TPU v7x, 256 devices: a whole 4x4x8 slice. The times are simulated.
256 devices in a mesh: seq: 64 (over y, z, core), tp: 4 (over x).
Axes of the slice: x: 4, y: 4, z: 8, core: 2. Of those that a mesh axis runs over, the one named last changes fastest.
Arguments:
- tier_source_concatenated: bfloat16 [8192, 2048], P('seq', 'tp'), may hold values from -6 to 6
- prompt_sizes_ordered: int32 [4], replicated, may hold values from 1 to 4096, 8192 in all
- tier_standardize_scale: float32 [2048], replicated, may hold values from 0.1 to 1.9
- tier_standardize_offset: float32 [2048], replicated, may hold values from -3 to 3
- previous_item_mixers: float32 [5, 2048], replicated, may hold values from 0 to 1
- mapping_matrices_pile: bfloat16 [4, 2048, 2048], P(None, None, 'tp'), may hold values from -0.125 to 0.125
- fading_narrow_left: bfloat16 [2048, 64], replicated, may hold values from -0.125 to 0.125
- fading_narrow_right: bfloat16 [64, 2048], P(None, 'tp'), may hold values from -0.75 to 0.75
- feature_fading_baseline: float32 [2048], P('tp'), may hold values from 5e-05 to 0.04
- diagonal_boost_coefficient: float32 [2048], P('tp'), may hold values from -4 to 4
- cluster_standardize_scale: float32 [2048], P('tp'), may hold values from 0.1 to 1.9
- cluster_standardize_offset: float32 [2048], P('tp'), may hold values from -3 to 3
- emitted_mapping_matrix: bfloat16 [2048, 2048], P('tp'), may hold values from -0.125 to 0.125
Outputs:
- hidden_out: bfloat16 [8192, 2048], P('seq', 'tp')
Inputs may be any that keep to these rules, and one draw needn't show every extreme that they name: `prompt_sizes_ordered`: the prompt lengths sum to 8192, and the longest is exactly 4096.
All inputs are finite; a program needn't handle non-finite values.
Results may differ from a plain program's by a relative error of at most 0.025.
Values may be sent and summed in bfloat16 or wider, within the bound.
No kernel may reach another device: no remote copies, remote signals or barrier semaphores. Data moves between devices by JAX's collectives and lax.ppermute only.
A program may use at most 128 MiB of HBM per device.

v0:
```python
import jax
import jax.numpy as jnp
from jax import lax
from jax.sharding import PartitionSpec as P

CHANNELS_ONE_HEAD = 64


highest = lax.Precision.HIGHEST


def from_behind(block, axis, distance):
    devices = range(lax.axis_size(axis))
    route = [(i - distance, i) for i in devices if i - distance in devices]
    return lax.ppermute(block, axis, route)


def layer_norm(rows, gain, bias, eps):
    mean = jnp.mean(rows, axis=-1, keepdims=True)
    centred = rows - mean
    spread = jnp.mean(centred * centred, axis=-1, keepdims=True)
    return centred * lax.rsqrt(spread + eps) * gain + bias


def body(
    tier_source_concatenated,
    prompt_sizes_ordered,
    tier_standardize_scale,
    tier_standardize_offset,
    previous_item_mixers,
    mapping_matrices_pile,
    fading_narrow_left,
    fading_narrow_right,
    feature_fading_baseline,
    diagonal_boost_coefficient,
    cluster_standardize_scale,
    cluster_standardize_offset,
    emitted_mapping_matrix,
):
    rows = tier_source_concatenated.shape[0]
    local_width = mapping_matrices_pile.shape[2]
    mixing_values_divided = local_width // CHANNELS_ONE_HEAD
    block = min(32, rows)
    blocks = rows // block
    full = lax.all_gather(tier_source_concatenated, "tp", axis=1, tiled=True)
    normed = layer_norm(
        full.astype(jnp.float32), tier_standardize_scale, tier_standardize_offset, 1e-05
    ).astype(jnp.bfloat16)
    first = jnp.cumsum(prompt_sizes_ordered) - prompt_sizes_ordered
    position = lax.axis_index("seq") * rows + jnp.arange(rows, dtype=jnp.int32)
    is_start = jnp.any(position[:, None] == first[None, :], axis=1)
    segment = jnp.sum((first[None, :] <= position[:, None]).astype(jnp.int32), axis=1)
    edge = from_behind(normed[rows - 1 :], "seq", 1)
    previous = jnp.concatenate([edge, normed[: rows - 1]], axis=0)
    previous = jnp.where(is_start[:, None], jnp.zeros_like(previous), previous)
    base = normed.astype(jnp.float32)
    delta = previous.astype(jnp.float32) - base
    shifted_blend = (base[None] + delta[None] * previous_item_mixers[:, None, :]).astype(
        jnp.bfloat16
    )
    projected = jnp.einsum(
        "itd,ide->ite", shifted_blend[:4], mapping_matrices_pile, preferred_element_type=jnp.float32
    )
    recept = projected[0].astype(jnp.bfloat16)
    key_rows = projected[1].astype(jnp.bfloat16)
    value_rows = projected[2].astype(jnp.bfloat16)
    gate = jax.nn.silu(projected[3]).astype(jnp.bfloat16)
    lowrank_decay_delta = jnp.tanh(
        jnp.dot(shifted_blend[4], fading_narrow_left, preferred_element_type=jnp.float32)
    ).astype(jnp.bfloat16)
    decay_logarithm = -feature_fading_baseline[None, :] * jnp.exp(
        jnp.dot(lowrank_decay_delta, fading_narrow_right, preferred_element_type=jnp.float32)
    )

    def split_heads(values):
        return (
            values.astype(jnp.float32)
            .reshape(blocks, block, mixing_values_divided, CHANNELS_ONE_HEAD)
            .transpose(0, 2, 1, 3)
        )

    inputs = (
        split_heads(recept),
        split_heads(key_rows),
        split_heads(value_rows),
        split_heads(decay_logarithm),
        segment.reshape(blocks, block),
        is_start.astype(jnp.float32).reshape(blocks, block),
    )
    order = jnp.arange(block)
    lower_incl = (order[None, :] <= order[:, None]).astype(jnp.float32)
    strictly = order[None, :] < order[:, None]
    diagonal_extra_contribution = diagonal_boost_coefficient.reshape(
        mixing_values_divided, CHANNELS_ONE_HEAD
    )

    def block_step(carry, item):
        running_recurrence_array, offset, alive = carry
        gating_rows_tile, query_array_tile, content_slab, lw_b, seg_b, start_b = item
        incl = jnp.einsum("ts,hsc->htc", lower_incl, lw_b, precision=highest)
        excl = incl - lw_b
        pair_ok = strictly & (seg_b[None, :] == seg_b[:, None])
        gap = jnp.minimum(excl[:, :, None, :] - incl[:, None, :, :], 0.0)
        weight = jnp.where(pair_ok[None, :, :, None], jnp.exp(gap), 0.0)
        scores = jnp.einsum(
            "htc,hsc,htsc->hts", gating_rows_tile, query_array_tile, weight, precision=highest
        )
        present_item_reward = jnp.sum(
            gating_rows_tile * diagonal_extra_contribution[:, None, :] * query_array_tile, axis=-1
        )
        seen = jnp.dot(lower_incl, start_b, precision=highest)
        valid = (seen == 0.0).astype(jnp.float32)
        carried = gating_rows_tile * jnp.exp(excl) * valid[None, :, None]
        level_ultimate_outcome = (
            jnp.einsum("hts,hsv->htv", scores, content_slab, precision=highest)
            + present_item_reward[..., None] * content_slab
        )
        level_ultimate_outcome = level_ultimate_outcome + jnp.einsum(
            "htc,hcv->htv", carried, running_recurrence_array, precision=highest
        )
        from_start = carried * alive * jnp.exp(offset)[:, None, :]
        total = incl[:, block - 1, :]
        keep = (seen[block - 1] == 0.0).astype(jnp.float32)
        tail_ok = (seg_b == seg_b[block - 1]).astype(jnp.float32)
        tail = query_array_tile * jnp.exp(total[:, None, :] - incl) * tail_ok[None, :, None]
        running_recurrence_array = keep * jnp.exp(total)[
            :, :, None
        ] * running_recurrence_array + jnp.einsum(
            "hsc,hsv->hcv", tail, content_slab, precision=highest
        )
        return (
            (running_recurrence_array, offset + total, alive * keep),
            (level_ultimate_outcome, from_start),
        )

    init = (
        jnp.zeros((mixing_values_divided, CHANNELS_ONE_HEAD, CHANNELS_ONE_HEAD), jnp.float32),
        jnp.zeros((mixing_values_divided, CHANNELS_ONE_HEAD), jnp.float32),
        jnp.float32(1.0),
    )
    (end_state, offset, alive), (outs, from_start) = lax.scan(block_step, init, inputs)
    decay_total = alive * jnp.exp(offset)

    def relay_turn(turn, entering):
        leaving = decay_total[..., None] * entering + end_state
        return from_behind(leaving, "seq", 1)

    incoming = lax.fori_loop(0, lax.axis_size("seq") - 1, relay_turn, jnp.zeros_like(end_state))
    outs = outs + jnp.einsum("bhtc,hcv->bhtv", from_start, incoming, precision=highest)
    wkv = outs.transpose(0, 2, 1, 3).reshape(rows, mixing_values_divided, CHANNELS_ONE_HEAD)
    mean = jnp.mean(wkv, axis=-1, keepdims=True)
    centred = wkv - mean
    spread = jnp.mean(centred * centred, axis=-1, keepdims=True)
    grouped = (centred * lax.rsqrt(spread + 0.00064)).reshape(
        rows, local_width
    ) * cluster_standardize_scale + cluster_standardize_offset
    gated = (grouped * gate.astype(jnp.float32)).astype(jnp.bfloat16)
    partial_sum = jnp.dot(gated, emitted_mapping_matrix, preferred_element_type=jnp.float32)
    summed = lax.psum(partial_sum.astype(jnp.bfloat16), "tp").astype(jnp.float32)
    mine = lax.dynamic_slice_in_dim(summed, lax.axis_index("tp") * local_width, local_width, 1)
    return (tier_source_concatenated.astype(jnp.float32) + mine).astype(jnp.bfloat16)


def solution(mesh):
    in_specs = (
        P("seq", "tp"),
        P(),
        P(),
        P(),
        P(),
        P(None, None, "tp"),
        P(),
        P(None, "tp"),
        P("tp"),
        P("tp"),
        P("tp"),
        P("tp"),
        P("tp", None),
    )
    out_specs = P("seq", "tp")
    return jax.shard_map(body, mesh=mesh, in_specs=in_specs, out_specs=out_specs, check_vma=False)
```

profile of v0, /device:TPU:48, one launch (start us, length us, event | category | flops | bytes accessed | tf_op | source)
XLA Modules:
  0.0 798.6 jit_solution(16465226275542968937)
XLA Ops:
  6.5 13.5 %all_gather.3 = bf16[128,2048]{1,0:T(8,128)(2,1)S(1)} all-gather(bf16[128,512]{1,0:T(8,128)(2,1)} %param.17), channel_id=1, replica_groups=mesh['seq'=64,'tp'=4] {'tp'}, dimensions={1}, use_global_device_ids=true | all-gather | bytes 655360 | tf_op jit(solution)/shard_map/all_gather | solution.py:45
  47.8 64.4 %while.31 = (s32[]{:T(128)}, f32[8,64,64]{2,1,0:T(8,128)S(1)}, f32[8,64]{1,0:T(8,128)S(1)}, f32[]{:T(128)}, f32[4,8,32,64]{3,2,0,1:T(8,128)}, /*index=5*/f32[4,8...) while((s32[]{:T(128)}, f32[8,64,64]{2,1,0:T(8,128)S(1)}, ...), condition=%wide.region_7.8_spmd.clone.clone, body=%wide.region_5.7_spmd.clone.clone.sunk | while | flops 41284548 | bytes 7640688 | solution.py:141
  112.3 617.8 %while.30 = (s32[]{:T(128)}, f32[8,64,64]{2,1,0:T(8,128)S(1)}, f32[8,64]{1,0:T(8,128)S(1)}, f32[8,64,64]{2,1,0:T(8,128)S(1)}, s32[]{:T(128)}) while((s32[]{:T(128)}, f32[8,64,64]{2,1,0:T(8,128)S(1)}, f32[8,64]{1,0:T(8,128)S(1)}, f32[8,64,64]{2,1,0:T(8,128)S(1)}, s32[]{:T(128)}) %tuple.61), condition=%wide.region_9.10_spmd, body=%wide.region_8.9_spmd.sunk | while | flops 65538 | bytes 919653 | solution.py:148
  145.8 7.9 collective-permute-done
  155.8 7.9 collective-permute-done
  165.7 7.9 collective-permute-done
  175.7 7.9 collective-permute-done
  185.6 7.9 collective-permute-done
  195.5 7.9 collective-permute-done
  205.5 7.9 collective-permute-done
  215.4 7.9 collective-permute-done
  225.3 7.9 collective-permute-done
  235.3 7.9 collective-permute-done
  245.2 7.9 collective-permute-done
  255.2 7.9 collective-permute-done
  265.1 7.9 collective-permute-done
  275.0 7.9 collective-permute-done
  285.0 7.9 collective-permute-done
  294.9 7.9 collective-permute-done
  304.8 7.9 collective-permute-done
  314.8 7.9 collective-permute-done
  424.1 7.9 collective-permute-done
  612.9 7.9 collective-permute-done
  735.6 54.6 %all-reduce.2.cloned.1.call-done = bf16[128,2048]{1,0:T(8,128)(2,1)} async-done(((bf16[128,2048]{1,0:T(8,128)(2,1)}), bf16[128,2048]{1,0:T(8,128)(2,1)}) %all-reduce.2.cloned.1.call-update) | async-done | bytes 524304 | tf_op jit(solution)/shard_map/psum | solution.py:159
  (313 shorter events, 555.6 us)
Async XLA Ops:
  6.5 783.6 %all-reduce.2.cloned.1.call-start = ((), (), s32[]{:S(2)}) async-start(), calls=%async_computation | async-start | bytes 1048576 | tf_op jit(solution)/shard_map/psum | solution.py:159
  143.9 9.8 %collective-permute-start = (f32[8,64,64]{2,1,0:T(8,128)S(1)}, f32[8,64,64]{2,1,0:T(8,128)S(1)}, u32[]{:S(2)}, u32[]{:S(2)}) collective-permute-start(f32[8,64,64]{2,1,0:T(8,128)S(1)} %multiply_add_fusion.2), channel_id=1, source_target_pairs={{0,4},{4,8},{8,12},{12,16},{16,20},{20,24},{24,28},{28,32},{32,36}... | collective-permute-start | bytes 393224 | tf_op jit(solution)/shard_map/while/body/eval_jaxpr/ppermute | solution.py:15
  153.9 9.8 %collective-permute-start = (f32[8,64,64]{2,1,0:T(8,128)S(1)}, f32[8,64,64]{2,1,0:T(8,128)S(1)}, u32[]{:S(2)}, u32[]{:S(2)}) collective-permute-start(f32[8,64,64]{2,1,0:T(8,128)S(1)} %multiply_add_fusion.2), channel_id=1, source_target_pairs={{0,4},{4,8},{8,12},{12,16},{16,20},{20,24},{24,28},{28,32},{32,36}... | collective-permute-start | bytes 393224 | tf_op jit(solution)/shard_map/while/body/eval_jaxpr/ppermute | solution.py:15
  163.8 9.8 %collective-permute-start = (f32[8,64,64]{2,1,0:T(8,128)S(1)}, f32[8,64,64]{2,1,0:T(8,128)S(1)}, u32[]{:S(2)}, u32[]{:S(2)}) collective-permute-start(f32[8,64,64]{2,1,0:T(8,128)S(1)} %multiply_add_fusion.2), channel_id=1, source_target_pairs={{0,4},{4,8},{8,12},{12,16},{16,20},{20,24},{24,28},{28,32},{32,36}... | collective-permute-start | bytes 393224 | tf_op jit(solution)/shard_map/while/body/eval_jaxpr/ppermute | solution.py:15
  173.7 9.8 %collective-permute-start = (f32[8,64,64]{2,1,0:T(8,128)S(1)}, f32[8,64,64]{2,1,0:T(8,128)S(1)}, u32[]{:S(2)}, u32[]{:S(2)}) collective-permute-start(f32[8,64,64]{2,1,0:T(8,128)S(1)} %multiply_add_fusion.2), channel_id=1, source_target_pairs={{0,4},{4,8},{8,12},{12,16},{16,20},{20,24},{24,28},{28,32},{32,36}... | collective-permute-start | bytes 393224 | tf_op jit(solution)/shard_map/while/body/eval_jaxpr/ppermute | solution.py:15
  183.7 9.8 %collective-permute-start = (f32[8,64,64]{2,1,0:T(8,128)S(1)}, f32[8,64,64]{2,1,0:T(8,128)S(1)}, u32[]{:S(2)}, u32[]{:S(2)}) collective-permute-start(f32[8,64,64]{2,1,0:T(8,128)S(1)} %multiply_add_fusion.2), channel_id=1, source_target_pairs={{0,4},{4,8},{8,12},{12,16},{16,20},{20,24},{24,28},{28,32},{32,36}... | collective-permute-start | bytes 393224 | tf_op jit(solution)/shard_map/while/body/eval_jaxpr/ppermute | solution.py:15
  193.6 9.8 %collective-permute-start = (f32[8,64,64]{2,1,0:T(8,128)S(1)}, f32[8,64,64]{2,1,0:T(8,128)S(1)}, u32[]{:S(2)}, u32[]{:S(2)}) collective-permute-start(f32[8,64,64]{2,1,0:T(8,128)S(1)} %multiply_add_fusion.2), channel_id=1, source_target_pairs={{0,4},{4,8},{8,12},{12,16},{16,20},{20,24},{24,28},{28,32},{32,36}... | collective-permute-start | bytes 393224 | tf_op jit(solution)/shard_map/while/body/eval_jaxpr/ppermute | solution.py:15
  213.5 9.8 %collective-permute-start = (f32[8,64,64]{2,1,0:T(8,128)S(1)}, f32[8,64,64]{2,1,0:T(8,128)S(1)}, u32[]{:S(2)}, u32[]{:S(2)}) collective-permute-start(f32[8,64,64]{2,1,0:T(8,128)S(1)} %multiply_add_fusion.2), channel_id=1, source_target_pairs={{0,4},{4,8},{8,12},{12,16},{16,20},{20,24},{24,28},{28,32},{32,36}... | collective-permute-start | bytes 393224 | tf_op jit(solution)/shard_map/while/body/eval_jaxpr/ppermute | solution.py:15
  233.4 9.8 %collective-permute-start = (f32[8,64,64]{2,1,0:T(8,128)S(1)}, f32[8,64,64]{2,1,0:T(8,128)S(1)}, u32[]{:S(2)}, u32[]{:S(2)}) collective-permute-start(f32[8,64,64]{2,1,0:T(8,128)S(1)} %multiply_add_fusion.2), channel_id=1, source_target_pairs={{0,4},{4,8},{8,12},{12,16},{16,20},{20,24},{24,28},{28,32},{32,36}... | collective-permute-start | bytes 393224 | tf_op jit(solution)/shard_map/while/body/eval_jaxpr/ppermute | solution.py:15
  263.2 9.8 %collective-permute-start = (f32[8,64,64]{2,1,0:T(8,128)S(1)}, f32[8,64,64]{2,1,0:T(8,128)S(1)}, u32[]{:S(2)}, u32[]{:S(2)}) collective-permute-start(f32[8,64,64]{2,1,0:T(8,128)S(1)} %multiply_add_fusion.2), channel_id=1, source_target_pairs={{0,4},{4,8},{8,12},{12,16},{16,20},{20,24},{24,28},{28,32},{32,36}... | collective-permute-start | bytes 393224 | tf_op jit(solution)/shard_map/while/body/eval_jaxpr/ppermute | solution.py:15
  283.0 9.8 %collective-permute-start = (f32[8,64,64]{2,1,0:T(8,128)S(1)}, f32[8,64,64]{2,1,0:T(8,128)S(1)}, u32[]{:S(2)}, u32[]{:S(2)}) collective-permute-start(f32[8,64,64]{2,1,0:T(8,128)S(1)} %multiply_add_fusion.2), channel_id=1, source_target_pairs={{0,4},{4,8},{8,12},{12,16},{16,20},{20,24},{24,28},{28,32},{32,36}... | collective-permute-start | bytes 393224 | tf_op jit(solution)/shard_map/while/body/eval_jaxpr/ppermute | solution.py:15
  332.7 9.8 %collective-permute-start = (f32[8,64,64]{2,1,0:T(8,128)S(1)}, f32[8,64,64]{2,1,0:T(8,128)S(1)}, u32[]{:S(2)}, u32[]{:S(2)}) collective-permute-start(f32[8,64,64]{2,1,0:T(8,128)S(1)} %multiply_add_fusion.2), channel_id=1, source_target_pairs={{0,4},{4,8},{8,12},{12,16},{16,20},{20,24},{24,28},{28,32},{32,36}... | collective-permute-start | bytes 393224 | tf_op jit(solution)/shard_map/while/body/eval_jaxpr/ppermute | solution.py:15
  352.6 9.8 %collective-permute-start = (f32[8,64,64]{2,1,0:T(8,128)S(1)}, f32[8,64,64]{2,1,0:T(8,128)S(1)}, u32[]{:S(2)}, u32[]{:S(2)}) collective-permute-start(f32[8,64,64]{2,1,0:T(8,128)S(1)} %multiply_add_fusion.2), channel_id=1, source_target_pairs={{0,4},{4,8},{8,12},{12,16},{16,20},{20,24},{24,28},{28,32},{32,36}... | collective-permute-start | bytes 393224 | tf_op jit(solution)/shard_map/while/body/eval_jaxpr/ppermute | solution.py:15
  402.3 9.8 %collective-permute-start = (f32[8,64,64]{2,1,0:T(8,128)S(1)}, f32[8,64,64]{2,1,0:T(8,128)S(1)}, u32[]{:S(2)}, u32[]{:S(2)}) collective-permute-start(f32[8,64,64]{2,1,0:T(8,128)S(1)} %multiply_add_fusion.2), channel_id=1, source_target_pairs={{0,4},{4,8},{8,12},{12,16},{16,20},{20,24},{24,28},{28,32},{32,36}... | collective-permute-start | bytes 393224 | tf_op jit(solution)/shard_map/while/body/eval_jaxpr/ppermute | solution.py:15
  422.2 9.8 %collective-permute-start = (f32[8,64,64]{2,1,0:T(8,128)S(1)}, f32[8,64,64]{2,1,0:T(8,128)S(1)}, u32[]{:S(2)}, u32[]{:S(2)}) collective-permute-start(f32[8,64,64]{2,1,0:T(8,128)S(1)} %multiply_add_fusion.2), channel_id=1, source_target_pairs={{0,4},{4,8},{8,12},{12,16},{16,20},{20,24},{24,28},{28,32},{32,36}... | collective-permute-start | bytes 393224 | tf_op jit(solution)/shard_map/while/body/eval_jaxpr/ppermute | solution.py:15
  452.0 9.8 %collective-permute-start = (f32[8,64,64]{2,1,0:T(8,128)S(1)}, f32[8,64,64]{2,1,0:T(8,128)S(1)}, u32[]{:S(2)}, u32[]{:S(2)}) collective-permute-start(f32[8,64,64]{2,1,0:T(8,128)S(1)} %multiply_add_fusion.2), channel_id=1, source_target_pairs={{0,4},{4,8},{8,12},{12,16},{16,20},{20,24},{24,28},{28,32},{32,36}... | collective-permute-start | bytes 393224 | tf_op jit(solution)/shard_map/while/body/eval_jaxpr/ppermute | solution.py:15
  471.9 9.8 %collective-permute-start = (f32[8,64,64]{2,1,0:T(8,128)S(1)}, f32[8,64,64]{2,1,0:T(8,128)S(1)}, u32[]{:S(2)}, u32[]{:S(2)}) collective-permute-start(f32[8,64,64]{2,1,0:T(8,128)S(1)} %multiply_add_fusion.2), channel_id=1, source_target_pairs={{0,4},{4,8},{8,12},{12,16},{16,20},{20,24},{24,28},{28,32},{32,36}... | collective-permute-start | bytes 393224 | tf_op jit(solution)/shard_map/while/body/eval_jaxpr/ppermute | solution.py:15
  521.5 9.8 %collective-permute-start = (f32[8,64,64]{2,1,0:T(8,128)S(1)}, f32[8,64,64]{2,1,0:T(8,128)S(1)}, u32[]{:S(2)}, u32[]{:S(2)}) collective-permute-start(f32[8,64,64]{2,1,0:T(8,128)S(1)} %multiply_add_fusion.2), channel_id=1, source_target_pairs={{0,4},{4,8},{8,12},{12,16},{16,20},{20,24},{24,28},{28,32},{32,36}... | collective-permute-start | bytes 393224 | tf_op jit(solution)/shard_map/while/body/eval_jaxpr/ppermute | solution.py:15
  541.4 9.8 %collective-permute-start = (f32[8,64,64]{2,1,0:T(8,128)S(1)}, f32[8,64,64]{2,1,0:T(8,128)S(1)}, u32[]{:S(2)}, u32[]{:S(2)}) collective-permute-start(f32[8,64,64]{2,1,0:T(8,128)S(1)} %multiply_add_fusion.2), channel_id=1, source_target_pairs={{0,4},{4,8},{8,12},{12,16},{16,20},{20,24},{24,28},{28,32},{32,36}... | collective-permute-start | bytes 393224 | tf_op jit(solution)/shard_map/while/body/eval_jaxpr/ppermute | solution.py:15
  591.1 9.8 %collective-permute-start = (f32[8,64,64]{2,1,0:T(8,128)S(1)}, f32[8,64,64]{2,1,0:T(8,128)S(1)}, u32[]{:S(2)}, u32[]{:S(2)}) collective-permute-start(f32[8,64,64]{2,1,0:T(8,128)S(1)} %multiply_add_fusion.2), channel_id=1, source_target_pairs={{0,4},{4,8},{8,12},{12,16},{16,20},{20,24},{24,28},{28,32},{32,36}... | collective-permute-start | bytes 393224 | tf_op jit(solution)/shard_map/while/body/eval_jaxpr/ppermute | solution.py:15
  611.0 9.8 %collective-permute-start = (f32[8,64,64]{2,1,0:T(8,128)S(1)}, f32[8,64,64]{2,1,0:T(8,128)S(1)}, u32[]{:S(2)}, u32[]{:S(2)}) collective-permute-start(f32[8,64,64]{2,1,0:T(8,128)S(1)} %multiply_add_fusion.2), channel_id=1, source_target_pairs={{0,4},{4,8},{8,12},{12,16},{16,20},{20,24},{24,28},{28,32},{32,36}... | collective-permute-start | bytes 393224 | tf_op jit(solution)/shard_map/while/body/eval_jaxpr/ppermute | solution.py:15
  640.8 9.8 %collective-permute-start = (f32[8,64,64]{2,1,0:T(8,128)S(1)}, f32[8,64,64]{2,1,0:T(8,128)S(1)}, u32[]{:S(2)}, u32[]{:S(2)}) collective-permute-start(f32[8,64,64]{2,1,0:T(8,128)S(1)} %multiply_add_fusion.2), channel_id=1, source_target_pairs={{0,4},{4,8},{8,12},{12,16},{16,20},{20,24},{24,28},{28,32},{32,36}... | collective-permute-start | bytes 393224 | tf_op jit(solution)/shard_map/while/body/eval_jaxpr/ppermute | solution.py:15
  660.7 9.8 %collective-permute-start = (f32[8,64,64]{2,1,0:T(8,128)S(1)}, f32[8,64,64]{2,1,0:T(8,128)S(1)}, u32[]{:S(2)}, u32[]{:S(2)}) collective-permute-start(f32[8,64,64]{2,1,0:T(8,128)S(1)} %multiply_add_fusion.2), channel_id=1, source_target_pairs={{0,4},{4,8},{8,12},{12,16},{16,20},{20,24},{24,28},{28,32},{32,36}... | collective-permute-start | bytes 393224 | tf_op jit(solution)/shard_map/while/body/eval_jaxpr/ppermute | solution.py:15
  710.3 9.8 %collective-permute-start = (f32[8,64,64]{2,1,0:T(8,128)S(1)}, f32[8,64,64]{2,1,0:T(8,128)S(1)}, u32[]{:S(2)}, u32[]{:S(2)}) collective-permute-start(f32[8,64,64]{2,1,0:T(8,128)S(1)} %multiply_add_fusion.2), channel_id=1, source_target_pairs={{0,4},{4,8},{8,12},{12,16},{16,20},{20,24},{24,28},{28,32},{32,36}... | collective-permute-start | bytes 393224 | tf_op jit(solution)/shard_map/while/body/eval_jaxpr/ppermute | solution.py:15
  (50 other events, 3078.7 us)
Sparse Core Ops, SparseCore 0:
  735.7 54.4 all-reduce.1
where the time goes:
time: 802 us; the launch traced here: 799 us
  waiting for transfers between devices  541 us (67%)
  starting transfers between devices  125 us (16%)
  other arithmetic  50.5 us (6%)
  matrix products  32.7 us (4%)
  local copies, waits for them, and re-layouts  18.9 us (2%)
  between operations  13.6 us (2%)
  blocking collectives  13.5 us (2%)
    ppermute x64, waiting for transfers between devices, from_behind(): return lax.ppermute(block, axis, route)  486 us
    ppermute x64, starting transfers between devices, from_behind(): return lax.ppermute(block, axis, route)  125 us
    psum x1, waiting for transfers between devices, body(): lax.psum(partial_sum.astype(jnp.bfloat16), 'tp').astype(jnp.float32)  54.6 us
  transfers between devices with their start and end apart: 65, of which 65 were waited for; matrix products, arithmetic and copies ran while one was open for 0% of the time, Pallas kernels for 0%

commit v1 on v0

--- a/solution.py
+++ b/solution.py
@@ -141,11 +141,21 @@
     (end_state, offset, alive), (outs, from_start) = lax.scan(block_step, init, inputs)
     decay_total = alive * jnp.exp(offset)
 
-    def relay_turn(turn, entering):
-        leaving = decay_total[..., None] * entering + end_state
-        return from_behind(leaving, "seq", 1)
+    devices = lax.axis_size("seq")
+    packed = jnp.concatenate([end_state, decay_total[:, None, :]], axis=1)
 
-    incoming = lax.fori_loop(0, lax.axis_size("seq") - 1, relay_turn, jnp.zeros_like(end_state))
+    def combine(received, own):
+        own_state, own_decay = own[:, :CHANNELS_ONE_HEAD], own[:, CHANNELS_ONE_HEAD:]
+        got_state, got_decay = received[:, :CHANNELS_ONE_HEAD], received[:, CHANNELS_ONE_HEAD:]
+        state = jnp.transpose(own_decay, (0, 2, 1)) * got_state + own_state
+        return jnp.concatenate([state, own_decay * got_decay], axis=1)
+
+    prefix = from_behind(packed, "seq", 1)
+    distance = 1
+    while distance < devices:
+        prefix = combine(from_behind(prefix, "seq", distance), prefix)
+        distance *= 2
+    incoming = prefix[:, :CHANNELS_ONE_HEAD]
     outs = outs + jnp.einsum("bhtc,hcv->bhtv", from_start, incoming, precision=highest)
     wkv = outs.transpose(0, 2, 1, 3).reshape(rows, mixing_values_divided, CHANNELS_ONE_HEAD)
     mean = jnp.mean(wkv, axis=-1, keepdims=True)

time: 802 us -> 264 us (0.33)
  waiting for transfers between devices: 541 us -> 106 us
  starting transfers between devices: 125 us -> 32.3 us
    ppermute x64 -> x8, waiting for transfers between devices: 486 us -> 55.1 us  [from_behind(): return lax.ppermute(block, axis, route)]
    ppermute x64 -> x8, starting transfers between devices: 125 us -> 32.3 us  [from_behind(): return lax.ppermute(block, axis, route)]
  transfers between devices with their start and end apart: 65 -> 9, of which waited for: 65 -> 9; matrix products, arithmetic and copies ran while one was open for 0% -> 1% of each run, Pallas kernels for 0% -> 0%
where the time goes in v1:
time: 264 us; the launch traced here: 262 us
  waiting for transfers between devices  106 us (40%)
  other arithmetic  43.2 us (16%)
  starting transfers between devices  32.3 us (12%)
  matrix products  31.7 us (12%)
  local copies, waits for them, and re-layouts  18.9 us (7%)
  between operations  13.7 us (5%)
  blocking collectives  13.5 us (5%)
  loops' own time  3.16 us (1%)
    ppermute x8, waiting for transfers between devices, from_behind(): return lax.ppermute(block, axis, route)  55.1 us
    psum x1, waiting for transfers between devices, body(): lax.psum(partial_sum.astype(jnp.bfloat16), 'tp').astype(jnp.float32)  50.7 us
    ppermute x8, starting transfers between devices, from_behind(): return lax.ppermute(block, axis, route)  32.3 us
    dot_general x4, other arithmetic, block_step(): jnp.einsum('htc,hsc,htsc->hts', gating_rows_tile, query_array_tile, weigh...  13.8 us
    all_gather x1, blocking collectives, body(): full = lax.all_gather(tier_source_concatenated, 'tp', axis=1, tiled=True)  13.5 us
    transpose x5, local copies, waits for them, and re-layouts, split_heads(): return values.astype(jnp.float32).reshape(blocks, block, mixing_values_di...  7.39 us
    dynamic_update_slice x4, other arithmetic, body(): lax.scan(block_step, init, inputs)  6.66 us
    dot_general x4, matrix products, block_step(): jnp.einsum('hsc,hsv->hcv', tail, content_slab, precision=highest)  6.64 us
  transfers between devices with their start and end apart: 9, of which 9 were waited for; matrix products, arithmetic and copies ran while one was open for 1% of the time, Pallas kernels for 0%

profile of v1, /device:TPU:48, one launch (start us, length us, event | category | flops | bytes accessed | tf_op | source)
XLA Modules:
  0.0 262.3 jit_solution(8254443867008987985)
XLA Ops:
  6.5 13.5 %all_gather.3 = bf16[128,2048]{1,0:T(8,128)(2,1)S(1)} all-gather(bf16[128,512]{1,0:T(8,128)(2,1)} %param.15), channel_id=1, replica_groups=mesh['seq'=64,'tp'=4] {'tp'}, dimensions={1}, use_global_device_ids=true | all-gather | bytes 655360 | tf_op jit(solution)/shard_map/all_gather | solution.py:45
  20.5 2.1 fusion.65
  27.9 3.3 %add_convert_fusion = bf16[5,128,2048]{2,1,0:T(8,128)(2,1)} fusion(f32[5,2048]{1,0:T(8,128)S(1)} %copy-done.5, f32[128,2048]{1,0:T(8,128)S(1)} %convert_subtract_fusion.1, f32[128,2048]{1,0:T(8,128)} %get-tuple-element.202), kind=kLoop, calls=%fused_computation.59 | loop fusion | flops 3932160 | bytes 4759552 | tf_op jit(solution)/shard_map/convert_element_type | solution.py:58
  31.2 5.7 %fusion.67 = (bf16[4,128,512]{2,1,0:T(8,128)(2,1)S(1)}, f32[4,128,512]{2,1,0:T(8,128)}) fusion(bf16[4,2048,512]{2,1,0:T(8,128)(2,1)} %param.20, f32[5,2048]{1,0:T(8,128)S(1)} %copy-done.5, f32[128,2048]{1,0:T(8,128)S(1)} %convert_subtract_fusion.1, f32[128,2048]{1,0:T(8,128)S(1)} %copy-done.1), kind=kOutput, calls=%fused_computation.131 | convolution fusion | flops 1077936128 | bytes 12099584 | tf_op jit(solution)/shard_map/itd,ide->ite/dot_general | solution.py:61
  45.4 2.4 copy_bitcast_fusion.2
  47.7 65.0 %while.20 = (s32[]{:T(128)}, f32[8,64,64]{2,1,0:T(8,128)S(1)}, f32[8,64]{1,0:T(8,128)S(1)}, f32[]{:T(128)}, f32[4,8,32,64]{3,2,0,1:T(8,128)}, /*index=5*/f32[4,8...) while((s32[]{:T(128)}, f32[8,64,64]{2,1,0:T(8,128)S(1)}, ...), condition=%wide.region_7.8_spmd.clone.clone, body=%wide.region_5.7_spmd.clone.clone.sunk | while | flops 41284548 | bytes 7640688 | solution.py:141
  53.9 3.4 %fusion.100 = f32[8,32,32]{1,2,0:T(8,128)S(1)} fusion(f32[8,32,32,64]{3,2,1,0:T(8,128)S(1)} %exponential_select_fusion.2, f32[8,64,32]{1,2,0:T(8,128)S(1)} %get-tuple-element.318, f32[8,64,32]{1,2,0:T(8,128)S(1)} %get-tuple-element.319), kind=kLoop, calls=%fused_computation.4.clone.1 | loop fusion | flops 1564672 | bytes 2260992 | tf_op jit(solution)/shard_map/while/body/eval_jaxpr/htc,hsc,htsc->hts/dot_general | solution.py:105
  70.2 3.4 %fusion.100 = f32[8,32,32]{1,2,0:T(8,128)S(1)} fusion(f32[8,32,32,64]{3,2,1,0:T(8,128)S(1)} %exponential_select_fusion.2, f32[8,64,32]{1,2,0:T(8,128)S(1)} %get-tuple-element.318, f32[8,64,32]{1,2,0:T(8,128)S(1)} %get-tuple-element.319), kind=kLoop, calls=%fused_computation.4.clone.1 | loop fusion | flops 1564672 | bytes 2260992 | tf_op jit(solution)/shard_map/while/body/eval_jaxpr/htc,hsc,htsc->hts/dot_general | solution.py:105
  86.4 3.4 %fusion.100 = f32[8,32,32]{1,2,0:T(8,128)S(1)} fusion(f32[8,32,32,64]{3,2,1,0:T(8,128)S(1)} %exponential_select_fusion.2, f32[8,64,32]{1,2,0:T(8,128)S(1)} %get-tuple-element.318, f32[8,64,32]{1,2,0:T(8,128)S(1)} %get-tuple-element.319), kind=kLoop, calls=%fused_computation.4.clone.1 | loop fusion | flops 1564672 | bytes 2260992 | tf_op jit(solution)/shard_map/while/body/eval_jaxpr/htc,hsc,htsc->hts/dot_general | solution.py:105
  102.7 3.4 %fusion.100 = f32[8,32,32]{1,2,0:T(8,128)S(1)} fusion(f32[8,32,32,64]{3,2,1,0:T(8,128)S(1)} %exponential_select_fusion.2, f32[8,64,32]{1,2,0:T(8,128)S(1)} %get-tuple-element.318, f32[8,64,32]{1,2,0:T(8,128)S(1)} %get-tuple-element.319), kind=kLoop, calls=%fused_computation.4.clone.1 | loop fusion | flops 1564672 | bytes 2260992 | tf_op jit(solution)/shard_map/while/body/eval_jaxpr/htc,hsc,htsc->hts/dot_general | solution.py:105
  112.8 3.6 %collective-permute-start.1 = (f32[8,65,64]{2,1,0:T(8,128)S(1)}, f32[8,65,64]{2,1,0:T(8,128)S(1)}, u32[]{:S(2)}, u32[]{:S(2)}) collective-permute-start(f32[8,65,64]{2,1,0:T(8,128)S(1)} %pad_maximum_fusion), channel_id=1, source_target_pairs={{0,4},{4,8},{8,12},{12,16},{16,20},{20,24},{24,28},{28,32},{32,36}... | collective-permute-start | bytes 399368 | tf_op jit(solution)/shard_map/ppermute | solution.py:15
  116.4 4.6 %collective-permute-done.1 = f32[8,65,64]{2,1,0:T(8,128)S(1)} collective-permute-done((f32[8,65,64]{2,1,0:T(8,128)S(1)}, f32[8,65,64]{2,1,0:T(8,128)S(1)}, u32[]{:S(2)}, u32[]{:S(2)}) %collective-permute-start.1) | collective-permute-done | bytes 133152 | tf_op jit(solution)/shard_map/ppermute | solution.py:15
  122.8 6.1 %collective-permute-done.2 = f32[8,65,64]{2,1,0:T(8,128)S(1)} collective-permute-done((f32[8,65,64]{2,1,0:T(8,128)S(1)}, f32[8,65,64]{2,1,0:T(8,128)S(1)}, u32[]{:S(2)}, u32[]{:S(2)}) %collective-permute-start.2) | collective-permute-done | bytes 133152 | tf_op jit(solution)/shard_map/ppermute | solution.py:15
  129.1 3.8 %collective-permute-start.3 = (f32[8,65,64]{2,1,0:T(8,128)S(1)}, f32[8,65,64]{2,1,0:T(8,128)S(1)}, u32[]{:S(2)}, u32[]{:S(2)}) collective-permute-start(f32[8,65,64]{2,1,0:T(8,128)S(1)} %pad_maximum_fusion.1), channel_id=1, source_target_pairs={{0,8},{4,12},{8,16},{12,20},{16,24},{20,28},{24,32},{28,36},{32,40... | collective-permute-start | bytes 399368 | tf_op jit(solution)/shard_map/ppermute | solution.py:15
  133.0 9.2 %collective-permute-done.3 = f32[8,65,64]{2,1,0:T(8,128)S(1)} collective-permute-done((f32[8,65,64]{2,1,0:T(8,128)S(1)}, f32[8,65,64]{2,1,0:T(8,128)S(1)}, u32[]{:S(2)}, u32[]{:S(2)}) %collective-permute-start.3) | collective-permute-done | bytes 133152 | tf_op jit(solution)/shard_map/ppermute | solution.py:15
  142.4 5.0 %collective-permute-start.4 = (f32[8,65,64]{2,1,0:T(8,128)S(1)}, f32[8,65,64]{2,1,0:T(8,128)S(1)}, u32[]{:S(2)}, u32[]{:S(2)}) collective-permute-start(f32[8,65,64]{2,1,0:T(8,128)S(1)} %pad_maximum_fusion.2), channel_id=1, source_target_pairs={{0,16},{4,20},{8,24},{12,28},{16,32},{20,36},{24,40},{28,44},{32,4... | collective-permute-start | bytes 399368 | tf_op jit(solution)/shard_map/ppermute | solution.py:15
  147.4 11.5 %collective-permute-done.4 = f32[8,65,64]{2,1,0:T(8,128)S(1)} collective-permute-done((f32[8,65,64]{2,1,0:T(8,128)S(1)}, f32[8,65,64]{2,1,0:T(8,128)S(1)}, u32[]{:S(2)}, u32[]{:S(2)}) %collective-permute-start.4) | collective-permute-done | bytes 133152 | tf_op jit(solution)/shard_map/ppermute | solution.py:15
  159.1 5.1 %collective-permute-start.5 = (f32[8,65,64]{2,1,0:T(8,128)S(1)}, f32[8,65,64]{2,1,0:T(8,128)S(1)}, u32[]{:S(2)}, u32[]{:S(2)}) collective-permute-start(f32[8,65,64]{2,1,0:T(8,128)S(1)} %pad_maximum_fusion.3), channel_id=1, source_target_pairs={{0,32},{4,36},{8,40},{12,44},{16,48},{20,52},{24,56},{28,60},{32,6... | collective-permute-start | bytes 399368 | tf_op jit(solution)/shard_map/ppermute | solution.py:15
  164.2 9.7 %collective-permute-done.5 = f32[8,65,64]{2,1,0:T(8,128)S(1)} collective-permute-done((f32[8,65,64]{2,1,0:T(8,128)S(1)}, f32[8,65,64]{2,1,0:T(8,128)S(1)}, u32[]{:S(2)}, u32[]{:S(2)}) %collective-permute-start.5) | collective-permute-done | bytes 133152 | tf_op jit(solution)/shard_map/ppermute | solution.py:15
  174.1 9.6 %collective-permute-start.6 = (f32[8,65,64]{2,1,0:T(8,128)S(1)}, f32[8,65,64]{2,1,0:T(8,128)S(1)}, u32[]{:S(2)}, u32[]{:S(2)}) collective-permute-start(f32[8,65,64]{2,1,0:T(8,128)S(1)} %pad_maximum_fusion.4), channel_id=1, source_target_pairs={{0,64},{4,68},{8,72},{12,76},{16,80},{20,84},{24,88},{28,92},{32,9... | collective-permute-start | bytes 399368 | tf_op jit(solution)/shard_map/ppermute | solution.py:15
  183.7 4.7 %collective-permute-done.6 = f32[8,65,64]{2,1,0:T(8,128)S(1)} collective-permute-done((f32[8,65,64]{2,1,0:T(8,128)S(1)}, f32[8,65,64]{2,1,0:T(8,128)S(1)}, u32[]{:S(2)}, u32[]{:S(2)}) %collective-permute-start.6) | collective-permute-done | bytes 133152 | tf_op jit(solution)/shard_map/ppermute | solution.py:15
  189.9 8.8 %collective-permute-done.7 = f32[8,65,64]{2,1,0:T(8,128)S(1)} collective-permute-done((f32[8,65,64]{2,1,0:T(8,128)S(1)}, f32[8,65,64]{2,1,0:T(8,128)S(1)}, u32[]{:S(2)}, u32[]{:S(2)}) %collective-permute-start.7) | collective-permute-done | bytes 133152 | tf_op jit(solution)/shard_map/ppermute | solution.py:15
  200.9 2.2 convolution_convert_fusion
  203.2 50.7 %all-reduce.2.cloned.1.call-done = bf16[128,2048]{1,0:T(8,128)(2,1)} async-done(((bf16[128,2048]{1,0:T(8,128)(2,1)}), bf16[128,2048]{1,0:T(8,128)(2,1)}) %all-reduce.2.cloned.1.call-update) | async-done | bytes 524304 | tf_op jit(solution)/shard_map/psum | solution.py:169
  (154 shorter events, 70.0 us)
Async XLA Ops:
  6.5 194.4 %copy-start = (bf16[512,2048]{1,0:T(8,128)(2,1)S(1)}, bf16[512,2048]{1,0:T(8,128)(2,1)}, u32[]{:S(2)}) copy-start(bf16[512,2048]{1,0:T(8,128)(2,1)} %param.27) | copy-start | bytes 6291460
  6.5 21.3 %copy-start.5 = (f32[5,2048]{1,0:T(8,128)S(1)}, f32[5,2048]{1,0:T(8,128)}, u32[]{:S(2)}) copy-start(f32[5,2048]{1,0:T(8,128)} %param.19) | copy-start | bytes 122884
  6.5 247.3 %all-reduce.2.cloned.1.call-start = ((), (), s32[]{:S(2)}) async-start(), calls=%async_computation | async-start | bytes 1048576 | tf_op jit(solution)/shard_map/psum | solution.py:169
  22.6 5.0 %collective-permute-start = (bf16[1,2048]{1,0:T(2,128)(2,1)S(1)}, bf16[1,2048]{1,0:T(2,128)(2,1)S(1)}, u32[]{:S(2)}, u32[]{:S(2)}) collective-permute-start(bf16[1,2048]{1,0:T(2,128)(2,1)S(1)} %slice.104), channel_id=1, source_target_pairs={{0,4},{4,8},{8,12},{12,16},{16,20},{20,24},{24,28},{28,32},{32,36}... | collective-permute-start | bytes 12296 | tf_op jit(solution)/shard_map/ppermute | solution.py:15
  27.1 4.1 %copy-start.1 = (f32[128,2048]{1,0:T(8,128)S(1)}, f32[128,2048]{1,0:T(8,128)}, u32[]{:S(2)}) copy-start(f32[128,2048]{1,0:T(8,128)} %get-tuple-element.202) | copy-start | bytes 3145732
  31.2 9.5 %copy-start.6 = (bf16[64,512]{1,0:T(8,128)(2,1)S(1)}, bf16[64,512]{1,0:T(8,128)(2,1)}, u32[]{:S(2)}) copy-start(bf16[64,512]{1,0:T(8,128)(2,1)} %param.22) | copy-start | bytes 196612
  37.7 10.0 %copy-start.7 = (f32[512]{0:T(512)S(1)}, f32[512]{0:T(512)}, u32[]{:S(2)}) copy-start(f32[512]{0:T(512)} %param.24) | copy-start | bytes 6148
  112.7 86.0 %copy-start.3 = (f32[4,8,32,64]{3,2,0,1:T(8,128)S(1)}, f32[4,8,32,64]{3,2,0,1:T(8,128)}, u32[]{:S(2)}) copy-start(f32[4,8,32,64]{3,2,0,1:T(8,128)} %get-tuple-element.89) | copy-start | bytes 786436
  112.7 86.0 %copy-start.4 = (f32[4,8,32,64]{3,2,0,1:T(8,128)S(1)}, f32[4,8,32,64]{3,2,0,1:T(8,128)}, u32[]{:S(2)}) copy-start(f32[4,8,32,64]{3,2,0,1:T(8,128)} %get-tuple-element.93) | copy-start | bytes 786436
  112.8 8.2 %collective-permute-start.1 = (f32[8,65,64]{2,1,0:T(8,128)S(1)}, f32[8,65,64]{2,1,0:T(8,128)S(1)}, u32[]{:S(2)}, u32[]{:S(2)}) collective-permute-start(f32[8,65,64]{2,1,0:T(8,128)S(1)} %pad_maximum_fusion), channel_id=1, source_target_pairs={{0,4},{4,8},{8,12},{12,16},{16,20},{20,24},{24,28},{28,32},{32,36}... | collective-permute-start | bytes 399368 | tf_op jit(solution)/shard_map/ppermute | solution.py:15
  120.9 8.0 %collective-permute-start.2 = (f32[8,65,64]{2,1,0:T(8,128)S(1)}, f32[8,65,64]{2,1,0:T(8,128)S(1)}, u32[]{:S(2)}, u32[]{:S(2)}) collective-permute-start(f32[8,65,64]{2,1,0:T(8,128)S(1)} %collective-permute-done.1), channel_id=1, source_target_pairs={{0,4},{4,8},{8,12},{12,16},{16,20},{20,24},{24,28},{28,32},{32,36}... | collective-permute-start | bytes 399368 | tf_op jit(solution)/shard_map/ppermute | solution.py:15
  129.1 13.0 %collective-permute-start.3 = (f32[8,65,64]{2,1,0:T(8,128)S(1)}, f32[8,65,64]{2,1,0:T(8,128)S(1)}, u32[]{:S(2)}, u32[]{:S(2)}) collective-permute-start(f32[8,65,64]{2,1,0:T(8,128)S(1)} %pad_maximum_fusion.1), channel_id=1, source_target_pairs={{0,8},{4,12},{8,16},{12,20},{16,24},{20,28},{24,32},{28,36},{32,40... | collective-permute-start | bytes 399368 | tf_op jit(solution)/shard_map/ppermute | solution.py:15
  142.4 16.5 %collective-permute-start.4 = (f32[8,65,64]{2,1,0:T(8,128)S(1)}, f32[8,65,64]{2,1,0:T(8,128)S(1)}, u32[]{:S(2)}, u32[]{:S(2)}) collective-permute-start(f32[8,65,64]{2,1,0:T(8,128)S(1)} %pad_maximum_fusion.2), channel_id=1, source_target_pairs={{0,16},{4,20},{8,24},{12,28},{16,32},{20,36},{24,40},{28,44},{32,4... | collective-permute-start | bytes 399368 | tf_op jit(solution)/shard_map/ppermute | solution.py:15
  159.1 14.9 %collective-permute-start.5 = (f32[8,65,64]{2,1,0:T(8,128)S(1)}, f32[8,65,64]{2,1,0:T(8,128)S(1)}, u32[]{:S(2)}, u32[]{:S(2)}) collective-permute-start(f32[8,65,64]{2,1,0:T(8,128)S(1)} %pad_maximum_fusion.3), channel_id=1, source_target_pairs={{0,32},{4,36},{8,40},{12,44},{16,48},{20,52},{24,56},{28,60},{32,6... | collective-permute-start | bytes 399368 | tf_op jit(solution)/shard_map/ppermute | solution.py:15
  174.0 26.9 %copy-start.8 = (f32[512]{0:T(512)S(1)}, f32[512]{0:T(512)}, u32[]{:S(2)}) copy-start(f32[512]{0:T(512)} %param.26) | copy-start | bytes 6148
  174.1 26.9 %copy-start.9 = (f32[512]{0:T(512)S(1)}, f32[512]{0:T(512)}, u32[]{:S(2)}) copy-start(f32[512]{0:T(512)} %param.25) | copy-start | bytes 6148
  174.1 14.3 %collective-permute-start.6 = (f32[8,65,64]{2,1,0:T(8,128)S(1)}, f32[8,65,64]{2,1,0:T(8,128)S(1)}, u32[]{:S(2)}, u32[]{:S(2)}) collective-permute-start(f32[8,65,64]{2,1,0:T(8,128)S(1)} %pad_maximum_fusion.4), channel_id=1, source_target_pairs={{0,64},{4,68},{8,72},{12,76},{16,80},{20,84},{24,88},{28,92},{32,9... | collective-permute-start | bytes 399368 | tf_op jit(solution)/shard_map/ppermute | solution.py:15
  188.6 10.1 %collective-permute-start.7 = (f32[8,65,64]{2,1,0:T(8,128)S(1)}, f32[8,65,64]{2,1,0:T(8,128)S(1)}, u32[]{:S(2)}, u32[]{:S(2)}) collective-permute-start(f32[8,65,64]{2,1,0:T(8,128)S(1)} %pad_maximum_fusion.5), channel_id=1, source_target_pairs={{0,128},{4,132},{8,136},{12,140},{16,144},{20,148},{24,152},{28,15... | collective-permute-start | bytes 399368 | tf_op jit(solution)/shard_map/ppermute | solution.py:15
  199.5 54.4 %copy-start.2 = (bf16[128,512]{1,0:T(8,128)(2,1)S(1)}, bf16[128,512]{1,0:T(8,128)(2,1)}, u32[]{:S(2)}) copy-start(bf16[128,512]{1,0:T(8,128)(2,1)} %param.15) | copy-start | bytes 393220
Sparse Core Ops, SparseCore 0:
  203.3 50.5 all-reduce.1

commit v2 on v1

--- a/solution.py
+++ b/solution.py
@@ -138,8 +138,23 @@
         jnp.zeros((mixing_values_divided, CHANNELS_ONE_HEAD), jnp.float32),
         jnp.float32(1.0),
     )
-    (end_state, offset, alive), (outs, from_start) = lax.scan(block_step, init, inputs)
-    decay_total = alive * jnp.exp(offset)
+    decay_heads = decay_logarithm.reshape(rows, mixing_values_divided, CHANNELS_ONE_HEAD).transpose(1, 0, 2)
+    suffix_incl = jnp.flip(jnp.cumsum(jnp.flip(decay_heads, 1), axis=1), 1)
+    suffix_excl = jnp.concatenate([suffix_incl[:, 1:], jnp.zeros_like(suffix_incl[:, :1])], axis=1)
+    in_tail = (segment == segment[rows - 1]).astype(jnp.float32)
+    key_heads = key_rows.astype(jnp.float32).reshape(rows, mixing_values_divided, CHANNELS_ONE_HEAD)
+    value_heads = value_rows.astype(jnp.float32).reshape(rows, mixing_values_divided, CHANNELS_ONE_HEAD)
+    tail_keys = key_heads.transpose(1, 0, 2) * jnp.exp(suffix_excl) * in_tail[None, :, None]
+    end_state = jnp.einsum("hsc,shv->hcv", tail_keys, value_heads, precision=highest)
+    decay_total = jnp.all(jnp.logical_not(is_start)).astype(jnp.float32) * jnp.exp(suffix_incl[:, 0])
+    carry = init
+    outs, from_start = [], []
+    for index in range(blocks):
+        carry, (block_out, block_from_start) = block_step(carry, tuple(part[index] for part in inputs))
+        outs.append(block_out)
+        from_start.append(block_from_start)
+    outs = jnp.stack(outs)
+    from_start = jnp.stack(from_start)
 
     devices = lax.axis_size("seq")
     packed = jnp.concatenate([end_state, decay_total[:, None, :]], axis=1)
@@ -166,8 +181,10 @@
     ) * cluster_standardize_scale + cluster_standardize_offset
     gated = (grouped * gate.astype(jnp.float32)).astype(jnp.bfloat16)
     partial_sum = jnp.dot(gated, emitted_mapping_matrix, preferred_element_type=jnp.float32)
-    summed = lax.psum(partial_sum.astype(jnp.bfloat16), "tp").astype(jnp.float32)
-    mine = lax.dynamic_slice_in_dim(summed, lax.axis_index("tp") * local_width, local_width, 1)
+    parts = lax.axis_size("tp")
+    pieces = partial_sum.astype(jnp.bfloat16).reshape(rows, parts, local_width).transpose(1, 0, 2)
+    pieces = lax.all_to_all(pieces, "tp", 0, 0, tiled=True)
+    mine = jnp.sum(pieces.astype(jnp.float32), axis=0)
     return (tier_source_concatenated.astype(jnp.float32) + mine).astype(jnp.bfloat16)
 
 

time: 264 us -> 196 us (0.74)
  waiting for transfers between devices: 106 us -> 50 us
  matrix products: 31.7 us -> 19 us
  blocking collectives: 13.5 us -> 25.6 us
  between operations: 13.7 us -> 3.48 us
  starting transfers between devices: 32.3 us -> 27.1 us
  other arithmetic: 43.2 us -> 47.6 us
  loops' own time: 3.16 us -> 0 us
    psum x1 -> x0, waiting for transfers between devices: 50.7 us -> none  [body(): lax.psum(partial_sum.astype(jnp.bfloat16), 'tp').astype(jnp.float32)]
    all_to_all x0 -> x1, blocking collectives: none -> 12.1 us  [body(): pieces = lax.all_to_all(pieces, 'tp', 0, 0, tiled=True)]
    dynamic_update_slice x4 -> x0, other arithmetic: 6.66 us -> none  [body(): lax.scan(block_step, init, inputs)]
    dot_general x4 -> x3, matrix products: 6.64 us -> 1.42 us  [block_step(): jnp.einsum('hsc,hsv->hcv', tail, content_slab, precision=highest)]
    ppermute x8, starting transfers between devices: 32.3 us -> 27.1 us  [from_behind(): return lax.ppermute(block, axis, route)]
    ppermute x8, waiting for transfers between devices: 55.1 us -> 50 us  [from_behind(): return lax.ppermute(block, axis, route)]
    transpose x5 -> x2, local copies, waits for them, and re-layouts: 7.39 us -> 2.78 us  [body(): key_heads.transpose(1, 0, 2) * jnp.exp(suffix_excl) * in_tail[None, :, None]]
    convert_element_type x1 -> x4, local copies, waits for them, and re-layouts: 0.08 us -> 4.38 us  [the longest x1 1.8 us: body(): recept = projected[0].astype(jnp.bfloat16)]
  transfers between devices with their start and end apart: 9 -> 8, of which waited for: 9 -> 6; matrix products, arithmetic and copies ran while one was open for 1% -> 19% of each run, Pallas kernels for 0% -> 0%
where the time goes in v2:
time: 196 us; the launch traced here: 194 us
  waiting for transfers between devices  50 us (26%)
  other arithmetic  47.6 us (24%)
  starting transfers between devices  27.1 us (14%)
  blocking collectives  25.6 us (13%)
  local copies, waits for them, and re-layouts  21 us (11%)
  matrix products  19 us (10%)
  between operations  3.48 us (2%)
    ppermute x8, waiting for transfers between devices, from_behind(): return lax.ppermute(block, axis, route)  50 us
    ppermute x8, starting transfers between devices, from_behind(): return lax.ppermute(block, axis, route)  27.1 us
    dot_general x4, other arithmetic, block_step(): jnp.einsum('htc,hsc,htsc->hts', gating_rows_tile, query_array_tile, weigh...  13.8 us
    all_gather x1, blocking collectives, body(): full = lax.all_gather(tier_source_concatenated, 'tp', axis=1, tiled=True)  13.5 us
    all_to_all x1, blocking collectives, body(): pieces = lax.all_to_all(pieces, 'tp', 0, 0, tiled=True)  12.1 us
    dot_general x1, matrix products, body(): jnp.einsum('itd,ide->ite', shifted_blend[:4], mapping_matrices_pile, pref...  5.37 us
    select_n x3, other arithmetic, block_step(): weight = jnp.where(pair_ok[None, :, :, None], jnp.exp(gap), 0.0)  4.14 us
  transfers between devices with their start and end apart: 8, of which 6 were waited for; matrix products, arithmetic and copies ran while one was open for 19% of the time, Pallas kernels for 0%

profile of v2, /device:TPU:48, one launch (start us, length us, event | category | flops | bytes accessed | tf_op | source)
XLA Modules:
  0.0 193.9 jit_solution(2850467474836239887)
XLA Ops:
  0.0 13.5 %all_gather.3 = bf16[128,2048]{1,0:T(8,128)(2,1)S(1)} all-gather(bf16[128,512]{1,0:T(8,128)(2,1)} %param.13), channel_id=1, replica_groups=mesh['seq'=64,'tp'=4] {'tp'}, dimensions={1}, use_global_device_ids=true | all-gather | bytes 655360 | tf_op jit(solution)/shard_map/all_gather | solution.py:45
  13.9 2.1 %fusion.105 = (f32[128,2048]{1,0:T(8,128)}, bf16[128,2048]{1,0:T(8,128)(2,1)S(1)}) fusion(f32[2048]{0:T(1024)} %param.16, f32[2048]{0:T(1024)} %param.15, f32[128]{0:T(128)S(1)} %add_rsqrt_fusion.1, f32[128]{0:T(128)S(1)} %broadcast_multiply_fusion.1, bf16[128,2048]{1,0:T(8,128)(2,1)S(1)} %all_gather.3), kind=kLoop, calls=%fused_computation.241 | loop fusion | flops 1835008 | bytes 2114560 | tf_op jit(solution)/shard_map/convert_element_type | solution.py:56
  25.3 2.5 %compare_convert_fusion.1 = (f32[32]{0:T(128)}, f32[32]{0:T(128)}, f32[32]{0:T(128)}) fusion(s32[]{:T(128)} %bitcast.79, s32[128]{0:T(128)S(1)} %convert_reduce_fusion.2, s32[]{:T(128)} %bitcast.43, s32[]{:T(128)} %bitcast.61), kind=kLoop, calls=%fused_computation.212 | loop fusion | flops 192 | bytes 780 | tf_op jit(solution)/shard_map/convert_element_type | solution.py:124
  35.1 5.4 %fusion.95 = f32[4,128,512]{2,1,0:T(8,128)S(1)} fusion(bf16[4,2048,512]{2,1,0:T(8,128)(2,1)} %param.18, f32[5,2048]{1,0:T(8,128)S(1)} %copy-done.15, f32[128,2048]{1,0:T(8,128)S(1)} %convert_subtract_fusion.1, f32[128,2048]{1,0:T(8,128)} %get-tuple-element.23), kind=kOutput, calls=%fused_computation.235 | convolution fusion | flops 1077673984 | bytes 11575296 | tf_op jit(solution)/shard_map/itd,ide->ite/dot_general | solution.py:61
  45.0 3.4 %add_convert_fusion = bf16[5,128,2048]{2,1,0:T(8,128)(2,1)} fusion(f32[5,2048]{1,0:T(8,128)} %param.17, f32[128,2048]{1,0:T(8,128)} %copy-done.1, f32[128,2048]{1,0:T(8,128)S(1)} %copy-done.2), kind=kLoop, calls=%fused_computation.4 | loop fusion | flops 3932160 | bytes 4759552 | tf_op jit(solution)/shard_map/convert_element_type | solution.py:58
  56.1 2.0 %copy_bitcast_fusion.1 = (bf16[4,8,32,64]{3,2,1,0:T(8,128)(2,1)}, f32[4,8,32,64]{3,2,1,0:T(8,128)S(1)}, f32[4,8,32,64]{3,2,1,0:T(8,128)S(1)}, bf16[4,8,32,64]{3,2,1,0:T(8,128)(2,1)}) fusion(bf16[4,32,8,64]{3,2,1,0:T(8,128)(2,1)} %convert_element_type.139, bf16[4,32,8,64]{3,2,1,0:T(8,128)(2,1)} %convert_element_type.136), kind=kLoop, calls=%fused_computation.108 | loop fusion | flops 131072 | bytes 1048576 | tf_op jit(solution)/shard_map/transpose | solution.py:79
  61.2 2.0 %copy.179 = f32[128,8,64]{2,1,0:T(8,128)} copy(f32[128,8,64]{0,2,1:T(8,128)} %bitcast.382) | data formatting | bytes 524288 | tf_op jit(solution)/shard_map/transpose | solution.py:147
  65.0 2.0 %copy.181 = f32[8,128,64]{2,0,1:T(8,128)} copy(f32[8,128,64]{1,2,0:T(8,128)} %rev.5) | data formatting | bytes 524288 | tf_op jit(solution)/shard_map/jit(_flip)/rev | solution.py:142
  75.8 4.1 %collective-permute-start.1 = (f32[8,65,64]{1,2,0:T(8,128)S(1)}, f32[8,65,64]{1,2,0:T(8,128)S(1)}, u32[]{:S(2)}, u32[]{:S(2)}) collective-permute-start(f32[8,65,64]{1,2,0:T(8,128)S(1)} %pad_maximum_fusion), channel_id=1, source_target_pairs={{0,4},{4,8},{8,12},{12,16},{16,20},{20,24},{24,28},{28,32},{32,36}... | collective-permute-start | bytes 399368 | tf_op jit(solution)/shard_map/ppermute | solution.py:15
  85.1 3.4 %fusion.6 = f32[8,32,32]{1,2,0:T(8,128)S(1)} fusion(f32[8,32,32,64]{3,2,1,0:T(8,128)S(1)} %exponential_select_fusion.2, f32[8,64,32]{1,2,0:T(8,128)S(1)} %get-tuple-element.39, f32[8,64,32]{1,2,0:T(8,128)S(1)} %get-tuple-element.35), kind=kLoop, calls=%fused_computation.10 | loop fusion | flops 1564672 | bytes 2260992 | tf_op jit(solution)/shard_map/htc,hsc,htsc->hts/dot_general | solution.py:105
  88.6 3.4 %fusion.7 = f32[8,32,32]{1,2,0:T(8,128)S(1)} fusion(f32[8,32,32,64]{3,2,1,0:T(8,128)S(1)} %exponential_select_fusion.3, f32[8,64,32]{1,2,0:T(8,128)S(1)} %get-tuple-element.37, f32[8,64,32]{1,2,0:T(8,128)S(1)} %get-tuple-element.33), kind=kLoop, calls=%fused_computation.12 | loop fusion | flops 1564672 | bytes 2260992 | tf_op jit(solution)/shard_map/htc,hsc,htsc->hts/dot_general | solution.py:105
  93.9 3.4 %fusion.5 = f32[8,32,32]{1,2,0:T(8,128)S(1)} fusion(f32[8,32,32,64]{3,2,1,0:T(8,128)S(1)} %get-tuple-element.73, f32[8,64,32]{1,2,0:T(8,128)S(1)} %get-tuple-element.38, f32[8,64,32]{1,2,0:T(8,128)S(1)} %get-tuple-element.34), kind=kLoop, calls=%fused_computation.8 | loop fusion | flops 1564672 | bytes 2260992 | tf_op jit(solution)/shard_map/htc,hsc,htsc->hts/dot_general | solution.py:105
  97.4 3.4 %fusion.4 = f32[8,32,32]{1,2,0:T(8,128)S(1)} fusion(f32[8,32,32,64]{3,2,1,0:T(8,128)S(1)} %get-tuple-element.72, f32[8,64,32]{1,2,0:T(8,128)S(1)} %get-tuple-element.40, f32[8,64,32]{1,2,0:T(8,128)S(1)} %get-tuple-element.36), kind=kLoop, calls=%fused_computation.6 | loop fusion | flops 1564672 | bytes 2260992 | tf_op jit(solution)/shard_map/htc,hsc,htsc->hts/dot_general | solution.py:105
  101.1 1.9 collective-permute-start.2
  103.4 5.5 %collective-permute-done.2 = f32[8,65,64]{1,2,0:T(8,128)S(1)} collective-permute-done((f32[8,65,64]{1,2,0:T(8,128)S(1)}, f32[8,65,64]{1,2,0:T(8,128)S(1)}, u32[]{:S(2)}, u32[]{:S(2)}) %collective-permute-start.2) | collective-permute-done | bytes 133152 | tf_op jit(solution)/shard_map/ppermute | solution.py:15
  109.4 3.8 %collective-permute-start.3 = (f32[8,65,64]{1,2,0:T(8,128)S(1)}, f32[8,65,64]{1,2,0:T(8,128)S(1)}, u32[]{:S(2)}, u32[]{:S(2)}) collective-permute-start(f32[8,65,64]{1,2,0:T(8,128)S(1)} %pad_maximum_fusion.1), channel_id=1, source_target_pairs={{0,8},{4,12},{8,16},{12,20},{16,24},{20,28},{24,32},{28,36},{32,40... | collective-permute-start | bytes 399368 | tf_op jit(solution)/shard_map/ppermute | solution.py:15
  113.6 6.2 %collective-permute-done.3 = f32[8,65,64]{1,2,0:T(8,128)S(1)} collective-permute-done((f32[8,65,64]{1,2,0:T(8,128)S(1)}, f32[8,65,64]{1,2,0:T(8,128)S(1)}, u32[]{:S(2)}, u32[]{:S(2)}) %collective-permute-start.3) | collective-permute-done | bytes 133152 | tf_op jit(solution)/shard_map/ppermute | solution.py:15
  120.2 4.8 %collective-permute-start.4 = (f32[8,65,64]{1,2,0:T(8,128)S(1)}, f32[8,65,64]{1,2,0:T(8,128)S(1)}, u32[]{:S(2)}, u32[]{:S(2)}) collective-permute-start(f32[8,65,64]{1,2,0:T(8,128)S(1)} %pad_maximum_fusion.2), channel_id=1, source_target_pairs={{0,16},{4,20},{8,24},{12,28},{16,32},{20,36},{24,40},{28,44},{32,4... | collective-permute-start | bytes 399368 | tf_op jit(solution)/shard_map/ppermute | solution.py:15
  125.7 11.4 %collective-permute-done.4 = f32[8,65,64]{1,2,0:T(8,128)S(1)} collective-permute-done((f32[8,65,64]{1,2,0:T(8,128)S(1)}, f32[8,65,64]{1,2,0:T(8,128)S(1)}, u32[]{:S(2)}, u32[]{:S(2)}) %collective-permute-start.4) | collective-permute-done | bytes 133152 | tf_op jit(solution)/shard_map/ppermute | solution.py:15
  139.9 12.9 %collective-permute-done.5 = f32[8,65,64]{1,2,0:T(8,128)S(1)} collective-permute-done((f32[8,65,64]{1,2,0:T(8,128)S(1)}, f32[8,65,64]{1,2,0:T(8,128)S(1)}, u32[]{:S(2)}, u32[]{:S(2)}) %collective-permute-start.5) | collective-permute-done | bytes 133152 | tf_op jit(solution)/shard_map/ppermute | solution.py:15
  153.2 7.0 %collective-permute-start.6 = (f32[8,65,64]{1,2,0:T(8,128)S(1)}, f32[8,65,64]{1,2,0:T(8,128)S(1)}, u32[]{:S(2)}, u32[]{:S(2)}) collective-permute-start(f32[8,65,64]{1,2,0:T(8,128)S(1)} %pad_maximum_fusion.4), channel_id=1, source_target_pairs={{0,64},{4,68},{8,72},{12,76},{16,80},{20,84},{24,88},{28,92},{32,9... | collective-permute-start | bytes 399368 | tf_op jit(solution)/shard_map/ppermute | solution.py:15
  160.7 5.3 %collective-permute-done.6 = f32[8,65,64]{1,2,0:T(8,128)S(1)} collective-permute-done((f32[8,65,64]{1,2,0:T(8,128)S(1)}, f32[8,65,64]{1,2,0:T(8,128)S(1)}, u32[]{:S(2)}, u32[]{:S(2)}) %collective-permute-start.6) | collective-permute-done | bytes 133152 | tf_op jit(solution)/shard_map/ppermute | solution.py:15
  168.5 8.8 %collective-permute-done.7 = f32[8,65,64]{1,2,0:T(8,128)S(1)} collective-permute-done((f32[8,65,64]{1,2,0:T(8,128)S(1)}, f32[8,65,64]{1,2,0:T(8,128)S(1)}, u32[]{:S(2)}, u32[]{:S(2)}) %collective-permute-start.7) | collective-permute-done | bytes 133152 | tf_op jit(solution)/shard_map/ppermute | solution.py:15
  181.0 12.1 %all_to_all.5 = bf16[4,128,512]{2,1,0:T(8,128)(2,1)S(1)} all-to-all(bf16[4,128,512]{2,1,0:T(8,128)(2,1)S(1)} %bitcast.380), channel_id=1, replica_groups=mesh['seq'=64,'tp'=4] {'tp'}, dimensions={0} | all-to-all | bytes 1048576 | tf_op jit(solution)/shard_map/all_to_all | solution.py:186
  (169 shorter events, 59.9 us)
Async XLA Ops:
  0.0 179.4 %copy-start = (bf16[512,2048]{1,0:T(8,128)(2,1)S(1)}, bf16[512,2048]{1,0:T(8,128)(2,1)}, u32[]{:S(2)}) copy-start(bf16[512,2048]{1,0:T(8,128)(2,1)} %param.25) | copy-start | bytes 6291460
  0.0 35.1 %copy-start.15 = (f32[5,2048]{1,0:T(8,128)S(1)}, f32[5,2048]{1,0:T(8,128)}, u32[]{:S(2)}) copy-start(f32[5,2048]{1,0:T(8,128)} %param.17) | copy-start | bytes 122884
  16.1 18.7 %collective-permute-start = (bf16[1,2048]{1,0:T(2,128)(2,1)S(1)}, bf16[1,2048]{1,0:T(2,128)(2,1)S(1)}, u32[]{:S(2)}, u32[]{:S(2)}) collective-permute-start(bf16[1,2048]{1,0:T(2,128)(2,1)S(1)} %slice.281), channel_id=1, source_target_pairs={{0,4},{4,8},{8,12},{12,16},{16,20},{20,24},{24,28},{28,32},{32,36}... | collective-permute-start | bytes 12296 | tf_op jit(solution)/shard_map/ppermute | solution.py:15
  35.1 9.8 %copy-start.2 = (f32[128,2048]{1,0:T(8,128)S(1)}, f32[128,2048]{1,0:T(8,128)}, u32[]{:S(2)}) copy-start(f32[128,2048]{1,0:T(8,128)} %get-tuple-element.23) | copy-start | bytes 3145732
  71.8 9.1 %copy-start.7 = (bf16[4,8,32,64]{3,2,1,0:T(8,128)(2,1)S(1)}, bf16[4,8,32,64]{3,2,1,0:T(8,128)(2,1)}, u32[]{:S(2)}) copy-start(bf16[4,8,32,64]{3,2,1,0:T(8,128)(2,1)} %get-tuple-element.75) | copy-start | bytes 393220
  71.8 9.2 %copy-start.25 = (f32[32]{0:T(128)S(1)}, f32[32]{0:T(128)}, u32[]{:S(2)}) copy-start(f32[32]{0:T(128)} %get-tuple-element.68) | copy-start | bytes 388
  73.2 9.4 %copy-start.6 = (f32[8,32,64]{2,1,0:T(8,128)S(1)}, f32[8,32,64]{2,1,0:T(8,128)}, u32[]{:S(2)}) copy-start(f32[8,32,64]{2,1,0:T(8,128)} %convolution_bitcast_fusion.1) | copy-start | bytes 196612
  73.3 9.4 %copy-start.20 = (f32[32]{0:T(128)S(1)}, f32[32]{0:T(128)}, u32[]{:S(2)}) copy-start(f32[32]{0:T(128)} %get-tuple-element.64) | copy-start | bytes 388
  73.3 9.4 %copy-start.23 = (f32[32]{0:T(128)S(1)}, f32[32]{0:T(128)}, u32[]{:S(2)}) copy-start(f32[32]{0:T(128)} %fusion.23) | copy-start | bytes 388
  73.3 9.4 %copy-start.24 = (f32[32]{0:T(128)S(1)}, f32[32]{0:T(128)}, u32[]{:S(2)}) copy-start(f32[32]{0:T(128)} %get-tuple-element.66) | copy-start | bytes 388
  75.8 25.4 %collective-permute-start.1 = (f32[8,65,64]{1,2,0:T(8,128)S(1)}, f32[8,65,64]{1,2,0:T(8,128)S(1)}, u32[]{:S(2)}, u32[]{:S(2)}) collective-permute-start(f32[8,65,64]{1,2,0:T(8,128)S(1)} %pad_maximum_fusion), channel_id=1, source_target_pairs={{0,4},{4,8},{8,12},{12,16},{16,20},{20,24},{24,28},{28,32},{32,36}... | collective-permute-start | bytes 399368 | tf_op jit(solution)/shard_map/ppermute | solution.py:15
  93.9 6.9 %copy-start.12 = (f32[8,32,64]{2,1,0:T(8,128)S(1)}, f32[8,32,64]{2,1,0:T(8,128)}, u32[]{:S(2)}) copy-start(f32[8,32,64]{2,1,0:T(8,128)} %fusion.18) | copy-start | bytes 196612
  93.9 9.2 %copy-start.11 = (f32[8,32,64]{2,1,0:T(8,128)S(1)}, f32[8,32,64]{2,1,0:T(8,128)}, u32[]{:S(2)}) copy-start(f32[8,32,64]{2,1,0:T(8,128)} %fusion.17) | copy-start | bytes 196612
  97.4 15.9 %copy-start.10 = (f32[8,32,64]{2,1,0:T(8,128)S(1)}, f32[8,32,64]{2,1,0:T(8,128)}, u32[]{:S(2)}) copy-start(f32[8,32,64]{2,1,0:T(8,128)} %fusion.19) | copy-start | bytes 196612
  100.8 24.2 %copy-start.9 = (f32[8,32,64]{2,1,0:T(8,128)S(1)}, f32[8,32,64]{2,1,0:T(8,128)}, u32[]{:S(2)}) copy-start(f32[8,32,64]{2,1,0:T(8,128)} %fusion.20) | copy-start | bytes 196612
  101.1 7.7 %collective-permute-start.2 = (f32[8,65,64]{1,2,0:T(8,128)S(1)}, f32[8,65,64]{1,2,0:T(8,128)S(1)}, u32[]{:S(2)}, u32[]{:S(2)}) collective-permute-start(f32[8,65,64]{1,2,0:T(8,128)S(1)} %collective-permute-done.1), channel_id=1, source_target_pairs={{0,4},{4,8},{8,12},{12,16},{16,20},{20,24},{24,28},{28,32},{32,36}... | collective-permute-start | bytes 399368 | tf_op jit(solution)/shard_map/ppermute | solution.py:15
  109.4 10.3 %collective-permute-start.3 = (f32[8,65,64]{1,2,0:T(8,128)S(1)}, f32[8,65,64]{1,2,0:T(8,128)S(1)}, u32[]{:S(2)}, u32[]{:S(2)}) collective-permute-start(f32[8,65,64]{1,2,0:T(8,128)S(1)} %pad_maximum_fusion.1), channel_id=1, source_target_pairs={{0,8},{4,12},{8,16},{12,20},{16,24},{20,28},{24,32},{28,36},{32,40... | collective-permute-start | bytes 399368 | tf_op jit(solution)/shard_map/ppermute | solution.py:15
  120.2 16.9 %collective-permute-start.4 = (f32[8,65,64]{1,2,0:T(8,128)S(1)}, f32[8,65,64]{1,2,0:T(8,128)S(1)}, u32[]{:S(2)}, u32[]{:S(2)}) collective-permute-start(f32[8,65,64]{1,2,0:T(8,128)S(1)} %pad_maximum_fusion.2), channel_id=1, source_target_pairs={{0,16},{4,20},{8,24},{12,28},{16,32},{20,36},{24,40},{28,44},{32,4... | collective-permute-start | bytes 399368 | tf_op jit(solution)/shard_map/ppermute | solution.py:15
  137.5 15.2 %collective-permute-start.5 = (f32[8,65,64]{1,2,0:T(8,128)S(1)}, f32[8,65,64]{1,2,0:T(8,128)S(1)}, u32[]{:S(2)}, u32[]{:S(2)}) collective-permute-start(f32[8,65,64]{1,2,0:T(8,128)S(1)} %pad_maximum_fusion.3), channel_id=1, source_target_pairs={{0,32},{4,36},{8,40},{12,44},{16,48},{20,52},{24,56},{28,60},{32,6... | collective-permute-start | bytes 399368 | tf_op jit(solution)/shard_map/ppermute | solution.py:15
  153.2 12.8 %collective-permute-start.6 = (f32[8,65,64]{1,2,0:T(8,128)S(1)}, f32[8,65,64]{1,2,0:T(8,128)S(1)}, u32[]{:S(2)}, u32[]{:S(2)}) collective-permute-start(f32[8,65,64]{1,2,0:T(8,128)S(1)} %pad_maximum_fusion.4), channel_id=1, source_target_pairs={{0,64},{4,68},{8,72},{12,76},{16,80},{20,84},{24,88},{28,92},{32,9... | collective-permute-start | bytes 399368 | tf_op jit(solution)/shard_map/ppermute | solution.py:15
  166.3 13.2 %copy-start.18 = (f32[512]{0:T(512)S(1)}, f32[512]{0:T(512)}, u32[]{:S(2)}) copy-start(f32[512]{0:T(512)} %param.24) | copy-start | bytes 6148
  166.3 13.2 %copy-start.19 = (f32[512]{0:T(512)S(1)}, f32[512]{0:T(512)}, u32[]{:S(2)}) copy-start(f32[512]{0:T(512)} %param.23) | copy-start | bytes 6148
  166.5 10.8 %collective-permute-start.7 = (f32[8,65,64]{1,2,0:T(8,128)S(1)}, f32[8,65,64]{1,2,0:T(8,128)S(1)}, u32[]{:S(2)}, u32[]{:S(2)}) collective-permute-start(f32[8,65,64]{1,2,0:T(8,128)S(1)} %pad_maximum_fusion.5), channel_id=1, source_target_pairs={{0,128},{4,132},{8,136},{12,140},{16,144},{20,148},{24,152},{28,15... | collective-permute-start | bytes 399368 | tf_op jit(solution)/shard_map/ppermute | solution.py:15
  179.0 14.2 %copy-start.8 = (bf16[128,512]{1,0:T(8,128)(2,1)S(1)}, bf16[128,512]{1,0:T(8,128)(2,1)}, u32[]{:S(2)}) copy-start(bf16[128,512]{1,0:T(8,128)(2,1)} %param.13) | copy-start | bytes 393220
  (11 other events, 27.6 us)

commit v3 on v2

--- a/solution.py
+++ b/solution.py
@@ -1,3 +1,5 @@
+import math
+
 import jax
 import jax.numpy as jnp
 from jax import lax
@@ -9,8 +11,15 @@
 highest = lax.Precision.HIGHEST
 
 
+SEQ = ("seq_hi", "seq_lo")
+
+
+def size_of(axes):
+    return math.prod(lax.axis_size(axis) for axis in axes)
+
+
 def from_behind(block, axis, distance):
-    devices = range(lax.axis_size(axis))
+    devices = range(size_of(axis))
     route = [(i - distance, i) for i in devices if i - distance in devices]
     return lax.ppermute(block, axis, route)
 
@@ -47,10 +56,10 @@
         full.astype(jnp.float32), tier_standardize_scale, tier_standardize_offset, 1e-05
     ).astype(jnp.bfloat16)
     first = jnp.cumsum(prompt_sizes_ordered) - prompt_sizes_ordered
-    position = lax.axis_index("seq") * rows + jnp.arange(rows, dtype=jnp.int32)
+    position = lax.axis_index(SEQ) * rows + jnp.arange(rows, dtype=jnp.int32)
     is_start = jnp.any(position[:, None] == first[None, :], axis=1)
     segment = jnp.sum((first[None, :] <= position[:, None]).astype(jnp.int32), axis=1)
-    edge = from_behind(normed[rows - 1 :], "seq", 1)
+    edge = from_behind(normed[rows - 1 :], SEQ, 1)
     previous = jnp.concatenate([edge, normed[: rows - 1]], axis=0)
     previous = jnp.where(is_start[:, None], jnp.zeros_like(previous), previous)
     base = normed.astype(jnp.float32)
@@ -147,30 +156,27 @@
     tail_keys = key_heads.transpose(1, 0, 2) * jnp.exp(suffix_excl) * in_tail[None, :, None]
     end_state = jnp.einsum("hsc,shv->hcv", tail_keys, value_heads, precision=highest)
     decay_total = jnp.all(jnp.logical_not(is_start)).astype(jnp.float32) * jnp.exp(suffix_incl[:, 0])
-    carry = init
-    outs, from_start = [], []
-    for index in range(blocks):
-        carry, (block_out, block_from_start) = block_step(carry, tuple(part[index] for part in inputs))
-        outs.append(block_out)
-        from_start.append(block_from_start)
-    outs = jnp.stack(outs)
-    from_start = jnp.stack(from_start)
-
-    devices = lax.axis_size("seq")
+    _, (outs, from_start) = lax.scan(block_step, init, inputs)
+
     packed = jnp.concatenate([end_state, decay_total[:, None, :]], axis=1)
 
-    def combine(received, own):
-        own_state, own_decay = own[:, :CHANNELS_ONE_HEAD], own[:, CHANNELS_ONE_HEAD:]
-        got_state, got_decay = received[:, :CHANNELS_ONE_HEAD], received[:, CHANNELS_ONE_HEAD:]
-        state = jnp.transpose(own_decay, (0, 2, 1)) * got_state + own_state
-        return jnp.concatenate([state, own_decay * got_decay], axis=1)
-
-    prefix = from_behind(packed, "seq", 1)
-    distance = 1
-    while distance < devices:
-        prefix = combine(from_behind(prefix, "seq", distance), prefix)
-        distance *= 2
-    incoming = prefix[:, :CHANNELS_ONE_HEAD]
+    def fold(gathered, count):
+        state = jnp.zeros_like(end_state)
+        decay = jnp.ones_like(decay_total)
+        for index in range(gathered.shape[0]):
+            take = index < count
+            piece = gathered[index]
+            state = jnp.where(take, piece[:, CHANNELS_ONE_HEAD, :, None] * state + piece[:, :CHANNELS_ONE_HEAD], state)
+            decay = jnp.where(take, piece[:, CHANNELS_ONE_HEAD] * decay, decay)
+        return state, decay
+
+    low = lax.axis_index("seq_lo")
+    neighbours = lax.all_gather(packed, "seq_lo")
+    inner_state, inner_decay = fold(neighbours, low)
+    group_state, group_decay = fold(neighbours, lax.axis_size("seq_lo"))
+    group = jnp.concatenate([group_state, group_decay[:, None, :]], axis=1)
+    entering, _ = fold(lax.all_gather(group, "seq_hi"), lax.axis_index("seq_hi"))
+    incoming = inner_decay[:, :, None] * entering + inner_state
     outs = outs + jnp.einsum("bhtc,hcv->bhtv", from_start, incoming, precision=highest)
     wkv = outs.transpose(0, 2, 1, 3).reshape(rows, mixing_values_divided, CHANNELS_ONE_HEAD)
     mean = jnp.mean(wkv, axis=-1, keepdims=True)
@@ -189,8 +195,11 @@
 
 
 def solution(mesh):
+    groups = 8 if mesh.shape["seq"] % 8 == 0 else 1
+    devices = mesh.devices.reshape(mesh.shape["seq"] // groups, groups, mesh.shape["tp"])
+    mesh = jax.sharding.Mesh(devices, ("seq_hi", "seq_lo", "tp"))
     in_specs = (
-        P("seq", "tp"),
+        P(SEQ, "tp"),
         P(),
         P(),
         P(),
@@ -204,5 +213,5 @@
         P("tp"),
         P("tp", None),
     )
-    out_specs = P("seq", "tp")
+    out_specs = P(SEQ, "tp")
     return jax.shard_map(body, mesh=mesh, in_specs=in_specs, out_specs=out_specs, check_vma=False)

time: 196 us -> 240 us (1.22)
  starting transfers between devices: 27.1 us -> 1.96 us
  other arithmetic: 47.6 us -> 70.8 us
  local copies, waits for them, and re-layouts: 21 us -> 43.7 us
  matrix products: 19 us -> 34.1 us
  between operations: 3.48 us -> 14.4 us
  waiting for transfers between devices: 50 us -> 41.7 us
  loops' own time: 0 us -> 3.32 us
    ppermute x8 -> x1, waiting for transfers between devices: 50 us -> 0.01 us  [from_behind(): return lax.ppermute(block, axis, route)]
    all_gather x0 -> x2, waiting for transfers between devices: none -> 41.7 us  [the longest x1 30.1 us: body(): neighbours = lax.all_gather(packed, 'seq_lo')]
    ppermute x8 -> x1, starting transfers between devices: 27.1 us -> 1.92 us  [from_behind(): return lax.ppermute(block, axis, route)]
    another operation x1, other arithmetic: 1.18 us -> 23.3 us  [body(): suffix_incl = jnp.flip(jnp.cumsum(jnp.flip(decay_heads, 1), axis=1), 1)]
    unnamed x54 -> x36, local copies, waits for them, and re-layouts: 0.43 us -> 11.7 us
    transpose x0 -> x6, local copies, waits for them, and re-layouts: none -> 8.25 us  [split_heads(): return values.astype(jnp.float32).reshape(blocks, block, mixing_values_di...]
    slice x3 -> x11, local copies, waits for them, and re-layouts: 0.88 us -> 8.85 us  [the longest x1 3.24 us: fold(): decay = jnp.where(take, piece[:, CHANNELS_ONE_HEAD] * decay, decay)]
    dynamic_update_slice x0 -> x4, other arithmetic: none -> 6.61 us  [body(): _, (outs, from_start) = lax.scan(block_step, init, inputs)]
  transfers between devices with their start and end apart: 8 -> 3, of which waited for: 6 -> 2; matrix products, arithmetic and copies ran while one was open for 19% -> 32% of each run, Pallas kernels for 0% -> 0%
where the time goes in v3:
time: 240 us; the launch traced here: 236 us
  other arithmetic  70.8 us (30%)
  local copies, waits for them, and re-layouts  43.7 us (18%)
  waiting for transfers between devices  41.7 us (17%)
  matrix products  34.1 us (14%)
  blocking collectives  25.8 us (11%)
  between operations  14.4 us (6%)
  loops' own time  3.32 us (1%)
    all_gather x1, waiting for transfers between devices, body(): neighbours = lax.all_gather(packed, 'seq_lo')  30.1 us
    another operation x1, other arithmetic, body(): suffix_incl = jnp.flip(jnp.cumsum(jnp.flip(decay_heads, 1), axis=1), 1)  23.3 us
    dot_general x4, other arithmetic, block_step(): jnp.einsum('htc,hsc,htsc->hts', gating_rows_tile, query_array_tile, weigh...  13.8 us
    all_gather x1, blocking collectives, body(): full = lax.all_gather(tier_source_concatenated, 'tp', axis=1, tiled=True)  13.5 us
    all_to_all x1, blocking collectives, body(): pieces = lax.all_to_all(pieces, 'tp', 0, 0, tiled=True)  12.3 us
    unnamed x36, local copies, waits for them, and re-layouts  11.7 us
    all_gather x1, waiting for transfers between devices, body(): lax.all_gather(group, 'seq_hi')  11.6 us
    transpose x6, local copies, waits for them, and re-layouts, split_heads(): return values.astype(jnp.float32).reshape(blocks, block, mixing_values_di...  8.25 us
  transfers between devices with their start and end apart: 3, of which 2 were waited for; matrix products, arithmetic and copies ran while one was open for 32% of the time, Pallas kernels for 0%

profile of v3, /device:TPU:48, one launch (start us, length us, event | category | flops | bytes accessed | tf_op | source)
XLA Modules:
  0.0 235.9 jit_solution(6184946986443270659)
XLA Ops:
  6.5 13.5 %all_gather.15 = bf16[128,2048]{1,0:T(8,128)(2,1)S(1)} all-gather(bf16[128,512]{1,0:T(8,128)(2,1)} %param.15), channel_id=1, replica_groups=mesh['seq_hi'=8,'seq_lo'=8,'tp'=4] {'tp'}, dimensions={1}, use_global_device_ids=true | all-gather | bytes 655360 | tf_op jit(solution)/shard_map/all_gather | solution.py:54
  20.5 2.1 fusion.153
  22.6 1.9 collective-permute-start
  29.9 3.3 %add_convert_fusion = bf16[5,128,2048]{2,1,0:T(8,128)(2,1)} fusion(f32[5,2048]{1,0:T(8,128)S(1)} %copy-done.5, f32[128,2048]{1,0:T(8,128)S(1)} %convert_subtract_fusion.1, f32[128,2048]{1,0:T(8,128)} %get-tuple-element.196), kind=kLoop, calls=%fused_computation.59 | loop fusion | flops 3932160 | bytes 4759552 | tf_op jit(solution)/shard_map/convert_element_type | solution.py:67
  33.2 4.7 %fusion.152 = f32[4,128,512]{2,1,0:T(8,128)S(1)} fusion(bf16[4,2048,512]{2,1,0:T(8,128)(2,1)} %param.20, f32[5,2048]{1,0:T(8,128)S(1)} %copy-done.5, f32[128,2048]{1,0:T(8,128)S(1)} %convert_subtract_fusion.1, f32[128,2048]{1,0:T(8,128)S(1)} %copy-done.1), kind=kOutput, calls=%fused_computation.219 | convolution fusion | flops 1077673984 | bytes 11575296 | tf_op jit(solution)/shard_map/itd,ide->ite/dot_general | solution.py:70
  41.8 23.3 %fusion.158 = f32[8,128,64]{2,0,1:T(8,128)S(1)} fusion(f32[8,128,64]{2,0,1:T(8,128)S(1)} %copy.314), kind=kOutput, calls=%fused_computation.224 | output fusion | flops 8323072 | bytes 524288 | tf_op jit(solution)/shard_map/jit(cumsum)/reduce_window_sum | solution.py:151
  68.9 1.9 slice.240
  76.6 1.9 reshape.272
  78.5 2.4 %copy_bitcast_fusion.2 = (f32[4,8,32,64]{3,2,1,0:T(8,128)}, f32[4,8,32,64]{3,2,1,0:T(8,128)}) fusion(f32[4,32,8,64]{3,2,1,0:T(8,128)} %reshape.270, f32[4,32,8,64]{3,2,1,0:T(8,128)} %reshape.264), kind=kLoop, calls=%fused_computation.87 | loop fusion | bytes 1048576 | tf_op jit(solution)/shard_map/transpose | solution.py:88
  80.9 2.0 copy_bitcast_fusion
  82.9 30.1 %all-gather.5.cloned.1.call-done = f32[64,65,64]{1,2,0:T(8,128)} async-done(((f32[8,65,64]{1,2,0:T(8,128)}), f32[64,65,64]{1,2,0:T(8,128)}) %all-gather.5.cloned.1.call-update) | async-done | bytes 1064976 | tf_op jit(solution)/shard_map/all_gather | solution.py:174
  113.0 3.2 %fusion.156 = (f32[8,1,64]{1,2,0:T(8,128)}, f32[8,1,64]{1,2,0:T(8,128)}, f32[8,1,64]{1,2,0:T(8,128)}, f32[8,1,64]{1,2,0:T(8,128)}, f32[8,1,64]{1,2,0:T(8,128)}, ...) fusion(f32[64,65,64]{1,2,0:T(8,128)} %all-gather.5.cloned.1.call-done), kind=kLoop, calls=%fused_computation.222 | loop fusion | bytes 32768 | tf_op jit(solution)/shard_map/slice | solution.py:170
  123.2 1.8 multiply_add_fusion
  125.8 64.9 %while.20 = (s32[]{:T(128)}, f32[8,64,64]{2,1,0:T(8,128)S(1)}, f32[8,64]{1,0:T(8,128)S(1)}, f32[]{:T(128)}, f32[4,8,32,64]{3,2,0,1:T(8,128)}, /*index=5*/f32[4,8...) while((s32[]{:T(128)}, f32[8,64,64]{2,1,0:T(8,128)S(1)}, ...), condition=%wide.region_7.8_spmd.clone.clone, body=%wide.region_5.7_spmd.clone.clone.sunk | while | flops 41284548 | bytes 7640194 | solution.py:159
  132.2 3.4 %fusion.192 = f32[8,32,32]{1,2,0:T(8,128)S(1)} fusion(f32[8,32,32,64]{3,2,1,0:T(8,128)S(1)} %exponential_select_fusion.2, f32[8,64,32]{1,2,0:T(8,128)S(1)} %get-tuple-element.328, f32[8,64,32]{1,2,0:T(8,128)S(1)} %get-tuple-element.329), kind=kLoop, calls=%fused_computation.4.clone.1 | loop fusion | flops 1564672 | bytes 2260992 | tf_op jit(solution)/shard_map/while/body/eval_jaxpr/htc,hsc,htsc->hts/dot_general | solution.py:114
  140.5 1.7 convolution_add_fusion.3
  148.4 3.4 %fusion.192 = f32[8,32,32]{1,2,0:T(8,128)S(1)} fusion(f32[8,32,32,64]{3,2,1,0:T(8,128)S(1)} %exponential_select_fusion.2, f32[8,64,32]{1,2,0:T(8,128)S(1)} %get-tuple-element.328, f32[8,64,32]{1,2,0:T(8,128)S(1)} %get-tuple-element.329), kind=kLoop, calls=%fused_computation.4.clone.1 | loop fusion | flops 1564672 | bytes 2260992 | tf_op jit(solution)/shard_map/while/body/eval_jaxpr/htc,hsc,htsc->hts/dot_general | solution.py:114
  164.6 3.4 %fusion.192 = f32[8,32,32]{1,2,0:T(8,128)S(1)} fusion(f32[8,32,32,64]{3,2,1,0:T(8,128)S(1)} %exponential_select_fusion.2, f32[8,64,32]{1,2,0:T(8,128)S(1)} %get-tuple-element.328, f32[8,64,32]{1,2,0:T(8,128)S(1)} %get-tuple-element.329), kind=kLoop, calls=%fused_computation.4.clone.1 | loop fusion | flops 1564672 | bytes 2260992 | tf_op jit(solution)/shard_map/while/body/eval_jaxpr/htc,hsc,htsc->hts/dot_general | solution.py:114
  177.3 1.7 bitcast_dynamic-update-slice_fusion.2
  180.8 3.4 %fusion.192 = f32[8,32,32]{1,2,0:T(8,128)S(1)} fusion(f32[8,32,32,64]{3,2,1,0:T(8,128)S(1)} %exponential_select_fusion.2, f32[8,64,32]{1,2,0:T(8,128)S(1)} %get-tuple-element.328, f32[8,64,32]{1,2,0:T(8,128)S(1)} %get-tuple-element.329), kind=kLoop, calls=%fused_computation.4.clone.1 | loop fusion | flops 1564672 | bytes 2260992 | tf_op jit(solution)/shard_map/while/body/eval_jaxpr/htc,hsc,htsc->hts/dot_general | solution.py:114
  190.8 11.6 %all-gather.7.cloned.1.call-done = f32[64,65,64]{1,2,0:T(8,128)} async-done(((f32[8,65,64]{1,2,0:T(8,128)}), f32[64,65,64]{1,2,0:T(8,128)}) %all-gather.7.cloned.1.call-update) | async-done | bytes 1064976 | tf_op jit(solution)/shard_map/all_gather | solution.py:178
  202.4 3.0 %fusion.155 = (f32[8,1,64]{1,2,0:T(8,128)S(1)}, f32[8,1,64]{1,2,0:T(8,128)S(1)}, f32[8,1,64]{1,2,0:T(8,128)S(1)}, f32[8,1,64]{1,2,0:T(8,128)S(1)}, f32[8,1,64]{1...) fusion(f32[64,65,64]{1,2,0:T(8,128)} %all-gather.7.cloned.1.call-done), kind=kLoop, calls=%fused_computation.221 | loop fusion | bytes 32768 | tf_op jit(solution)/shard_map/slice | solution.py:169
  209.3 3.7 %fusion.157 = (f32[4,32,8]{1,0,2:T(4,128)S(1)}, f32[4,32,8,64]{3,1,0,2:T(8,128)S(1)}) fusion(f32[4,8,32,64]{3,2,0,1:T(8,128)} %get-tuple-element.86, f32[4,8,32,64]{3,2,0,1:T(8,128)} %get-tuple-element.87, f32[64,65,64]{1,2,0:T(8,128)} %all-gather.7.cloned.1.call-done, f32[64,65,64]{1,2,0:T(8,128)} %all-gather.5.cloned.1.call-done, ...), kind=kOutput, calls=%fused_computation.223 | convolution fusion | flops 52034560 | bytes 2955280 | tf_op jit(solution)/shard_map/bhtc,hcv->bhtv/dot_general | solution.py:180
  215.9 12.3 %all_to_all.5 = bf16[4,128,512]{2,1,0:T(8,128)(2,1)S(1)} all-to-all(bf16[4,128,512]{2,1,0:T(8,128)(2,1)S(1)} %bitcast.217), channel_id=1, replica_groups=mesh['seq_hi'=8,'seq_lo'=8,'tp'=4] {'tp'}, dimensions={0} | all-to-all | bytes 1048576 | tf_op jit(solution)/shard_map/all_to_all | solution.py:192
  (169 shorter events, 78.3 us)
Async XLA Ops:
  6.5 207.9 %copy-start = (bf16[512,2048]{1,0:T(8,128)(2,1)S(1)}, bf16[512,2048]{1,0:T(8,128)(2,1)}, u32[]{:S(2)}) copy-start(bf16[512,2048]{1,0:T(8,128)(2,1)} %param.27) | copy-start | bytes 6291460
  6.5 23.3 %copy-start.5 = (f32[5,2048]{1,0:T(8,128)S(1)}, f32[5,2048]{1,0:T(8,128)}, u32[]{:S(2)}) copy-start(f32[5,2048]{1,0:T(8,128)} %param.19) | copy-start | bytes 122884
  6.5 106.5 %all-gather.5.cloned.1.call-start = ((), (), s32[]{:S(2)}) async-start(), calls=%async_computation.1 | async-start | bytes 2359296 | tf_op jit(solution)/shard_map/all_gather | solution.py:174
  22.6 7.0 %collective-permute-start = (bf16[1,2048]{1,0:T(2,128)(2,1)S(1)}, bf16[1,2048]{1,0:T(2,128)(2,1)S(1)}, u32[]{:S(2)}, u32[]{:S(2)}) collective-permute-start(bf16[1,2048]{1,0:T(2,128)(2,1)S(1)} %slice.347), channel_id=1, source_target_pairs={{0,4},{4,8},{8,12},{12,16},{16,20},{20,24},{24,28},{28,32},{32,36}... | collective-permute-start | bytes 12296 | tf_op jit(solution)/shard_map/ppermute | solution.py:24
  29.6 3.7 %copy-start.1 = (f32[128,2048]{1,0:T(8,128)S(1)}, f32[128,2048]{1,0:T(8,128)}, u32[]{:S(2)}) copy-start(f32[128,2048]{1,0:T(8,128)} %get-tuple-element.196) | copy-start | bytes 3145732
  33.2 6.5 %copy-start.4 = (bf16[2048,64]{0,1:T(8,128)(2,1)S(1)}, bf16[2048,64]{0,1:T(8,128)(2,1)}, u32[]{:S(2)}) copy-start(bf16[2048,64]{0,1:T(8,128)(2,1)} %param.21) | copy-start | bytes 786436
  33.2 6.5 %copy-start.6 = (bf16[64,512]{1,0:T(8,128)(2,1)S(1)}, bf16[64,512]{1,0:T(8,128)(2,1)}, u32[]{:S(2)}) copy-start(bf16[64,512]{1,0:T(8,128)(2,1)} %param.22) | copy-start | bytes 196612
  37.9 1.0 copy-start.3
  74.3 128.1 %all-gather.7.cloned.1.call-start = ((), (), s32[]{:S(2)}) async-start(), calls=%async_computation.2 | async-start | bytes 2359296 | tf_op jit(solution)/shard_map/all_gather | solution.py:178
  82.9 42.9 %copy-start.7 = (f32[512]{0:T(512)S(1)}, f32[512]{0:T(512)}, u32[]{:S(2)}) copy-start(f32[512]{0:T(512)} %param.24) | copy-start | bytes 6148
  209.3 5.1 %copy-start.8 = (f32[512]{0:T(512)S(1)}, f32[512]{0:T(512)}, u32[]{:S(2)}) copy-start(f32[512]{0:T(512)} %param.26) | copy-start | bytes 6148
  209.3 5.1 %copy-start.9 = (f32[512]{0:T(512)S(1)}, f32[512]{0:T(512)}, u32[]{:S(2)}) copy-start(f32[512]{0:T(512)} %param.25) | copy-start | bytes 6148
  214.1 14.2 %copy-start.2 = (bf16[128,512]{1,0:T(8,128)(2,1)S(1)}, bf16[128,512]{1,0:T(8,128)(2,1)}, u32[]{:S(2)}) copy-start(bf16[128,512]{1,0:T(8,128)(2,1)} %param.15) | copy-start | bytes 393220
Sparse Core Ops, SparseCore 0:
  74.4 38.5 all-gather.4
  125.9 76.4 all-gather.6

commit v4 on v3

--- a/solution.py
+++ b/solution.py
@@ -12,6 +12,11 @@
 
 
 SEQ = ("seq_hi", "seq_lo")
+
+
+def gather(block, axis):
+    copies = jnp.broadcast_to(block[None], (lax.axis_size(axis),) + block.shape)
+    return lax.all_to_all(copies, axis, 0, 0, tiled=True)
 
 
 def size_of(axes):
@@ -148,14 +153,15 @@
         jnp.float32(1.0),
     )
     decay_heads = decay_logarithm.reshape(rows, mixing_values_divided, CHANNELS_ONE_HEAD).transpose(1, 0, 2)
-    suffix_incl = jnp.flip(jnp.cumsum(jnp.flip(decay_heads, 1), axis=1), 1)
-    suffix_excl = jnp.concatenate([suffix_incl[:, 1:], jnp.zeros_like(suffix_incl[:, :1])], axis=1)
+    later = (jnp.arange(rows)[None, :] > jnp.arange(rows)[:, None]).astype(jnp.float32)
+    suffix_excl = jnp.einsum("sj,hjc->hsc", later, decay_heads, precision=highest)
+    decay_sum = jnp.sum(decay_heads, axis=1)
     in_tail = (segment == segment[rows - 1]).astype(jnp.float32)
     key_heads = key_rows.astype(jnp.float32).reshape(rows, mixing_values_divided, CHANNELS_ONE_HEAD)
     value_heads = value_rows.astype(jnp.float32).reshape(rows, mixing_values_divided, CHANNELS_ONE_HEAD)
     tail_keys = key_heads.transpose(1, 0, 2) * jnp.exp(suffix_excl) * in_tail[None, :, None]
     end_state = jnp.einsum("hsc,shv->hcv", tail_keys, value_heads, precision=highest)
-    decay_total = jnp.all(jnp.logical_not(is_start)).astype(jnp.float32) * jnp.exp(suffix_incl[:, 0])
+    decay_total = jnp.all(jnp.logical_not(is_start)).astype(jnp.float32) * jnp.exp(decay_sum)
     _, (outs, from_start) = lax.scan(block_step, init, inputs)
 
     packed = jnp.concatenate([end_state, decay_total[:, None, :]], axis=1)
@@ -171,11 +177,11 @@
         return state, decay
 
     low = lax.axis_index("seq_lo")
-    neighbours = lax.all_gather(packed, "seq_lo")
+    neighbours = gather(packed, "seq_lo")
     inner_state, inner_decay = fold(neighbours, low)
     group_state, group_decay = fold(neighbours, lax.axis_size("seq_lo"))
     group = jnp.concatenate([group_state, group_decay[:, None, :]], axis=1)
-    entering, _ = fold(lax.all_gather(group, "seq_hi"), lax.axis_index("seq_hi"))
+    entering, _ = fold(gather(group, "seq_hi"), lax.axis_index("seq_hi"))
     incoming = inner_decay[:, :, None] * entering + inner_state
     outs = outs + jnp.einsum("bhtc,hcv->bhtv", from_start, incoming, precision=highest)
     wkv = outs.transpose(0, 2, 1, 3).reshape(rows, mixing_values_divided, CHANNELS_ONE_HEAD)

time: 240 us -> 268 us (1.12)
  the two profiles are of different devices: /device:TPU:48 before, /device:TPU:8 now
where the time goes in v4:
time: 268 us; the launch traced here: 265 us
  local copies, waits for them, and re-layouts  83.3 us (31%)
  other arithmetic  57.9 us (22%)
  waiting for transfers between devices  39.7 us (15%)
  matrix products  36.5 us (14%)
  blocking collectives  26.2 us (10%)
  starting transfers between devices  17.5 us (7%)
  loops' own time  3.12 us (1%)
    all_to_all x2, waiting for transfers between devices, gather(): return lax.all_to_all(copies, axis, 0, 0, tiled=True)  39.4 us
    unnamed x60, local copies, waits for them, and re-layouts  27.3 us
    all_to_all x2, starting transfers between devices, gather(): return lax.all_to_all(copies, axis, 0, 0, tiled=True)  15.6 us
    dot_general x4, other arithmetic, block_step(): jnp.einsum('htc,hsc,htsc->hts', gating_rows_tile, query_array_tile, weigh...  13.8 us
    all_gather x1, blocking collectives, body(): full = lax.all_gather(tier_source_concatenated, 'tp', axis=1, tiled=True)  13.5 us
    all_to_all x1, blocking collectives, body(): pieces = lax.all_to_all(pieces, 'tp', 0, 0, tiled=True)  12.7 us
    mul x16, local copies, waits for them, and re-layouts, fold(): piece[:, CHANNELS_ONE_HEAD, :, None] * state + piece[:, :CHANNELS_ONE_HEAD]  10.9 us
    transpose x6, local copies, waits for them, and re-layouts, split_heads(): return values.astype(jnp.float32).reshape(blocks, block, mixing_values_di...  7.52 us
  transfers between devices with their start and end apart: 3, of which 2 were waited for; matrix products, arithmetic and copies ran while one was open for 37% of the time, Pallas kernels for 0%

profile of v4, /device:TPU:8, one launch (start us, length us, event | category | flops | bytes accessed | tf_op | source)
XLA Modules:
  0.0 265.3 jit_solution(1014636811761653934)
XLA Ops:
  0.0 13.5 %all_gather.3 = bf16[128,2048]{1,0:T(8,128)(2,1)S(1)} all-gather(bf16[128,512]{1,0:T(8,128)(2,1)} %param.15), channel_id=1, replica_groups=mesh['seq_hi'=8,'seq_lo'=8,'tp'=4] {'tp'}, dimensions={1}, use_global_device_ids=true | all-gather | bytes 655360 | tf_op jit(solution)/shard_map/all_gather | solution.py:59
  13.9 2.1 fusion.77
  16.1 1.9 collective-permute-start
  23.4 3.4 %add_convert_fusion = bf16[5,128,2048]{2,1,0:T(8,128)(2,1)} fusion(f32[5,2048]{1,0:T(8,128)S(1)} %copy-done.18, f32[128,2048]{1,0:T(8,128)S(1)} %convert_subtract_fusion.1, f32[128,2048]{1,0:T(8,128)} %get-tuple-element.196), kind=kLoop, calls=%fused_computation.59 | loop fusion | flops 3932160 | bytes 4759552 | tf_op jit(solution)/shard_map/convert_element_type | solution.py:72
  26.8 4.7 %fusion.76 = f32[4,128,512]{2,1,0:T(8,128)S(1)} fusion(bf16[4,2048,512]{2,1,0:T(8,128)(2,1)} %param.20, f32[5,2048]{1,0:T(8,128)S(1)} %copy-done.18, f32[128,2048]{1,0:T(8,128)S(1)} %convert_subtract_fusion.1, f32[128,2048]{1,0:T(8,128)S(1)} %copy-done.1), kind=kOutput, calls=%fused_computation.165 | convolution fusion | flops 1077673984 | bytes 11575296 | tf_op jit(solution)/shard_map/itd,ide->ite/dot_general | solution.py:75
  38.8 8.5 %all-to-all-start = ((f32[8,8,65,64]{2,3,1,0:T(8,128)}), f32[8,8,65,64]{2,3,1,0:T(8,128)}, u32[]{:S(2)}, u32[]{:S(2)}) async-start(f32[8,8,65,64]{2,3,1,0:T(8,128)} %broadcast_in_dim.33), calls=%async_computation | async-start | bytes 4194304 | tf_op jit(solution)/shard_map/all_to_all | solution.py:19
  50.8 1.9 reshape.287
  52.7 2.0 copy_bitcast_fusion
  54.7 2.4 copy_bitcast_fusion.2
  57.1 39.4 %all-to-all-done = f32[8,8,65,64]{2,3,1,0:T(8,128)} async-done(((f32[8,8,65,64]{2,3,1,0:T(8,128)}), f32[8,8,65,64]{2,3,1,0:T(8,128)}, u32[]{:S(2)}, u32[]{:S(2)}) %all-to-all-start) | async-done | bytes 1064992 | tf_op jit(solution)/shard_map/all_to_all | solution.py:19
  96.5 2.8 %fusion.80 = (f32[1,8,65,64]{2,3,1,0:T(8,128)}, f32[1,8,65,64]{2,3,1,0:T(8,128)}, f32[1,8,65,64]{2,3,1,0:T(8,128)}, f32[1,8,65,64]{2,3,1,0:T(8,128)}, f32[1,8,65...) fusion(f32[8,8,65,64]{2,3,1,0:T(8,128)} %all-to-all-done), kind=kLoop, calls=%fused_computation.168 | loop fusion | bytes 2129920 | tf_op jit(solution)/shard_map/slice | solution.py:174
  100.6 2.0 copy.251
  109.9 1.8 copy.256
  116.2 2.0 multiply_add_fusion
  120.8 2.5 broadcast_in_dim.35
  123.3 7.1 %all-to-all-start.1 = ((f32[8,8,65,64]{2,3,1,0:T(8,128)}), f32[8,8,65,64]{2,3,1,0:T(8,128)}, u32[]{:S(2)}, u32[]{:S(2)}) async-start(f32[8,8,65,64]{2,3,1,0:T(8,128)} %broadcast_in_dim.35), calls=%async_computation.1 | async-start | bytes 4194304 | tf_op jit(solution)/shard_map/all_to_all | solution.py:19
  130.4 84.7 %while.20 = (s32[]{:T(128)}, f32[8,64,64]{2,1,0:T(8,128)S(1)}, f32[8,64]{1,0:T(8,128)}, f32[]{:T(128)}, f32[4,8,32,64]{3,2,0,1:T(8,128)}, /*index=5*/f32[4,8,32,...) while((s32[]{:T(128)}, f32[8,64,64]{2,1,0:T(8,128)S(1)}, ...), condition=%wide.region_7.8_spmd.clone.clone, body=%wide.region_5.7_spmd.clone.clone.sunk | while | flops 41284548 | bytes 7641736 | solution.py:165
  138.5 3.4 %fusion.117 = f32[8,32,32]{1,2,0:T(8,128)S(1)} fusion(f32[8,32,32,64]{3,2,1,0:T(8,128)S(1)} %exponential_select_fusion.2, f32[8,64,32]{1,2,0:T(8,128)S(1)} %get-tuple-element.335, f32[8,64,32]{1,2,0:T(8,128)S(1)} %get-tuple-element.336), kind=kLoop, calls=%fused_computation.4.clone.1 | loop fusion | flops 1564672 | bytes 2260992 | tf_op jit(solution)/shard_map/while/body/eval_jaxpr/htc,hsc,htsc->hts/dot_general | solution.py:119
  159.9 3.4 %fusion.117 = f32[8,32,32]{1,2,0:T(8,128)S(1)} fusion(f32[8,32,32,64]{3,2,1,0:T(8,128)S(1)} %exponential_select_fusion.2, f32[8,64,32]{1,2,0:T(8,128)S(1)} %get-tuple-element.335, f32[8,64,32]{1,2,0:T(8,128)S(1)} %get-tuple-element.336), kind=kLoop, calls=%fused_computation.4.clone.1 | loop fusion | flops 1564672 | bytes 2260992 | tf_op jit(solution)/shard_map/while/body/eval_jaxpr/htc,hsc,htsc->hts/dot_general | solution.py:119
  181.2 3.4 %fusion.117 = f32[8,32,32]{1,2,0:T(8,128)S(1)} fusion(f32[8,32,32,64]{3,2,1,0:T(8,128)S(1)} %exponential_select_fusion.2, f32[8,64,32]{1,2,0:T(8,128)S(1)} %get-tuple-element.335, f32[8,64,32]{1,2,0:T(8,128)S(1)} %get-tuple-element.336), kind=kLoop, calls=%fused_computation.4.clone.1 | loop fusion | flops 1564672 | bytes 2260992 | tf_op jit(solution)/shard_map/while/body/eval_jaxpr/htc,hsc,htsc->hts/dot_general | solution.py:119
  202.5 3.4 %fusion.117 = f32[8,32,32]{1,2,0:T(8,128)S(1)} fusion(f32[8,32,32,64]{3,2,1,0:T(8,128)S(1)} %exponential_select_fusion.2, f32[8,64,32]{1,2,0:T(8,128)S(1)} %get-tuple-element.335, f32[8,64,32]{1,2,0:T(8,128)S(1)} %get-tuple-element.336), kind=kLoop, calls=%fused_computation.4.clone.1 | loop fusion | flops 1564672 | bytes 2260992 | tf_op jit(solution)/shard_map/while/body/eval_jaxpr/htc,hsc,htsc->hts/dot_general | solution.py:119
  216.6 3.0 %fusion.79 = (f32[1,8,65,64]{2,3,1,0:T(8,128)}, f32[1,8,65,64]{2,3,1,0:T(8,128)}, f32[1,8,65,64]{2,3,1,0:T(8,128)}, f32[1,8,65,64]{2,3,1,0:T(8,128)}, f32[1,8,65...) fusion(f32[8,8,65,64]{2,3,1,0:T(8,128)} %all-to-all-done.1), kind=kLoop, calls=%fused_computation.167 | loop fusion | bytes 2129920 | tf_op jit(solution)/shard_map/slice | solution.py:174
  245.1 3.1 %fusion.58 = f32[8,64,64,1]{2,0,1,3:T(8,128)S(1)} fusion(f32[8,65,64]{2,0,1:T(8,128)} %bitcast.296, f32[8,65,64]{2,0,1:T(8,128)} %bitcast.298, f32[8,65,64]{2,0,1:T(8,128)} %bitcast.300, f32[8,65,64]{2,0,1:T(8,128)} %bitcast.302, f32[8,65,64]{2,0,1:T(8,128)} %bitcast.304, f32[8,65,64]{2,0,1:T(8,128)} %bitcast.306, f32[8,65,64]{2,0,1:T(8,128)} %bitcast.308, ...), kind=kLoop, calls=%fused_computation.96 | loop fusion | flops 1572864 | bytes 2263056 | tf_op jit(solution)/shard_map/add | solution.py:185
  251.9 12.7 %all_to_all.15 = bf16[4,128,512]{2,1,0:T(8,128)(2,1)S(1)} all-to-all(bf16[4,128,512]{2,1,0:T(8,128)(2,1)S(1)} %bitcast.293), channel_id=1, replica_groups=mesh['seq_hi'=8,'seq_lo'=8,'tp'=4] {'tp'}, dimensions={0} | all-to-all | bytes 1048576 | tf_op jit(solution)/shard_map/all_to_all | solution.py:198
  (221 shorter events, 130.6 us)
Async XLA Ops:
  0.0 250.3 %copy-start = (bf16[512,2048]{1,0:T(8,128)(2,1)S(1)}, bf16[512,2048]{1,0:T(8,128)(2,1)}, u32[]{:S(2)}) copy-start(bf16[512,2048]{1,0:T(8,128)(2,1)} %param.27) | copy-start | bytes 6291460
  0.0 23.4 %copy-start.18 = (f32[5,2048]{1,0:T(8,128)S(1)}, f32[5,2048]{1,0:T(8,128)}, u32[]{:S(2)}) copy-start(f32[5,2048]{1,0:T(8,128)} %param.19) | copy-start | bytes 122884
  16.1 7.1 %collective-permute-start = (bf16[1,2048]{1,0:T(2,128)(2,1)S(1)}, bf16[1,2048]{1,0:T(2,128)(2,1)S(1)}, u32[]{:S(2)}, u32[]{:S(2)}) collective-permute-start(bf16[1,2048]{1,0:T(2,128)(2,1)S(1)} %slice.286), channel_id=1, source_target_pairs={{0,4},{4,8},{8,12},{12,16},{16,20},{20,24},{24,28},{28,32},{32,36}... | collective-permute-start | bytes 12296 | tf_op jit(solution)/shard_map/ppermute | solution.py:29
  22.9 3.9 %copy-start.1 = (f32[128,2048]{1,0:T(8,128)S(1)}, f32[128,2048]{1,0:T(8,128)}, u32[]{:S(2)}) copy-start(f32[128,2048]{1,0:T(8,128)} %get-tuple-element.196) | copy-start | bytes 3145732
  26.8 5.9 %copy-start.17 = (bf16[2048,64]{0,1:T(8,128)(2,1)S(1)}, bf16[2048,64]{0,1:T(8,128)(2,1)}, u32[]{:S(2)}) copy-start(bf16[2048,64]{0,1:T(8,128)(2,1)} %param.21) | copy-start | bytes 786436
  26.8 5.9 %copy-start.19 = (bf16[64,512]{1,0:T(8,128)(2,1)S(1)}, bf16[64,512]{1,0:T(8,128)(2,1)}, u32[]{:S(2)}) copy-start(bf16[64,512]{1,0:T(8,128)(2,1)} %param.22) | copy-start | bytes 196612
  38.8 57.6 %all-to-all-start = ((f32[8,8,65,64]{2,3,1,0:T(8,128)}), f32[8,8,65,64]{2,3,1,0:T(8,128)}, u32[]{:S(2)}, u32[]{:S(2)}) async-start(f32[8,8,65,64]{2,3,1,0:T(8,128)} %broadcast_in_dim.33), calls=%async_computation | async-start | bytes 4194304 | tf_op jit(solution)/shard_map/all_to_all | solution.py:19
  100.6 22.6 %copy-start.2 = (f32[1,8,65,64]{3,1,2,0:T(8,128)}, f32[1,8,65,64]{3,1,2,0:T(8,128)S(1)}, u32[]{:S(2)}) copy-start(f32[1,8,65,64]{3,1,2,0:T(8,128)S(1)} %copy.250) | copy-start | bytes 399364
  112.6 10.7 %copy-start.11 = (f32[8,64]{0,1:T(8,128)}, f32[8,64]{0,1:T(8,128)S(1)}, u32[]{:S(2)}) copy-start(f32[8,64]{0,1:T(8,128)S(1)} %copy.203) | copy-start | bytes 6148
  112.7 10.6 %copy-start.13 = (f32[8,64]{0,1:T(8,128)}, f32[8,64]{0,1:T(8,128)S(1)}, u32[]{:S(2)}) copy-start(f32[8,64]{0,1:T(8,128)S(1)} %copy.204) | copy-start | bytes 6148
  112.8 10.5 %copy-start.15 = (f32[8,64]{0,1:T(8,128)}, f32[8,64]{0,1:T(8,128)S(1)}, u32[]{:S(2)}) copy-start(f32[8,64]{0,1:T(8,128)S(1)} %copy.205) | copy-start | bytes 6148
  123.3 93.3 %all-to-all-start.1 = ((f32[8,8,65,64]{2,3,1,0:T(8,128)}), f32[8,8,65,64]{2,3,1,0:T(8,128)}, u32[]{:S(2)}, u32[]{:S(2)}) async-start(f32[8,8,65,64]{2,3,1,0:T(8,128)} %broadcast_in_dim.35), calls=%async_computation.1 | async-start | bytes 4194304 | tf_op jit(solution)/shard_map/all_to_all | solution.py:19
  132.3 3.7 %copy-start.20 = (f32[32]{0:T(128)}, f32[32]{0:T(128)S(1)}, u32[]{:S(2)}) copy-start(f32[32]{0:T(128)S(1)} %get-tuple-element.333) | copy-start | bytes 388 | tf_op jit(solution)/shard_map/while
  153.0 4.4 %copy-start.20 = (f32[32]{0:T(128)}, f32[32]{0:T(128)S(1)}, u32[]{:S(2)}) copy-start(f32[32]{0:T(128)S(1)} %get-tuple-element.333) | copy-start | bytes 388 | tf_op jit(solution)/shard_map/while
  174.4 4.3 %copy-start.20 = (f32[32]{0:T(128)}, f32[32]{0:T(128)S(1)}, u32[]{:S(2)}) copy-start(f32[32]{0:T(128)S(1)} %get-tuple-element.333) | copy-start | bytes 388 | tf_op jit(solution)/shard_map/while
  195.7 4.3 %copy-start.20 = (f32[32]{0:T(128)}, f32[32]{0:T(128)S(1)}, u32[]{:S(2)}) copy-start(f32[32]{0:T(128)S(1)} %get-tuple-element.333) | copy-start | bytes 388 | tf_op jit(solution)/shard_map/while
  216.5 28.5 %copy-start.3 = (f32[1,8,65,64]{3,1,2,0:T(8,128)S(1)}, f32[1,8,65,64]{3,1,2,0:T(8,128)}, u32[]{:S(2)}) copy-start(f32[1,8,65,64]{3,1,2,0:T(8,128)} %copy-done.2) | copy-start | bytes 399364
  216.5 28.5 %copy-start.4 = (f32[1,8,65,64]{3,1,2,0:T(8,128)S(1)}, f32[1,8,65,64]{3,1,2,0:T(8,128)}, u32[]{:S(2)}) copy-start(f32[1,8,65,64]{3,1,2,0:T(8,128)} %copy.251) | copy-start | bytes 399364
  216.5 28.5 %copy-start.5 = (f32[1,8,65,64]{3,1,2,0:T(8,128)S(1)}, f32[1,8,65,64]{3,1,2,0:T(8,128)}, u32[]{:S(2)}) copy-start(f32[1,8,65,64]{3,1,2,0:T(8,128)} %copy.252) | copy-start | bytes 399364
  216.5 28.5 %copy-start.6 = (f32[1,8,65,64]{3,1,2,0:T(8,128)S(1)}, f32[1,8,65,64]{3,1,2,0:T(8,128)}, u32[]{:S(2)}) copy-start(f32[1,8,65,64]{3,1,2,0:T(8,128)} %copy.253) | copy-start | bytes 399364
  216.5 28.5 %copy-start.12 = (f32[8,64]{0,1:T(8,128)S(1)}, f32[8,64]{0,1:T(8,128)}, u32[]{:S(2)}) copy-start(f32[8,64]{0,1:T(8,128)} %copy-done.11) | copy-start | bytes 6148
  216.5 28.5 %copy-start.14 = (f32[8,64]{0,1:T(8,128)S(1)}, f32[8,64]{0,1:T(8,128)}, u32[]{:S(2)}) copy-start(f32[8,64]{0,1:T(8,128)} %copy-done.13) | copy-start | bytes 6148
  216.5 28.5 %copy-start.16 = (f32[8,64]{0,1:T(8,128)S(1)}, f32[8,64]{0,1:T(8,128)}, u32[]{:S(2)}) copy-start(f32[8,64]{0,1:T(8,128)} %copy-done.15) | copy-start | bytes 6148
  249.9 14.7 %copy-start.9 = (bf16[128,512]{1,0:T(8,128)(2,1)S(1)}, bf16[128,512]{1,0:T(8,128)(2,1)}, u32[]{:S(2)}) copy-start(bf16[128,512]{1,0:T(8,128)(2,1)} %param.15) | copy-start | bytes 393220
  (5 other events, 11.7 us)

commit v5 on v4

--- a/solution.py
+++ b/solution.py
@@ -12,11 +12,6 @@
 
 
 SEQ = ("seq_hi", "seq_lo")
-
-
-def gather(block, axis):
-    copies = jnp.broadcast_to(block[None], (lax.axis_size(axis),) + block.shape)
-    return lax.all_to_all(copies, axis, 0, 0, tiled=True)
 
 
 def size_of(axes):
@@ -166,23 +161,23 @@
 
     packed = jnp.concatenate([end_state, decay_total[:, None, :]], axis=1)
 
-    def fold(gathered, count):
-        state = jnp.zeros_like(end_state)
-        decay = jnp.ones_like(decay_total)
-        for index in range(gathered.shape[0]):
-            take = index < count
-            piece = gathered[index]
-            state = jnp.where(take, piece[:, CHANNELS_ONE_HEAD, :, None] * state + piece[:, :CHANNELS_ONE_HEAD], state)
-            decay = jnp.where(take, piece[:, CHANNELS_ONE_HEAD] * decay, decay)
-        return state, decay
-
-    low = lax.axis_index("seq_lo")
-    neighbours = gather(packed, "seq_lo")
-    inner_state, inner_decay = fold(neighbours, low)
-    group_state, group_decay = fold(neighbours, lax.axis_size("seq_lo"))
-    group = jnp.concatenate([group_state, group_decay[:, None, :]], axis=1)
-    entering, _ = fold(gather(group, "seq_hi"), lax.axis_index("seq_hi"))
-    incoming = inner_decay[:, :, None] * entering + inner_state
+    def fold(pieces):
+        state, decay = pieces[0][:, :CHANNELS_ONE_HEAD], pieces[0][:, CHANNELS_ONE_HEAD:]
+        for piece in pieces[1:]:
+            piece_decay = piece[:, CHANNELS_ONE_HEAD:]
+            state = jnp.transpose(piece_decay, (0, 2, 1)) * state + piece[:, :CHANNELS_ONE_HEAD]
+            decay = piece_decay * decay
+        return jnp.concatenate([state, decay], axis=1)
+
+    devices = size_of(SEQ)
+    radix = 4
+    prefix = fold([from_behind(packed, SEQ, distance) for distance in range(radix, 0, -1)])
+    window = radix
+    while window < devices:
+        behind = [from_behind(prefix, SEQ, window * step) for step in range(radix - 1, 0, -1)]
+        prefix = fold(behind + [prefix])
+        window *= radix
+    incoming = prefix[:, :CHANNELS_ONE_HEAD]
     outs = outs + jnp.einsum("bhtc,hcv->bhtv", from_start, incoming, precision=highest)
     wkv = outs.transpose(0, 2, 1, 3).reshape(rows, mixing_values_divided, CHANNELS_ONE_HEAD)
     mean = jnp.mean(wkv, axis=-1, keepdims=True)

time: 268 us -> 240 us (0.90)
  the two profiles are of different devices: /device:TPU:8 before, /device:TPU:24 now
where the time goes in v5:
time: 240 us; the launch traced here: 238 us
  other arithmetic  52.3 us (22%)
  waiting for transfers between devices  48.3 us (20%)
  matrix products  39.8 us (17%)
  local copies, waits for them, and re-layouts  36.3 us (15%)
  starting transfers between devices  31.6 us (13%)
  blocking collectives  26 us (11%)
  loops' own time  2.87 us (1%)
    ppermute x11, waiting for transfers between devices, from_behind(): return lax.ppermute(block, axis, route)  48.3 us
    ppermute x11, starting transfers between devices, from_behind(): return lax.ppermute(block, axis, route)  31.6 us
    dot_general x4, other arithmetic, block_step(): jnp.einsum('htc,hsc,htsc->hts', gating_rows_tile, query_array_tile, weigh...  13.8 us
    all_gather x1, blocking collectives, body(): full = lax.all_gather(tier_source_concatenated, 'tp', axis=1, tiled=True)  13.5 us
    all_to_all x1, blocking collectives, body(): pieces = lax.all_to_all(pieces, 'tp', 0, 0, tiled=True)  12.5 us
    transpose x6, local copies, waits for them, and re-layouts, split_heads(): return values.astype(jnp.float32).reshape(blocks, block, mixing_values_di...  7.38 us
    dot_general x4, matrix products, block_step(): jnp.einsum('htc,hcv->htv', carried, running_recurrence_array, precision=h...  6.72 us
    dynamic_update_slice x4, other arithmetic, body(): _, (outs, from_start) = lax.scan(block_step, init, inputs)  6.64 us
  transfers between devices with their start and end apart: 11, of which 6 were waited for; matrix products, arithmetic and copies ran while one was open for 38% of the time, Pallas kernels for 0%

profile of v5, /device:TPU:24, one launch (start us, length us, event | category | flops | bytes accessed | tf_op | source)
XLA Modules:
  0.0 238.4 jit_solution(10400541798867202281)
XLA Ops:
  0.0 13.5 %all_gather.3 = bf16[128,2048]{1,0:T(8,128)(2,1)S(1)} all-gather(bf16[128,512]{1,0:T(8,128)(2,1)} %param.15), channel_id=1, replica_groups=mesh['seq_hi'=8,'seq_lo'=8,'tp'=4] {'tp'}, dimensions={1}, use_global_device_ids=true | all-gather | bytes 655360 | tf_op jit(solution)/shard_map/all_gather | solution.py:54
  13.9 2.2 fusion.86
  25.9 3.3 %add_convert_fusion = bf16[5,128,2048]{2,1,0:T(8,128)(2,1)} fusion(f32[5,2048]{1,0:T(8,128)S(1)} %copy-done.6, f32[128,2048]{1,0:T(8,128)S(1)} %convert_subtract_fusion.1, f32[128,2048]{1,0:T(8,128)} %get-tuple-element.200), kind=kLoop, calls=%fused_computation.59 | loop fusion | flops 3932160 | bytes 4759552 | tf_op jit(solution)/shard_map/convert_element_type | solution.py:67
  29.3 2.4 %fusion.49 = f32[128,512]{1,0:T(8,128)} fusion(bf16[64,512]{1,0:T(8,128)(2,1)S(1)} %copy-done.7, bf16[2048,64]{0,1:T(8,128)(2,1)} %param.21, bf16[5,128,2048]{2,1,0:T(8,128)(2,1)} %add_convert_fusion, f32[512]{0:T(512)S(1)} %neg.8), kind=kOutput, calls=%fused_computation.73 | convolution fusion | flops 42016768 | bytes 1116160 | tf_op jit(solution)/shard_map/dot_general | solution.py:81
  35.4 5.0 %fusion.81 = f32[4,128,512]{2,1,0:T(8,128)S(1)} fusion(bf16[4,2048,512]{2,1,0:T(8,128)(2,1)} %param.20, f32[5,2048]{1,0:T(8,128)S(1)} %copy-done.6, f32[128,2048]{1,0:T(8,128)} %copy-done.1, f32[128,2048]{1,0:T(8,128)S(1)} %copy-done.2), kind=kOutput, calls=%fused_computation.154 | convolution fusion | flops 1077673984 | bytes 11575296 | tf_op jit(solution)/shard_map/itd,ide->ite/dot_general | solution.py:70
  48.6 3.9 %collective-permute-start.1 = (f32[8,65,64]{1,2,0:T(8,128)}, f32[8,65,64]{1,2,0:T(8,128)S(1)}, u32[]{:S(2)}, u32[]{:S(2)}) collective-permute-start(f32[8,65,64]{1,2,0:T(8,128)} %pad_maximum_fusion), channel_id=1, source_target_pairs={{0,4},{4,8},{8,12},{12,16},{16,20},{20,24},{24,28},{28,32},{32,36}... | collective-permute-start | bytes 399368 | tf_op jit(solution)/shard_map/ppermute | solution.py:24
  52.5 3.8 %collective-permute-start.2 = (f32[8,65,64]{1,2,0:T(8,128)}, f32[8,65,64]{1,2,0:T(8,128)}, u32[]{:S(2)}, u32[]{:S(2)}) collective-permute-start(f32[8,65,64]{1,2,0:T(8,128)} %pad_maximum_fusion), channel_id=1, source_target_pairs={{0,8},{4,12},{8,16},{12,20},{16,24},{20,28},{24,32},{28,36},{32,40... | collective-permute-start | bytes 399368 | tf_op jit(solution)/shard_map/ppermute | solution.py:24
  56.3 3.2 %collective-permute-start.3 = (f32[8,65,64]{1,2,0:T(8,128)}, f32[8,65,64]{1,2,0:T(8,128)}, u32[]{:S(2)}, u32[]{:S(2)}) collective-permute-start(f32[8,65,64]{1,2,0:T(8,128)} %pad_maximum_fusion), channel_id=1, source_target_pairs={{0,12},{4,16},{8,20},{12,24},{16,28},{20,32},{24,36},{28,40},{32,4... | collective-permute-start | bytes 399368 | tf_op jit(solution)/shard_map/ppermute | solution.py:24
  59.5 5.5 %collective-permute-start.4 = (f32[8,65,64]{1,2,0:T(8,128)}, f32[8,65,64]{1,2,0:T(8,128)}, u32[]{:S(2)}, u32[]{:S(2)}) collective-permute-start(f32[8,65,64]{1,2,0:T(8,128)} %pad_maximum_fusion), channel_id=1, source_target_pairs={{0,16},{4,20},{8,24},{12,28},{16,32},{20,36},{24,40},{28,44},{32,4... | collective-permute-start | bytes 399368 | tf_op jit(solution)/shard_map/ppermute | solution.py:24
  65.0 2.3 copy_bitcast_fusion.2
  69.3 7.2 %collective-permute-done.3 = f32[8,65,64]{1,2,0:T(8,128)} collective-permute-done((f32[8,65,64]{1,2,0:T(8,128)}, f32[8,65,64]{1,2,0:T(8,128)}, u32[]{:S(2)}, u32[]{:S(2)}) %collective-permute-start.3) | collective-permute-done | bytes 133152 | tf_op jit(solution)/shard_map/ppermute | solution.py:24
  76.5 10.6 %collective-permute-done.4 = f32[8,65,64]{1,2,0:T(8,128)} collective-permute-done((f32[8,65,64]{1,2,0:T(8,128)}, f32[8,65,64]{1,2,0:T(8,128)}, u32[]{:S(2)}, u32[]{:S(2)}) %collective-permute-start.4) | collective-permute-done | bytes 133152 | tf_op jit(solution)/shard_map/ppermute | solution.py:24
  92.2 5.4 %collective-permute-start.6 = (f32[8,65,64]{1,2,0:T(8,128)S(1)}, f32[8,65,64]{1,2,0:T(8,128)S(1)}, u32[]{:S(2)}, u32[]{:S(2)}) collective-permute-start(f32[8,65,64]{1,2,0:T(8,128)S(1)} %pad_maximum_fusion.1), channel_id=1, source_target_pairs={{0,32},{4,36},{8,40},{12,44},{16,48},{20,52},{24,56},{28,60},{32,6... | collective-permute-start | bytes 399368 | tf_op jit(solution)/shard_map/ppermute | solution.py:24
  101.5 3.8 %collective-permute-done.5 = f32[8,65,64]{1,2,0:T(8,128)S(1)} collective-permute-done((f32[8,65,64]{1,2,0:T(8,128)S(1)}, f32[8,65,64]{1,2,0:T(8,128)S(1)}, u32[]{:S(2)}, u32[]{:S(2)}) %collective-permute-start.5) | collective-permute-done | bytes 133152 | tf_op jit(solution)/shard_map/ppermute | solution.py:24
  105.3 13.9 %collective-permute-done.6 = f32[8,65,64]{1,2,0:T(8,128)S(1)} collective-permute-done((f32[8,65,64]{1,2,0:T(8,128)S(1)}, f32[8,65,64]{1,2,0:T(8,128)S(1)}, u32[]{:S(2)}, u32[]{:S(2)}) %collective-permute-start.6) | collective-permute-done | bytes 133152 | tf_op jit(solution)/shard_map/ppermute | solution.py:24
  119.2 2.8 %collective-permute-done.7 = f32[8,65,64]{1,2,0:T(8,128)S(1)} collective-permute-done((f32[8,65,64]{1,2,0:T(8,128)S(1)}, f32[8,65,64]{1,2,0:T(8,128)S(1)}, u32[]{:S(2)}, u32[]{:S(2)}) %collective-permute-start.7) | collective-permute-done | bytes 133152 | tf_op jit(solution)/shard_map/ppermute | solution.py:24
  126.7 79.5 %while.20 = (s32[]{:T(128)}, f32[8,64,64]{2,1,0:T(8,128)S(1)}, f32[8,64]{1,0:T(8,128)S(1)}, f32[]{:T(128)}, f32[4,8,32,64]{3,2,0,1:T(8,128)}, /*index=5*/f32[4,8...) while((s32[]{:T(128)}, f32[8,64,64]{2,1,0:T(8,128)S(1)}, ...), condition=%wide.region_7.8_spmd.clone.clone, body=%wide.region_5.7_spmd.clone.clone.sunk | while | flops 41284548 | bytes 7640734 | solution.py:160
  134.2 3.4 %fusion.124 = f32[8,32,32]{1,2,0:T(8,128)S(1)} fusion(f32[8,32,32,64]{3,2,1,0:T(8,128)S(1)} %exponential_select_fusion.2, f32[8,64,32]{1,2,0:T(8,128)S(1)} %get-tuple-element.319, f32[8,64,32]{1,2,0:T(8,128)S(1)} %get-tuple-element.320), kind=kLoop, calls=%fused_computation.4.clone.1 | loop fusion | flops 1564672 | bytes 2260992 | tf_op jit(solution)/shard_map/while/body/eval_jaxpr/htc,hsc,htsc->hts/dot_general | solution.py:114
  154.0 3.4 %fusion.124 = f32[8,32,32]{1,2,0:T(8,128)S(1)} fusion(f32[8,32,32,64]{3,2,1,0:T(8,128)S(1)} %exponential_select_fusion.2, f32[8,64,32]{1,2,0:T(8,128)S(1)} %get-tuple-element.319, f32[8,64,32]{1,2,0:T(8,128)S(1)} %get-tuple-element.320), kind=kLoop, calls=%fused_computation.4.clone.1 | loop fusion | flops 1564672 | bytes 2260992 | tf_op jit(solution)/shard_map/while/body/eval_jaxpr/htc,hsc,htsc->hts/dot_general | solution.py:114
  173.9 3.4 %fusion.124 = f32[8,32,32]{1,2,0:T(8,128)S(1)} fusion(f32[8,32,32,64]{3,2,1,0:T(8,128)S(1)} %exponential_select_fusion.2, f32[8,64,32]{1,2,0:T(8,128)S(1)} %get-tuple-element.319, f32[8,64,32]{1,2,0:T(8,128)S(1)} %get-tuple-element.320), kind=kLoop, calls=%fused_computation.4.clone.1 | loop fusion | flops 1564672 | bytes 2260992 | tf_op jit(solution)/shard_map/while/body/eval_jaxpr/htc,hsc,htsc->hts/dot_general | solution.py:114
  193.8 3.4 %fusion.124 = f32[8,32,32]{1,2,0:T(8,128)S(1)} fusion(f32[8,32,32,64]{3,2,1,0:T(8,128)S(1)} %exponential_select_fusion.2, f32[8,64,32]{1,2,0:T(8,128)S(1)} %get-tuple-element.319, f32[8,64,32]{1,2,0:T(8,128)S(1)} %get-tuple-element.320), kind=kLoop, calls=%fused_computation.4.clone.1 | loop fusion | flops 1564672 | bytes 2260992 | tf_op jit(solution)/shard_map/while/body/eval_jaxpr/htc,hsc,htsc->hts/dot_general | solution.py:114
  210.0 10.0 %collective-permute-done.10 = f32[8,65,64]{1,2,0:T(8,128)S(1)} collective-permute-done((f32[8,65,64]{1,2,0:T(8,128)}, f32[8,65,64]{1,2,0:T(8,128)S(1)}, u32[]{:S(2)}, u32[]{:S(2)}) %collective-permute-start.10) | collective-permute-done | bytes 133152 | tf_op jit(solution)/shard_map/ppermute | solution.py:24
  220.0 2.2 fusion.88
  225.1 12.5 %all_to_all.5 = bf16[4,128,512]{2,1,0:T(8,128)(2,1)S(1)} all-to-all(bf16[4,128,512]{2,1,0:T(8,128)(2,1)S(1)} %bitcast.202), channel_id=1, replica_groups=mesh['seq_hi'=8,'seq_lo'=8,'tp'=4] {'tp'}, dimensions={0} | all-to-all | bytes 1048576 | tf_op jit(solution)/shard_map/all_to_all | solution.py:193
  (172 shorter events, 107.3 us)
Async XLA Ops:
  0.0 223.6 %copy-start = (bf16[512,2048]{1,0:T(8,128)(2,1)S(1)}, bf16[512,2048]{1,0:T(8,128)(2,1)}, u32[]{:S(2)}) copy-start(bf16[512,2048]{1,0:T(8,128)(2,1)} %param.27) | copy-start | bytes 6291460
  0.0 25.9 %copy-start.6 = (f32[5,2048]{1,0:T(8,128)S(1)}, f32[5,2048]{1,0:T(8,128)}, u32[]{:S(2)}) copy-start(f32[5,2048]{1,0:T(8,128)} %param.19) | copy-start | bytes 122884
  13.9 15.4 %copy-start.7 = (bf16[64,512]{1,0:T(8,128)(2,1)S(1)}, bf16[64,512]{1,0:T(8,128)(2,1)}, u32[]{:S(2)}) copy-start(bf16[64,512]{1,0:T(8,128)(2,1)} %param.22) | copy-start | bytes 196612
  16.1 8.6 %collective-permute-start = (bf16[1,2048]{1,0:T(2,128)(2,1)S(1)}, bf16[1,2048]{1,0:T(2,128)(2,1)S(1)}, u32[]{:S(2)}, u32[]{:S(2)}) collective-permute-start(bf16[1,2048]{1,0:T(2,128)(2,1)S(1)} %slice.130), channel_id=1, source_target_pairs={{0,4},{4,8},{8,12},{12,16},{16,20},{20,24},{24,28},{28,32},{32,36}... | collective-permute-start | bytes 12296 | tf_op jit(solution)/shard_map/ppermute | solution.py:24
  25.0 10.4 %copy-start.2 = (f32[128,2048]{1,0:T(8,128)S(1)}, f32[128,2048]{1,0:T(8,128)}, u32[]{:S(2)}) copy-start(f32[128,2048]{1,0:T(8,128)} %get-tuple-element.200) | copy-start | bytes 3145732
  35.4 9.9 %copy-start.11 = (f32[128]{0:T(128)S(1)}, f32[128]{0:T(128)}, u32[]{:S(2)}) copy-start(f32[128]{0:T(128)} %compare_convert_fusion.2) | copy-start | bytes 1540
  41.4 23.7 %copy-start.3 = (f32[4,32,8,64]{3,2,1,0:T(8,128)S(1)}, f32[4,32,8,64]{3,2,1,0:T(8,128)}, u32[]{:S(2)}) copy-start(f32[4,32,8,64]{3,2,1,0:T(8,128)} %reshape.216) | copy-start | bytes 786436
  48.6 20.7 %collective-permute-start.1 = (f32[8,65,64]{1,2,0:T(8,128)}, f32[8,65,64]{1,2,0:T(8,128)S(1)}, u32[]{:S(2)}, u32[]{:S(2)}) collective-permute-start(f32[8,65,64]{1,2,0:T(8,128)} %pad_maximum_fusion), channel_id=1, source_target_pairs={{0,4},{4,8},{8,12},{12,16},{16,20},{20,24},{24,28},{28,32},{32,36}... | collective-permute-start | bytes 399368 | tf_op jit(solution)/shard_map/ppermute | solution.py:24
  52.5 16.8 %collective-permute-start.2 = (f32[8,65,64]{1,2,0:T(8,128)}, f32[8,65,64]{1,2,0:T(8,128)}, u32[]{:S(2)}, u32[]{:S(2)}) collective-permute-start(f32[8,65,64]{1,2,0:T(8,128)} %pad_maximum_fusion), channel_id=1, source_target_pairs={{0,8},{4,12},{8,16},{12,20},{16,24},{20,28},{24,32},{28,36},{32,40... | collective-permute-start | bytes 399368 | tf_op jit(solution)/shard_map/ppermute | solution.py:24
  56.3 20.2 %collective-permute-start.3 = (f32[8,65,64]{1,2,0:T(8,128)}, f32[8,65,64]{1,2,0:T(8,128)}, u32[]{:S(2)}, u32[]{:S(2)}) collective-permute-start(f32[8,65,64]{1,2,0:T(8,128)} %pad_maximum_fusion), channel_id=1, source_target_pairs={{0,12},{4,16},{8,20},{12,24},{16,28},{20,32},{24,36},{28,40},{32,4... | collective-permute-start | bytes 399368 | tf_op jit(solution)/shard_map/ppermute | solution.py:24
  59.5 27.6 %collective-permute-start.4 = (f32[8,65,64]{1,2,0:T(8,128)}, f32[8,65,64]{1,2,0:T(8,128)}, u32[]{:S(2)}, u32[]{:S(2)}) collective-permute-start(f32[8,65,64]{1,2,0:T(8,128)} %pad_maximum_fusion), channel_id=1, source_target_pairs={{0,16},{4,20},{8,24},{12,28},{16,32},{20,36},{24,40},{28,44},{32,4... | collective-permute-start | bytes 399368 | tf_op jit(solution)/shard_map/ppermute | solution.py:24
  90.2 15.0 %collective-permute-start.5 = (f32[8,65,64]{1,2,0:T(8,128)S(1)}, f32[8,65,64]{1,2,0:T(8,128)S(1)}, u32[]{:S(2)}, u32[]{:S(2)}) collective-permute-start(f32[8,65,64]{1,2,0:T(8,128)S(1)} %pad_maximum_fusion.1), channel_id=1, source_target_pairs={{0,16},{4,20},{8,24},{12,28},{16,32},{20,36},{24,40},{28,44},{32,4... | collective-permute-start | bytes 399368 | tf_op jit(solution)/shard_map/ppermute | solution.py:24
  92.2 27.0 %collective-permute-start.6 = (f32[8,65,64]{1,2,0:T(8,128)S(1)}, f32[8,65,64]{1,2,0:T(8,128)S(1)}, u32[]{:S(2)}, u32[]{:S(2)}) collective-permute-start(f32[8,65,64]{1,2,0:T(8,128)S(1)} %pad_maximum_fusion.1), channel_id=1, source_target_pairs={{0,32},{4,36},{8,40},{12,44},{16,48},{20,52},{24,56},{28,60},{32,6... | collective-permute-start | bytes 399368 | tf_op jit(solution)/shard_map/ppermute | solution.py:24
  97.5 24.5 %collective-permute-start.7 = (f32[8,65,64]{1,2,0:T(8,128)S(1)}, f32[8,65,64]{1,2,0:T(8,128)S(1)}, u32[]{:S(2)}, u32[]{:S(2)}) collective-permute-start(f32[8,65,64]{1,2,0:T(8,128)S(1)} %pad_maximum_fusion.1), channel_id=1, source_target_pairs={{0,48},{4,52},{8,56},{12,60},{16,64},{20,68},{24,72},{28,76},{32,8... | collective-permute-start | bytes 399368 | tf_op jit(solution)/shard_map/ppermute | solution.py:24
  124.0 84.8 %collective-permute-start.8 = (f32[8,65,64]{1,2,0:T(8,128)}, f32[8,65,64]{1,2,0:T(8,128)}, u32[]{:S(2)}, u32[]{:S(2)}) collective-permute-start(f32[8,65,64]{1,2,0:T(8,128)} %pad_maximum_fusion.2), channel_id=1, source_target_pairs={{0,64},{4,68},{8,72},{12,76},{16,80},{20,84},{24,88},{28,92},{32,9... | collective-permute-start | bytes 399368 | tf_op jit(solution)/shard_map/ppermute | solution.py:24
  125.2 82.3 %collective-permute-start.9 = (f32[8,65,64]{1,2,0:T(8,128)}, f32[8,65,64]{1,2,0:T(8,128)}, u32[]{:S(2)}, u32[]{:S(2)}) collective-permute-start(f32[8,65,64]{1,2,0:T(8,128)} %pad_maximum_fusion.2), channel_id=1, source_target_pairs={{0,128},{4,132},{8,136},{12,140},{16,144},{20,148},{24,152},{28,15... | collective-permute-start | bytes 399368 | tf_op jit(solution)/shard_map/ppermute | solution.py:24
  128.7 3.0 %copy-start.8 = (f32[32]{0:T(128)}, f32[32]{0:T(128)S(1)}, u32[]{:S(2)}) copy-start(f32[32]{0:T(128)S(1)} %get-tuple-element.317) | copy-start | bytes 388 | tf_op jit(solution)/shard_map/while
  148.6 3.0 %copy-start.8 = (f32[32]{0:T(128)}, f32[32]{0:T(128)S(1)}, u32[]{:S(2)}) copy-start(f32[32]{0:T(128)S(1)} %get-tuple-element.317) | copy-start | bytes 388 | tf_op jit(solution)/shard_map/while
  168.5 3.0 %copy-start.8 = (f32[32]{0:T(128)}, f32[32]{0:T(128)S(1)}, u32[]{:S(2)}) copy-start(f32[32]{0:T(128)S(1)} %get-tuple-element.317) | copy-start | bytes 388 | tf_op jit(solution)/shard_map/while
  188.3 3.0 %copy-start.8 = (f32[32]{0:T(128)}, f32[32]{0:T(128)S(1)}, u32[]{:S(2)}) copy-start(f32[32]{0:T(128)S(1)} %get-tuple-element.317) | copy-start | bytes 388 | tf_op jit(solution)/shard_map/while
  206.2 17.4 %copy-start.9 = (f32[512]{0:T(512)S(1)}, f32[512]{0:T(512)}, u32[]{:S(2)}) copy-start(f32[512]{0:T(512)} %param.26) | copy-start | bytes 6148
  206.2 17.4 %copy-start.10 = (f32[512]{0:T(512)S(1)}, f32[512]{0:T(512)}, u32[]{:S(2)}) copy-start(f32[512]{0:T(512)} %param.25) | copy-start | bytes 6148
  206.2 13.8 %collective-permute-start.10 = (f32[8,65,64]{1,2,0:T(8,128)}, f32[8,65,64]{1,2,0:T(8,128)S(1)}, u32[]{:S(2)}, u32[]{:S(2)}) collective-permute-start(f32[8,65,64]{1,2,0:T(8,128)} %pad_maximum_fusion.2), channel_id=1, source_target_pairs={{0,192},{4,196},{8,200},{12,204},{16,208},{20,212},{24,216},{28,22... | collective-permute-start | bytes 399368 | tf_op jit(solution)/shard_map/ppermute | solution.py:24
  223.2 14.4 %copy-start.4 = (bf16[128,512]{1,0:T(8,128)(2,1)S(1)}, bf16[128,512]{1,0:T(8,128)(2,1)}, u32[]{:S(2)}) copy-start(bf16[128,512]{1,0:T(8,128)(2,1)} %param.15) | copy-start | bytes 393220
  (2 other events, 2.0 us)

commit v6 on v1

v6 whole, which is shorter than its diff:
```python
import math

import jax
import jax.numpy as jnp
from jax import lax
from jax.sharding import PartitionSpec as P

CHANNELS_ONE_HEAD = 64


highest = lax.Precision.HIGHEST


SEQ = ("seq_hi", "seq_lo")


def size_of(axes):
    return math.prod(lax.axis_size(axis) for axis in axes)


def from_behind(block, axis, distance):
    devices = range(size_of(axis))
    route = [(i - distance, i) for i in devices if i - distance in devices]
    return lax.ppermute(block, axis, route)


def layer_norm(rows, gain, bias, eps):
    mean = jnp.mean(rows, axis=-1, keepdims=True)
    centred = rows - mean
    spread = jnp.mean(centred * centred, axis=-1, keepdims=True)
    return centred * lax.rsqrt(spread + eps) * gain + bias


def body(
    tier_source_concatenated,
    prompt_sizes_ordered,
    tier_standardize_scale,
    tier_standardize_offset,
    previous_item_mixers,
    mapping_matrices_pile,
    fading_narrow_left,
    fading_narrow_right,
    feature_fading_baseline,
    diagonal_boost_coefficient,
    cluster_standardize_scale,
    cluster_standardize_offset,
    emitted_mapping_matrix,
):
    rows = tier_source_concatenated.shape[0]
    local_width = mapping_matrices_pile.shape[2]
    mixing_values_divided = local_width // CHANNELS_ONE_HEAD
    block = min(32, rows)
    blocks = rows // block
    full = lax.all_gather(tier_source_concatenated, "tp", axis=1, tiled=True)
    normed = layer_norm(
        full.astype(jnp.float32), tier_standardize_scale, tier_standardize_offset, 1e-05
    ).astype(jnp.bfloat16)
    first = jnp.cumsum(prompt_sizes_ordered) - prompt_sizes_ordered
    position = lax.axis_index(SEQ) * rows + jnp.arange(rows, dtype=jnp.int32)
    is_start = jnp.any(position[:, None] == first[None, :], axis=1)
    segment = jnp.sum((first[None, :] <= position[:, None]).astype(jnp.int32), axis=1)
    edge = from_behind(normed[rows - 1 :], SEQ, 1)
    previous = jnp.concatenate([edge, normed[: rows - 1]], axis=0)
    previous = jnp.where(is_start[:, None], jnp.zeros_like(previous), previous)
    base = normed.astype(jnp.float32)
    delta = previous.astype(jnp.float32) - base
    shifted_blend = (base[None] + delta[None] * previous_item_mixers[:, None, :]).astype(
        jnp.bfloat16
    )
    projected = jnp.einsum(
        "itd,ide->ite", shifted_blend[:4], mapping_matrices_pile, preferred_element_type=jnp.float32
    )
    recept = projected[0].astype(jnp.bfloat16)
    key_rows = projected[1].astype(jnp.bfloat16)
    value_rows = projected[2].astype(jnp.bfloat16)
    gate = jax.nn.silu(projected[3]).astype(jnp.bfloat16)
    lowrank_decay_delta = jnp.tanh(
        jnp.dot(shifted_blend[4], fading_narrow_left, preferred_element_type=jnp.float32)
    ).astype(jnp.bfloat16)
    decay_logarithm = -feature_fading_baseline[None, :] * jnp.exp(
        jnp.dot(lowrank_decay_delta, fading_narrow_right, preferred_element_type=jnp.float32)
    )

    def split_heads(values):
        return (
            values.astype(jnp.float32)
            .reshape(blocks, block, mixing_values_divided, CHANNELS_ONE_HEAD)
            .transpose(0, 2, 1, 3)
        )

    inputs = (
        split_heads(recept),
        split_heads(key_rows),
        split_heads(value_rows),
        split_heads(decay_logarithm),
        segment.reshape(blocks, block),
        is_start.astype(jnp.float32).reshape(blocks, block),
    )
    order = jnp.arange(block)
    lower_incl = (order[None, :] <= order[:, None]).astype(jnp.float32)
    strictly = order[None, :] < order[:, None]
    diagonal_extra_contribution = diagonal_boost_coefficient.reshape(
        mixing_values_divided, CHANNELS_ONE_HEAD
    )

    gating_rows_tile, query_array_tile, content_slab, lw_b, seg_b, start_b = inputs
    incl = jnp.einsum("ts,bhsc->bhtc", lower_incl, lw_b, precision=highest)
    excl = incl - lw_b
    pair_ok = strictly[None] & (seg_b[:, None, :] == seg_b[:, :, None])
    gap = jnp.minimum(excl[:, :, :, None, :] - incl[:, :, None, :, :], 0.0)
    weight = jnp.where(pair_ok[:, None, :, :, None], jnp.exp(gap), 0.0)
    scores = jnp.einsum(
        "bhtc,bhsc,bhtsc->bhts", gating_rows_tile, query_array_tile, weight, precision=highest
    )
    present_item_reward = jnp.sum(
        gating_rows_tile * diagonal_extra_contribution[None, :, None, :] * query_array_tile, axis=-1
    )
    seen = jnp.einsum("ts,bs->bt", lower_incl, start_b, precision=highest)
    valid = (seen == 0.0).astype(jnp.float32)
    carried = gating_rows_tile * jnp.exp(excl) * valid[:, None, :, None]
    intra = (
        jnp.einsum("bhts,bhsv->bhtv", scores, content_slab, precision=highest)
        + present_item_reward[..., None] * content_slab
    )
    total = incl[:, :, block - 1, :]
    keep = (seen[:, block - 1] == 0.0).astype(jnp.float32)
    tail_ok = (seg_b == seg_b[:, block - 1 :]).astype(jnp.float32)
    tail = query_array_tile * jnp.exp(total[:, :, None, :] - incl) * tail_ok[:, None, :, None]
    block_state = jnp.einsum("bhsc,bhsv->bhcv", tail, content_slab, precision=highest)
    block_decay = keep[:, None, None] * jnp.exp(total)

    state = jnp.zeros_like(block_state[0])
    offset = jnp.zeros_like(total[0])
    alive = jnp.float32(1.0)
    entering, reach = [], []
    for index in range(blocks):
        entering.append(state)
        reach.append(alive * jnp.exp(offset))
        state = block_decay[index][:, :, None] * state + block_state[index]
        offset = offset + total[index]
        alive = alive * keep[index]
    entering = jnp.stack(entering)
    from_start = carried * jnp.stack(reach)[:, :, None, :]
    outs = intra + jnp.einsum("bhtc,bhcv->bhtv", carried, entering, precision=highest)
    end_state = state
    decay_total = alive * jnp.exp(offset)

    packed = jnp.concatenate([end_state, decay_total[:, None, :]], axis=1)

    def combine(received, own):
        own_state, own_decay = own[:, :CHANNELS_ONE_HEAD], own[:, CHANNELS_ONE_HEAD:]
        got_state, got_decay = received[:, :CHANNELS_ONE_HEAD], received[:, CHANNELS_ONE_HEAD:]
        state = jnp.transpose(own_decay, (0, 2, 1)) * got_state + own_state
        return jnp.concatenate([state, own_decay * got_decay], axis=1)

    devices = size_of(SEQ)
    prefix = from_behind(packed, SEQ, 1)
    distance = 1
    while distance < devices:
        prefix = combine(from_behind(prefix, SEQ, distance), prefix)
        distance *= 2
    incoming = prefix[:, :CHANNELS_ONE_HEAD]
    outs = outs + jnp.einsum("bhtc,hcv->bhtv", from_start, incoming, precision=highest)
    wkv = outs.transpose(0, 2, 1, 3).reshape(rows, mixing_values_divided, CHANNELS_ONE_HEAD)
    mean = jnp.mean(wkv, axis=-1, keepdims=True)
    centred = wkv - mean
    spread = jnp.mean(centred * centred, axis=-1, keepdims=True)
    grouped = (centred * lax.rsqrt(spread + 0.00064)).reshape(
        rows, local_width
    ) * cluster_standardize_scale + cluster_standardize_offset
    gated = (grouped * gate.astype(jnp.float32)).astype(jnp.bfloat16)
    partial_sum = jnp.dot(gated, emitted_mapping_matrix, preferred_element_type=jnp.float32)
    parts = lax.axis_size("tp")
    pieces = partial_sum.astype(jnp.bfloat16).reshape(rows, parts, local_width).transpose(1, 0, 2)
    pieces = lax.all_to_all(pieces, "tp", 0, 0, tiled=True)
    mine = jnp.sum(pieces.astype(jnp.float32), axis=0)
    return (tier_source_concatenated.astype(jnp.float32) + mine).astype(jnp.bfloat16)


def solution(mesh):
    groups = 8 if mesh.shape["seq"] % 8 == 0 else 1
    devices = mesh.devices.reshape(mesh.shape["seq"] // groups, groups, mesh.shape["tp"])
    mesh = jax.sharding.Mesh(devices, ("seq_hi", "seq_lo", "tp"))
    in_specs = (
        P(SEQ, "tp"),
        P(),
        P(),
        P(),
        P(),
        P(None, None, "tp"),
        P(),
        P(None, "tp"),
        P("tp"),
        P("tp"),
        P("tp"),
        P("tp"),
        P("tp", None),
    )
    out_specs = P(SEQ, "tp")
    return jax.shard_map(body, mesh=mesh, in_specs=in_specs, out_specs=out_specs, check_vma=False)
```

time: 264 us -> 182 us (0.69)
  the two profiles are of different devices: /device:TPU:48 before, /device:TPU:24 now
where the time goes in v6:
time: 182 us; the launch traced here: 181 us
  waiting for transfers between devices  50.8 us (28%)
  other arithmetic  48.1 us (26%)
  starting transfers between devices  26.2 us (14%)
  blocking collectives  25.6 us (14%)
  matrix products  15.8 us (9%)
  local copies, waits for them, and re-layouts  11.4 us (6%)
  between operations  3.11 us (2%)
    ppermute x8, waiting for transfers between devices, from_behind(): return lax.ppermute(block, axis, route)  50.8 us
    ppermute x8, starting transfers between devices, from_behind(): return lax.ppermute(block, axis, route)  26.2 us
    dot_general x1, other arithmetic, body(): jnp.einsum('bhtc,bhsc,bhtsc->bhts', gating_rows_tile, query_array_tile, w...  18.2 us
    all_gather x1, blocking collectives, body(): full = lax.all_gather(tier_source_concatenated, 'tp', axis=1, tiled=True)  13.5 us
    all_to_all x1, blocking collectives, body(): pieces = lax.all_to_all(pieces, 'tp', 0, 0, tiled=True)  12.2 us
    select_n x1, other arithmetic, body(): weight = jnp.where(pair_ok[:, None, :, :, None], jnp.exp(gap), 0.0)  7.66 us
    dot_general x1, matrix products, body(): jnp.einsum('itd,ide->ite', shifted_blend[:4], mapping_matrices_pile, pref...  6.32 us
  transfers between devices with their start and end apart: 8, of which 5 were waited for; matrix products, arithmetic and copies ran while one was open for 22% of the time, Pallas kernels for 0%

profile of v6, /device:TPU:24, one launch (start us, length us, event | category | flops | bytes accessed | tf_op | source)
XLA Modules:
  0.0 181.0 jit_solution(13988374477612887855)
XLA Ops:
  0.0 13.5 %all_gather.3 = bf16[128,2048]{1,0:T(8,128)(2,1)S(1)} all-gather(bf16[128,512]{1,0:T(8,128)(2,1)} %param.13), channel_id=1, replica_groups=mesh['seq_hi'=8,'seq_lo'=8,'tp'=4] {'tp'}, dimensions={1}, use_global_device_ids=true | all-gather | bytes 655360 | tf_op jit(solution)/shard_map/all_gather | solution.py:54
  13.9 2.1 %fusion.70 = (f32[128,2048]{1,0:T(8,128)}, bf16[128,2048]{1,0:T(8,128)(2,1)S(1)}) fusion(f32[2048]{0:T(1024)} %param.16, f32[2048]{0:T(1024)} %param.15, f32[128]{0:T(128)S(1)} %add_rsqrt_fusion.1, f32[128]{0:T(128)S(1)} %broadcast_multiply_fusion.1, bf16[128,2048]{1,0:T(8,128)(2,1)S(1)} %all_gather.3), kind=kLoop, calls=%fused_computation.146 | loop fusion | flops 1835008 | bytes 2114560 | tf_op jit(solution)/shard_map/convert_element_type | solution.py:65
  16.1 1.9 %collective-permute-start = (bf16[1,2048]{1,0:T(2,128)(2,1)S(1)}, bf16[1,2048]{1,0:T(2,128)(2,1)S(1)}, u32[]{:S(2)}, u32[]{:S(2)}) collective-permute-start(bf16[1,2048]{1,0:T(2,128)(2,1)S(1)} %slice.175), channel_id=1, source_target_pairs={{0,4},{4,8},{8,12},{12,16},{16,20},{20,24},{24,28},{28,32},{32,36}... | collective-permute-start | bytes 12296 | tf_op jit(solution)/shard_map/ppermute | solution.py:24
  30.5 3.3 %add_convert_fusion = bf16[5,128,2048]{2,1,0:T(8,128)(2,1)} fusion(f32[5,2048]{1,0:T(8,128)S(1)} %copy-done.9, f32[128,2048]{1,0:T(8,128)S(1)} %convert_subtract_fusion.1, f32[128,2048]{1,0:T(8,128)} %get-tuple-element.20), kind=kLoop, calls=%fused_computation.3 | loop fusion | flops 3932160 | bytes 4759552 | tf_op jit(solution)/shard_map/convert_element_type | solution.py:67
  33.8 1.6 fusion.6
  37.4 6.3 %fusion.75 = (bf16[4,128,512]{2,1,0:T(8,128)(2,1)S(1)}, f32[4,128,512]{2,1,0:T(8,128)}) fusion(bf16[4,2048,512]{2,1,0:T(8,128)(2,1)} %param.18, f32[5,2048]{1,0:T(8,128)S(1)} %copy-done.9, f32[128,2048]{1,0:T(8,128)} %copy-done.6, f32[128,2048]{1,0:T(8,128)} %get-tuple-element.20), kind=kOutput, calls=%fused_computation.150 | convolution fusion | flops 1077936128 | bytes 12099584 | tf_op jit(solution)/shard_map/itd,ide->ite/dot_general | solution.py:70
  48.6 1.8 fusion.21
  51.6 1.8 pad_maximum_fusion
  53.4 3.9 %collective-permute-start.1 = (f32[8,65,64]{1,2,0:T(8,128)}, f32[8,65,64]{1,2,0:T(8,128)}, u32[]{:S(2)}, u32[]{:S(2)}) collective-permute-start(f32[8,65,64]{1,2,0:T(8,128)} %pad_maximum_fusion), channel_id=1, source_target_pairs={{0,4},{4,8},{8,12},{12,16},{16,20},{20,24},{24,28},{28,32},{32,36}... | collective-permute-start | bytes 399368 | tf_op jit(solution)/shard_map/ppermute | solution.py:24
  57.3 7.7 %exponential_select_fusion = f32[4,8,32,32,64]{4,3,2,1,0:T(8,128)} fusion(f32[4,8,32,64]{3,2,1,0:T(8,128)} %copy-done.5, f32[4,8,32,64]{3,2,1,0:T(8,128)S(1)} %get-tuple-element.39, pred[4,32,32]{2,1,0:T(8,128)(4,1)} %compare_and_fusion), kind=kLoop, calls=%fused_computation.2 | loop fusion | flops 6291456 | bytes 8916992 | tf_op jit(solution)/shard_map/jit(_where)/select_n | solution.py:111
  67.3 2.1 %collective-permute-start.2 = (f32[8,65,64]{1,2,0:T(8,128)}, f32[8,65,64]{1,2,0:T(8,128)S(1)}, u32[]{:S(2)}, u32[]{:S(2)}) collective-permute-start(f32[8,65,64]{1,2,0:T(8,128)} %collective-permute-done.1), channel_id=1, source_target_pairs={{0,4},{4,8},{8,12},{12,16},{16,20},{20,24},{24,28},{28,32},{32,36}... | collective-permute-start | bytes 399368 | tf_op jit(solution)/shard_map/ppermute | solution.py:24
  69.4 18.2 %fusion = f32[4,8,32,32]{2,3,1,0:T(8,128)S(1)} fusion(f32[4,8,32,32,64]{4,3,2,1,0:T(8,128)} %exponential_select_fusion, f32[4,8,64,32]{2,3,1,0:T(8,128)S(1)} %copy.68, f32[4,8,64,32]{2,3,1,0:T(8,128)S(1)} %copy.67), kind=kLoop, calls=%fused_computation.1 | loop fusion | flops 6258688 | bytes 9043968 | tf_op jit(solution)/shard_map/bhtc,bhsc,bhtsc->bhts/dot_general | solution.py:112
  87.6 1.4 fusion.69
  90.2 4.0 %collective-permute-start.3 = (f32[8,65,64]{1,2,0:T(8,128)S(1)}, f32[8,65,64]{1,2,0:T(8,128)S(1)}, u32[]{:S(2)}, u32[]{:S(2)}) collective-permute-start(f32[8,65,64]{1,2,0:T(8,128)S(1)} %pad_maximum_fusion.1), channel_id=1, source_target_pairs={{0,8},{4,12},{8,16},{12,20},{16,24},{20,28},{24,32},{28,36},{32,40... | collective-permute-start | bytes 399368 | tf_op jit(solution)/shard_map/ppermute | solution.py:24
  94.5 7.8 %collective-permute-done.3 = f32[8,65,64]{1,2,0:T(8,128)S(1)} collective-permute-done((f32[8,65,64]{1,2,0:T(8,128)S(1)}, f32[8,65,64]{1,2,0:T(8,128)S(1)}, u32[]{:S(2)}, u32[]{:S(2)}) %collective-permute-start.3) | collective-permute-done | bytes 133152 | tf_op jit(solution)/shard_map/ppermute | solution.py:24
  102.8 4.6 %collective-permute-start.4 = (f32[8,65,64]{1,2,0:T(8,128)S(1)}, f32[8,65,64]{1,2,0:T(8,128)S(1)}, u32[]{:S(2)}, u32[]{:S(2)}) collective-permute-start(f32[8,65,64]{1,2,0:T(8,128)S(1)} %pad_maximum_fusion.2), channel_id=1, source_target_pairs={{0,16},{4,20},{8,24},{12,28},{16,32},{20,36},{24,40},{28,44},{32,4... | collective-permute-start | bytes 399368 | tf_op jit(solution)/shard_map/ppermute | solution.py:24
  108.1 13.7 %collective-permute-done.4 = f32[8,65,64]{1,2,0:T(8,128)S(1)} collective-permute-done((f32[8,65,64]{1,2,0:T(8,128)S(1)}, f32[8,65,64]{1,2,0:T(8,128)S(1)}, u32[]{:S(2)}, u32[]{:S(2)}) %collective-permute-start.4) | collective-permute-done | bytes 133152 | tf_op jit(solution)/shard_map/ppermute | solution.py:24
  122.2 7.1 %collective-permute-start.5 = (f32[8,65,64]{1,2,0:T(8,128)S(1)}, f32[8,65,64]{1,2,0:T(8,128)S(1)}, u32[]{:S(2)}, u32[]{:S(2)}) collective-permute-start(f32[8,65,64]{1,2,0:T(8,128)S(1)} %pad_maximum_fusion.3), channel_id=1, source_target_pairs={{0,32},{4,36},{8,40},{12,44},{16,48},{20,52},{24,56},{28,60},{32,6... | collective-permute-start | bytes 399368 | tf_op jit(solution)/shard_map/ppermute | solution.py:24
  129.4 13.4 %collective-permute-done.5 = f32[8,65,64]{1,2,0:T(8,128)S(1)} collective-permute-done((f32[8,65,64]{1,2,0:T(8,128)S(1)}, f32[8,65,64]{1,2,0:T(8,128)S(1)}, u32[]{:S(2)}, u32[]{:S(2)}) %collective-permute-start.5) | collective-permute-done | bytes 133152 | tf_op jit(solution)/shard_map/ppermute | solution.py:24
  144.6 1.9 %fusion.3 = f32[4,32,8,64]{3,1,2,0:T(8,128)S(1)} fusion(f32[4,32,8,64]{3,1,2,0:T(8,128)S(1)} %fusion.4, f32[1,8,64,64]{2,3,1,0:T(8,128)S(1)} %get-tuple-element.17, f32[1,8,64,64]{2,3,1,0:T(8,128)S(1)} %get-tuple-element.18, f32[1,8,64,64]{2,3,1,0:T(8,128)S(1)} %get-tuple-element.19, f32[4]{0:T(128)S(1)} %copy-done.16, ...), kind=kOutput, calls=%fused_computation.11 | convolution fusion | flops 50921472 | bytes 1442320 | tf_op jit(solution)/shard_map/bhtc,bhcv->bhtv/dot_general | solution.py:144
  146.5 6.7 %collective-permute-done.6 = f32[8,65,64]{1,2,0:T(8,128)S(1)} collective-permute-done((f32[8,65,64]{1,2,0:T(8,128)S(1)}, f32[8,65,64]{1,2,0:T(8,128)S(1)}, u32[]{:S(2)}, u32[]{:S(2)}) %collective-permute-start.6) | collective-permute-done | bytes 133152 | tf_op jit(solution)/shard_map/ppermute | solution.py:24
  155.1 9.2 %collective-permute-done.7 = f32[8,65,64]{1,2,0:T(8,128)S(1)} collective-permute-done((f32[8,65,64]{1,2,0:T(8,128)S(1)}, f32[8,65,64]{1,2,0:T(8,128)S(1)}, u32[]{:S(2)}, u32[]{:S(2)}) %collective-permute-start.7) | collective-permute-done | bytes 133152 | tf_op jit(solution)/shard_map/ppermute | solution.py:24
  166.6 1.4 convolution_convert_fusion
  168.1 12.2 %all_to_all.5 = bf16[4,128,512]{2,1,0:T(8,128)(2,1)S(1)} all-to-all(bf16[4,128,512]{2,1,0:T(8,128)(2,1)S(1)} %bitcast.152), channel_id=1, replica_groups=mesh['seq_hi'=8,'seq_lo'=8,'tp'=4] {'tp'}, dimensions={0} | all-to-all | bytes 1048576 | tf_op jit(solution)/shard_map/all_to_all | solution.py:175
  (115 shorter events, 30.2 us)
Async XLA Ops:
  0.0 166.5 %copy-start = (bf16[512,2048]{1,0:T(8,128)(2,1)S(1)}, bf16[512,2048]{1,0:T(8,128)(2,1)}, u32[]{:S(2)}) copy-start(bf16[512,2048]{1,0:T(8,128)(2,1)} %param.25) | copy-start | bytes 6291460
  0.0 30.4 %copy-start.9 = (f32[5,2048]{1,0:T(8,128)S(1)}, f32[5,2048]{1,0:T(8,128)}, u32[]{:S(2)}) copy-start(f32[5,2048]{1,0:T(8,128)} %param.17) | copy-start | bytes 122884
  13.5 20.3 %copy-start.8 = (bf16[2048,64]{0,1:T(8,128)(2,1)S(1)}, bf16[2048,64]{0,1:T(8,128)(2,1)}, u32[]{:S(2)}) copy-start(bf16[2048,64]{0,1:T(8,128)(2,1)} %param.19) | copy-start | bytes 786436
  13.5 20.3 %copy-start.10 = (bf16[64,512]{1,0:T(8,128)(2,1)S(1)}, bf16[64,512]{1,0:T(8,128)(2,1)}, u32[]{:S(2)}) copy-start(bf16[64,512]{1,0:T(8,128)(2,1)} %param.20) | copy-start | bytes 196612
  16.1 13.1 %collective-permute-start = (bf16[1,2048]{1,0:T(2,128)(2,1)S(1)}, bf16[1,2048]{1,0:T(2,128)(2,1)S(1)}, u32[]{:S(2)}, u32[]{:S(2)}) collective-permute-start(bf16[1,2048]{1,0:T(2,128)(2,1)S(1)} %slice.175), channel_id=1, source_target_pairs={{0,4},{4,8},{8,12},{12,16},{16,20},{20,24},{24,28},{28,32},{32,36}... | collective-permute-start | bytes 12296 | tf_op jit(solution)/shard_map/ppermute | solution.py:24
  29.5 1.0 copy-start.6
  44.6 20.3 %copy-start.1 = (f32[4,32,8,64]{3,2,1,0:T(8,128)}, f32[4,32,8,64]{3,2,1,0:T(8,128)S(1)}, u32[]{:S(2)}) copy-start(f32[4,32,8,64]{3,2,1,0:T(8,128)S(1)} %reshape.331) | copy-start | bytes 786436
  50.4 1.0 copy-start.3
  53.4 13.9 %collective-permute-start.1 = (f32[8,65,64]{1,2,0:T(8,128)}, f32[8,65,64]{1,2,0:T(8,128)}, u32[]{:S(2)}, u32[]{:S(2)}) collective-permute-start(f32[8,65,64]{1,2,0:T(8,128)} %pad_maximum_fusion), channel_id=1, source_target_pairs={{0,4},{4,8},{8,12},{12,16},{16,20},{20,24},{24,28},{28,32},{32,36}... | collective-permute-start | bytes 399368 | tf_op jit(solution)/shard_map/ppermute | solution.py:24
  67.3 26.9 %copy-start.2 = (f32[4,32,8,64]{3,2,1,0:T(8,128)S(1)}, f32[4,32,8,64]{3,2,1,0:T(8,128)}, u32[]{:S(2)}) copy-start(f32[4,32,8,64]{3,2,1,0:T(8,128)} %copy-done.1) | copy-start | bytes 786436
  67.3 26.9 %copy-start.11 = (f32[8,64]{1,0:T(8,128)S(1)}, f32[8,64]{1,0:T(8,128)}, u32[]{:S(2)}) copy-start(f32[8,64]{1,0:T(8,128)} %mul.350) | copy-start | bytes 6148
  67.3 20.3 %collective-permute-start.2 = (f32[8,65,64]{1,2,0:T(8,128)}, f32[8,65,64]{1,2,0:T(8,128)S(1)}, u32[]{:S(2)}, u32[]{:S(2)}) collective-permute-start(f32[8,65,64]{1,2,0:T(8,128)} %collective-permute-done.1), channel_id=1, source_target_pairs={{0,4},{4,8},{8,12},{12,16},{16,20},{20,24},{24,28},{28,32},{32,36}... | collective-permute-start | bytes 399368 | tf_op jit(solution)/shard_map/ppermute | solution.py:24
  87.6 41.7 %copy-start.4 = (f32[4,8,64,64]{2,3,1,0:T(8,128)S(1)}, f32[4,8,64,64]{2,3,1,0:T(8,128)}, u32[]{:S(2)}) copy-start(f32[4,8,64,64]{2,3,1,0:T(8,128)} %copy-done.3) | copy-start | bytes 1572868
  90.2 12.1 %collective-permute-start.3 = (f32[8,65,64]{1,2,0:T(8,128)S(1)}, f32[8,65,64]{1,2,0:T(8,128)S(1)}, u32[]{:S(2)}, u32[]{:S(2)}) collective-permute-start(f32[8,65,64]{1,2,0:T(8,128)S(1)} %pad_maximum_fusion.1), channel_id=1, source_target_pairs={{0,8},{4,12},{8,16},{12,20},{16,24},{20,28},{24,32},{28,36},{32,40... | collective-permute-start | bytes 399368 | tf_op jit(solution)/shard_map/ppermute | solution.py:24
  94.5 50.1 %copy-start.12 = (f32[4,32]{1,0:T(4,128)S(1)}, f32[4,32]{1,0:T(4,128)}, u32[]{:S(2)}) copy-start(f32[4,32]{1,0:T(4,128)} %get-tuple-element.43) | copy-start | bytes 1540
  94.5 50.1 %copy-start.16 = (f32[4]{0:T(128)S(1)}, f32[4]{0:T(128)}, u32[]{:S(2)}) copy-start(f32[4]{0:T(128)} %pad.16.clone) | copy-start | bytes 52
  102.8 19.0 %collective-permute-start.4 = (f32[8,65,64]{1,2,0:T(8,128)S(1)}, f32[8,65,64]{1,2,0:T(8,128)S(1)}, u32[]{:S(2)}, u32[]{:S(2)}) collective-permute-start(f32[8,65,64]{1,2,0:T(8,128)S(1)} %pad_maximum_fusion.2), channel_id=1, source_target_pairs={{0,16},{4,20},{8,24},{12,28},{16,32},{20,36},{24,40},{28,44},{32,4... | collective-permute-start | bytes 399368 | tf_op jit(solution)/shard_map/ppermute | solution.py:24
  122.0 33.0 %copy-start.15 = (f32[4]{0:T(128)S(1)}, f32[4]{0:T(128)}, u32[]{:S(2)}) copy-start(f32[4]{0:T(128)} %pad.clone) | copy-start | bytes 52
  122.2 20.6 %collective-permute-start.5 = (f32[8,65,64]{1,2,0:T(8,128)S(1)}, f32[8,65,64]{1,2,0:T(8,128)S(1)}, u32[]{:S(2)}, u32[]{:S(2)}) collective-permute-start(f32[8,65,64]{1,2,0:T(8,128)S(1)} %pad_maximum_fusion.3), channel_id=1, source_target_pairs={{0,32},{4,36},{8,40},{12,44},{16,48},{20,52},{24,56},{28,60},{32,6... | collective-permute-start | bytes 399368 | tf_op jit(solution)/shard_map/ppermute | solution.py:24
  143.3 9.9 %collective-permute-start.6 = (f32[8,65,64]{1,2,0:T(8,128)S(1)}, f32[8,65,64]{1,2,0:T(8,128)S(1)}, u32[]{:S(2)}, u32[]{:S(2)}) collective-permute-start(f32[8,65,64]{1,2,0:T(8,128)S(1)} %pad_maximum_fusion.4), channel_id=1, source_target_pairs={{0,64},{4,68},{8,72},{12,76},{16,80},{20,84},{24,88},{28,92},{32,9... | collective-permute-start | bytes 399368 | tf_op jit(solution)/shard_map/ppermute | solution.py:24
  146.5 20.1 %copy-start.13 = (f32[512]{0:T(512)S(1)}, f32[512]{0:T(512)}, u32[]{:S(2)}) copy-start(f32[512]{0:T(512)} %param.24) | copy-start | bytes 6148
  146.5 20.1 %copy-start.14 = (f32[512]{0:T(512)S(1)}, f32[512]{0:T(512)}, u32[]{:S(2)}) copy-start(f32[512]{0:T(512)} %param.23) | copy-start | bytes 6148
  153.7 10.6 %collective-permute-start.7 = (f32[8,65,64]{1,2,0:T(8,128)S(1)}, f32[8,65,64]{1,2,0:T(8,128)S(1)}, u32[]{:S(2)}, u32[]{:S(2)}) collective-permute-start(f32[8,65,64]{1,2,0:T(8,128)S(1)} %pad_maximum_fusion.5), channel_id=1, source_target_pairs={{0,128},{4,132},{8,136},{12,140},{16,144},{20,148},{24,152},{28,15... | collective-permute-start | bytes 399368 | tf_op jit(solution)/shard_map/ppermute | solution.py:24
  165.1 15.2 %copy-start.7 = (bf16[128,512]{1,0:T(8,128)(2,1)S(1)}, bf16[128,512]{1,0:T(8,128)(2,1)}, u32[]{:S(2)}) copy-start(bf16[128,512]{1,0:T(8,128)(2,1)} %param.13) | copy-start | bytes 393220
  (1 other events, 0.8 us)

commit v7 on v6

--- a/solution.py
+++ b/solution.py
@@ -145,21 +145,27 @@
     end_state = state
     decay_total = alive * jnp.exp(offset)
 
-    packed = jnp.concatenate([end_state, decay_total[:, None, :]], axis=1)
+    lanes = 128 if (mixing_values_divided * CHANNELS_ONE_HEAD) % 128 == 0 else CHANNELS_ONE_HEAD
+    state_rows = end_state.size // lanes
+
+    def pack(state, decay):
+        return jnp.concatenate([state.reshape(-1, lanes), decay.reshape(-1, lanes)], axis=0)
 
     def combine(received, own):
-        own_state, own_decay = own[:, :CHANNELS_ONE_HEAD], own[:, CHANNELS_ONE_HEAD:]
-        got_state, got_decay = received[:, :CHANNELS_ONE_HEAD], received[:, CHANNELS_ONE_HEAD:]
-        state = jnp.transpose(own_decay, (0, 2, 1)) * got_state + own_state
-        return jnp.concatenate([state, own_decay * got_decay], axis=1)
+        own_state = own[:state_rows].reshape(end_state.shape)
+        own_decay = own[state_rows:].reshape(decay_total.shape)
+        got_state = received[:state_rows].reshape(end_state.shape)
+        got_decay = received[state_rows:].reshape(decay_total.shape)
+        return pack(own_decay[:, :, None] * got_state + own_state, own_decay * got_decay)
 
     devices = size_of(SEQ)
-    prefix = from_behind(packed, SEQ, 1)
+    prefix = pack(end_state, decay_total)
     distance = 1
-    while distance < devices:
+    while 2 * distance < devices:
         prefix = combine(from_behind(prefix, SEQ, distance), prefix)
         distance *= 2
-    incoming = prefix[:, :CHANNELS_ONE_HEAD]
+    prefix = combine(from_behind(prefix, SEQ, distance + 1), from_behind(prefix, SEQ, 1))
+    incoming = prefix[:state_rows].reshape(end_state.shape)
     outs = outs + jnp.einsum("bhtc,hcv->bhtv", from_start, incoming, precision=highest)
     wkv = outs.transpose(0, 2, 1, 3).reshape(rows, mixing_values_divided, CHANNELS_ONE_HEAD)
     mean = jnp.mean(wkv, axis=-1, keepdims=True)

time: 182 us -> 206 us (1.13)
  the two profiles are of different devices: /device:TPU:24 before, /device:TPU:48 now
where the time goes in v7:
time: 206 us; the launch traced here: 204 us
  other arithmetic  63.7 us (31%)
  local copies, waits for them, and re-layouts  46 us (22%)
  blocking collectives  28.3 us (14%)
  starting transfers between devices  27.4 us (13%)
  matrix products  20.5 us (10%)
  waiting for transfers between devices  15.7 us (8%)
  between operations  2.91 us (1%)
    ppermute x8, starting transfers between devices, from_behind(): return lax.ppermute(block, axis, route)  27.4 us
    dot_general x1, other arithmetic, body(): jnp.einsum('bhtc,bhsc,bhtsc->bhts', gating_rows_tile, query_array_tile, w...  19.6 us
    ppermute x8, waiting for transfers between devices, from_behind(): return lax.ppermute(block, axis, route)  15.7 us
    all_to_all x1, blocking collectives, body(): pieces = lax.all_to_all(pieces, 'tp', 0, 0, tiled=True)  14.8 us
    all_gather x1, blocking collectives, body(): full = lax.all_gather(tier_source_concatenated, 'tp', axis=1, tiled=True)  13.5 us
    mul x8, local copies, waits for them, and re-layouts, body(): state = block_decay[index][:, :, None] * state + block_state[index]  10.2 us
    mul x11, local copies, waits for them, and re-layouts, combine(): own_decay[:, :, None] * got_state + own_state  10.1 us
    select_n x1, other arithmetic, body(): weight = jnp.where(pair_ok[:, None, :, :, None], jnp.exp(gap), 0.0)  7.64 us
  transfers between devices with their start and end apart: 8, of which 4 were waited for; matrix products, arithmetic and copies ran while one was open for 27% of the time, Pallas kernels for 0%

profile of v7, /device:TPU:48, one launch (start us, length us, event | category | flops | bytes accessed | tf_op | source)
XLA Modules:
  0.0 204.4 jit_solution(3655362769855931596)
XLA Ops:
  0.0 13.5 %all_gather.3 = bf16[128,2048]{1,0:T(8,128)(2,1)S(1)} all-gather(bf16[128,512]{1,0:T(8,128)(2,1)} %param.13), channel_id=1, replica_groups=mesh['seq_hi'=8,'seq_lo'=8,'tp'=4] {'tp'}, dimensions={1}, use_global_device_ids=true | all-gather | bytes 655360 | tf_op jit(solution)/shard_map/all_gather | solution.py:54
  13.9 2.1 %fusion.66 = (f32[128,2048]{1,0:T(8,128)}, bf16[128,2048]{1,0:T(8,128)(2,1)S(1)}) fusion(f32[2048]{0:T(1024)} %param.16, f32[2048]{0:T(1024)} %param.15, f32[128]{0:T(128)S(1)} %add_rsqrt_fusion.1, f32[128]{0:T(128)S(1)} %broadcast_multiply_fusion.1, bf16[128,2048]{1,0:T(8,128)(2,1)S(1)} %all_gather.3), kind=kLoop, calls=%fused_computation.136 | loop fusion | flops 1835008 | bytes 2114560 | tf_op jit(solution)/shard_map/convert_element_type | solution.py:65
  16.1 1.9 collective-permute-start
  30.4 3.3 %add_convert_fusion = bf16[5,128,2048]{2,1,0:T(8,128)(2,1)} fusion(f32[5,2048]{1,0:T(8,128)S(1)} %copy-done.10, f32[128,2048]{1,0:T(8,128)S(1)} %convert_subtract_fusion.1, f32[128,2048]{1,0:T(8,128)} %get-tuple-element.16), kind=kLoop, calls=%fused_computation.3 | loop fusion | flops 3932160 | bytes 4759552 | tf_op jit(solution)/shard_map/convert_element_type | solution.py:67
  37.3 6.3 %fusion.75 = (bf16[4,128,512]{2,1,0:T(8,128)(2,1)S(1)}, f32[4,128,512]{2,1,0:T(8,128)}) fusion(bf16[4,2048,512]{2,1,0:T(8,128)(2,1)} %param.18, f32[5,2048]{1,0:T(8,128)S(1)} %copy-done.10, f32[128,2048]{1,0:T(8,128)} %copy-done.3, f32[128,2048]{1,0:T(8,128)} %get-tuple-element.16), kind=kOutput, calls=%fused_computation.144 | convolution fusion | flops 1077936128 | bytes 12099584 | tf_op jit(solution)/shard_map/itd,ide->ite/dot_general | solution.py:70
  47.8 2.1 %fusion.64 = (f32[8,64]{1,0:T(8,128)S(1)}, f32[1,8,1,64]{3,2,1,0:T(1,128)}, f32[1,8,1,64]{3,2,1,0:T(1,128)}) fusion(f32[]{:T(128)} %broadcast.234, f32[4,8,32,64]{3,2,1,0:T(8,128)} %copy-done.2, f32[1,8,1,64]{3,2,1,0:T(1,128)S(1)} %bitcast.148, f32[]{:T(128)S(6)} %mul.493, f32[]{:T(128)S(6)} %mul.492), kind=kLoop, calls=%fused_computation.135 | loop fusion | flops 2048 | bytes 12300 | tf_op jit(solution)/shard_map/mul | solution.py:146
  50.5 2.1 %fusion.21 = f32[4,8,64,64]{3,2,1,0:T(8,128)S(1)} fusion(f32[4,8,32,64]{3,2,1,0:T(8,128)} %copy-done.2, f32[4,32,8,64]{3,2,1,0:T(8,128)S(1)} %reshape.525, f32[4,32]{1,0:T(4,128)} %compare_convert_fusion, f32[4,8,64]{2,1,0:T(8,128)S(1)} %bitcast.143, bf16[4,32,8,64]{3,2,1,0:T(8,128)(2,1)S(1)} %convert_element_type.96), kind=kOutput, calls=%fused_computation.40 | convolution fusion | flops 50528256 | bytes 1188352 | tf_op jit(solution)/shard_map/bhsc,bhsv->bhcv/dot_general | solution.py:129
  73.9 3.9 %collective-permute-start.1 = (f32[260,128]{1,0:T(8,128)}, f32[260,128]{1,0:T(8,128)}, u32[]{:S(2)}, u32[]{:S(2)}) collective-permute-start(f32[260,128]{1,0:T(8,128)} %pad_maximum_fusion), channel_id=1, source_target_pairs={{0,4},{4,8},{8,12},{12,16},{16,20},{20,24},{24,28},{28,32},{32,36}... | collective-permute-start | bytes 399368 | tf_op jit(solution)/shard_map/ppermute | solution.py:24
  77.8 7.6 %exponential_select_fusion = f32[4,8,32,32,64]{4,3,2,1,0:T(8,128)} fusion(f32[4,8,32,64]{3,2,1,0:T(8,128)} %copy-done.2, f32[4,8,32,64]{3,2,1,0:T(8,128)S(1)} %get-tuple-element.47, pred[4,32,32]{2,1,0:T(8,128)(4,1)S(1)} %copy-done.11), kind=kLoop, calls=%fused_computation.2 | loop fusion | flops 6291456 | bytes 8916992 | tf_op jit(solution)/shard_map/jit(_where)/select_n | solution.py:111
  87.4 2.0 copy.58
  95.6 4.1 %collective-permute-start.2 = (f32[260,128]{1,0:T(8,128)}, f32[260,128]{1,0:T(8,128)}, u32[]{:S(2)}, u32[]{:S(2)}) collective-permute-start(f32[260,128]{1,0:T(8,128)} %pad_maximum_fusion.1), channel_id=1, source_target_pairs={{0,8},{4,12},{8,16},{12,20},{16,24},{20,28},{24,32},{28,36},{32,40... | collective-permute-start | bytes 399368 | tf_op jit(solution)/shard_map/ppermute | solution.py:24
  99.7 19.6 %fusion = f32[4,8,32,32]{2,3,1,0:T(8,128)} fusion(f32[4,8,32,32,64]{4,3,2,1,0:T(8,128)} %exponential_select_fusion, f32[4,8,64,32]{2,3,1,0:T(8,128)} %copy.59, f32[4,8,64,32]{2,3,1,0:T(8,128)} %copy.58), kind=kLoop, calls=%fused_computation.1 | loop fusion | flops 6258688 | bytes 9043968 | tf_op jit(solution)/shard_map/bhtc,bhsc,bhtsc->bhts/dot_general | solution.py:112
  127.5 5.5 %collective-permute-start.3 = (f32[260,128]{1,0:T(8,128)S(1)}, f32[260,128]{1,0:T(8,128)}, u32[]{:S(2)}, u32[]{:S(2)}) collective-permute-start(f32[260,128]{1,0:T(8,128)S(1)} %pad_maximum_fusion.2), channel_id=1, source_target_pairs={{0,16},{4,20},{8,24},{12,28},{16,32},{20,36},{24,40},{28,44},{32,4... | collective-permute-start | bytes 399368 | tf_op jit(solution)/shard_map/ppermute | solution.py:24
  137.4 3.0 %collective-permute-done.3 = f32[260,128]{1,0:T(8,128)} collective-permute-done((f32[260,128]{1,0:T(8,128)S(1)}, f32[260,128]{1,0:T(8,128)}, u32[]{:S(2)}, u32[]{:S(2)}) %collective-permute-start.3) | collective-permute-done | bytes 133152 | tf_op jit(solution)/shard_map/ppermute | solution.py:24
  142.8 5.7 %collective-permute-start.4 = (f32[260,128]{1,0:T(8,128)}, f32[260,128]{1,0:T(8,128)}, u32[]{:S(2)}, u32[]{:S(2)}) collective-permute-start(f32[260,128]{1,0:T(8,128)} %pad_maximum_fusion.3), channel_id=1, source_target_pairs={{0,32},{4,36},{8,40},{12,44},{16,48},{20,52},{24,56},{28,60},{32,6... | collective-permute-start | bytes 399368 | tf_op jit(solution)/shard_map/ppermute | solution.py:24
  148.5 2.5 %fusion.4 = f32[4,32,8,64]{3,1,2,0:T(8,128)} fusion(f32[4,8,32,32]{2,3,1,0:T(8,128)} %fusion, f32[4,32,8]{1,2,0:T(8,128)} %bitcast.144, bf16[4,32,8,64]{3,2,1,0:T(8,128)(2,1)S(1)} %convert_element_type.96), kind=kOutput, calls=%fused_computation.14 | convolution fusion | flops 25362432 | bytes 528384 | tf_op jit(solution)/shard_map/bhts,bhsv->bhtv/dot_general | solution.py:122
  151.1 6.4 %collective-permute-done.4 = f32[260,128]{1,0:T(8,128)} collective-permute-done((f32[260,128]{1,0:T(8,128)}, f32[260,128]{1,0:T(8,128)}, u32[]{:S(2)}, u32[]{:S(2)}) %collective-permute-start.4) | collective-permute-done | bytes 133152 | tf_op jit(solution)/shard_map/ppermute | solution.py:24
  160.8 3.0 %collective-permute-start.5 = (f32[260,128]{1,0:T(8,128)}, f32[260,128]{1,0:T(8,128)}, u32[]{:S(2)}, u32[]{:S(2)}) collective-permute-start(f32[260,128]{1,0:T(8,128)} %pad_maximum_fusion.4), channel_id=1, source_target_pairs={{0,64},{4,68},{8,72},{12,76},{16,80},{20,84},{24,88},{28,92},{32,9... | collective-permute-start | bytes 399368 | tf_op jit(solution)/shard_map/ppermute | solution.py:24
  163.8 3.3 %fusion.3 = f32[4,32,8,64]{3,1,2,0:T(8,128)} fusion(f32[4,32,8,64]{3,1,2,0:T(8,128)} %fusion.4, f32[1,8,64,64]{3,2,1,0:T(8,128)} %get-tuple-element.13, f32[1,8,64,64]{3,2,1,0:T(8,128)} %get-tuple-element.14, f32[1,8,64,64]{3,2,1,0:T(8,128)} %get-tuple-element.15, f32[4]{0:T(128)} %pad.16.clone, f32[4,8,32,64]{3,2,1,0:T(8,128)S(1)} %get-tuple-element.47, ...), kind=kOutput, calls=%fused_computation.11 | convolution fusion | flops 50921472 | bytes 1442320 | tf_op jit(solution)/shard_map/bhtc,bhcv->bhtv/dot_general | solution.py:144
  170.3 1.9 collective-permute-start.6
  174.3 2.5 %collective-permute-done.6 = f32[260,128]{1,0:T(8,128)S(1)} collective-permute-done((f32[260,128]{1,0:T(8,128)}, f32[260,128]{1,0:T(8,128)S(1)}, u32[]{:S(2)}, u32[]{:S(2)}) %collective-permute-start.6) | collective-permute-done | bytes 133152 | tf_op jit(solution)/shard_map/ppermute | solution.py:24
  177.6 3.8 %collective-permute-done.7 = f32[260,128]{1,0:T(8,128)} collective-permute-done((f32[260,128]{1,0:T(8,128)}, f32[260,128]{1,0:T(8,128)}, u32[]{:S(2)}, u32[]{:S(2)}) %collective-permute-start.7) | collective-permute-done | bytes 133152 | tf_op jit(solution)/shard_map/ppermute | solution.py:24
  183.9 2.0 fusion.76
  188.8 14.8 %all_to_all.5 = bf16[4,128,512]{2,1,0:T(8,128)(2,1)S(1)} all-to-all(bf16[4,128,512]{2,1,0:T(8,128)(2,1)S(1)} %bitcast.138), channel_id=1, replica_groups=mesh['seq_hi'=8,'seq_lo'=8,'tp'=4] {'tp'}, dimensions={0} | all-to-all | bytes 1048576 | tf_op jit(solution)/shard_map/all_to_all | solution.py:181
  (150 shorter events, 78.6 us)
Async XLA Ops:
  0.0 187.3 %copy-start = (bf16[512,2048]{1,0:T(8,128)(2,1)S(1)}, bf16[512,2048]{1,0:T(8,128)(2,1)}, u32[]{:S(2)}) copy-start(bf16[512,2048]{1,0:T(8,128)(2,1)} %param.25) | copy-start | bytes 6291460
  0.0 30.3 %copy-start.10 = (f32[5,2048]{1,0:T(8,128)S(1)}, f32[5,2048]{1,0:T(8,128)}, u32[]{:S(2)}) copy-start(f32[5,2048]{1,0:T(8,128)} %param.17) | copy-start | bytes 122884
  13.5 20.2 %copy-start.8 = (bf16[2048,64]{0,1:T(8,128)(2,1)S(1)}, bf16[2048,64]{0,1:T(8,128)(2,1)}, u32[]{:S(2)}) copy-start(bf16[2048,64]{0,1:T(8,128)(2,1)} %param.19) | copy-start | bytes 786436
  13.5 20.2 %copy-start.12 = (bf16[64,512]{1,0:T(8,128)(2,1)S(1)}, bf16[64,512]{1,0:T(8,128)(2,1)}, u32[]{:S(2)}) copy-start(bf16[64,512]{1,0:T(8,128)(2,1)} %param.20) | copy-start | bytes 196612
  16.1 13.0 %collective-permute-start = (bf16[1,2048]{1,0:T(2,128)(2,1)S(1)}, bf16[1,2048]{1,0:T(2,128)(2,1)S(1)}, u32[]{:S(2)}, u32[]{:S(2)}) collective-permute-start(bf16[1,2048]{1,0:T(2,128)(2,1)S(1)} %slice.175), channel_id=1, source_target_pairs={{0,4},{4,8},{8,12},{12,16},{16,20},{20,24},{24,28},{28,32},{32,36}... | collective-permute-start | bytes 12296 | tf_op jit(solution)/shard_map/ppermute | solution.py:24
  29.4 1.0 copy-start.3
  35.9 0.8 copy-start.2
  44.5 28.1 %copy-start.1 = (f32[4,32,8,64]{3,2,1,0:T(8,128)}, f32[4,32,8,64]{3,2,1,0:T(8,128)S(1)}, u32[]{:S(2)}) copy-start(f32[4,32,8,64]{3,2,1,0:T(8,128)S(1)} %reshape.525) | copy-start | bytes 786436
  52.7 25.1 %copy-start.11 = (pred[4,32,32]{2,1,0:T(8,128)(4,1)S(1)}, pred[4,32,32]{2,1,0:T(8,128)(4,1)}, u32[]{:S(2)}) copy-start(pred[4,32,32]{2,1,0:T(8,128)(4,1)} %compare_and_fusion) | copy-start | bytes 12292
  73.9 18.7 %collective-permute-start.1 = (f32[260,128]{1,0:T(8,128)}, f32[260,128]{1,0:T(8,128)}, u32[]{:S(2)}, u32[]{:S(2)}) collective-permute-start(f32[260,128]{1,0:T(8,128)} %pad_maximum_fusion), channel_id=1, source_target_pairs={{0,4},{4,8},{8,12},{12,16},{16,20},{20,24},{24,28},{28,32},{32,36}... | collective-permute-start | bytes 399368 | tf_op jit(solution)/shard_map/ppermute | solution.py:24
  94.3 0.7 copy-start.4
  95.6 26.9 %copy-start.13 = (f32[1,8,1,64]{3,2,1,0:T(1,128)S(1)}, f32[1,8,1,64]{3,2,1,0:T(1,128)}, u32[]{:S(2)}) copy-start(f32[1,8,1,64]{3,2,1,0:T(1,128)} %get-tuple-element.10) | copy-start | bytes 6148
  95.6 30.2 %copy-start.5 = (f32[256,128]{1,0:T(8,128)S(1)}, f32[256,128]{1,0:T(8,128)}, u32[]{:S(2)}) copy-start(f32[256,128]{1,0:T(8,128)} %copy-done.4) | copy-start | bytes 393220
  95.6 37.4 %copy-start.14 = (f32[8,64]{1,0:T(8,128)S(1)}, f32[8,64]{1,0:T(8,128)}, u32[]{:S(2)}) copy-start(f32[8,64]{1,0:T(8,128)} %mul.467) | copy-start | bytes 6148
  95.6 24.4 %collective-permute-start.2 = (f32[260,128]{1,0:T(8,128)}, f32[260,128]{1,0:T(8,128)}, u32[]{:S(2)}, u32[]{:S(2)}) collective-permute-start(f32[260,128]{1,0:T(8,128)} %pad_maximum_fusion.1), channel_id=1, source_target_pairs={{0,8},{4,12},{8,16},{12,20},{16,24},{20,28},{24,32},{28,36},{32,40... | collective-permute-start | bytes 399368 | tf_op jit(solution)/shard_map/ppermute | solution.py:24
  126.8 0.7 copy-start.6
  127.5 12.9 %collective-permute-start.3 = (f32[260,128]{1,0:T(8,128)S(1)}, f32[260,128]{1,0:T(8,128)}, u32[]{:S(2)}, u32[]{:S(2)}) collective-permute-start(f32[260,128]{1,0:T(8,128)S(1)} %pad_maximum_fusion.2), channel_id=1, source_target_pairs={{0,16},{4,20},{8,24},{12,28},{16,32},{20,36},{24,40},{28,44},{32,4... | collective-permute-start | bytes 399368 | tf_op jit(solution)/shard_map/ppermute | solution.py:24
  142.8 14.7 %collective-permute-start.4 = (f32[260,128]{1,0:T(8,128)}, f32[260,128]{1,0:T(8,128)}, u32[]{:S(2)}, u32[]{:S(2)}) collective-permute-start(f32[260,128]{1,0:T(8,128)} %pad_maximum_fusion.3), channel_id=1, source_target_pairs={{0,32},{4,36},{8,40},{12,44},{16,48},{20,52},{24,56},{28,60},{32,6... | collective-permute-start | bytes 399368 | tf_op jit(solution)/shard_map/ppermute | solution.py:24
  160.8 7.2 %collective-permute-start.5 = (f32[260,128]{1,0:T(8,128)}, f32[260,128]{1,0:T(8,128)}, u32[]{:S(2)}, u32[]{:S(2)}) collective-permute-start(f32[260,128]{1,0:T(8,128)} %pad_maximum_fusion.4), channel_id=1, source_target_pairs={{0,64},{4,68},{8,72},{12,76},{16,80},{20,84},{24,88},{28,92},{32,9... | collective-permute-start | bytes 399368 | tf_op jit(solution)/shard_map/ppermute | solution.py:24
  170.3 6.5 %collective-permute-start.6 = (f32[260,128]{1,0:T(8,128)}, f32[260,128]{1,0:T(8,128)S(1)}, u32[]{:S(2)}, u32[]{:S(2)}) collective-permute-start(f32[260,128]{1,0:T(8,128)} %pad_maximum_fusion.5), channel_id=1, source_target_pairs={{0,4},{4,8},{8,12},{12,16},{16,20},{20,24},{24,28},{28,32},{32,36}... | collective-permute-start | bytes 399368 | tf_op jit(solution)/shard_map/ppermute | solution.py:24
  172.2 9.2 %collective-permute-start.7 = (f32[260,128]{1,0:T(8,128)}, f32[260,128]{1,0:T(8,128)}, u32[]{:S(2)}, u32[]{:S(2)}) collective-permute-start(f32[260,128]{1,0:T(8,128)} %pad_maximum_fusion.5), channel_id=1, source_target_pairs={{0,132},{4,136},{8,140},{12,144},{16,148},{20,152},{24,156},{28,16... | collective-permute-start | bytes 399368 | tf_op jit(solution)/shard_map/ppermute | solution.py:24
  183.1 4.2 %copy-start.15 = (f32[512]{0:T(512)S(1)}, f32[512]{0:T(512)}, u32[]{:S(2)}) copy-start(f32[512]{0:T(512)} %param.24) | copy-start | bytes 6148
  183.1 4.2 %copy-start.16 = (f32[512]{0:T(512)S(1)}, f32[512]{0:T(512)}, u32[]{:S(2)}) copy-start(f32[512]{0:T(512)} %param.23) | copy-start | bytes 6148
  185.9 17.8 %copy-start.7 = (bf16[128,512]{1,0:T(8,128)(2,1)S(1)}, bf16[128,512]{1,0:T(8,128)(2,1)}, u32[]{:S(2)}) copy-start(bf16[128,512]{1,0:T(8,128)(2,1)} %param.13) | copy-start | bytes 393220
  (1 other events, 0.6 us)

commit v8 on v6

--- a/solution.py
+++ b/solution.py
@@ -59,24 +59,32 @@
     position = lax.axis_index(SEQ) * rows + jnp.arange(rows, dtype=jnp.int32)
     is_start = jnp.any(position[:, None] == first[None, :], axis=1)
     segment = jnp.sum((first[None, :] <= position[:, None]).astype(jnp.int32), axis=1)
+    def blend(previous, rows_normed):
+        base = rows_normed.astype(jnp.float32)
+        delta = previous.astype(jnp.float32) - base
+        return (base[None] + delta[None] * previous_item_mixers[:, None, :]).astype(jnp.bfloat16)
+
+    def project(mixed):
+        return (
+            jnp.einsum(
+                "itd,ide->ite", mixed[:4], mapping_matrices_pile, preferred_element_type=jnp.float32
+            ),
+            jnp.dot(mixed[4], fading_narrow_left, preferred_element_type=jnp.float32),
+        )
+
+    previous = jnp.concatenate([jnp.zeros_like(normed[:1]), normed[: rows - 1]], axis=0)
+    previous = jnp.where(is_start[:, None], jnp.zeros_like(previous), previous)
+    projected, lowrank = project(blend(previous, normed))
     edge = from_behind(normed[rows - 1 :], SEQ, 1)
-    previous = jnp.concatenate([edge, normed[: rows - 1]], axis=0)
-    previous = jnp.where(is_start[:, None], jnp.zeros_like(previous), previous)
-    base = normed.astype(jnp.float32)
-    delta = previous.astype(jnp.float32) - base
-    shifted_blend = (base[None] + delta[None] * previous_item_mixers[:, None, :]).astype(
-        jnp.bfloat16
-    )
-    projected = jnp.einsum(
-        "itd,ide->ite", shifted_blend[:4], mapping_matrices_pile, preferred_element_type=jnp.float32
-    )
+    edge = jnp.where(is_start[0], jnp.zeros_like(edge), edge)
+    edge_projected, edge_lowrank = project(blend(edge, normed[:1]))
+    projected = lax.dynamic_update_slice(projected, edge_projected, (0, 0, 0))
+    lowrank = lax.dynamic_update_slice(lowrank, edge_lowrank, (0, 0))
     recept = projected[0].astype(jnp.bfloat16)
     key_rows = projected[1].astype(jnp.bfloat16)
     value_rows = projected[2].astype(jnp.bfloat16)
     gate = jax.nn.silu(projected[3]).astype(jnp.bfloat16)
-    lowrank_decay_delta = jnp.tanh(
-        jnp.dot(shifted_blend[4], fading_narrow_left, preferred_element_type=jnp.float32)
-    ).astype(jnp.bfloat16)
+    lowrank_decay_delta = jnp.tanh(lowrank).astype(jnp.bfloat16)
     decay_logarithm = -feature_fading_baseline[None, :] * jnp.exp(
         jnp.dot(lowrank_decay_delta, fading_narrow_right, preferred_element_type=jnp.float32)
     )
@@ -106,22 +114,12 @@
     gating_rows_tile, query_array_tile, content_slab, lw_b, seg_b, start_b = inputs
     incl = jnp.einsum("ts,bhsc->bhtc", lower_incl, lw_b, precision=highest)
     excl = incl - lw_b
-    pair_ok = strictly[None] & (seg_b[:, None, :] == seg_b[:, :, None])
-    gap = jnp.minimum(excl[:, :, :, None, :] - incl[:, :, None, :, :], 0.0)
-    weight = jnp.where(pair_ok[:, None, :, :, None], jnp.exp(gap), 0.0)
-    scores = jnp.einsum(
-        "bhtc,bhsc,bhtsc->bhts", gating_rows_tile, query_array_tile, weight, precision=highest
-    )
     present_item_reward = jnp.sum(
         gating_rows_tile * diagonal_extra_contribution[None, :, None, :] * query_array_tile, axis=-1
     )
     seen = jnp.einsum("ts,bs->bt", lower_incl, start_b, precision=highest)
     valid = (seen == 0.0).astype(jnp.float32)
     carried = gating_rows_tile * jnp.exp(excl) * valid[:, None, :, None]
-    intra = (
-        jnp.einsum("bhts,bhsv->bhtv", scores, content_slab, precision=highest)
-        + present_item_reward[..., None] * content_slab
-    )
     total = incl[:, :, block - 1, :]
     keep = (seen[:, block - 1] == 0.0).astype(jnp.float32)
     tail_ok = (seg_b == seg_b[:, block - 1 :]).astype(jnp.float32)
@@ -141,7 +139,6 @@
         alive = alive * keep[index]
     entering = jnp.stack(entering)
     from_start = carried * jnp.stack(reach)[:, :, None, :]
-    outs = intra + jnp.einsum("bhtc,bhcv->bhtv", carried, entering, precision=highest)
     end_state = state
     decay_total = alive * jnp.exp(offset)
 
@@ -154,11 +151,33 @@
         return jnp.concatenate([state, own_decay * got_decay], axis=1)
 
     devices = size_of(SEQ)
+    def block_scores(index, incl_b, excl_b, recept_b, key_b):
+        pair_ok = strictly & (seg_b[index][None, :] == seg_b[index][:, None])
+        gap = jnp.minimum(excl_b[:, :, None, :] - incl_b[:, None, :, :], 0.0)
+        weight = jnp.where(pair_ok[None, :, :, None], jnp.exp(gap), 0.0)
+        return jnp.einsum("htc,hsc,htsc->hts", recept_b, key_b, weight, precision=highest)
+
+    scores = []
     prefix = from_behind(packed, SEQ, 1)
     distance = 1
     while distance < devices:
         prefix = combine(from_behind(prefix, SEQ, distance), prefix)
         distance *= 2
+        index = len(scores)
+        if index < blocks:
+            operands = (incl[index], excl[index], gating_rows_tile[index], query_array_tile[index])
+            prefix, operands = lax.optimization_barrier((prefix, operands))
+            scores.append(block_scores(index, *operands))
+    for index in range(len(scores), blocks):
+        scores.append(
+            block_scores(index, incl[index], excl[index], gating_rows_tile[index], query_array_tile[index])
+        )
+    scores = jnp.stack(scores)
+    outs = (
+        jnp.einsum("bhts,bhsv->bhtv", scores, content_slab, precision=highest)
+        + present_item_reward[..., None] * content_slab
+        + jnp.einsum("bhtc,bhcv->bhtv", carried, entering, precision=highest)
+    )
     incoming = prefix[:, :CHANNELS_ONE_HEAD]
     outs = outs + jnp.einsum("bhtc,hcv->bhtv", from_start, incoming, precision=highest)
     wkv = outs.transpose(0, 2, 1, 3).reshape(rows, mixing_values_divided, CHANNELS_ONE_HEAD)

time: 182 us -> 163 us (0.90)
  the two profiles are of different devices: /device:TPU:24 before, /device:TPU:48 now
where the time goes in v8:
time: 163 us; the launch traced here: 160 us
  other arithmetic  42.7 us (26%)
  starting transfers between devices  29.9 us (18%)
  blocking collectives  25.8 us (16%)
  matrix products  21.7 us (13%)
  waiting for transfers between devices  21.4 us (13%)
  local copies, waits for them, and re-layouts  15.7 us (10%)
  between operations  3.27 us (2%)
    ppermute x8, starting transfers between devices, from_behind(): return lax.ppermute(block, axis, route)  29.9 us
    ppermute x8, waiting for transfers between devices, from_behind(): return lax.ppermute(block, axis, route)  21.4 us
    unnamed x4, other arithmetic  15.1 us
    all_gather x1, blocking collectives, body(): full = lax.all_gather(tier_source_concatenated, 'tp', axis=1, tiled=True)  13.5 us
    all_to_all x1, blocking collectives, body(): pieces = lax.all_to_all(pieces, 'tp', 0, 0, tiled=True)  12.3 us
    dot_general x2, matrix products, project(): jnp.einsum('itd,ide->ite', mixed[:4], mapping_matrices_pile, preferred_el...  10.3 us
    select_n x4, other arithmetic, block_scores(): weight = jnp.where(pair_ok[None, :, :, None], jnp.exp(gap), 0.0)  5.7 us
    dot_general x4, local copies, waits for them, and re-layouts, block_scores(): jnp.einsum('htc,hsc,htsc->hts', recept_b, key_b, weight, precision=highest)  4.81 us
  transfers between devices with their start and end apart: 8, of which 6 were waited for; matrix products, arithmetic and copies ran while one was open for 30% of the time, Pallas kernels for 0%

profile of v8, /device:TPU:48, one launch (start us, length us, event | category | flops | bytes accessed | tf_op | source)
XLA Modules:
  0.0 160.4 jit_solution(1241402684486712582)
XLA Ops:
  0.0 13.5 %all_gather.3 = bf16[128,2048]{1,0:T(8,128)(2,1)S(1)} all-gather(bf16[128,512]{1,0:T(8,128)(2,1)} %param.13), channel_id=1, replica_groups=mesh['seq_hi'=8,'seq_lo'=8,'tp'=4] {'tp'}, dimensions={1}, use_global_device_ids=true | all-gather | bytes 655360 | tf_op jit(solution)/shard_map/all_gather | solution.py:54
  13.9 2.1 %fusion.81 = (f32[128,2048]{1,0:T(8,128)}, bf16[128,2048]{1,0:T(8,128)(2,1)S(1)}) fusion(f32[2048]{0:T(1024)} %param.16, f32[2048]{0:T(1024)} %param.15, f32[128]{0:T(128)S(1)} %add_rsqrt_fusion.1, f32[128]{0:T(128)S(1)} %broadcast_multiply_fusion.1, bf16[128,2048]{1,0:T(8,128)(2,1)S(1)} %all_gather.3), kind=kLoop, calls=%fused_computation.190 | loop fusion | flops 1835008 | bytes 2114560 | tf_op jit(solution)/shard_map/convert_element_type | solution.py:63
  16.1 1.9 %collective-permute-start = (bf16[1,2048]{1,0:T(2,128)(2,1)S(1)}, bf16[1,2048]{1,0:T(2,128)(2,1)S(1)}, u32[]{:S(2)}, u32[]{:S(2)}) collective-permute-start(bf16[1,2048]{1,0:T(2,128)(2,1)S(1)} %get-tuple-element.78), channel_id=1, source_target_pairs={{0,4},{4,8},{8,12},{12,16},{16,20},{20,24},{24,28},{28,32},{32,36}... | collective-permute-start | bytes 12296 | tf_op jit(solution)/shard_map/ppermute | solution.py:24
  22.4 1.8 %add_convert_fusion = bf16[5,128,2048]{2,1,0:T(8,128)(2,1)S(1)} fusion(f32[5,2048]{1,0:T(8,128)S(1)} %copy-done.20, f32[128,2048]{1,0:T(8,128)S(1)} %convert_subtract_fusion.1, f32[128,2048]{1,0:T(8,128)} %get-tuple-element.52), kind=kLoop, calls=%fused_computation | loop fusion | flops 3932160 | bytes 4759552 | tf_op jit(solution)/shard_map/convert_element_type | solution.py:65
  24.3 5.7 %fusion.79 = f32[4,128,512]{2,1,0:T(8,128)} fusion(bf16[4,2048,512]{2,1,0:T(8,128)(2,1)} %param.18, f32[5,2048]{1,0:T(8,128)S(1)} %copy-done.20, f32[128,2048]{1,0:T(8,128)S(1)} %convert_subtract_fusion.1, f32[128,2048]{1,0:T(8,128)S(1)} %copy-done.5), kind=kOutput, calls=%fused_computation.188 | convolution fusion | flops 1077673984 | bytes 11575296 | tf_op jit(solution)/shard_map/itd,ide->ite/dot_general | solution.py:69
  39.5 4.6 %fusion.59 = f32[4,1,512]{2,1,0:T(1,128)S(1)} fusion(bf16[4,2048,512]{2,1,0:T(8,128)(2,1)} %param.18, bf16[4,2048,1]{1,0,2:T(4,128)(2,1)S(1)} %slice_bitcast_fusion.20), kind=kOutput, calls=%fused_computation.138 | convolution fusion | flops 8388608 | bytes 8413184 | tf_op jit(solution)/shard_map/itd,ide->ite/dot_general | solution.py:69
  50.0 2.0 %multiply_bitcast_fusion = (f32[1,8,64]{2,1,0:T(8,128)}, f32[1,8,1,64]{3,1,2,0:T(8,128)S(1)}, f32[1,8,64]{2,1,0:T(8,128)}) fusion(f32[]{:T(128)S(6)} %mul.381, f32[1,8,1,64]{3,1,2,0:T(8,128)} %bitcast.250, f32[1,8,1,64]{3,1,2,0:T(8,128)} %bitcast.249, f32[]{:T(128)} %bitcast.28), kind=kLoop, calls=%fused_computation.170 | loop fusion | flops 1536 | bytes 10248 | tf_op jit(solution)/shard_map/mul | solution.py:136
  53.5 2.0 %fusion.31 = f32[4,8,64,64]{2,3,1,0:T(8,128)S(1)} fusion(f32[4,8,32,64]{3,2,1,0:T(8,128)} %copy-done.3, f32[4,32]{1,0:T(4,128)} %compare_convert_fusion.1, f32[4,8,64]{2,1,0:T(8,128)S(1)} %bitcast.238, bf16[4,32,8,64]{3,2,1,0:T(8,128)(2,1)} %convert_element_type.115, f32[4,32,8,64]{3,2,1,0:T(8,128)S(1)} %reshape.504), kind=kOutput, calls=%fused_computation.58 | convolution fusion | flops 50528256 | bytes 1188352 | tf_op jit(solution)/shard_map/bhsc,bhsv->bhcv/dot_general | solution.py:127
  56.8 3.9 %collective-permute-start.1 = (f32[8,65,64]{1,2,0:T(8,128)S(1)}, f32[8,65,64]{1,2,0:T(8,128)S(1)}, u32[]{:S(2)}, u32[]{:S(2)}) collective-permute-start(f32[8,65,64]{1,2,0:T(8,128)S(1)} %pad_maximum_fusion), channel_id=1, source_target_pairs={{0,4},{4,8},{8,12},{12,16},{16,20},{20,24},{24,28},{28,32},{32,36}... | collective-permute-start | bytes 399368 | tf_op jit(solution)/shard_map/ppermute | solution.py:24
  62.5 2.0 %collective-permute-done.1 = f32[8,65,64]{1,2,0:T(8,128)S(1)} collective-permute-done((f32[8,65,64]{1,2,0:T(8,128)S(1)}, f32[8,65,64]{1,2,0:T(8,128)S(1)}, u32[]{:S(2)}, u32[]{:S(2)}) %collective-permute-start.1) | collective-permute-done | bytes 133152 | tf_op jit(solution)/shard_map/ppermute | solution.py:24
  64.5 1.9 %collective-permute-start.2 = (f32[8,65,64]{1,2,0:T(8,128)S(1)}, f32[8,65,64]{1,2,0:T(8,128)S(1)}, u32[]{:S(2)}, u32[]{:S(2)}) collective-permute-start(f32[8,65,64]{1,2,0:T(8,128)S(1)} %collective-permute-done.1), channel_id=1, source_target_pairs={{0,4},{4,8},{8,12},{12,16},{16,20},{20,24},{24,28},{28,32},{32,36}... | collective-permute-start | bytes 399368 | tf_op jit(solution)/shard_map/ppermute | solution.py:24
  67.3 4.9 %collective-permute-done.2 = f32[8,65,64]{1,2,0:T(8,128)S(1)} collective-permute-done((f32[8,65,64]{1,2,0:T(8,128)S(1)}, f32[8,65,64]{1,2,0:T(8,128)S(1)}, u32[]{:S(2)}, u32[]{:S(2)}) %collective-permute-start.2) | collective-permute-done | bytes 133152 | tf_op jit(solution)/shard_map/ppermute | solution.py:24
  72.7 4.0 %collective-permute-start.3 = (f32[8,65,64]{1,2,0:T(8,128)S(1)}, f32[8,65,64]{1,2,0:T(8,128)S(1)}, u32[]{:S(2)}, u32[]{:S(2)}) collective-permute-start(f32[8,65,64]{1,2,0:T(8,128)S(1)} %pad_maximum_fusion.1), channel_id=1, source_target_pairs={{0,8},{4,12},{8,16},{12,20},{16,24},{20,28},{24,32},{28,36},{32,40... | collective-permute-start | bytes 399368 | tf_op jit(solution)/shard_map/ppermute | solution.py:24
  77.5 4.1 %fusion.3 = f32[8,32,32]{1,2,0:T(8,128)} fusion(f32[8,32,32,64]{3,2,1,0:T(8,128)S(1)} %exponential_select_fusion.3, f32[8,64,32]{1,2,0:T(8,128)S(1)} %bitcast.236, f32[8,64,32]{1,2,0:T(8,128)S(1)} %bitcast.235), kind=kLoop, calls=%fused_computation.8 | loop fusion | flops 1564672 | bytes 2260992
  83.8 8.8 %collective-permute-start.4 = (f32[8,65,64]{1,2,0:T(8,128)S(1)}, f32[8,65,64]{1,2,0:T(8,128)S(1)}, u32[]{:S(2)}, u32[]{:S(2)}) collective-permute-start(f32[8,65,64]{1,2,0:T(8,128)S(1)} %pad_maximum_fusion.2), channel_id=1, source_target_pairs={{0,16},{4,20},{8,24},{12,28},{16,32},{20,36},{24,40},{28,44},{32,4... | collective-permute-start | bytes 399368 | tf_op jit(solution)/shard_map/ppermute | solution.py:24
  94.4 4.1 %fusion.2 = f32[8,32,32]{1,2,0:T(8,128)} fusion(f32[8,32,32,64]{3,2,1,0:T(8,128)S(1)} %exponential_select_fusion.2, f32[8,64,32]{1,2,0:T(8,128)S(1)} %bitcast.234, f32[8,64,32]{1,2,0:T(8,128)S(1)} %bitcast.233), kind=kLoop, calls=%fused_computation.6 | loop fusion | flops 1564672 | bytes 2260992
  101.0 5.8 %collective-permute-start.5 = (f32[8,65,64]{1,2,0:T(8,128)S(1)}, f32[8,65,64]{1,2,0:T(8,128)S(1)}, u32[]{:S(2)}, u32[]{:S(2)}) collective-permute-start(f32[8,65,64]{1,2,0:T(8,128)S(1)} %pad_maximum_fusion.3), channel_id=1, source_target_pairs={{0,32},{4,36},{8,40},{12,44},{16,48},{20,52},{24,56},{28,60},{32,6... | collective-permute-start | bytes 399368 | tf_op jit(solution)/shard_map/ppermute | solution.py:24
  108.3 3.4 %fusion.1 = f32[8,32,32]{1,2,0:T(8,128)S(1)} fusion(f32[8,32,32,64]{3,2,1,0:T(8,128)S(1)} %exponential_select_fusion.1, f32[8,64,32]{1,2,0:T(8,128)S(1)} %bitcast.232, f32[8,64,32]{1,2,0:T(8,128)S(1)} %bitcast.231), kind=kLoop, calls=%fused_computation.4 | loop fusion | flops 1564672 | bytes 2260992
  112.5 6.7 %collective-permute-done.5 = f32[8,65,64]{1,2,0:T(8,128)S(1)} collective-permute-done((f32[8,65,64]{1,2,0:T(8,128)S(1)}, f32[8,65,64]{1,2,0:T(8,128)S(1)}, u32[]{:S(2)}, u32[]{:S(2)}) %collective-permute-start.5) | collective-permute-done | bytes 133152 | tf_op jit(solution)/shard_map/ppermute | solution.py:24
  119.8 1.9 %collective-permute-start.6 = (f32[8,65,64]{1,2,0:T(8,128)S(1)}, f32[8,65,64]{1,2,0:T(8,128)}, u32[]{:S(2)}, u32[]{:S(2)}) collective-permute-start(f32[8,65,64]{1,2,0:T(8,128)S(1)} %pad_maximum_fusion.4), channel_id=1, source_target_pairs={{0,64},{4,68},{8,72},{12,76},{16,80},{20,84},{24,88},{28,92},{32,9... | collective-permute-start | bytes 399368 | tf_op jit(solution)/shard_map/ppermute | solution.py:24
  123.4 3.4 %fusion = f32[8,32,32]{1,2,0:T(8,128)S(1)} fusion(f32[8,32,32,64]{3,2,1,0:T(8,128)S(1)} %exponential_select_fusion, f32[8,64,32]{1,2,0:T(8,128)S(1)} %bitcast.230, f32[8,64,32]{1,2,0:T(8,128)S(1)} %bitcast.229), kind=kLoop, calls=%fused_computation.2 | loop fusion | flops 1564672 | bytes 2260992
  134.0 2.6 %fusion.6 = f32[4,32,8,64]{3,1,2,0:T(8,128)S(1)} fusion(f32[4,32,8,64]{3,1,2,0:T(8,128)S(1)} %fusion.7, f32[1,8,64,64]{2,3,1,0:T(8,128)S(1)} %copy-done.10, f32[1,8,64,64]{2,3,1,0:T(8,128)S(1)} %copy-done.11, f32[1,8,64,64]{2,3,1,0:T(8,128)S(1)} %copy-done.12, f32[4]{0:T(128)} %pad.7.clone, f32[4,8,32,64]{3,2,1,0:T(8,128)S(1)} %copy-done.2, ...), kind=kOutput, calls=%fused_computation.20 | convolution fusion | flops 50921472 | bytes 1442320 | tf_op jit(solution)/shard_map/bhtc,bhcv->bhtv/dot_general | solution.py:179
  136.6 6.9 %collective-permute-done.7 = f32[8,65,64]{1,2,0:T(8,128)S(1)} collective-permute-done((f32[8,65,64]{1,2,0:T(8,128)S(1)}, f32[8,65,64]{1,2,0:T(8,128)S(1)}, u32[]{:S(2)}, u32[]{:S(2)}) %collective-permute-start.7) | collective-permute-done | bytes 133152 | tf_op jit(solution)/shard_map/ppermute | solution.py:24
  147.3 12.3 %all_to_all.5 = bf16[4,128,512]{2,1,0:T(8,128)(2,1)S(1)} all-to-all(bf16[4,128,512]{2,1,0:T(8,128)(2,1)S(1)} %bitcast.223), channel_id=1, replica_groups=mesh['seq_hi'=8,'seq_lo'=8,'tp'=4] {'tp'}, dimensions={0} | all-to-all | bytes 1048576 | tf_op jit(solution)/shard_map/all_to_all | solution.py:194
  (173 shorter events, 46.7 us)
Async XLA Ops:
  0.0 145.8 %copy-start = (bf16[512,2048]{1,0:T(8,128)(2,1)S(1)}, bf16[512,2048]{1,0:T(8,128)(2,1)}, u32[]{:S(2)}) copy-start(bf16[512,2048]{1,0:T(8,128)(2,1)} %param.25) | copy-start | bytes 6291460
  0.0 22.4 %copy-start.20 = (f32[5,2048]{1,0:T(8,128)S(1)}, f32[5,2048]{1,0:T(8,128)}, u32[]{:S(2)}) copy-start(f32[5,2048]{1,0:T(8,128)} %param.17) | copy-start | bytes 122884
  16.1 20.5 %collective-permute-start = (bf16[1,2048]{1,0:T(2,128)(2,1)S(1)}, bf16[1,2048]{1,0:T(2,128)(2,1)S(1)}, u32[]{:S(2)}, u32[]{:S(2)}) collective-permute-start(bf16[1,2048]{1,0:T(2,128)(2,1)S(1)} %get-tuple-element.78), channel_id=1, source_target_pairs={{0,4},{4,8},{8,12},{12,16},{16,20},{20,24},{24,28},{28,32},{32,36}... | collective-permute-start | bytes 12296 | tf_op jit(solution)/shard_map/ppermute | solution.py:24
  24.3 9.2 %copy-start.31 = (f32[512]{0:T(512)S(1)}, f32[512]{0:T(512)}, u32[]{:S(2)}) copy-start(f32[512]{0:T(512)} %param.21) | copy-start | bytes 6148
  24.3 9.2 %copy-start.30 = (f32[512]{0:T(512)S(1)}, f32[512]{0:T(512)}, u32[]{:S(2)}) copy-start(f32[512]{0:T(512)} %param.22) | copy-start | bytes 6148
  24.3 12.7 %copy-start.21 = (bf16[64,512]{1,0:T(8,128)(2,1)S(1)}, bf16[64,512]{1,0:T(8,128)(2,1)}, u32[]{:S(2)}) copy-start(bf16[64,512]{1,0:T(8,128)(2,1)} %param.20) | copy-start | bytes 196612
  55.6 10.8 %copy-start.23 = (f32[8,64]{1,0:T(8,128)S(1)}, f32[8,64]{1,0:T(8,128)}, u32[]{:S(2)}) copy-start(f32[8,64]{1,0:T(8,128)} %mul.402) | copy-start | bytes 6148
  56.6 20.0 %copy-start.22 = (pred[32,32]{1,0:T(8,128)(4,1)S(1)}, pred[32,32]{1,0:T(8,128)(4,1)}, u32[]{:S(2)}) copy-start(pred[32,32]{1,0:T(8,128)(4,1)} %get-tuple-element.118) | copy-start | bytes 3076
  56.8 7.7 %collective-permute-start.1 = (f32[8,65,64]{1,2,0:T(8,128)S(1)}, f32[8,65,64]{1,2,0:T(8,128)S(1)}, u32[]{:S(2)}, u32[]{:S(2)}) collective-permute-start(f32[8,65,64]{1,2,0:T(8,128)S(1)} %pad_maximum_fusion), channel_id=1, source_target_pairs={{0,4},{4,8},{8,12},{12,16},{16,20},{20,24},{24,28},{28,32},{32,36}... | collective-permute-start | bytes 399368 | tf_op jit(solution)/shard_map/ppermute | solution.py:24
  64.5 7.7 %collective-permute-start.2 = (f32[8,65,64]{1,2,0:T(8,128)S(1)}, f32[8,65,64]{1,2,0:T(8,128)S(1)}, u32[]{:S(2)}, u32[]{:S(2)}) collective-permute-start(f32[8,65,64]{1,2,0:T(8,128)S(1)} %collective-permute-done.1), channel_id=1, source_target_pairs={{0,4},{4,8},{8,12},{12,16},{16,20},{20,24},{24,28},{28,32},{32,36}... | collective-permute-start | bytes 399368 | tf_op jit(solution)/shard_map/ppermute | solution.py:24
  72.7 10.6 %collective-permute-start.3 = (f32[8,65,64]{1,2,0:T(8,128)S(1)}, f32[8,65,64]{1,2,0:T(8,128)S(1)}, u32[]{:S(2)}, u32[]{:S(2)}) collective-permute-start(f32[8,65,64]{1,2,0:T(8,128)S(1)} %pad_maximum_fusion.1), channel_id=1, source_target_pairs={{0,8},{4,12},{8,16},{12,20},{16,24},{20,28},{24,32},{28,36},{32,40... | collective-permute-start | bytes 399368 | tf_op jit(solution)/shard_map/ppermute | solution.py:24
  83.2 11.1 %copy-start.17 = (f32[8,32,64]{2,1,0:T(8,128)S(1)}, f32[8,32,64]{2,1,0:T(8,128)}, u32[]{:S(2)}) copy-start(f32[8,32,64]{2,1,0:T(8,128)} %get-tuple-element.32) | copy-start | bytes 196612
  83.2 11.1 %copy-start.18 = (f32[8,32,64]{2,1,0:T(8,128)S(1)}, f32[8,32,64]{2,1,0:T(8,128)}, u32[]{:S(2)}) copy-start(f32[8,32,64]{2,1,0:T(8,128)} %get-tuple-element.33) | copy-start | bytes 196612
  83.8 16.7 %collective-permute-start.4 = (f32[8,65,64]{1,2,0:T(8,128)S(1)}, f32[8,65,64]{1,2,0:T(8,128)S(1)}, u32[]{:S(2)}, u32[]{:S(2)}) collective-permute-start(f32[8,65,64]{1,2,0:T(8,128)S(1)} %pad_maximum_fusion.2), channel_id=1, source_target_pairs={{0,16},{4,20},{8,24},{12,28},{16,32},{20,36},{24,40},{28,44},{32,4... | collective-permute-start | bytes 399368 | tf_op jit(solution)/shard_map/ppermute | solution.py:24
  101.0 18.3 %collective-permute-start.5 = (f32[8,65,64]{1,2,0:T(8,128)S(1)}, f32[8,65,64]{1,2,0:T(8,128)S(1)}, u32[]{:S(2)}, u32[]{:S(2)}) collective-permute-start(f32[8,65,64]{1,2,0:T(8,128)S(1)} %pad_maximum_fusion.3), channel_id=1, source_target_pairs={{0,32},{4,36},{8,40},{12,44},{16,48},{20,52},{24,56},{28,60},{32,6... | collective-permute-start | bytes 399368 | tf_op jit(solution)/shard_map/ppermute | solution.py:24
  112.5 10.9 %copy-start.13 = (f32[8,32,64]{2,1,0:T(8,128)S(1)}, f32[8,32,64]{2,1,0:T(8,128)}, u32[]{:S(2)}) copy-start(f32[8,32,64]{2,1,0:T(8,128)} %get-tuple-element.42) | copy-start | bytes 196612
  112.5 10.9 %copy-start.14 = (f32[8,32,64]{2,1,0:T(8,128)S(1)}, f32[8,32,64]{2,1,0:T(8,128)}, u32[]{:S(2)}) copy-start(f32[8,32,64]{2,1,0:T(8,128)} %get-tuple-element.43) | copy-start | bytes 196612
  119.8 10.2 %collective-permute-start.6 = (f32[8,65,64]{1,2,0:T(8,128)S(1)}, f32[8,65,64]{1,2,0:T(8,128)}, u32[]{:S(2)}, u32[]{:S(2)}) collective-permute-start(f32[8,65,64]{1,2,0:T(8,128)S(1)} %pad_maximum_fusion.4), channel_id=1, source_target_pairs={{0,64},{4,68},{8,72},{12,76},{16,80},{20,84},{24,88},{28,92},{32,9... | collective-permute-start | bytes 399368 | tf_op jit(solution)/shard_map/ppermute | solution.py:24
  123.4 10.6 %copy-start.2 = (f32[4,8,32,64]{3,2,1,0:T(8,128)S(1)}, f32[4,8,32,64]{3,2,1,0:T(8,128)}, u32[]{:S(2)}) copy-start(f32[4,8,32,64]{3,2,1,0:T(8,128)} %get-tuple-element.101) | copy-start | bytes 786436
  127.6 15.9 %copy-start.27 = (f32[4,32]{1,0:T(4,128)S(1)}, f32[4,32]{1,0:T(4,128)}, u32[]{:S(2)}) copy-start(f32[4,32]{1,0:T(4,128)} %get-tuple-element.103) | copy-start | bytes 1540
  132.4 11.1 %collective-permute-start.7 = (f32[8,65,64]{1,2,0:T(8,128)S(1)}, f32[8,65,64]{1,2,0:T(8,128)S(1)}, u32[]{:S(2)}, u32[]{:S(2)}) collective-permute-start(f32[8,65,64]{1,2,0:T(8,128)S(1)} %pad_maximum_fusion.5), channel_id=1, source_target_pairs={{0,128},{4,132},{8,136},{12,140},{16,144},{20,148},{24,152},{28,15... | collective-permute-start | bytes 399368 | tf_op jit(solution)/shard_map/ppermute | solution.py:24
  134.0 11.8 %copy-start.28 = (f32[512]{0:T(512)S(1)}, f32[512]{0:T(512)}, u32[]{:S(2)}) copy-start(f32[512]{0:T(512)} %param.24) | copy-start | bytes 6148
  134.0 11.8 %copy-start.29 = (f32[512]{0:T(512)S(1)}, f32[512]{0:T(512)}, u32[]{:S(2)}) copy-start(f32[512]{0:T(512)} %param.23) | copy-start | bytes 6148
  145.3 14.4 %copy-start.19 = (bf16[128,512]{1,0:T(8,128)(2,1)S(1)}, bf16[128,512]{1,0:T(8,128)(2,1)}, u32[]{:S(2)}) copy-start(bf16[128,512]{1,0:T(8,128)(2,1)} %param.13) | copy-start | bytes 393220
  (18 other events, 111.7 us)

commit v9 on v8

--- a/solution.py
+++ b/solution.py
@@ -64,26 +64,25 @@
         delta = previous.astype(jnp.float32) - base
         return (base[None] + delta[None] * previous_item_mixers[:, None, :]).astype(jnp.bfloat16)
 
-    def project(mixed):
-        return (
-            jnp.einsum(
-                "itd,ide->ite", mixed[:4], mapping_matrices_pile, preferred_element_type=jnp.float32
-            ),
-            jnp.dot(mixed[4], fading_narrow_left, preferred_element_type=jnp.float32),
-        )
+    def project(mixed, index):
+        return jnp.dot(mixed[index], mapping_matrices_pile[index], preferred_element_type=jnp.float32)
+
+    def fixed(index, mixed, edge_mixed):
+        return lax.dynamic_update_slice(project(mixed, index), project(edge_mixed, index), (0, 0))
 
     previous = jnp.concatenate([jnp.zeros_like(normed[:1]), normed[: rows - 1]], axis=0)
     previous = jnp.where(is_start[:, None], jnp.zeros_like(previous), previous)
-    projected, lowrank = project(blend(previous, normed))
+    mixed = blend(previous, normed)
     edge = from_behind(normed[rows - 1 :], SEQ, 1)
     edge = jnp.where(is_start[0], jnp.zeros_like(edge), edge)
-    edge_projected, edge_lowrank = project(blend(edge, normed[:1]))
-    projected = lax.dynamic_update_slice(projected, edge_projected, (0, 0, 0))
-    lowrank = lax.dynamic_update_slice(lowrank, edge_lowrank, (0, 0))
-    recept = projected[0].astype(jnp.bfloat16)
-    key_rows = projected[1].astype(jnp.bfloat16)
-    value_rows = projected[2].astype(jnp.bfloat16)
-    gate = jax.nn.silu(projected[3]).astype(jnp.bfloat16)
+    edge_mixed = blend(edge, normed[:1])
+    key_rows = fixed(1, mixed, edge_mixed).astype(jnp.bfloat16)
+    value_rows = fixed(2, mixed, edge_mixed).astype(jnp.bfloat16)
+    lowrank = lax.dynamic_update_slice(
+        jnp.dot(mixed[4], fading_narrow_left, preferred_element_type=jnp.float32),
+        jnp.dot(edge_mixed[4], fading_narrow_left, preferred_element_type=jnp.float32),
+        (0, 0),
+    )
     lowrank_decay_delta = jnp.tanh(lowrank).astype(jnp.bfloat16)
     decay_logarithm = -feature_fading_baseline[None, :] * jnp.exp(
         jnp.dot(lowrank_decay_delta, fading_narrow_right, preferred_element_type=jnp.float32)
@@ -97,7 +96,6 @@
         )
 
     inputs = (
-        split_heads(recept),
         split_heads(key_rows),
         split_heads(value_rows),
         split_heads(decay_logarithm),
@@ -111,15 +109,12 @@
         mixing_values_divided, CHANNELS_ONE_HEAD
     )
 
-    gating_rows_tile, query_array_tile, content_slab, lw_b, seg_b, start_b = inputs
+    query_array_tile, content_slab, lw_b, seg_b, start_b = inputs
     incl = jnp.einsum("ts,bhsc->bhtc", lower_incl, lw_b, precision=highest)
     excl = incl - lw_b
-    present_item_reward = jnp.sum(
-        gating_rows_tile * diagonal_extra_contribution[None, :, None, :] * query_array_tile, axis=-1
-    )
     seen = jnp.einsum("ts,bs->bt", lower_incl, start_b, precision=highest)
     valid = (seen == 0.0).astype(jnp.float32)
-    carried = gating_rows_tile * jnp.exp(excl) * valid[:, None, :, None]
+    decay_factor = jnp.exp(excl) * valid[:, None, :, None]
     total = incl[:, :, block - 1, :]
     keep = (seen[:, block - 1] == 0.0).astype(jnp.float32)
     tail_ok = (seg_b == seg_b[:, block - 1 :]).astype(jnp.float32)
@@ -138,7 +133,7 @@
         offset = offset + total[index]
         alive = alive * keep[index]
     entering = jnp.stack(entering)
-    from_start = carried * jnp.stack(reach)[:, :, None, :]
+    reach = jnp.stack(reach)[:, :, None, :]
     end_state = state
     decay_total = alive * jnp.exp(offset)
 
@@ -159,6 +154,15 @@
 
     scores = []
     prefix = from_behind(packed, SEQ, 1)
+    prefix, late = lax.optimization_barrier((prefix, (mixed, edge_mixed)))
+    recept = fixed(0, *late).astype(jnp.bfloat16)
+    gate = jax.nn.silu(fixed(3, *late)).astype(jnp.bfloat16)
+    gating_rows_tile = split_heads(recept)
+    carried = gating_rows_tile * decay_factor
+    from_start = carried * reach
+    present_item_reward = jnp.sum(
+        gating_rows_tile * diagonal_extra_contribution[None, :, None, :] * query_array_tile, axis=-1
+    )
     distance = 1
     while distance < devices:
         prefix = combine(from_behind(prefix, SEQ, distance), prefix)

time: 163 us -> 174 us (1.067)
  matrix products: 21.7 us -> 29.7 us
  local copies, waits for them, and re-layouts: 15.7 us -> 17.5 us
    dot_general x4 -> x10, matrix products: 10.8 us -> 19.9 us  [the longest x8 19.3 us: project(): jnp.dot(mixed[index], mapping_matrices_pile[index], preferred_element_typ...]
    dynamic_update_slice x2 -> x5, local copies, waits for them, and re-layouts: 0.24 us -> 2.83 us  [the longest x4 2.73 us: fixed(): lax.dynamic_update_slice(project(mixed, index), project(edge_mixed, index...]
  transfers between devices with their start and end apart: 8 -> 8, of which waited for: 6 -> 5; matrix products, arithmetic and copies ran while one was open for 30% -> 30% of each run, Pallas kernels for 0% -> 0%
where the time goes in v9:
time: 174 us; the launch traced here: 172 us
  other arithmetic  43.1 us (25%)
  starting transfers between devices  30.9 us (18%)
  matrix products  29.7 us (17%)
  blocking collectives  25.6 us (15%)
  waiting for transfers between devices  22.3 us (13%)
  local copies, waits for them, and re-layouts  17.5 us (10%)
  between operations  3.4 us (2%)
    ppermute x8, starting transfers between devices, from_behind(): return lax.ppermute(block, axis, route)  30.9 us
    ppermute x8, waiting for transfers between devices, from_behind(): return lax.ppermute(block, axis, route)  22.3 us
    dot_general x8, matrix products, project(): jnp.dot(mixed[index], mapping_matrices_pile[index], preferred_element_typ...  19.3 us
    unnamed x4, other arithmetic  15.1 us
    all_gather x1, blocking collectives, body(): full = lax.all_gather(tier_source_concatenated, 'tp', axis=1, tiled=True)  13.5 us
    all_to_all x1, blocking collectives, body(): pieces = lax.all_to_all(pieces, 'tp', 0, 0, tiled=True)  12.1 us
    select_n x4, other arithmetic, block_scores(): weight = jnp.where(pair_ok[None, :, :, None], jnp.exp(gap), 0.0)  6.37 us
    dot_general x4, local copies, waits for them, and re-layouts, block_scores(): jnp.einsum('htc,hsc,htsc->hts', recept_b, key_b, weight, precision=highest)  4.82 us
  transfers between devices with their start and end apart: 8, of which 5 were waited for; matrix products, arithmetic and copies ran while one was open for 30% of the time, Pallas kernels for 0%

profile of v9, /device:TPU:48, one launch (start us, length us, event | category | flops | bytes accessed | tf_op | source)
XLA Modules:
  0.0 172.4 jit_solution(14887884325997624019)
XLA Ops:
  0.0 13.5 %all_gather.3 = bf16[128,2048]{1,0:T(8,128)(2,1)S(1)} all-gather(bf16[128,512]{1,0:T(8,128)(2,1)} %param.13), channel_id=1, replica_groups=mesh['seq_hi'=8,'seq_lo'=8,'tp'=4] {'tp'}, dimensions={1}, use_global_device_ids=true | all-gather | bytes 655360 | tf_op jit(solution)/shard_map/all_gather | solution.py:54
  13.9 2.1 %fusion.111 = (f32[128,2048]{1,0:T(8,128)}, bf16[128,2048]{1,0:T(8,128)(2,1)S(1)}) fusion(f32[2048]{0:T(1024)} %param.16, f32[2048]{0:T(1024)} %param.15, f32[128]{0:T(128)S(1)} %add_rsqrt_fusion.1, f32[128]{0:T(128)S(1)} %broadcast_multiply_fusion.1, bf16[128,2048]{1,0:T(8,128)(2,1)S(1)} %all_gather.3), kind=kLoop, calls=%fused_computation.220 | loop fusion | flops 1835008 | bytes 2114560 | tf_op jit(solution)/shard_map/convert_element_type | solution.py:63
  22.1 3.0 %fusion.14 = bf16[128,512]{1,0:T(8,128)(2,1)S(1)} fusion(bf16[4,2048,512]{2,1,0:T(8,128)(2,1)} %param.18, bf16[5,128,2048]{2,1,0:T(8,128)(2,1)S(1)} %add_convert_fusion), kind=kOutput, calls=%fused_computation.24 | convolution fusion | flops 268435456 | bytes 2752512 | tf_op jit(solution)/shard_map/dot_general | solution.py:68
  25.1 2.1 %fusion.18 = bf16[128,512]{1,0:T(8,128)(2,1)S(1)} fusion(bf16[4,2048,512]{2,1,0:T(8,128)(2,1)} %param.18, bf16[5,128,2048]{2,1,0:T(8,128)(2,1)S(1)} %add_convert_fusion), kind=kOutput, calls=%fused_computation.28 | convolution fusion | flops 268435456 | bytes 2752512 | tf_op jit(solution)/shard_map/dot_general | solution.py:68
  35.1 2.0 %fusion.12 = bf16[1,512]{1,0:T(2,128)(2,1)S(1)} fusion(bf16[4,2048,512]{2,1,0:T(8,128)(2,1)} %param.18, bf16[5,2048]{1,0:T(8,128)(2,1)S(1)} %add_convert_fusion.2), kind=kOutput, calls=%fused_computation.22 | convolution fusion | flops 2097152 | bytes 2106368 | tf_op jit(solution)/shard_map/dot_general | solution.py:68
  37.1 2.0 %fusion.16 = bf16[1,512]{1,0:T(2,128)(2,1)S(1)} fusion(bf16[4,2048,512]{2,1,0:T(8,128)(2,1)} %param.18, bf16[5,2048]{1,0:T(8,128)(2,1)S(1)} %add_convert_fusion.2), kind=kOutput, calls=%fused_computation.26 | convolution fusion | flops 2097152 | bytes 2106368 | tf_op jit(solution)/shard_map/dot_general | solution.py:68
  49.7 3.9 %collective-permute-start.1 = (f32[8,65,64]{1,2,0:T(8,128)S(1)}, f32[8,65,64]{1,2,0:T(8,128)S(1)}, u32[]{:S(2)}, u32[]{:S(2)}) collective-permute-start(f32[8,65,64]{1,2,0:T(8,128)S(1)} %pad_maximum_fusion), channel_id=1, source_target_pairs={{0,4},{4,8},{8,12},{12,16},{16,20},{20,24},{24,28},{28,32},{32,36}... | collective-permute-start | bytes 399368 | tf_op jit(solution)/shard_map/ppermute | solution.py:24
  54.6 2.7 %collective-permute-done.1 = f32[8,65,64]{1,2,0:T(8,128)S(1)} collective-permute-done((f32[8,65,64]{1,2,0:T(8,128)S(1)}, f32[8,65,64]{1,2,0:T(8,128)S(1)}, u32[]{:S(2)}, u32[]{:S(2)}) %collective-permute-start.1) | collective-permute-done | bytes 133152 | tf_op jit(solution)/shard_map/ppermute | solution.py:24
  57.4 2.6 %fusion.4 = f32[1,512]{1,0:T(1,128)} fusion(bf16[4,2048,512]{2,1,0:T(8,128)(2,1)} %param.18, bf16[5,1,2048]{2,0,1:T(8,128)(2,1)S(1)} %copy-done.23), kind=kOutput, calls=%fused_computation.14 | convolution fusion | flops 2097152 | bytes 2107392 | tf_op jit(solution)/shard_map/dot_general | solution.py:68
  61.9 2.9 %fusion.10 = bf16[128,512]{1,0:T(8,128)(2,1)} fusion(bf16[4,2048,512]{2,1,0:T(8,128)(2,1)} %param.18, bf16[5,128,2048]{2,1,0:T(8,128)(2,1)} %copy-done.5), kind=kOutput, calls=%fused_computation.20 | convolution fusion | flops 268435456 | bytes 2752512 | tf_op jit(solution)/shard_map/dot_general | solution.py:68
  64.8 2.9 %fusion.6 = f32[128,512]{1,0:T(8,128)} fusion(bf16[4,2048,512]{2,1,0:T(8,128)(2,1)} %param.18, bf16[5,128,2048]{2,1,0:T(8,128)(2,1)} %copy-done.5), kind=kOutput, calls=%fused_computation.16 | convolution fusion | flops 268435456 | bytes 2883584 | tf_op jit(solution)/shard_map/dot_general | solution.py:68
  78.2 4.0 %collective-permute-start.3 = (f32[8,65,64]{1,2,0:T(8,128)S(1)}, f32[8,65,64]{1,2,0:T(8,128)S(1)}, u32[]{:S(2)}, u32[]{:S(2)}) collective-permute-start(f32[8,65,64]{1,2,0:T(8,128)S(1)} %pad_maximum_fusion.1), channel_id=1, source_target_pairs={{0,8},{4,12},{8,16},{12,20},{16,24},{20,28},{24,32},{28,36},{32,40... | collective-permute-start | bytes 399368 | tf_op jit(solution)/shard_map/ppermute | solution.py:24
  84.0 4.1 %fusion.3 = f32[8,32,32]{1,2,0:T(8,128)} fusion(f32[8,32,32,64]{3,2,1,0:T(8,128)S(1)} %exponential_select_fusion.3, f32[8,64,32]{1,2,0:T(8,128)S(1)} %bitcast.272, f32[8,64,32]{1,2,0:T(8,128)S(1)} %bitcast.268), kind=kLoop, calls=%fused_computation.8 | loop fusion | flops 1564672 | bytes 2260992
  90.9 7.9 %collective-permute-start.4 = (f32[8,65,64]{1,2,0:T(8,128)S(1)}, f32[8,65,64]{1,2,0:T(8,128)S(1)}, u32[]{:S(2)}, u32[]{:S(2)}) collective-permute-start(f32[8,65,64]{1,2,0:T(8,128)S(1)} %pad_maximum_fusion.2), channel_id=1, source_target_pairs={{0,16},{4,20},{8,24},{12,28},{16,32},{20,36},{24,40},{28,44},{32,4... | collective-permute-start | bytes 399368 | tf_op jit(solution)/shard_map/ppermute | solution.py:24
  100.3 4.1 %fusion.2 = f32[8,32,32]{1,2,0:T(8,128)} fusion(f32[8,32,32,64]{3,2,1,0:T(8,128)S(1)} %exponential_select_fusion.2, f32[8,64,32]{1,2,0:T(8,128)S(1)} %bitcast.271, f32[8,64,32]{1,2,0:T(8,128)S(1)} %bitcast.267), kind=kLoop, calls=%fused_computation.6 | loop fusion | flops 1564672 | bytes 2260992
  106.1 4.1 %collective-permute-done.4 = f32[8,65,64]{1,2,0:T(8,128)S(1)} collective-permute-done((f32[8,65,64]{1,2,0:T(8,128)S(1)}, f32[8,65,64]{1,2,0:T(8,128)S(1)}, u32[]{:S(2)}, u32[]{:S(2)}) %collective-permute-start.4) | collective-permute-done | bytes 133152 | tf_op jit(solution)/shard_map/ppermute | solution.py:24
  110.7 6.0 %collective-permute-start.5 = (f32[8,65,64]{1,2,0:T(8,128)S(1)}, f32[8,65,64]{1,2,0:T(8,128)S(1)}, u32[]{:S(2)}, u32[]{:S(2)}) collective-permute-start(f32[8,65,64]{1,2,0:T(8,128)S(1)} %pad_maximum_fusion.3), channel_id=1, source_target_pairs={{0,32},{4,36},{8,40},{12,44},{16,48},{20,52},{24,56},{28,60},{32,6... | collective-permute-start | bytes 399368 | tf_op jit(solution)/shard_map/ppermute | solution.py:24
  118.2 3.4 %fusion.1 = f32[8,32,32]{1,2,0:T(8,128)S(1)} fusion(f32[8,32,32,64]{3,2,1,0:T(8,128)S(1)} %exponential_select_fusion.1, f32[8,64,32]{1,2,0:T(8,128)S(1)} %bitcast.270, f32[8,64,32]{1,2,0:T(8,128)S(1)} %bitcast.266), kind=kLoop, calls=%fused_computation.4 | loop fusion | flops 1564672 | bytes 2260992
  122.4 8.3 %collective-permute-done.5 = f32[8,65,64]{1,2,0:T(8,128)S(1)} collective-permute-done((f32[8,65,64]{1,2,0:T(8,128)S(1)}, f32[8,65,64]{1,2,0:T(8,128)S(1)}, u32[]{:S(2)}, u32[]{:S(2)}) %collective-permute-start.5) | collective-permute-done | bytes 133152 | tf_op jit(solution)/shard_map/ppermute | solution.py:24
  131.3 3.6 %collective-permute-start.6 = (f32[8,65,64]{1,2,0:T(8,128)S(1)}, f32[8,65,64]{1,2,0:T(8,128)}, u32[]{:S(2)}, u32[]{:S(2)}) collective-permute-start(f32[8,65,64]{1,2,0:T(8,128)S(1)} %pad_maximum_fusion.4), channel_id=1, source_target_pairs={{0,64},{4,68},{8,72},{12,76},{16,80},{20,84},{24,88},{28,92},{32,9... | collective-permute-start | bytes 399368 | tf_op jit(solution)/shard_map/ppermute | solution.py:24
  136.6 3.4 %fusion = f32[8,32,32]{1,2,0:T(8,128)S(1)} fusion(f32[8,32,32,64]{3,2,1,0:T(8,128)S(1)} %exponential_select_fusion, f32[8,64,32]{1,2,0:T(8,128)S(1)} %bitcast.269, f32[8,64,32]{1,2,0:T(8,128)S(1)} %bitcast.265), kind=kLoop, calls=%fused_computation.2 | loop fusion | flops 1564672 | bytes 2260992
  146.8 2.6 %fusion.30 = f32[4,32,8,64]{3,1,2,0:T(8,128)S(1)} fusion(f32[4,32,8,64]{3,1,2,0:T(8,128)S(1)} %fusion.31, f32[1,8,64,64]{2,3,1,0:T(8,128)S(1)} %copy-done.6, f32[1,8,64,64]{2,3,1,0:T(8,128)S(1)} %copy-done.7, f32[1,8,64,64]{2,3,1,0:T(8,128)S(1)} %copy-done.8, f32[4]{0:T(128)} %pad.7.clone, f32[4,8,32,64]{3,2,1,0:T(8,128)S(1)} %copy-done.2, ...), kind=kOutput, calls=%fused_computation.44 | convolution fusion | flops 50921472 | bytes 1442320 | tf_op jit(solution)/shard_map/bhtc,bhcv->bhtv/dot_general | solution.py:183
  149.3 6.6 %collective-permute-done.7 = f32[8,65,64]{1,2,0:T(8,128)S(1)} collective-permute-done((f32[8,65,64]{1,2,0:T(8,128)S(1)}, f32[8,65,64]{1,2,0:T(8,128)S(1)}, u32[]{:S(2)}, u32[]{:S(2)}) %collective-permute-start.7) | collective-permute-done | bytes 133152 | tf_op jit(solution)/shard_map/ppermute | solution.py:24
  159.5 12.1 %all_to_all.5 = bf16[4,128,512]{2,1,0:T(8,128)(2,1)S(1)} all-to-all(bf16[4,128,512]{2,1,0:T(8,128)(2,1)S(1)} %bitcast.261), channel_id=1, replica_groups=mesh['seq_hi'=8,'seq_lo'=8,'tp'=4] {'tp'}, dimensions={0} | all-to-all | bytes 1048576 | tf_op jit(solution)/shard_map/all_to_all | solution.py:198
  (179 shorter events, 59.0 us)
Async XLA Ops:
  0.0 158.2 %copy-start = (bf16[512,2048]{1,0:T(8,128)(2,1)S(1)}, bf16[512,2048]{1,0:T(8,128)(2,1)}, u32[]{:S(2)}) copy-start(bf16[512,2048]{1,0:T(8,128)(2,1)} %param.25) | copy-start | bytes 6291460
  0.0 20.2 %copy-start.9 = (f32[5,2048]{1,0:T(8,128)S(1)}, f32[5,2048]{1,0:T(8,128)}, u32[]{:S(2)}) copy-start(f32[5,2048]{1,0:T(8,128)} %param.17) | copy-start | bytes 122884
  16.1 19.0 %collective-permute-start = (bf16[1,2048]{1,0:T(2,128)(2,1)S(1)}, bf16[1,2048]{1,0:T(2,128)(2,1)S(1)}, u32[]{:S(2)}, u32[]{:S(2)}) collective-permute-start(bf16[1,2048]{1,0:T(2,128)(2,1)S(1)} %get-tuple-element.81), channel_id=1, source_target_pairs={{0,4},{4,8},{8,12},{12,16},{16,20},{20,24},{24,28},{28,32},{32,36}... | collective-permute-start | bytes 12296 | tf_op jit(solution)/shard_map/ppermute | solution.py:24
  25.1 14.9 %copy-start.25 = (bf16[64,512]{1,0:T(8,128)(2,1)S(1)}, bf16[64,512]{1,0:T(8,128)(2,1)}, u32[]{:S(2)}) copy-start(bf16[64,512]{1,0:T(8,128)(2,1)} %param.20) | copy-start | bytes 196612
  40.9 12.7 %copy-start.1 = (f32[4,8,32,64]{3,2,1,0:T(8,128)}, f32[4,8,32,64]{3,2,1,0:T(8,128)S(1)}, u32[]{:S(2)}) copy-start(f32[4,8,32,64]{3,2,1,0:T(8,128)S(1)} %get-tuple-element.104) | copy-start | bytes 786436
  46.5 10.8 %copy-start.23 = (bf16[5,1,2048]{2,0,1:T(8,128)(2,1)S(1)}, bf16[5,1,2048]{2,0,1:T(8,128)(2,1)}, u32[]{:S(2)}) copy-start(bf16[5,1,2048]{2,0,1:T(8,128)(2,1)} %fusion.122) | copy-start | bytes 61444
  49.7 7.7 %collective-permute-start.1 = (f32[8,65,64]{1,2,0:T(8,128)S(1)}, f32[8,65,64]{1,2,0:T(8,128)S(1)}, u32[]{:S(2)}, u32[]{:S(2)}) collective-permute-start(f32[8,65,64]{1,2,0:T(8,128)S(1)} %pad_maximum_fusion), channel_id=1, source_target_pairs={{0,4},{4,8},{8,12},{12,16},{16,20},{20,24},{24,28},{28,32},{32,36}... | collective-permute-start | bytes 399368 | tf_op jit(solution)/shard_map/ppermute | solution.py:24
  67.7 8.1 %collective-permute-start.2 = (f32[8,65,64]{1,2,0:T(8,128)S(1)}, f32[8,65,64]{1,2,0:T(8,128)}, u32[]{:S(2)}, u32[]{:S(2)}) collective-permute-start(f32[8,65,64]{1,2,0:T(8,128)S(1)} %collective-permute-done.1), channel_id=1, source_target_pairs={{0,4},{4,8},{8,12},{12,16},{16,20},{20,24},{24,28},{28,32},{32,36}... | collective-permute-start | bytes 399368 | tf_op jit(solution)/shard_map/ppermute | solution.py:24
  78.2 12.1 %collective-permute-start.3 = (f32[8,65,64]{1,2,0:T(8,128)S(1)}, f32[8,65,64]{1,2,0:T(8,128)S(1)}, u32[]{:S(2)}, u32[]{:S(2)}) collective-permute-start(f32[8,65,64]{1,2,0:T(8,128)S(1)} %pad_maximum_fusion.1), channel_id=1, source_target_pairs={{0,8},{4,12},{8,16},{12,20},{16,24},{20,28},{24,32},{28,36},{32,40... | collective-permute-start | bytes 399368 | tf_op jit(solution)/shard_map/ppermute | solution.py:24
  84.0 14.8 %copy-start.12 = (f32[8,32,64]{2,1,0:T(8,128)S(1)}, f32[8,32,64]{2,1,0:T(8,128)}, u32[]{:S(2)}) copy-start(f32[8,32,64]{2,1,0:T(8,128)} %get-tuple-element.36) | copy-start | bytes 196612
  84.0 14.8 %copy-start.13 = (f32[8,32,64]{2,1,0:T(8,128)S(1)}, f32[8,32,64]{2,1,0:T(8,128)}, u32[]{:S(2)}) copy-start(f32[8,32,64]{2,1,0:T(8,128)} %get-tuple-element.37) | copy-start | bytes 196612
  90.9 19.3 %collective-permute-start.4 = (f32[8,65,64]{1,2,0:T(8,128)S(1)}, f32[8,65,64]{1,2,0:T(8,128)S(1)}, u32[]{:S(2)}, u32[]{:S(2)}) collective-permute-start(f32[8,65,64]{1,2,0:T(8,128)S(1)} %pad_maximum_fusion.2), channel_id=1, source_target_pairs={{0,16},{4,20},{8,24},{12,28},{16,32},{20,36},{24,40},{28,44},{32,4... | collective-permute-start | bytes 399368 | tf_op jit(solution)/shard_map/ppermute | solution.py:24
  100.3 16.4 %copy-start.10 = (f32[8,32,64]{2,1,0:T(8,128)S(1)}, f32[8,32,64]{2,1,0:T(8,128)}, u32[]{:S(2)}) copy-start(f32[8,32,64]{2,1,0:T(8,128)} %get-tuple-element.41) | copy-start | bytes 196612
  100.3 16.4 %copy-start.11 = (f32[8,32,64]{2,1,0:T(8,128)S(1)}, f32[8,32,64]{2,1,0:T(8,128)}, u32[]{:S(2)}) copy-start(f32[8,32,64]{2,1,0:T(8,128)} %get-tuple-element.42) | copy-start | bytes 196612
  106.1 12.1 %copy-start.16 = (f32[8,32,64]{2,1,0:T(8,128)S(1)}, f32[8,32,64]{2,1,0:T(8,128)}, u32[]{:S(2)}) copy-start(f32[8,32,64]{2,1,0:T(8,128)} %get-tuple-element.43) | copy-start | bytes 196612
  106.1 12.1 %copy-start.20 = (f32[8,32,64]{2,1,0:T(8,128)S(1)}, f32[8,32,64]{2,1,0:T(8,128)}, u32[]{:S(2)}) copy-start(f32[8,32,64]{2,1,0:T(8,128)} %get-tuple-element.44) | copy-start | bytes 196612
  110.7 20.0 %collective-permute-start.5 = (f32[8,65,64]{1,2,0:T(8,128)S(1)}, f32[8,65,64]{1,2,0:T(8,128)S(1)}, u32[]{:S(2)}, u32[]{:S(2)}) collective-permute-start(f32[8,65,64]{1,2,0:T(8,128)S(1)} %pad_maximum_fusion.3), channel_id=1, source_target_pairs={{0,32},{4,36},{8,40},{12,44},{16,48},{20,52},{24,56},{28,60},{32,6... | collective-permute-start | bytes 399368 | tf_op jit(solution)/shard_map/ppermute | solution.py:24
  122.4 14.2 %copy-start.15 = (f32[8,32,64]{2,1,0:T(8,128)S(1)}, f32[8,32,64]{2,1,0:T(8,128)}, u32[]{:S(2)}) copy-start(f32[8,32,64]{2,1,0:T(8,128)} %get-tuple-element.48) | copy-start | bytes 196612
  122.4 14.2 %copy-start.19 = (f32[8,32,64]{2,1,0:T(8,128)S(1)}, f32[8,32,64]{2,1,0:T(8,128)}, u32[]{:S(2)}) copy-start(f32[8,32,64]{2,1,0:T(8,128)} %get-tuple-element.49) | copy-start | bytes 196612
  131.3 11.4 %collective-permute-start.6 = (f32[8,65,64]{1,2,0:T(8,128)S(1)}, f32[8,65,64]{1,2,0:T(8,128)}, u32[]{:S(2)}, u32[]{:S(2)}) collective-permute-start(f32[8,65,64]{1,2,0:T(8,128)S(1)} %pad_maximum_fusion.4), channel_id=1, source_target_pairs={{0,64},{4,68},{8,72},{12,76},{16,80},{20,84},{24,88},{28,92},{32,9... | collective-permute-start | bytes 399368 | tf_op jit(solution)/shard_map/ppermute | solution.py:24
  140.8 15.1 %copy-start.29 = (f32[4,32]{1,0:T(4,128)S(1)}, f32[4,32]{1,0:T(4,128)}, u32[]{:S(2)}) copy-start(f32[4,32]{1,0:T(4,128)} %get-tuple-element.106) | copy-start | bytes 1540
  145.2 10.8 %collective-permute-start.7 = (f32[8,65,64]{1,2,0:T(8,128)S(1)}, f32[8,65,64]{1,2,0:T(8,128)S(1)}, u32[]{:S(2)}, u32[]{:S(2)}) collective-permute-start(f32[8,65,64]{1,2,0:T(8,128)S(1)} %pad_maximum_fusion.5), channel_id=1, source_target_pairs={{0,128},{4,132},{8,136},{12,140},{16,144},{20,148},{24,152},{28,15... | collective-permute-start | bytes 399368 | tf_op jit(solution)/shard_map/ppermute | solution.py:24
  146.8 11.5 %copy-start.24 = (f32[128,512]{1,0:T(8,128)S(1)}, f32[128,512]{1,0:T(8,128)}, u32[]{:S(2)}) copy-start(f32[128,512]{1,0:T(8,128)} %dynamic_update_slice.19) | copy-start | bytes 786436
  157.8 13.9 %copy-start.14 = (bf16[128,512]{1,0:T(8,128)(2,1)S(1)}, bf16[128,512]{1,0:T(8,128)(2,1)}, u32[]{:S(2)}) copy-start(bf16[128,512]{1,0:T(8,128)(2,1)} %param.13) | copy-start | bytes 393220
  (18 other events, 141.6 us)

commit v10 on v8

--- a/solution.py
+++ b/solution.py
@@ -158,9 +158,9 @@
         return jnp.einsum("htc,hsc,htsc->hts", recept_b, key_b, weight, precision=highest)
 
     scores = []
-    prefix = from_behind(packed, SEQ, 1)
+    prefix = packed
     distance = 1
-    while distance < devices:
+    while 2 * distance < devices:
         prefix = combine(from_behind(prefix, SEQ, distance), prefix)
         distance *= 2
         index = len(scores)
@@ -168,6 +168,7 @@
             operands = (incl[index], excl[index], gating_rows_tile[index], query_array_tile[index])
             prefix, operands = lax.optimization_barrier((prefix, operands))
             scores.append(block_scores(index, *operands))
+    prefix = combine(from_behind(prefix, SEQ, distance + 1), from_behind(prefix, SEQ, 1))
     for index in range(len(scores), blocks):
         scores.append(
             block_scores(index, incl[index], excl[index], gating_rows_tile[index], query_array_tile[index])

time: 163 us -> 184 us (1.13)
  the two profiles are of different devices: /device:TPU:48 before, /device:TPU:81 now
where the time goes in v10:
time: 184 us; the launch traced here: 182 us
  other arithmetic  51.2 us (28%)
  starting transfers between devices  31 us (17%)
  local copies, waits for them, and re-layouts  25.1 us (14%)
  blocking collectives  24.2 us (13%)
  matrix products  24.2 us (13%)
  waiting for transfers between devices  22.9 us (12%)
  between operations  3.34 us (2%)
    ppermute x8, starting transfers between devices, from_behind(): return lax.ppermute(block, axis, route)  31 us
    ppermute x8, waiting for transfers between devices, from_behind(): return lax.ppermute(block, axis, route)  22.9 us
    unnamed x4, other arithmetic  17.4 us
    all_to_all x1, blocking collectives, body(): pieces = lax.all_to_all(pieces, 'tp', 0, 0, tiled=True)  12.4 us
    all_gather x1, blocking collectives, body(): full = lax.all_gather(tier_source_concatenated, 'tp', axis=1, tiled=True)  11.8 us
    dot_general x2, matrix products, project(): jnp.einsum('itd,ide->ite', mixed[:4], mapping_matrices_pile, preferred_el...  10.3 us
    unnamed x60, local copies, waits for them, and re-layouts  6.61 us
    add x6, other arithmetic, combine(): state = jnp.transpose(own_decay, (0, 2, 1)) * got_state + own_state  5.54 us
  transfers between devices with their start and end apart: 8, of which 3 were waited for; matrix products, arithmetic and copies ran while one was open for 29% of the time, Pallas kernels for 0%

profile of v10, /device:TPU:81, one launch (start us, length us, event | category | flops | bytes accessed | tf_op | source)
XLA Modules:
  0.0 182.1 jit_solution(211580946521780230)
XLA Ops:
  0.0 11.8 %all_gather.3 = bf16[128,2048]{1,0:T(8,128)(2,1)S(1)} all-gather(bf16[128,512]{1,0:T(8,128)(2,1)} %param.13), channel_id=1, replica_groups=mesh['seq_hi'=8,'seq_lo'=8,'tp'=4] {'tp'}, dimensions={1}, use_global_device_ids=true | all-gather | bytes 655360 | tf_op jit(solution)/shard_map/all_gather | solution.py:54
  12.2 2.1 %fusion.71 = (f32[128,2048]{1,0:T(8,128)}, bf16[128,2048]{1,0:T(8,128)(2,1)S(1)}) fusion(f32[2048]{0:T(1024)} %param.16, f32[2048]{0:T(1024)} %param.15, f32[128]{0:T(128)S(1)} %add_rsqrt_fusion.1, f32[128]{0:T(128)S(1)} %broadcast_multiply_fusion.1, bf16[128,2048]{1,0:T(8,128)(2,1)S(1)} %all_gather.3), kind=kLoop, calls=%fused_computation.182 | loop fusion | flops 1835008 | bytes 2114560 | tf_op jit(solution)/shard_map/convert_element_type | solution.py:63
  14.4 5.8 %collective-permute-start = (bf16[1,2048]{1,0:T(2,128)(2,1)S(1)}, bf16[1,2048]{1,0:T(2,128)(2,1)S(1)}, u32[]{:S(2)}, u32[]{:S(2)}) collective-permute-start(bf16[1,2048]{1,0:T(2,128)(2,1)S(1)} %get-tuple-element.80), channel_id=1, source_target_pairs={{0,4},{4,8},{8,12},{12,16},{16,20},{20,24},{24,28},{28,32},{32,36}... | collective-permute-start | bytes 12296 | tf_op jit(solution)/shard_map/ppermute | solution.py:24
  26.5 5.7 %fusion.70 = f32[4,128,512]{2,1,0:T(8,128)} fusion(bf16[4,2048,512]{2,1,0:T(8,128)(2,1)} %param.18, f32[5,2048]{1,0:T(8,128)S(1)} %copy-done.9, f32[128,2048]{1,0:T(8,128)S(1)} %convert_subtract_fusion.1, f32[128,2048]{1,0:T(8,128)S(1)} %copy-done.3), kind=kOutput, calls=%fused_computation.181 | convolution fusion | flops 1077673984 | bytes 11575296 | tf_op jit(solution)/shard_map/itd,ide->ite/dot_general | solution.py:69
  41.2 4.6 %fusion.51 = f32[4,1,512]{2,1,0:T(1,128)S(1)} fusion(bf16[4,2048,512]{2,1,0:T(8,128)(2,1)} %param.18, bf16[4,2048,1]{1,0,2:T(4,128)(2,1)S(1)} %slice_bitcast_fusion.19), kind=kOutput, calls=%fused_computation.122 | convolution fusion | flops 8388608 | bytes 8413184 | tf_op jit(solution)/shard_map/itd,ide->ite/dot_general | solution.py:69
  52.0 1.9 %multiply_bitcast_fusion = (f32[1,8,64]{2,1,0:T(8,128)}, f32[1,8,1,64]{3,1,2,0:T(8,128)S(1)}, f32[1,8,64]{2,1,0:T(8,128)}) fusion(f32[]{:T(128)S(6)} %mul.357, f32[1,8,1,64]{3,1,2,0:T(8,128)} %bitcast.261, f32[1,8,1,64]{3,1,2,0:T(8,128)} %bitcast.260, f32[]{:T(128)} %bitcast.6), kind=kLoop, calls=%fused_computation.160 | loop fusion | flops 1536 | bytes 10248 | tf_op jit(solution)/shard_map/mul | solution.py:136
  68.3 1.9 %collective-permute-start.1 = (f32[8,65,64]{2,0,1:T(8,128)S(1)}, f32[8,65,64]{2,0,1:T(8,128)S(1)}, u32[]{:S(2)}, u32[]{:S(2)}) collective-permute-start(f32[8,65,64]{2,0,1:T(8,128)S(1)} %pad_maximum_fusion.1), channel_id=1, source_target_pairs={{0,4},{4,8},{8,12},{12,16},{16,20},{20,24},{24,28},{28,32},{32,36}... | collective-permute-start | bytes 399368 | tf_op jit(solution)/shard_map/ppermute | solution.py:24
  70.2 2.0 %slice_bitcast_fusion.5 = (f32[8,32,64]{2,1,0:T(8,128)S(1)}, f32[8,32,64]{2,1,0:T(8,128)S(1)}, f32[8,32,64]{2,1,0:T(8,128)}, f32[8,32,64]{2,1,0:T(8,128)S(1)}, f...) fusion(f32[4,8,32,64]{3,2,1,0:T(8,128)} %get-tuple-element.102, ...), kind=kLoop, calls=%fused_computation.101 | loop fusion | bytes 1048576 | tf_op jit(solution)/shard_map/squeeze | solution.py:168
  76.7 4.9 %collective-permute-start.2 = (f32[8,65,64]{2,0,1:T(8,128)S(1)}, f32[8,65,64]{2,0,1:T(8,128)}, u32[]{:S(2)}, u32[]{:S(2)}) collective-permute-start(f32[8,65,64]{2,0,1:T(8,128)S(1)} %pad_maximum_fusion.2), channel_id=1, source_target_pairs={{0,8},{4,12},{8,16},{12,20},{16,24},{20,28},{24,32},{28,36},{32,40... | collective-permute-start | bytes 399368 | tf_op jit(solution)/shard_map/ppermute | solution.py:24
  82.5 4.1 %fusion.3 = f32[8,32,32]{1,2,0:T(8,128)} fusion(f32[8,32,32,64]{3,2,1,0:T(8,128)S(1)} %exponential_select_fusion.3, f32[8,64,32]{1,2,0:T(8,128)S(1)} %bitcast.245, f32[8,64,32]{1,2,0:T(8,128)S(1)} %bitcast.244), kind=kLoop, calls=%fused_computation.8 | loop fusion | flops 1564672 | bytes 2260992
  90.2 4.3 %collective-permute-start.3 = (f32[8,65,64]{2,0,1:T(8,128)S(1)}, f32[8,65,64]{2,0,1:T(8,128)}, u32[]{:S(2)}, u32[]{:S(2)}) collective-permute-start(f32[8,65,64]{2,0,1:T(8,128)S(1)} %pad_maximum_fusion.3), channel_id=1, source_target_pairs={{0,16},{4,20},{8,24},{12,28},{16,32},{20,36},{24,40},{28,44},{32,4... | collective-permute-start | bytes 399368 | tf_op jit(solution)/shard_map/ppermute | solution.py:24
  96.2 4.4 %fusion.2 = f32[8,32,32]{1,2,0:T(8,128)S(1)} fusion(f32[8,32,32,64]{3,2,1,0:T(8,128)S(1)} %exponential_select_fusion.2, f32[8,64,32]{1,2,0:T(8,128)} %bitcast.243, f32[8,64,32]{1,2,0:T(8,128)} %bitcast.242), kind=kLoop, calls=%fused_computation.6 | loop fusion | flops 1564672 | bytes 2260992
  101.4 5.5 %collective-permute-done.3 = f32[8,65,64]{2,0,1:T(8,128)} collective-permute-done((f32[8,65,64]{2,0,1:T(8,128)S(1)}, f32[8,65,64]{2,0,1:T(8,128)}, u32[]{:S(2)}, u32[]{:S(2)}) %collective-permute-start.3) | collective-permute-done | bytes 133152 | tf_op jit(solution)/shard_map/ppermute | solution.py:24
  108.8 3.0 %collective-permute-start.4 = (f32[8,65,64]{2,0,1:T(8,128)S(1)}, f32[8,65,64]{2,0,1:T(8,128)}, u32[]{:S(2)}, u32[]{:S(2)}) collective-permute-start(f32[8,65,64]{2,0,1:T(8,128)S(1)} %pad_maximum_fusion.4), channel_id=1, source_target_pairs={{0,32},{4,36},{8,40},{12,44},{16,48},{20,52},{24,56},{28,60},{32,6... | collective-permute-start | bytes 399368 | tf_op jit(solution)/shard_map/ppermute | solution.py:24
  112.6 4.4 %fusion.1 = f32[8,32,32]{1,2,0:T(8,128)S(1)} fusion(f32[8,32,32,64]{3,2,1,0:T(8,128)S(1)} %exponential_select_fusion.1, f32[8,64,32]{1,2,0:T(8,128)} %bitcast.241, f32[8,64,32]{1,2,0:T(8,128)} %bitcast.240), kind=kLoop, calls=%fused_computation.4 | loop fusion | flops 1564672 | bytes 2260992
  117.7 6.7 %collective-permute-done.4 = f32[8,65,64]{2,0,1:T(8,128)} collective-permute-done((f32[8,65,64]{2,0,1:T(8,128)S(1)}, f32[8,65,64]{2,0,1:T(8,128)}, u32[]{:S(2)}, u32[]{:S(2)}) %collective-permute-start.4) | collective-permute-done | bytes 133152 | tf_op jit(solution)/shard_map/ppermute | solution.py:24
  126.3 1.9 %collective-permute-start.5 = (f32[8,65,64]{2,0,1:T(8,128)S(1)}, f32[8,65,64]{2,0,1:T(8,128)}, u32[]{:S(2)}, u32[]{:S(2)}) collective-permute-start(f32[8,65,64]{2,0,1:T(8,128)S(1)} %pad_maximum_fusion.5), channel_id=1, source_target_pairs={{0,64},{4,68},{8,72},{12,76},{16,80},{20,84},{24,88},{28,92},{32,9... | collective-permute-start | bytes 399368 | tf_op jit(solution)/shard_map/ppermute | solution.py:24
  129.1 4.5 %fusion = f32[8,32,32]{1,2,0:T(8,128)S(1)} fusion(f32[8,32,32,64]{3,2,1,0:T(8,128)S(1)} %exponential_select_fusion, f32[8,64,32]{1,2,0:T(8,128)} %bitcast.239, f32[8,64,32]{1,2,0:T(8,128)} %bitcast.238), kind=kLoop, calls=%fused_computation.2 | loop fusion | flops 1564672 | bytes 2260992
  134.3 2.6 %fusion.7 = f32[4,32,8,64]{3,1,2,0:T(8,128)} fusion(f32[1,8,32,32]{3,2,1,0:T(8,128)} %bitcast.251, f32[1,8,32,32]{3,2,1,0:T(8,128)} %bitcast.250, f32[1,8,32,32]{3,2,1,0:T(8,128)} %bitcast.249, f32[1,8,32,32]{3,2,1,0:T(8,128)} %bitcast.248, f32[4,32,8]{1,2,0:T(8,128)} %bitcast.258, bf16[4,32,8,64]{3,2,1,0:T(8,128)(2,1)} %convert_element_type.115), kind=kOutput, calls=%fused_computation.23 | convolution fusion | flops 25460736 | bytes 528384 | tf_op jit(solution)/shard_map/bhts,bhsv->bhtv/dot_general | solution.py:178
  139.4 7.5 %collective-permute-start.6 = (f32[8,65,64]{2,0,1:T(8,128)}, f32[8,65,64]{2,0,1:T(8,128)S(1)}, u32[]{:S(2)}, u32[]{:S(2)}) collective-permute-start(f32[8,65,64]{2,0,1:T(8,128)} %pad_maximum_fusion.6), channel_id=1, source_target_pairs={{0,4},{4,8},{8,12},{12,16},{16,20},{20,24},{24,28},{28,32},{32,36}... | collective-permute-start | bytes 399368 | tf_op jit(solution)/shard_map/ppermute | solution.py:24
  147.0 3.4 %fusion.6 = f32[4,32,8,64]{3,1,2,0:T(8,128)} fusion(f32[4,32,8,64]{3,1,2,0:T(8,128)} %fusion.7, f32[4,8,64,64]{3,1,2,0:T(8,128)} %pad_maximum_fusion, f32[4,8,32,64]{3,2,1,0:T(8,128)S(1)} %copy-done.1, f32[4,32]{1,0:T(4,128)S(1)} %copy-done.21, f32[4,32,8,64]{3,2,1,0:T(8,128)S(1)} %reshape.531), kind=kOutput, calls=%fused_computation.20 | convolution fusion | flops 50528256 | bytes 1573376 | tf_op jit(solution)/shard_map/bhtc,bhcv->bhtv/dot_general | solution.py:180
  152.2 10.7 %collective-permute-done.7 = f32[8,65,64]{2,0,1:T(8,128)} collective-permute-done((f32[8,65,64]{2,0,1:T(8,128)}, f32[8,65,64]{2,0,1:T(8,128)}, u32[]{:S(2)}, u32[]{:S(2)}) %collective-permute-start.7) | collective-permute-done | bytes 133152 | tf_op jit(solution)/shard_map/ppermute | solution.py:24
  164.1 1.9 %fusion.77 = (f32[4,32,8]{1,2,0:T(8,128)S(1)}, f32[4,32,8,64]{3,1,2,0:T(8,128)S(1)}) fusion(f32[4,32,8,64]{3,1,2,0:T(8,128)} %fusion.6, f32[4,8,64]{2,1,0:T(8,128)S(1)} %copy-done.11, f32[4,32]{1,0:T(4,128)S(1)} %copy-done.21, f32[4,8,32,64]{3,2,1,0:T(8,128)S(1)} %copy-done.1, f32[4,32,8,64]{3,2,1,0:T(8,128)S(1)} %reshape.531, ...), kind=kOutput, calls=%fused_computation.187 | convolution fusion | flops 50658304 | bytes 1192448 | tf_op jit(solution)/shard_map/bhtc,hcv->bhtv/dot_general | solution.py:183
  168.9 12.4 %all_to_all.5 = bf16[4,128,512]{2,1,0:T(8,128)(2,1)S(1)} all-to-all(bf16[4,128,512]{2,1,0:T(8,128)(2,1)S(1)} %bitcast.232), channel_id=1, replica_groups=mesh['seq_hi'=8,'seq_lo'=8,'tp'=4] {'tp'}, dimensions={0} | all-to-all | bytes 1048576 | tf_op jit(solution)/shard_map/all_to_all | solution.py:195
  (178 shorter events, 60.6 us)
Async XLA Ops:
  0.0 167.4 %copy-start = (bf16[512,2048]{1,0:T(8,128)(2,1)S(1)}, bf16[512,2048]{1,0:T(8,128)(2,1)}, u32[]{:S(2)}) copy-start(bf16[512,2048]{1,0:T(8,128)(2,1)} %param.25) | copy-start | bytes 6291460
  0.0 24.6 %copy-start.9 = (f32[5,2048]{1,0:T(8,128)S(1)}, f32[5,2048]{1,0:T(8,128)}, u32[]{:S(2)}) copy-start(f32[5,2048]{1,0:T(8,128)} %param.17) | copy-start | bytes 122884
  14.4 24.0 %collective-permute-start = (bf16[1,2048]{1,0:T(2,128)(2,1)S(1)}, bf16[1,2048]{1,0:T(2,128)(2,1)S(1)}, u32[]{:S(2)}, u32[]{:S(2)}) collective-permute-start(bf16[1,2048]{1,0:T(2,128)(2,1)S(1)} %get-tuple-element.80), channel_id=1, source_target_pairs={{0,4},{4,8},{8,12},{12,16},{16,20},{20,24},{24,28},{28,32},{32,36}... | collective-permute-start | bytes 12296 | tf_op jit(solution)/shard_map/ppermute | solution.py:24
  26.5 12.4 %copy-start.15 = (bf16[64,512]{1,0:T(8,128)(2,1)S(1)}, bf16[64,512]{1,0:T(8,128)(2,1)}, u32[]{:S(2)}) copy-start(bf16[64,512]{1,0:T(8,128)(2,1)} %param.20) | copy-start | bytes 196612
  58.9 9.4 %copy-start.13 = (f32[1,8,1,64]{3,2,1,0:T(1,128)S(1)}, f32[1,8,1,64]{3,2,1,0:T(1,128)}, u32[]{:S(2)}) copy-start(f32[1,8,1,64]{3,2,1,0:T(1,128)} %copy-done.12) | copy-start | bytes 6148
  68.3 8.3 %collective-permute-start.1 = (f32[8,65,64]{2,0,1:T(8,128)S(1)}, f32[8,65,64]{2,0,1:T(8,128)S(1)}, u32[]{:S(2)}, u32[]{:S(2)}) collective-permute-start(f32[8,65,64]{2,0,1:T(8,128)S(1)} %pad_maximum_fusion.1), channel_id=1, source_target_pairs={{0,4},{4,8},{8,12},{12,16},{16,20},{20,24},{24,28},{28,32},{32,36}... | collective-permute-start | bytes 399368 | tf_op jit(solution)/shard_map/ppermute | solution.py:24
  70.2 11.5 %copy-start.19 = (pred[32,32]{1,0:T(8,128)(4,1)S(1)}, pred[32,32]{1,0:T(8,128)(4,1)}, u32[]{:S(2)}) copy-start(pred[32,32]{1,0:T(8,128)(4,1)} %get-tuple-element.119) | copy-start | bytes 3076
  76.7 11.5 %collective-permute-start.2 = (f32[8,65,64]{2,0,1:T(8,128)S(1)}, f32[8,65,64]{2,0,1:T(8,128)}, u32[]{:S(2)}, u32[]{:S(2)}) collective-permute-start(f32[8,65,64]{2,0,1:T(8,128)S(1)} %pad_maximum_fusion.2), channel_id=1, source_target_pairs={{0,8},{4,12},{8,16},{12,20},{16,24},{20,28},{24,32},{28,36},{32,40... | collective-permute-start | bytes 399368 | tf_op jit(solution)/shard_map/ppermute | solution.py:24
  82.5 12.0 %copy-start.7 = (f32[8,32,64]{2,1,0:T(8,128)S(1)}, f32[8,32,64]{2,1,0:T(8,128)}, u32[]{:S(2)}) copy-start(f32[8,32,64]{2,1,0:T(8,128)} %get-tuple-element.30) | copy-start | bytes 196612
  82.5 12.0 %copy-start.18 = (pred[32,32]{1,0:T(8,128)(4,1)S(1)}, pred[32,32]{1,0:T(8,128)(4,1)}, u32[]{:S(2)}) copy-start(pred[32,32]{1,0:T(8,128)(4,1)} %get-tuple-element.118) | copy-start | bytes 3076
  90.2 16.7 %collective-permute-start.3 = (f32[8,65,64]{2,0,1:T(8,128)S(1)}, f32[8,65,64]{2,0,1:T(8,128)}, u32[]{:S(2)}, u32[]{:S(2)}) collective-permute-start(f32[8,65,64]{2,0,1:T(8,128)S(1)} %pad_maximum_fusion.3), channel_id=1, source_target_pairs={{0,16},{4,20},{8,24},{12,28},{16,32},{20,36},{24,40},{28,44},{32,4... | collective-permute-start | bytes 399368 | tf_op jit(solution)/shard_map/ppermute | solution.py:24
  96.2 15.5 %copy-start.17 = (pred[32,32]{1,0:T(8,128)(4,1)S(1)}, pred[32,32]{1,0:T(8,128)(4,1)}, u32[]{:S(2)}) copy-start(pred[32,32]{1,0:T(8,128)(4,1)} %get-tuple-element.117) | copy-start | bytes 3076
  108.8 15.7 %collective-permute-start.4 = (f32[8,65,64]{2,0,1:T(8,128)S(1)}, f32[8,65,64]{2,0,1:T(8,128)}, u32[]{:S(2)}, u32[]{:S(2)}) collective-permute-start(f32[8,65,64]{2,0,1:T(8,128)S(1)} %pad_maximum_fusion.4), channel_id=1, source_target_pairs={{0,32},{4,36},{8,40},{12,44},{16,48},{20,52},{24,56},{28,60},{32,6... | collective-permute-start | bytes 399368 | tf_op jit(solution)/shard_map/ppermute | solution.py:24
  112.5 15.7 %copy-start.6 = (f32[8,32,64]{2,1,0:T(8,128)S(1)}, f32[8,32,64]{2,1,0:T(8,128)}, u32[]{:S(2)}) copy-start(f32[8,32,64]{2,1,0:T(8,128)} %get-tuple-element.41) | copy-start | bytes 196612
  112.5 15.7 %copy-start.16 = (pred[32,32]{1,0:T(8,128)(4,1)S(1)}, pred[32,32]{1,0:T(8,128)(4,1)}, u32[]{:S(2)}) copy-start(pred[32,32]{1,0:T(8,128)(4,1)} %get-tuple-element.116) | copy-start | bytes 3076
  126.3 10.5 %collective-permute-start.5 = (f32[8,65,64]{2,0,1:T(8,128)S(1)}, f32[8,65,64]{2,0,1:T(8,128)}, u32[]{:S(2)}, u32[]{:S(2)}) collective-permute-start(f32[8,65,64]{2,0,1:T(8,128)S(1)} %pad_maximum_fusion.5), channel_id=1, source_target_pairs={{0,64},{4,68},{8,72},{12,76},{16,80},{20,84},{24,88},{28,92},{32,9... | collective-permute-start | bytes 399368 | tf_op jit(solution)/shard_map/ppermute | solution.py:24
  129.1 17.9 %copy-start.1 = (f32[4,8,32,64]{3,2,1,0:T(8,128)S(1)}, f32[4,8,32,64]{3,2,1,0:T(8,128)}, u32[]{:S(2)}) copy-start(f32[4,8,32,64]{3,2,1,0:T(8,128)} %get-tuple-element.102) | copy-start | bytes 786436
  129.1 17.9 %copy-start.21 = (f32[4,32]{1,0:T(4,128)S(1)}, f32[4,32]{1,0:T(4,128)}, u32[]{:S(2)}) copy-start(f32[4,32]{1,0:T(4,128)} %get-tuple-element.104) | copy-start | bytes 1540
  134.3 29.7 %copy-start.11 = (f32[4,8,64]{2,1,0:T(8,128)S(1)}, f32[4,8,64]{2,1,0:T(8,128)}, u32[]{:S(2)}) copy-start(f32[4,8,64]{2,1,0:T(8,128)} %pad_maximum_fusion.7) | copy-start | bytes 24580
  139.4 12.7 %collective-permute-start.6 = (f32[8,65,64]{2,0,1:T(8,128)}, f32[8,65,64]{2,0,1:T(8,128)S(1)}, u32[]{:S(2)}, u32[]{:S(2)}) collective-permute-start(f32[8,65,64]{2,0,1:T(8,128)} %pad_maximum_fusion.6), channel_id=1, source_target_pairs={{0,4},{4,8},{8,12},{12,16},{16,20},{20,24},{24,28},{28,32},{32,36}... | collective-permute-start | bytes 399368 | tf_op jit(solution)/shard_map/ppermute | solution.py:24
  150.4 17.0 %copy-start.22 = (f32[512]{0:T(512)S(1)}, f32[512]{0:T(512)}, u32[]{:S(2)}) copy-start(f32[512]{0:T(512)} %param.24) | copy-start | bytes 6148
  150.4 17.0 %copy-start.23 = (f32[512]{0:T(512)S(1)}, f32[512]{0:T(512)}, u32[]{:S(2)}) copy-start(f32[512]{0:T(512)} %param.23) | copy-start | bytes 6148
  150.4 12.5 %collective-permute-start.7 = (f32[8,65,64]{2,0,1:T(8,128)}, f32[8,65,64]{2,0,1:T(8,128)}, u32[]{:S(2)}, u32[]{:S(2)}) collective-permute-start(f32[8,65,64]{2,0,1:T(8,128)} %pad_maximum_fusion.6), channel_id=1, source_target_pairs={{0,132},{4,136},{8,140},{12,144},{16,148},{20,152},{24,156},{28,16... | collective-permute-start | bytes 399368 | tf_op jit(solution)/shard_map/ppermute | solution.py:24
  166.9 14.5 %copy-start.8 = (bf16[128,512]{1,0:T(8,128)(2,1)S(1)}, bf16[128,512]{1,0:T(8,128)(2,1)}, u32[]{:S(2)}) copy-start(bf16[128,512]{1,0:T(8,128)(2,1)} %param.13) | copy-start | bytes 393220
  (12 other events, 86.2 us)

commit v11 on v9

--- a/solution.py
+++ b/solution.py
@@ -64,25 +64,31 @@
         delta = previous.astype(jnp.float32) - base
         return (base[None] + delta[None] * previous_item_mixers[:, None, :]).astype(jnp.bfloat16)
 
-    def project(mixed, index):
-        return jnp.dot(mixed[index], mapping_matrices_pile[index], preferred_element_type=jnp.float32)
-
-    def fixed(index, mixed, edge_mixed):
-        return lax.dynamic_update_slice(project(mixed, index), project(edge_mixed, index), (0, 0))
+    def project(mixed):
+        return (
+            jnp.einsum(
+                "itd,ide->ite", mixed[:4], mapping_matrices_pile, preferred_element_type=jnp.float32
+            ),
+            jnp.dot(mixed[4], fading_narrow_left, preferred_element_type=jnp.float32),
+        )
 
     previous = jnp.concatenate([jnp.zeros_like(normed[:1]), normed[: rows - 1]], axis=0)
     previous = jnp.where(is_start[:, None], jnp.zeros_like(previous), previous)
-    mixed = blend(previous, normed)
+    projected, lowrank = project(blend(previous, normed))
     edge = from_behind(normed[rows - 1 :], SEQ, 1)
     edge = jnp.where(is_start[0], jnp.zeros_like(edge), edge)
     edge_mixed = blend(edge, normed[:1])
-    key_rows = fixed(1, mixed, edge_mixed).astype(jnp.bfloat16)
-    value_rows = fixed(2, mixed, edge_mixed).astype(jnp.bfloat16)
-    lowrank = lax.dynamic_update_slice(
-        jnp.dot(mixed[4], fading_narrow_left, preferred_element_type=jnp.float32),
-        jnp.dot(edge_mixed[4], fading_narrow_left, preferred_element_type=jnp.float32),
-        (0, 0),
-    )
+    edge_pair = jnp.einsum(
+        "itd,ide->ite", edge_mixed[1:3], mapping_matrices_pile[1:3], preferred_element_type=jnp.float32
+    )
+    key_rows = lax.dynamic_update_slice(projected[1], edge_pair[0], (0, 0)).astype(jnp.bfloat16)
+    value_rows = lax.dynamic_update_slice(projected[2], edge_pair[1], (0, 0)).astype(jnp.bfloat16)
+    edge_lowrank = jnp.dot(edge_mixed[4], fading_narrow_left, preferred_element_type=jnp.float32)
+    lowrank = lax.dynamic_update_slice(lowrank, edge_lowrank, (0, 0))
+
+    def late_rows(projected, edge_mixed, index):
+        edge_row = jnp.dot(edge_mixed[index], mapping_matrices_pile[index], preferred_element_type=jnp.float32)
+        return lax.dynamic_update_slice(projected[index], edge_row, (0, 0))
     lowrank_decay_delta = jnp.tanh(lowrank).astype(jnp.bfloat16)
     decay_logarithm = -feature_fading_baseline[None, :] * jnp.exp(
         jnp.dot(lowrank_decay_delta, fading_narrow_right, preferred_element_type=jnp.float32)
@@ -154,9 +160,9 @@
 
     scores = []
     prefix = from_behind(packed, SEQ, 1)
-    prefix, late = lax.optimization_barrier((prefix, (mixed, edge_mixed)))
-    recept = fixed(0, *late).astype(jnp.bfloat16)
-    gate = jax.nn.silu(fixed(3, *late)).astype(jnp.bfloat16)
+    prefix, late = lax.optimization_barrier((prefix, (projected, edge_mixed)))
+    recept = late_rows(*late, 0).astype(jnp.bfloat16)
+    gate = jax.nn.silu(late_rows(*late, 3)).astype(jnp.bfloat16)
     gating_rows_tile = split_heads(recept)
     carried = gating_rows_tile * decay_factor
     from_start = carried * reach

time: 174 us -> 170 us (0.977)
  matrix products: 29.7 us -> 22.3 us
  local copies, waits for them, and re-layouts: 17.5 us -> 20.8 us
    dot_general x9 -> x5, matrix products: 19.7 us -> 12.3 us  [the longest x1 4.7 us: project(): jnp.einsum('itd,ide->ite', mixed[:4], mapping_matrices_pile, preferred_el...]
    squeeze x0 -> x3, local copies, waits for them, and re-layouts: none -> 3.34 us  [the longest x2 3.31 us: late_rows(): return lax.dynamic_update_slice(projected[index], edge_row, (0, 0))]
  transfers between devices with their start and end apart: 8 -> 8, of which waited for: 5 -> 5; matrix products, arithmetic and copies ran while one was open for 30% -> 31% of each run, Pallas kernels for 0% -> 0%
where the time goes in v11:
time: 170 us; the launch traced here: 169 us
  other arithmetic  43.3 us (25%)
  starting transfers between devices  30.9 us (18%)
  blocking collectives  25.6 us (15%)
  matrix products  22.3 us (13%)
  waiting for transfers between devices  22.3 us (13%)
  local copies, waits for them, and re-layouts  20.8 us (12%)
  between operations  3.36 us (2%)
    ppermute x8, starting transfers between devices, from_behind(): return lax.ppermute(block, axis, route)  30.9 us
    ppermute x8, waiting for transfers between devices, from_behind(): return lax.ppermute(block, axis, route)  22.3 us
    unnamed x4, other arithmetic  15.1 us
    all_gather x1, blocking collectives, body(): full = lax.all_gather(tier_source_concatenated, 'tp', axis=1, tiled=True)  13.5 us
    all_to_all x1, blocking collectives, body(): pieces = lax.all_to_all(pieces, 'tp', 0, 0, tiled=True)  12.2 us
    select_n x4, other arithmetic, block_scores(): weight = jnp.where(pair_ok[None, :, :, None], jnp.exp(gap), 0.0)  6.35 us
    dot_general x4, local copies, waits for them, and re-layouts, block_scores(): jnp.einsum('htc,hsc,htsc->hts', recept_b, key_b, weight, precision=highest)  4.82 us
    dot_general x1, matrix products, project(): jnp.einsum('itd,ide->ite', mixed[:4], mapping_matrices_pile, preferred_el...  4.7 us
  transfers between devices with their start and end apart: 8, of which 5 were waited for; matrix products, arithmetic and copies ran while one was open for 31% of the time, Pallas kernels for 0%

profile of v11, /device:TPU:48, one launch (start us, length us, event | category | flops | bytes accessed | tf_op | source)
XLA Modules:
  0.0 168.6 jit_solution(15440966798054275504)
XLA Ops:
  0.0 13.5 %all_gather.3 = bf16[128,2048]{1,0:T(8,128)(2,1)S(1)} all-gather(bf16[128,512]{1,0:T(8,128)(2,1)} %param.13), channel_id=1, replica_groups=mesh['seq_hi'=8,'seq_lo'=8,'tp'=4] {'tp'}, dimensions={1}, use_global_device_ids=true | all-gather | bytes 655360 | tf_op jit(solution)/shard_map/all_gather | solution.py:54
  13.9 2.1 %fusion.93 = (f32[128,2048]{1,0:T(8,128)}, bf16[128,2048]{1,0:T(8,128)(2,1)S(1)}) fusion(f32[2048]{0:T(1024)} %param.16, f32[2048]{0:T(1024)} %param.15, f32[128]{0:T(128)S(1)} %add_rsqrt_fusion.1, f32[128]{0:T(128)S(1)} %broadcast_multiply_fusion.1, bf16[128,2048]{1,0:T(8,128)(2,1)S(1)} %all_gather.3), kind=kLoop, calls=%fused_computation.204 | loop fusion | flops 1835008 | bytes 2114560 | tf_op jit(solution)/shard_map/convert_element_type | solution.py:63
  16.1 1.9 %collective-permute-start = (bf16[1,2048]{1,0:T(2,128)(2,1)S(1)}, bf16[1,2048]{1,0:T(2,128)(2,1)S(1)}, u32[]{:S(2)}, u32[]{:S(2)}) collective-permute-start(bf16[1,2048]{1,0:T(2,128)(2,1)S(1)} %get-tuple-element.83), channel_id=1, source_target_pairs={{0,4},{4,8},{8,12},{12,16},{16,20},{20,24},{24,28},{28,32},{32,36}... | collective-permute-start | bytes 12296 | tf_op jit(solution)/shard_map/ppermute | solution.py:24
  23.7 4.7 %fusion.91 = f32[4,128,512]{2,1,0:T(8,128)S(1)} fusion(bf16[4,2048,512]{2,1,0:T(8,128)(2,1)} %param.18, f32[5,2048]{1,0:T(8,128)S(1)} %copy-done.10, f32[128,2048]{1,0:T(8,128)S(1)} %convert_subtract_fusion.1, f32[128,2048]{1,0:T(8,128)S(1)} %copy-done.5), kind=kOutput, calls=%fused_computation.202 | convolution fusion | flops 1077673984 | bytes 11575296 | tf_op jit(solution)/shard_map/itd,ide->ite/dot_general | solution.py:69
  37.4 2.8 %fusion.4 = bf16[2,1,512]{2,1,0:T(2,128)(2,1)S(1)} fusion(bf16[4,2048,512]{2,1,0:T(8,128)(2,1)} %param.18, bf16[2,2048,1]{1,0,2:T(2,128)(2,1)S(1)} %slice_bitcast_fusion.23), kind=kOutput, calls=%fused_computation.13 | convolution fusion | flops 4194304 | bytes 4204544 | tf_op jit(solution)/shard_map/itd,ide->ite/dot_general | solution.py:81
  45.2 1.9 %fusion.39 = f32[4,8,64,64]{2,3,1,0:T(8,128)S(1)} fusion(f32[4,8,32,64]{3,2,1,0:T(8,128)} %copy-done.3, f32[4,32]{1,0:T(4,128)S(1)} %compare_convert_fusion.1, f32[4,8,64]{2,1,0:T(8,128)S(1)} %bitcast.254, bf16[4,32,8,64]{3,2,1,0:T(8,128)(2,1)} %reshape.515, f32[4,32,8,64]{3,2,1,0:T(8,128)S(1)} %reshape.524), kind=kOutput, calls=%fused_computation.66 | convolution fusion | flops 50528256 | bytes 1188352 | tf_op jit(solution)/shard_map/bhsc,bhsv->bhcv/dot_general | solution.py:128
  48.3 3.9 %collective-permute-start.1 = (f32[8,65,64]{1,2,0:T(8,128)S(1)}, f32[8,65,64]{1,2,0:T(8,128)S(1)}, u32[]{:S(2)}, u32[]{:S(2)}) collective-permute-start(f32[8,65,64]{1,2,0:T(8,128)S(1)} %pad_maximum_fusion), channel_id=1, source_target_pairs={{0,4},{4,8},{8,12},{12,16},{16,20},{20,24},{24,28},{28,32},{32,36}... | collective-permute-start | bytes 399368 | tf_op jit(solution)/shard_map/ppermute | solution.py:24
  53.3 2.7 %collective-permute-done.1 = f32[8,65,64]{1,2,0:T(8,128)S(1)} collective-permute-done((f32[8,65,64]{1,2,0:T(8,128)S(1)}, f32[8,65,64]{1,2,0:T(8,128)S(1)}, u32[]{:S(2)}, u32[]{:S(2)}) %collective-permute-start.1) | collective-permute-done | bytes 133152 | tf_op jit(solution)/shard_map/ppermute | solution.py:24
  56.0 2.6 %fusion.6 = f32[1,512]{1,0:T(1,128)} fusion(bf16[4,2048,512]{2,1,0:T(8,128)(2,1)} %param.18, bf16[5,1,2048]{2,0,1:T(8,128)(2,1)S(1)} %copy-done.25), kind=kOutput, calls=%fused_computation.16 | convolution fusion | flops 2097152 | bytes 2107392 | tf_op jit(solution)/shard_map/dot_general | solution.py:90
  58.6 2.0 %fusion.8 = bf16[1,512]{1,0:T(2,128)(2,1)S(1)} fusion(bf16[4,2048,512]{2,1,0:T(8,128)(2,1)} %param.18, bf16[5,1,2048]{2,0,1:T(8,128)(2,1)S(1)} %copy-done.25), kind=kOutput, calls=%fused_computation.18 | convolution fusion | flops 2097152 | bytes 2106368 | tf_op jit(solution)/shard_map/dot_general | solution.py:90
  63.8 1.9 %collective-permute-start.2 = (f32[8,65,64]{1,2,0:T(8,128)S(1)}, f32[8,65,64]{1,2,0:T(8,128)}, u32[]{:S(2)}, u32[]{:S(2)}) collective-permute-start(f32[8,65,64]{1,2,0:T(8,128)S(1)} %collective-permute-done.1), channel_id=1, source_target_pairs={{0,4},{4,8},{8,12},{12,16},{16,20},{20,24},{24,28},{28,32},{32,36}... | collective-permute-start | bytes 399368 | tf_op jit(solution)/shard_map/ppermute | solution.py:24
  74.3 4.0 %collective-permute-start.3 = (f32[8,65,64]{1,2,0:T(8,128)S(1)}, f32[8,65,64]{1,2,0:T(8,128)S(1)}, u32[]{:S(2)}, u32[]{:S(2)}) collective-permute-start(f32[8,65,64]{1,2,0:T(8,128)S(1)} %pad_maximum_fusion.1), channel_id=1, source_target_pairs={{0,8},{4,12},{8,16},{12,20},{16,24},{20,28},{24,32},{28,36},{32,40... | collective-permute-start | bytes 399368 | tf_op jit(solution)/shard_map/ppermute | solution.py:24
  80.2 4.1 %fusion.3 = f32[8,32,32]{1,2,0:T(8,128)} fusion(f32[8,32,32,64]{3,2,1,0:T(8,128)S(1)} %exponential_select_fusion.3, f32[8,64,32]{1,2,0:T(8,128)S(1)} %bitcast.252, f32[8,64,32]{1,2,0:T(8,128)S(1)} %bitcast.248), kind=kLoop, calls=%fused_computation.8 | loop fusion | flops 1564672 | bytes 2260992
  87.0 7.9 %collective-permute-start.4 = (f32[8,65,64]{1,2,0:T(8,128)S(1)}, f32[8,65,64]{1,2,0:T(8,128)S(1)}, u32[]{:S(2)}, u32[]{:S(2)}) collective-permute-start(f32[8,65,64]{1,2,0:T(8,128)S(1)} %pad_maximum_fusion.2), channel_id=1, source_target_pairs={{0,16},{4,20},{8,24},{12,28},{16,32},{20,36},{24,40},{28,44},{32,4... | collective-permute-start | bytes 399368 | tf_op jit(solution)/shard_map/ppermute | solution.py:24
  96.4 4.1 %fusion.2 = f32[8,32,32]{1,2,0:T(8,128)} fusion(f32[8,32,32,64]{3,2,1,0:T(8,128)S(1)} %exponential_select_fusion.2, f32[8,64,32]{1,2,0:T(8,128)S(1)} %bitcast.251, f32[8,64,32]{1,2,0:T(8,128)S(1)} %bitcast.247), kind=kLoop, calls=%fused_computation.6 | loop fusion | flops 1564672 | bytes 2260992
  102.2 4.1 %collective-permute-done.4 = f32[8,65,64]{1,2,0:T(8,128)S(1)} collective-permute-done((f32[8,65,64]{1,2,0:T(8,128)S(1)}, f32[8,65,64]{1,2,0:T(8,128)S(1)}, u32[]{:S(2)}, u32[]{:S(2)}) %collective-permute-start.4) | collective-permute-done | bytes 133152 | tf_op jit(solution)/shard_map/ppermute | solution.py:24
  106.8 6.0 %collective-permute-start.5 = (f32[8,65,64]{1,2,0:T(8,128)S(1)}, f32[8,65,64]{1,2,0:T(8,128)S(1)}, u32[]{:S(2)}, u32[]{:S(2)}) collective-permute-start(f32[8,65,64]{1,2,0:T(8,128)S(1)} %pad_maximum_fusion.3), channel_id=1, source_target_pairs={{0,32},{4,36},{8,40},{12,44},{16,48},{20,52},{24,56},{28,60},{32,6... | collective-permute-start | bytes 399368 | tf_op jit(solution)/shard_map/ppermute | solution.py:24
  114.3 3.4 %fusion.1 = f32[8,32,32]{1,2,0:T(8,128)S(1)} fusion(f32[8,32,32,64]{3,2,1,0:T(8,128)S(1)} %exponential_select_fusion.1, f32[8,64,32]{1,2,0:T(8,128)S(1)} %bitcast.250, f32[8,64,32]{1,2,0:T(8,128)S(1)} %bitcast.246), kind=kLoop, calls=%fused_computation.4 | loop fusion | flops 1564672 | bytes 2260992
  118.5 8.3 %collective-permute-done.5 = f32[8,65,64]{1,2,0:T(8,128)S(1)} collective-permute-done((f32[8,65,64]{1,2,0:T(8,128)S(1)}, f32[8,65,64]{1,2,0:T(8,128)S(1)}, u32[]{:S(2)}, u32[]{:S(2)}) %collective-permute-start.5) | collective-permute-done | bytes 133152 | tf_op jit(solution)/shard_map/ppermute | solution.py:24
  127.4 3.7 %collective-permute-start.6 = (f32[8,65,64]{1,2,0:T(8,128)S(1)}, f32[8,65,64]{1,2,0:T(8,128)}, u32[]{:S(2)}, u32[]{:S(2)}) collective-permute-start(f32[8,65,64]{1,2,0:T(8,128)S(1)} %pad_maximum_fusion.4), channel_id=1, source_target_pairs={{0,64},{4,68},{8,72},{12,76},{16,80},{20,84},{24,88},{28,92},{32,9... | collective-permute-start | bytes 399368 | tf_op jit(solution)/shard_map/ppermute | solution.py:24
  132.8 3.4 %fusion = f32[8,32,32]{1,2,0:T(8,128)S(1)} fusion(f32[8,32,32,64]{3,2,1,0:T(8,128)S(1)} %exponential_select_fusion, f32[8,64,32]{1,2,0:T(8,128)S(1)} %bitcast.249, f32[8,64,32]{1,2,0:T(8,128)S(1)} %bitcast.245), kind=kLoop, calls=%fused_computation.2 | loop fusion | flops 1564672 | bytes 2260992
  142.9 2.6 %fusion.14 = f32[4,32,8,64]{3,1,2,0:T(8,128)S(1)} fusion(f32[4,32,8,64]{3,1,2,0:T(8,128)S(1)} %fusion.15, f32[1,8,64,64]{2,3,1,0:T(8,128)S(1)} %copy-done.7, f32[1,8,64,64]{2,3,1,0:T(8,128)S(1)} %copy-done.8, f32[1,8,64,64]{2,3,1,0:T(8,128)S(1)} %copy-done.9, f32[4]{0:T(128)} %pad.7.clone, f32[4,8,32,64]{3,2,1,0:T(8,128)S(1)} %copy-done.2, ...), kind=kOutput, calls=%fused_computation.28 | convolution fusion | flops 50921472 | bytes 1442320 | tf_op jit(solution)/shard_map/bhtc,bhcv->bhtv/dot_general | solution.py:189
  145.5 6.6 %collective-permute-done.7 = f32[8,65,64]{1,2,0:T(8,128)S(1)} collective-permute-done((f32[8,65,64]{1,2,0:T(8,128)S(1)}, f32[8,65,64]{1,2,0:T(8,128)S(1)}, u32[]{:S(2)}, u32[]{:S(2)}) %collective-permute-start.7) | collective-permute-done | bytes 133152 | tf_op jit(solution)/shard_map/ppermute | solution.py:24
  155.6 12.2 %all_to_all.5 = bf16[4,128,512]{2,1,0:T(8,128)(2,1)S(1)} all-to-all(bf16[4,128,512]{2,1,0:T(8,128)(2,1)S(1)} %bitcast.241), channel_id=1, replica_groups=mesh['seq_hi'=8,'seq_lo'=8,'tp'=4] {'tp'}, dimensions={0} | all-to-all | bytes 1048576 | tf_op jit(solution)/shard_map/all_to_all | solution.py:204
  (183 shorter events, 54.7 us)
Async XLA Ops:
  0.0 154.4 %copy-start = (bf16[512,2048]{1,0:T(8,128)(2,1)S(1)}, bf16[512,2048]{1,0:T(8,128)(2,1)}, u32[]{:S(2)}) copy-start(bf16[512,2048]{1,0:T(8,128)(2,1)} %param.25) | copy-start | bytes 6291460
  0.0 21.8 %copy-start.10 = (f32[5,2048]{1,0:T(8,128)S(1)}, f32[5,2048]{1,0:T(8,128)}, u32[]{:S(2)}) copy-start(f32[5,2048]{1,0:T(8,128)} %param.17) | copy-start | bytes 122884
  16.1 18.6 %collective-permute-start = (bf16[1,2048]{1,0:T(2,128)(2,1)S(1)}, bf16[1,2048]{1,0:T(2,128)(2,1)S(1)}, u32[]{:S(2)}, u32[]{:S(2)}) collective-permute-start(bf16[1,2048]{1,0:T(2,128)(2,1)S(1)} %get-tuple-element.83), channel_id=1, source_target_pairs={{0,4},{4,8},{8,12},{12,16},{16,20},{20,24},{24,28},{28,32},{32,36}... | collective-permute-start | bytes 12296 | tf_op jit(solution)/shard_map/ppermute | solution.py:24
  23.7 12.0 %copy-start.26 = (bf16[64,512]{1,0:T(8,128)(2,1)S(1)}, bf16[64,512]{1,0:T(8,128)(2,1)}, u32[]{:S(2)}) copy-start(bf16[64,512]{1,0:T(8,128)(2,1)} %param.20) | copy-start | bytes 196612
  36.6 15.6 %copy-start.1 = (f32[4,8,32,64]{3,2,1,0:T(8,128)}, f32[4,8,32,64]{3,2,1,0:T(8,128)S(1)}, u32[]{:S(2)}) copy-start(f32[4,8,32,64]{3,2,1,0:T(8,128)S(1)} %get-tuple-element.108) | copy-start | bytes 786436
  45.1 10.8 %copy-start.25 = (bf16[5,1,2048]{2,0,1:T(8,128)(2,1)S(1)}, bf16[5,1,2048]{2,0,1:T(8,128)(2,1)}, u32[]{:S(2)}) copy-start(bf16[5,1,2048]{2,0,1:T(8,128)(2,1)} %fusion.106) | copy-start | bytes 61444
  48.3 7.7 %collective-permute-start.1 = (f32[8,65,64]{1,2,0:T(8,128)S(1)}, f32[8,65,64]{1,2,0:T(8,128)S(1)}, u32[]{:S(2)}, u32[]{:S(2)}) collective-permute-start(f32[8,65,64]{1,2,0:T(8,128)S(1)} %pad_maximum_fusion), channel_id=1, source_target_pairs={{0,4},{4,8},{8,12},{12,16},{16,20},{20,24},{24,28},{28,32},{32,36}... | collective-permute-start | bytes 399368 | tf_op jit(solution)/shard_map/ppermute | solution.py:24
  63.8 8.1 %collective-permute-start.2 = (f32[8,65,64]{1,2,0:T(8,128)S(1)}, f32[8,65,64]{1,2,0:T(8,128)}, u32[]{:S(2)}, u32[]{:S(2)}) collective-permute-start(f32[8,65,64]{1,2,0:T(8,128)S(1)} %collective-permute-done.1), channel_id=1, source_target_pairs={{0,4},{4,8},{8,12},{12,16},{16,20},{20,24},{24,28},{28,32},{32,36}... | collective-permute-start | bytes 399368 | tf_op jit(solution)/shard_map/ppermute | solution.py:24
  74.3 12.1 %collective-permute-start.3 = (f32[8,65,64]{1,2,0:T(8,128)S(1)}, f32[8,65,64]{1,2,0:T(8,128)S(1)}, u32[]{:S(2)}, u32[]{:S(2)}) collective-permute-start(f32[8,65,64]{1,2,0:T(8,128)S(1)} %pad_maximum_fusion.1), channel_id=1, source_target_pairs={{0,8},{4,12},{8,16},{12,20},{16,24},{20,28},{24,32},{28,36},{32,40... | collective-permute-start | bytes 399368 | tf_op jit(solution)/shard_map/ppermute | solution.py:24
  80.1 14.8 %copy-start.13 = (f32[8,32,64]{2,1,0:T(8,128)S(1)}, f32[8,32,64]{2,1,0:T(8,128)}, u32[]{:S(2)}) copy-start(f32[8,32,64]{2,1,0:T(8,128)} %get-tuple-element.36) | copy-start | bytes 196612
  80.1 14.8 %copy-start.14 = (f32[8,32,64]{2,1,0:T(8,128)S(1)}, f32[8,32,64]{2,1,0:T(8,128)}, u32[]{:S(2)}) copy-start(f32[8,32,64]{2,1,0:T(8,128)} %get-tuple-element.37) | copy-start | bytes 196612
  87.0 19.4 %collective-permute-start.4 = (f32[8,65,64]{1,2,0:T(8,128)S(1)}, f32[8,65,64]{1,2,0:T(8,128)S(1)}, u32[]{:S(2)}, u32[]{:S(2)}) collective-permute-start(f32[8,65,64]{1,2,0:T(8,128)S(1)} %pad_maximum_fusion.2), channel_id=1, source_target_pairs={{0,16},{4,20},{8,24},{12,28},{16,32},{20,36},{24,40},{28,44},{32,4... | collective-permute-start | bytes 399368 | tf_op jit(solution)/shard_map/ppermute | solution.py:24
  96.4 16.4 %copy-start.11 = (f32[8,32,64]{2,1,0:T(8,128)S(1)}, f32[8,32,64]{2,1,0:T(8,128)}, u32[]{:S(2)}) copy-start(f32[8,32,64]{2,1,0:T(8,128)} %get-tuple-element.41) | copy-start | bytes 196612
  96.4 16.4 %copy-start.12 = (f32[8,32,64]{2,1,0:T(8,128)S(1)}, f32[8,32,64]{2,1,0:T(8,128)}, u32[]{:S(2)}) copy-start(f32[8,32,64]{2,1,0:T(8,128)} %get-tuple-element.42) | copy-start | bytes 196612
  102.2 12.1 %copy-start.17 = (f32[8,32,64]{2,1,0:T(8,128)S(1)}, f32[8,32,64]{2,1,0:T(8,128)}, u32[]{:S(2)}) copy-start(f32[8,32,64]{2,1,0:T(8,128)} %get-tuple-element.43) | copy-start | bytes 196612
  102.2 12.1 %copy-start.21 = (f32[8,32,64]{2,1,0:T(8,128)S(1)}, f32[8,32,64]{2,1,0:T(8,128)}, u32[]{:S(2)}) copy-start(f32[8,32,64]{2,1,0:T(8,128)} %get-tuple-element.44) | copy-start | bytes 196612
  106.8 20.0 %collective-permute-start.5 = (f32[8,65,64]{1,2,0:T(8,128)S(1)}, f32[8,65,64]{1,2,0:T(8,128)S(1)}, u32[]{:S(2)}, u32[]{:S(2)}) collective-permute-start(f32[8,65,64]{1,2,0:T(8,128)S(1)} %pad_maximum_fusion.3), channel_id=1, source_target_pairs={{0,32},{4,36},{8,40},{12,44},{16,48},{20,52},{24,56},{28,60},{32,6... | collective-permute-start | bytes 399368 | tf_op jit(solution)/shard_map/ppermute | solution.py:24
  118.5 14.2 %copy-start.16 = (f32[8,32,64]{2,1,0:T(8,128)S(1)}, f32[8,32,64]{2,1,0:T(8,128)}, u32[]{:S(2)}) copy-start(f32[8,32,64]{2,1,0:T(8,128)} %get-tuple-element.48) | copy-start | bytes 196612
  118.5 14.2 %copy-start.20 = (f32[8,32,64]{2,1,0:T(8,128)S(1)}, f32[8,32,64]{2,1,0:T(8,128)}, u32[]{:S(2)}) copy-start(f32[8,32,64]{2,1,0:T(8,128)} %get-tuple-element.49) | copy-start | bytes 196612
  127.4 11.4 %collective-permute-start.6 = (f32[8,65,64]{1,2,0:T(8,128)S(1)}, f32[8,65,64]{1,2,0:T(8,128)}, u32[]{:S(2)}, u32[]{:S(2)}) collective-permute-start(f32[8,65,64]{1,2,0:T(8,128)S(1)} %pad_maximum_fusion.4), channel_id=1, source_target_pairs={{0,64},{4,68},{8,72},{12,76},{16,80},{20,84},{24,88},{28,92},{32,9... | collective-permute-start | bytes 399368 | tf_op jit(solution)/shard_map/ppermute | solution.py:24
  137.0 15.1 %copy-start.30 = (f32[4,32]{1,0:T(4,128)S(1)}, f32[4,32]{1,0:T(4,128)}, u32[]{:S(2)}) copy-start(f32[4,32]{1,0:T(4,128)} %get-tuple-element.110) | copy-start | bytes 1540
  141.3 10.8 %collective-permute-start.7 = (f32[8,65,64]{1,2,0:T(8,128)S(1)}, f32[8,65,64]{1,2,0:T(8,128)S(1)}, u32[]{:S(2)}, u32[]{:S(2)}) collective-permute-start(f32[8,65,64]{1,2,0:T(8,128)S(1)} %pad_maximum_fusion.5), channel_id=1, source_target_pairs={{0,128},{4,132},{8,136},{12,140},{16,144},{20,148},{24,152},{28,15... | collective-permute-start | bytes 399368 | tf_op jit(solution)/shard_map/ppermute | solution.py:24
  142.9 11.5 %copy-start.6 = (f32[128,512]{1,0:T(8,128)S(1)}, f32[128,512]{1,0:T(8,128)}, u32[]{:S(2)}) copy-start(f32[128,512]{1,0:T(8,128)} %dynamic_update_slice.19) | copy-start | bytes 786436
  153.9 14.0 %copy-start.15 = (bf16[128,512]{1,0:T(8,128)(2,1)S(1)}, bf16[128,512]{1,0:T(8,128)(2,1)}, u32[]{:S(2)}) copy-start(bf16[128,512]{1,0:T(8,128)(2,1)} %param.13) | copy-start | bytes 393220
  (19 other events, 136.2 us)

commit v12 on v8

--- a/solution.py
+++ b/solution.py
@@ -155,7 +155,8 @@
         pair_ok = strictly & (seg_b[index][None, :] == seg_b[index][:, None])
         gap = jnp.minimum(excl_b[:, :, None, :] - incl_b[:, None, :, :], 0.0)
         weight = jnp.where(pair_ok[None, :, :, None], jnp.exp(gap), 0.0)
-        return jnp.einsum("htc,hsc,htsc->hts", recept_b, key_b, weight, precision=highest)
+        scores = jnp.einsum("htc,hsc,htsc->hts", recept_b, key_b, weight, precision=highest)
+        return jnp.einsum("hts,hsv->htv", scores, content_slab[index], precision=highest)
 
     scores = []
     prefix = from_behind(packed, SEQ, 1)
@@ -172,9 +173,8 @@
         scores.append(
             block_scores(index, incl[index], excl[index], gating_rows_tile[index], query_array_tile[index])
         )
-    scores = jnp.stack(scores)
     outs = (
-        jnp.einsum("bhts,bhsv->bhtv", scores, content_slab, precision=highest)
+        jnp.stack(scores)
         + present_item_reward[..., None] * content_slab
         + jnp.einsum("bhtc,bhcv->bhtv", carried, entering, precision=highest)
     )

time: 163 us -> 169 us (1.037)
  the two profiles are of different devices: /device:TPU:48 before, /device:TPU:120 now
where the time goes in v12:
time: 169 us; the launch traced here: 168 us
  other arithmetic  40.8 us (24%)
  waiting for transfers between devices  40.4 us (24%)
  blocking collectives  25.6 us (15%)
  starting transfers between devices  23.6 us (14%)
  matrix products  20.3 us (12%)
  local copies, waits for them, and re-layouts  13.5 us (8%)
  between operations  3.42 us (2%)
    ppermute x8, waiting for transfers between devices, from_behind(): return lax.ppermute(block, axis, route)  40.4 us
    ppermute x8, starting transfers between devices, from_behind(): return lax.ppermute(block, axis, route)  23.6 us
    dot_general x4, other arithmetic, block_scores(): jnp.einsum('htc,hsc,htsc->hts', recept_b, key_b, weight, precision=highest)  13.8 us
    all_gather x1, blocking collectives, body(): full = lax.all_gather(tier_source_concatenated, 'tp', axis=1, tiled=True)  13.5 us
    all_to_all x1, blocking collectives, body(): pieces = lax.all_to_all(pieces, 'tp', 0, 0, tiled=True)  12.1 us
    dot_general x2, matrix products, project(): jnp.einsum('itd,ide->ite', mixed[:4], mapping_matrices_pile, preferred_el...  10.2 us
  transfers between devices with their start and end apart: 8, of which 5 were waited for; matrix products, arithmetic and copies ran while one was open for 23% of the time, Pallas kernels for 0%

profile of v12, /device:TPU:120, one launch (start us, length us, event | category | flops | bytes accessed | tf_op | source)
XLA Modules:
  0.0 167.7 jit_solution(1064736691147563108)
XLA Ops:
  0.0 13.5 %all_gather.3 = bf16[128,2048]{1,0:T(8,128)(2,1)S(1)} all-gather(bf16[128,512]{1,0:T(8,128)(2,1)} %param.13), channel_id=1, replica_groups=mesh['seq_hi'=8,'seq_lo'=8,'tp'=4] {'tp'}, dimensions={1}, use_global_device_ids=true | all-gather | bytes 655360 | tf_op jit(solution)/shard_map/all_gather | solution.py:54
  13.9 2.1 %fusion.72 = (f32[128,2048]{1,0:T(8,128)}, bf16[128,2048]{1,0:T(8,128)(2,1)S(1)}) fusion(f32[2048]{0:T(1024)} %param.16, f32[2048]{0:T(1024)} %param.15, f32[128]{0:T(128)S(1)} %add_rsqrt_fusion.1, f32[128]{0:T(128)S(1)} %broadcast_multiply_fusion.1, bf16[128,2048]{1,0:T(8,128)(2,1)S(1)} %all_gather.3), kind=kLoop, calls=%fused_computation.189 | loop fusion | flops 1835008 | bytes 2114560 | tf_op jit(solution)/shard_map/convert_element_type | solution.py:63
  16.1 1.9 %collective-permute-start = (bf16[1,2048]{1,0:T(2,128)(2,1)S(1)}, bf16[1,2048]{1,0:T(2,128)(2,1)S(1)}, u32[]{:S(2)}, u32[]{:S(2)}) collective-permute-start(bf16[1,2048]{1,0:T(2,128)(2,1)S(1)} %get-tuple-element.78), channel_id=1, source_target_pairs={{0,4},{4,8},{8,12},{12,16},{16,20},{20,24},{24,28},{28,32},{32,36}... | collective-permute-start | bytes 12296 | tf_op jit(solution)/shard_map/ppermute | solution.py:24
  20.2 1.9 %add_convert_fusion = bf16[5,128,2048]{2,1,0:T(8,128)(2,1)S(1)} fusion(f32[5,2048]{1,0:T(8,128)S(1)} %copy-done.8, f32[128,2048]{1,0:T(8,128)S(1)} %convert_subtract_fusion.1, f32[128,2048]{1,0:T(8,128)} %get-tuple-element.52), kind=kLoop, calls=%fused_computation.1 | loop fusion | flops 3932160 | bytes 4759552 | tf_op jit(solution)/shard_map/convert_element_type | solution.py:65
  22.2 5.7 %fusion.70 = f32[4,128,512]{2,1,0:T(8,128)} fusion(bf16[4,2048,512]{2,1,0:T(8,128)(2,1)} %param.18, f32[5,2048]{1,0:T(8,128)S(1)} %copy-done.8, f32[128,2048]{1,0:T(8,128)S(1)} %convert_subtract_fusion.1, f32[128,2048]{1,0:T(8,128)S(1)} %copy-done.5), kind=kOutput, calls=%fused_computation.187 | convolution fusion | flops 1077673984 | bytes 11575296 | tf_op jit(solution)/shard_map/itd,ide->ite/dot_general | solution.py:69
  39.5 4.6 %fusion.51 = f32[4,1,512]{2,1,0:T(1,128)S(1)} fusion(bf16[4,2048,512]{2,1,0:T(8,128)(2,1)} %param.18, bf16[4,2048,1]{1,0,2:T(4,128)(2,1)S(1)} %slice_bitcast_fusion.28), kind=kOutput, calls=%fused_computation.138 | convolution fusion | flops 8388608 | bytes 8413184 | tf_op jit(solution)/shard_map/itd,ide->ite/dot_general | solution.py:69
  49.6 2.8 %fusion.26 = f32[4,8,64,64]{2,3,1,0:T(8,128)} fusion(f32[4,8,32,64]{3,2,1,0:T(8,128)} %copy-done.4, f32[4,32]{1,0:T(4,128)} %compare_convert_fusion.1, f32[4,8,64]{2,1,0:T(8,128)S(1)} %bitcast.257, bf16[4,32,8,64]{3,2,1,0:T(8,128)(2,1)S(1)} %convert_element_type.113, f32[4,32,8,64]{3,2,1,0:T(8,128)S(1)} %reshape.504), kind=kOutput, calls=%fused_computation.56 | convolution fusion | flops 50528256 | bytes 1188352 | tf_op jit(solution)/shard_map/bhsc,bhsv->bhcv/dot_general | solution.py:127
  57.5 1.8 %pad_maximum_fusion = f32[8,65,64]{1,2,0:T(8,128)} fusion(f32[8,1,64]{1,2,0:T(8,128)} %copy.152, f32[8,64,64]{1,2,0:T(8,128)S(1)} %fusion.39), kind=kLoop, calls=%fused_computation.83 | loop fusion | flops 33280 | bytes 266240 | tf_op jit(solution)/shard_map/concatenate | solution.py:145
  59.3 5.1 %collective-permute-start.1 = (f32[8,65,64]{1,2,0:T(8,128)}, f32[8,65,64]{1,2,0:T(8,128)}, u32[]{:S(2)}, u32[]{:S(2)}) collective-permute-start(f32[8,65,64]{1,2,0:T(8,128)} %pad_maximum_fusion), channel_id=1, source_target_pairs={{0,4},{4,8},{8,12},{12,16},{16,20},{20,24},{24,28},{28,32},{32,36}... | collective-permute-start | bytes 399368 | tf_op jit(solution)/shard_map/ppermute | solution.py:24
  68.2 1.9 %collective-permute-start.2 = (f32[8,65,64]{1,2,0:T(8,128)}, f32[8,65,64]{1,2,0:T(8,128)S(1)}, u32[]{:S(2)}, u32[]{:S(2)}) collective-permute-start(f32[8,65,64]{1,2,0:T(8,128)} %collective-permute-done.1), channel_id=1, source_target_pairs={{0,4},{4,8},{8,12},{12,16},{16,20},{20,24},{24,28},{28,32},{32,36}... | collective-permute-start | bytes 399368 | tf_op jit(solution)/shard_map/ppermute | solution.py:24
  70.2 5.9 %collective-permute-done.2 = f32[8,65,64]{1,2,0:T(8,128)S(1)} collective-permute-done((f32[8,65,64]{1,2,0:T(8,128)}, f32[8,65,64]{1,2,0:T(8,128)S(1)}, u32[]{:S(2)}, u32[]{:S(2)}) %collective-permute-start.2) | collective-permute-done | bytes 133152 | tf_op jit(solution)/shard_map/ppermute | solution.py:24
  78.5 6.7 %collective-permute-start.3 = (f32[8,65,64]{1,2,0:T(8,128)S(1)}, f32[8,65,64]{1,2,0:T(8,128)S(1)}, u32[]{:S(2)}, u32[]{:S(2)}) collective-permute-start(f32[8,65,64]{1,2,0:T(8,128)S(1)} %pad_maximum_fusion.1), channel_id=1, source_target_pairs={{0,8},{4,12},{8,16},{12,20},{16,24},{20,28},{24,32},{28,36},{32,40... | collective-permute-start | bytes 399368 | tf_op jit(solution)/shard_map/ppermute | solution.py:24
  86.0 3.4 %fusion.4 = f32[8,32,32]{1,2,0:T(8,128)S(1)} fusion(f32[8,32,32,64]{3,2,1,0:T(8,128)S(1)} %exponential_select_fusion.3, f32[8,64,32]{1,2,0:T(8,128)S(1)} %bitcast.256, f32[8,64,32]{1,2,0:T(8,128)S(1)} %bitcast.255), kind=kLoop, calls=%fused_computation.9 | loop fusion | flops 1564672 | bytes 2260992 | tf_op jit(solution)/shard_map/htc,hsc,htsc->hts/dot_general | solution.py:158
  90.3 2.9 %collective-permute-start.4 = (f32[8,65,64]{1,2,0:T(8,128)S(1)}, f32[8,65,64]{1,2,0:T(8,128)S(1)}, u32[]{:S(2)}, u32[]{:S(2)}) collective-permute-start(f32[8,65,64]{1,2,0:T(8,128)S(1)} %pad_maximum_fusion.2), channel_id=1, source_target_pairs={{0,16},{4,20},{8,24},{12,28},{16,32},{20,36},{24,40},{28,44},{32,4... | collective-permute-start | bytes 399368 | tf_op jit(solution)/shard_map/ppermute | solution.py:24
  94.1 3.4 %fusion.3 = f32[8,32,32]{1,2,0:T(8,128)S(1)} fusion(f32[8,32,32,64]{3,2,1,0:T(8,128)S(1)} %exponential_select_fusion.2, f32[8,64,32]{1,2,0:T(8,128)S(1)} %bitcast.254, f32[8,64,32]{1,2,0:T(8,128)S(1)} %bitcast.253), kind=kLoop, calls=%fused_computation.7 | loop fusion | flops 1564672 | bytes 2260992 | tf_op jit(solution)/shard_map/htc,hsc,htsc->hts/dot_general | solution.py:158
  97.8 10.9 %collective-permute-done.4 = f32[8,65,64]{1,2,0:T(8,128)S(1)} collective-permute-done((f32[8,65,64]{1,2,0:T(8,128)S(1)}, f32[8,65,64]{1,2,0:T(8,128)S(1)}, u32[]{:S(2)}, u32[]{:S(2)}) %collective-permute-start.4) | collective-permute-done | bytes 133152 | tf_op jit(solution)/shard_map/ppermute | solution.py:24
  109.2 2.1 %collective-permute-start.5 = (f32[8,65,64]{1,2,0:T(8,128)S(1)}, f32[8,65,64]{1,2,0:T(8,128)S(1)}, u32[]{:S(2)}, u32[]{:S(2)}) collective-permute-start(f32[8,65,64]{1,2,0:T(8,128)S(1)} %pad_maximum_fusion.3), channel_id=1, source_target_pairs={{0,32},{4,36},{8,40},{12,44},{16,48},{20,52},{24,56},{28,60},{32,6... | collective-permute-start | bytes 399368 | tf_op jit(solution)/shard_map/ppermute | solution.py:24
  112.2 3.4 %fusion.2 = f32[8,32,32]{1,2,0:T(8,128)S(1)} fusion(f32[8,32,32,64]{3,2,1,0:T(8,128)S(1)} %exponential_select_fusion.1, f32[8,64,32]{1,2,0:T(8,128)S(1)} %bitcast.252, f32[8,64,32]{1,2,0:T(8,128)S(1)} %bitcast.251), kind=kLoop, calls=%fused_computation.5 | loop fusion | flops 1564672 | bytes 2260992 | tf_op jit(solution)/shard_map/htc,hsc,htsc->hts/dot_general | solution.py:158
  115.9 13.1 %collective-permute-done.5 = f32[8,65,64]{1,2,0:T(8,128)S(1)} collective-permute-done((f32[8,65,64]{1,2,0:T(8,128)S(1)}, f32[8,65,64]{1,2,0:T(8,128)S(1)}, u32[]{:S(2)}, u32[]{:S(2)}) %collective-permute-start.5) | collective-permute-done | bytes 133152 | tf_op jit(solution)/shard_map/ppermute | solution.py:24
  131.7 3.4 %fusion.1 = f32[8,32,32]{1,2,0:T(8,128)S(1)} fusion(f32[8,32,32,64]{3,2,1,0:T(8,128)S(1)} %exponential_select_fusion, f32[8,64,32]{1,2,0:T(8,128)S(1)} %bitcast.250, f32[8,64,32]{1,2,0:T(8,128)S(1)} %bitcast.249), kind=kLoop, calls=%fused_computation.3 | loop fusion | flops 1564672 | bytes 2260992 | tf_op jit(solution)/shard_map/htc,hsc,htsc->hts/dot_general | solution.py:158
  135.4 3.3 %collective-permute-done.6 = f32[8,65,64]{1,2,0:T(8,128)S(1)} collective-permute-done((f32[8,65,64]{1,2,0:T(8,128)S(1)}, f32[8,65,64]{1,2,0:T(8,128)S(1)}, u32[]{:S(2)}, u32[]{:S(2)}) %collective-permute-start.6) | collective-permute-done | bytes 133152 | tf_op jit(solution)/shard_map/ppermute | solution.py:24
  141.9 7.2 %collective-permute-done.7 = f32[8,65,64]{1,2,0:T(8,128)S(1)} collective-permute-done((f32[8,65,64]{1,2,0:T(8,128)S(1)}, f32[8,65,64]{1,2,0:T(8,128)S(1)}, u32[]{:S(2)}, u32[]{:S(2)}) %collective-permute-start.7) | collective-permute-done | bytes 133152 | tf_op jit(solution)/shard_map/ppermute | solution.py:24
  149.9 2.0 %fusion.77 = (f32[4,32,8]{1,2,0:T(8,128)S(1)}, f32[4,32,8,64]{3,1,2,0:T(8,128)S(1)}) fusion(f32[4,8,32,64]{3,2,1,0:T(8,128)S(1)} %convolution_bitcast_fusion, f32[4,8,32,64]{3,2,1,0:T(8,128)S(1)} %fusion.10, f32[1,8,64,64]{2,3,1,0:T(8,128)S(1)} %get-tuple-element.45, f32[1,8,64,64]{2,3,1,0:T(8,128)S(1)} %get-tuple-element.46, ...), kind=kOutput, calls=%fused_computation.193 | convolution fusion | flops 51051520 | bytes 1708560 | tf_op jit(solution)/shard_map/bhtc,bhcv->bhtv/dot_general | solution.py:179
  154.8 12.1 %all_to_all.5 = bf16[4,128,512]{2,1,0:T(8,128)(2,1)S(1)} all-to-all(bf16[4,128,512]{2,1,0:T(8,128)(2,1)S(1)} %bitcast.239), channel_id=1, replica_groups=mesh['seq_hi'=8,'seq_lo'=8,'tp'=4] {'tp'}, dimensions={0} | all-to-all | bytes 1048576 | tf_op jit(solution)/shard_map/all_to_all | solution.py:194
  (151 shorter events, 42.9 us)
Async XLA Ops:
  0.0 153.2 %copy-start = (bf16[512,2048]{1,0:T(8,128)(2,1)S(1)}, bf16[512,2048]{1,0:T(8,128)(2,1)}, u32[]{:S(2)}) copy-start(bf16[512,2048]{1,0:T(8,128)(2,1)} %param.25) | copy-start | bytes 6291460
  0.0 20.2 %copy-start.8 = (f32[5,2048]{1,0:T(8,128)S(1)}, f32[5,2048]{1,0:T(8,128)}, u32[]{:S(2)}) copy-start(f32[5,2048]{1,0:T(8,128)} %param.17) | copy-start | bytes 122884
  16.1 20.7 %collective-permute-start = (bf16[1,2048]{1,0:T(2,128)(2,1)S(1)}, bf16[1,2048]{1,0:T(2,128)(2,1)S(1)}, u32[]{:S(2)}, u32[]{:S(2)}) collective-permute-start(bf16[1,2048]{1,0:T(2,128)(2,1)S(1)} %get-tuple-element.78), channel_id=1, source_target_pairs={{0,4},{4,8},{8,12},{12,16},{16,20},{20,24},{24,28},{28,32},{32,36}... | collective-permute-start | bytes 12296 | tf_op jit(solution)/shard_map/ppermute | solution.py:24
  22.1 8.0 %copy-start.22 = (bf16[2048,64]{0,1:T(8,128)(2,1)S(1)}, bf16[2048,64]{0,1:T(8,128)(2,1)}, u32[]{:S(2)}) copy-start(bf16[2048,64]{0,1:T(8,128)(2,1)} %param.19) | copy-start | bytes 786436
  22.1 10.3 %copy-start.19 = (f32[512]{0:T(512)S(1)}, f32[512]{0:T(512)}, u32[]{:S(2)}) copy-start(f32[512]{0:T(512)} %param.21) | copy-start | bytes 6148
  22.1 10.3 %copy-start.18 = (f32[512]{0:T(512)S(1)}, f32[512]{0:T(512)}, u32[]{:S(2)}) copy-start(f32[512]{0:T(512)} %param.22) | copy-start | bytes 6148
  22.1 15.1 %copy-start.9 = (bf16[64,512]{1,0:T(8,128)(2,1)S(1)}, bf16[64,512]{1,0:T(8,128)(2,1)}, u32[]{:S(2)}) copy-start(bf16[64,512]{1,0:T(8,128)(2,1)} %param.20) | copy-start | bytes 196612
  47.8 16.6 %copy-start.1 = (f32[4,32,8,64]{3,2,1,0:T(8,128)}, f32[4,32,8,64]{3,2,1,0:T(8,128)S(1)}, u32[]{:S(2)}) copy-start(f32[4,32,8,64]{3,2,1,0:T(8,128)S(1)} %reshape.504) | copy-start | bytes 786436
  57.5 12.6 %copy-start.21 = (f32[4]{0:T(128)S(1)}, f32[4]{0:T(128)}, u32[]{:S(2)}) copy-start(f32[4]{0:T(128)} %pad.1.clone) | copy-start | bytes 52
  59.3 8.9 %collective-permute-start.1 = (f32[8,65,64]{1,2,0:T(8,128)}, f32[8,65,64]{1,2,0:T(8,128)}, u32[]{:S(2)}, u32[]{:S(2)}) collective-permute-start(f32[8,65,64]{1,2,0:T(8,128)} %pad_maximum_fusion), channel_id=1, source_target_pairs={{0,4},{4,8},{8,12},{12,16},{16,20},{20,24},{24,28},{28,32},{32,36}... | collective-permute-start | bytes 399368 | tf_op jit(solution)/shard_map/ppermute | solution.py:24
  65.6 19.6 %copy-start.14 = (pred[32,32]{1,0:T(8,128)(4,1)S(1)}, pred[32,32]{1,0:T(8,128)(4,1)}, u32[]{:S(2)}) copy-start(pred[32,32]{1,0:T(8,128)(4,1)} %get-tuple-element.118) | copy-start | bytes 3076
  68.2 7.9 %collective-permute-start.2 = (f32[8,65,64]{1,2,0:T(8,128)}, f32[8,65,64]{1,2,0:T(8,128)S(1)}, u32[]{:S(2)}, u32[]{:S(2)}) collective-permute-start(f32[8,65,64]{1,2,0:T(8,128)} %collective-permute-done.1), channel_id=1, source_target_pairs={{0,4},{4,8},{8,12},{12,16},{16,20},{20,24},{24,28},{28,32},{32,36}... | collective-permute-start | bytes 399368 | tf_op jit(solution)/shard_map/ppermute | solution.py:24
  78.5 11.3 %collective-permute-start.3 = (f32[8,65,64]{1,2,0:T(8,128)S(1)}, f32[8,65,64]{1,2,0:T(8,128)S(1)}, u32[]{:S(2)}, u32[]{:S(2)}) collective-permute-start(f32[8,65,64]{1,2,0:T(8,128)S(1)} %pad_maximum_fusion.1), channel_id=1, source_target_pairs={{0,8},{4,12},{8,16},{12,20},{16,24},{20,28},{24,32},{28,36},{32,40... | collective-permute-start | bytes 399368 | tf_op jit(solution)/shard_map/ppermute | solution.py:24
  90.3 18.4 %collective-permute-start.4 = (f32[8,65,64]{1,2,0:T(8,128)S(1)}, f32[8,65,64]{1,2,0:T(8,128)S(1)}, u32[]{:S(2)}, u32[]{:S(2)}) collective-permute-start(f32[8,65,64]{1,2,0:T(8,128)S(1)} %pad_maximum_fusion.2), channel_id=1, source_target_pairs={{0,16},{4,20},{8,24},{12,28},{16,32},{20,36},{24,40},{28,44},{32,4... | collective-permute-start | bytes 399368 | tf_op jit(solution)/shard_map/ppermute | solution.py:24
  94.1 17.3 %copy-start.12 = (pred[32,32]{1,0:T(8,128)(4,1)S(1)}, pred[32,32]{1,0:T(8,128)(4,1)}, u32[]{:S(2)}) copy-start(pred[32,32]{1,0:T(8,128)(4,1)} %get-tuple-element.116) | copy-start | bytes 3076
  109.2 19.8 %collective-permute-start.5 = (f32[8,65,64]{1,2,0:T(8,128)S(1)}, f32[8,65,64]{1,2,0:T(8,128)S(1)}, u32[]{:S(2)}, u32[]{:S(2)}) collective-permute-start(f32[8,65,64]{1,2,0:T(8,128)S(1)} %pad_maximum_fusion.3), channel_id=1, source_target_pairs={{0,32},{4,36},{8,40},{12,44},{16,48},{20,52},{24,56},{28,60},{32,6... | collective-permute-start | bytes 399368 | tf_op jit(solution)/shard_map/ppermute | solution.py:24
  112.2 18.7 %copy-start.11 = (pred[32,32]{1,0:T(8,128)(4,1)S(1)}, pred[32,32]{1,0:T(8,128)(4,1)}, u32[]{:S(2)}) copy-start(pred[32,32]{1,0:T(8,128)(4,1)} %get-tuple-element.115) | copy-start | bytes 3076
  129.5 9.2 %collective-permute-start.6 = (f32[8,65,64]{1,2,0:T(8,128)S(1)}, f32[8,65,64]{1,2,0:T(8,128)S(1)}, u32[]{:S(2)}, u32[]{:S(2)}) collective-permute-start(f32[8,65,64]{1,2,0:T(8,128)S(1)} %pad_maximum_fusion.4), channel_id=1, source_target_pairs={{0,64},{4,68},{8,72},{12,76},{16,80},{20,84},{24,88},{28,92},{32,9... | collective-permute-start | bytes 399368 | tf_op jit(solution)/shard_map/ppermute | solution.py:24
  131.6 9.2 %copy-start.2 = (f32[4,32,8,64]{3,2,1,0:T(8,128)S(1)}, f32[4,32,8,64]{3,2,1,0:T(8,128)}, u32[]{:S(2)}) copy-start(f32[4,32,8,64]{3,2,1,0:T(8,128)} %copy-done.1) | copy-start | bytes 786436
  131.7 9.2 %copy-start.10 = (f32[8,64]{1,0:T(8,128)S(1)}, f32[8,64]{1,0:T(8,128)}, u32[]{:S(2)}) copy-start(f32[8,64]{1,0:T(8,128)} %mul.399) | copy-start | bytes 6148
  131.7 17.4 %copy-start.15 = (f32[4,32]{1,0:T(4,128)S(1)}, f32[4,32]{1,0:T(4,128)}, u32[]{:S(2)}) copy-start(f32[4,32]{1,0:T(4,128)} %get-tuple-element.103) | copy-start | bytes 1540
  135.1 14.7 %copy-start.20 = (f32[4]{0:T(128)S(1)}, f32[4]{0:T(128)}, u32[]{:S(2)}) copy-start(f32[4]{0:T(128)} %pad.7.clone) | copy-start | bytes 52
  139.3 9.8 %collective-permute-start.7 = (f32[8,65,64]{1,2,0:T(8,128)S(1)}, f32[8,65,64]{1,2,0:T(8,128)S(1)}, u32[]{:S(2)}, u32[]{:S(2)}) collective-permute-start(f32[8,65,64]{1,2,0:T(8,128)S(1)} %pad_maximum_fusion.5), channel_id=1, source_target_pairs={{0,128},{4,132},{8,136},{12,140},{16,144},{20,148},{24,152},{28,15... | collective-permute-start | bytes 399368 | tf_op jit(solution)/shard_map/ppermute | solution.py:24
  152.7 14.3 %copy-start.7 = (bf16[128,512]{1,0:T(8,128)(2,1)S(1)}, bf16[128,512]{1,0:T(8,128)(2,1)}, u32[]{:S(2)}) copy-start(bf16[128,512]{1,0:T(8,128)(2,1)} %param.13) | copy-start | bytes 393220
  (7 other events, 23.8 us)

commit v13 on v8

--- a/solution.py
+++ b/solution.py
@@ -49,7 +49,7 @@
     rows = tier_source_concatenated.shape[0]
     local_width = mapping_matrices_pile.shape[2]
     mixing_values_divided = local_width // CHANNELS_ONE_HEAD
-    block = min(32, rows)
+    block = min(16, rows)
     blocks = rows // block
     full = lax.all_gather(tier_source_concatenated, "tp", axis=1, tiled=True)
     normed = layer_norm(
@@ -151,11 +151,18 @@
         return jnp.concatenate([state, own_decay * got_decay], axis=1)
 
     devices = size_of(SEQ)
-    def block_scores(index, incl_b, excl_b, recept_b, key_b):
-        pair_ok = strictly & (seg_b[index][None, :] == seg_b[index][:, None])
-        gap = jnp.minimum(excl_b[:, :, None, :] - incl_b[:, None, :, :], 0.0)
-        weight = jnp.where(pair_ok[None, :, :, None], jnp.exp(gap), 0.0)
-        return jnp.einsum("htc,hsc,htsc->hts", recept_b, key_b, weight, precision=highest)
+    def block_scores(seg_g, incl_g, excl_g, recept_g, key_g):
+        pair_ok = strictly[None] & (seg_g[:, None, :] == seg_g[:, :, None])
+        gap = jnp.minimum(excl_g[:, :, :, None, :] - incl_g[:, :, None, :, :], 0.0)
+        weight = jnp.where(pair_ok[:, None, :, :, None], jnp.exp(gap), 0.0)
+        return jnp.einsum("bhtc,bhsc,bhtsc->bhts", recept_g, key_g, weight, precision=highest)
+
+    group = max(1, blocks // 4)
+    groups = blocks // group
+
+    def group_operands(index):
+        part = slice(index * group, (index + 1) * group)
+        return (incl[part], excl[part], gating_rows_tile[part], query_array_tile[part])
 
     scores = []
     prefix = from_behind(packed, SEQ, 1)
@@ -164,15 +171,12 @@
         prefix = combine(from_behind(prefix, SEQ, distance), prefix)
         distance *= 2
         index = len(scores)
-        if index < blocks:
-            operands = (incl[index], excl[index], gating_rows_tile[index], query_array_tile[index])
-            prefix, operands = lax.optimization_barrier((prefix, operands))
-            scores.append(block_scores(index, *operands))
-    for index in range(len(scores), blocks):
-        scores.append(
-            block_scores(index, incl[index], excl[index], gating_rows_tile[index], query_array_tile[index])
-        )
-    scores = jnp.stack(scores)
+        if index < groups:
+            prefix, operands = lax.optimization_barrier((prefix, group_operands(index)))
+            scores.append(block_scores(seg_b[index * group : (index + 1) * group], *operands))
+    for index in range(len(scores), groups):
+        scores.append(block_scores(seg_b[index * group : (index + 1) * group], *group_operands(index)))
+    scores = jnp.concatenate(scores, axis=0)
     outs = (
         jnp.einsum("bhts,bhsv->bhtv", scores, content_slab, precision=highest)
         + present_item_reward[..., None] * content_slab

time: 163 us -> 173 us (1.061)
  waiting for transfers between devices: 21.4 us -> 36.4 us
  other arithmetic: 42.7 us -> 35.5 us
  starting transfers between devices: 29.9 us -> 26 us
  between operations: 3.27 us -> 6.09 us
  local copies, waits for them, and re-layouts: 15.7 us -> 18 us
    ppermute x8, waiting for transfers between devices: 21.4 us -> 36.4 us  [from_behind(): return lax.ppermute(block, axis, route)]
    select_n x4, other arithmetic: 5.7 us -> 1.61 us  [block_scores(): weight = jnp.where(pair_ok[:, None, :, :, None], jnp.exp(gap), 0.0)]
    ppermute x8, starting transfers between devices: 29.9 us -> 26 us  [from_behind(): return lax.ppermute(block, axis, route)]
    slice x4, other arithmetic: 1.28 us -> 4.13 us  [combine(): own[:, CHANNELS_ONE_HEAD:]]
    mul x2 -> x1, other arithmetic: 3.33 us -> 0.62 us  [body(): reach.append(alive * jnp.exp(offset))]
    unnamed x4 -> x16, other arithmetic: 15.1 us -> 12.4 us
    add x5, other arithmetic: 1.12 us -> 3.14 us  [combine(): state = jnp.transpose(own_decay, (0, 2, 1)) * got_state + own_state]
    slice x1 -> x3, local copies, waits for them, and re-layouts: 0.07 us -> 1.91 us  [the longest x1 0.92 us: group_operands(): excl[part]]
  transfers between devices with their start and end apart: 8 -> 8, of which waited for: 6 -> 6; matrix products, arithmetic and copies ran while one was open for 30% -> 24% of each run, Pallas kernels for 0% -> 0%
where the time goes in v13:
time: 173 us; the launch traced here: 171 us
  waiting for transfers between devices  36.4 us (21%)
  other arithmetic  35.5 us (21%)
  starting transfers between devices  26 us (15%)
  blocking collectives  25.6 us (15%)
  matrix products  23 us (13%)
  local copies, waits for them, and re-layouts  18 us (10%)
  between operations  6.09 us (4%)
    ppermute x8, waiting for transfers between devices, from_behind(): return lax.ppermute(block, axis, route)  36.4 us
    ppermute x8, starting transfers between devices, from_behind(): return lax.ppermute(block, axis, route)  26 us
    all_gather x1, blocking collectives, body(): full = lax.all_gather(tier_source_concatenated, 'tp', axis=1, tiled=True)  13.5 us
    unnamed x16, other arithmetic  12.4 us
    all_to_all x1, blocking collectives, body(): pieces = lax.all_to_all(pieces, 'tp', 0, 0, tiled=True)  12.2 us
    dot_general x2, matrix products, project(): jnp.einsum('itd,ide->ite', mixed[:4], mapping_matrices_pile, preferred_el...  10.3 us
    dot_general x4, local copies, waits for them, and re-layouts, block_scores(): jnp.einsum('bhtc,bhsc,bhtsc->bhts', recept_g, key_g, weight, precision=hi...  5.71 us
    slice x4, other arithmetic, combine(): own[:, CHANNELS_ONE_HEAD:]  4.13 us
  transfers between devices with their start and end apart: 8, of which 6 were waited for; matrix products, arithmetic and copies ran while one was open for 24% of the time, Pallas kernels for 0%

profile of v13, /device:TPU:48, one launch (start us, length us, event | category | flops | bytes accessed | tf_op | source)
XLA Modules:
  0.0 170.6 jit_solution(15497258497653780678)
XLA Ops:
  0.0 13.5 %all_gather.3 = bf16[128,2048]{1,0:T(8,128)(2,1)S(1)} all-gather(bf16[128,512]{1,0:T(8,128)(2,1)} %param.13), channel_id=1, replica_groups=mesh['seq_hi'=8,'seq_lo'=8,'tp'=4] {'tp'}, dimensions={1}, use_global_device_ids=true | all-gather | bytes 655360 | tf_op jit(solution)/shard_map/all_gather | solution.py:54
  13.9 2.1 %fusion.76 = (f32[128,2048]{1,0:T(8,128)}, bf16[128,2048]{1,0:T(8,128)(2,1)S(1)}) fusion(f32[2048]{0:T(1024)} %param.16, f32[2048]{0:T(1024)} %param.15, f32[128]{0:T(128)S(1)} %add_rsqrt_fusion.1, f32[128]{0:T(128)S(1)} %broadcast_multiply_fusion.1, bf16[128,2048]{1,0:T(8,128)(2,1)S(1)} %all_gather.3), kind=kLoop, calls=%fused_computation.196 | loop fusion | flops 1835008 | bytes 2114560 | tf_op jit(solution)/shard_map/convert_element_type | solution.py:63
  16.1 1.9 %collective-permute-start = (bf16[1,2048]{1,0:T(2,128)(2,1)S(1)}, bf16[1,2048]{1,0:T(2,128)(2,1)S(1)}, u32[]{:S(2)}, u32[]{:S(2)}) collective-permute-start(bf16[1,2048]{1,0:T(2,128)(2,1)S(1)} %get-tuple-element.87), channel_id=1, source_target_pairs={{0,4},{4,8},{8,12},{12,16},{16,20},{20,24},{24,28},{28,32},{32,36}... | collective-permute-start | bytes 12296 | tf_op jit(solution)/shard_map/ppermute | solution.py:24
  21.6 2.1 %add_convert_fusion = bf16[5,128,2048]{2,1,0:T(8,128)(2,1)} fusion(f32[5,2048]{1,0:T(8,128)S(1)} %copy-done.24, f32[128,2048]{1,0:T(8,128)S(1)} %convert_subtract_fusion.1, f32[128,2048]{1,0:T(8,128)S(1)} %copy-done.7), kind=kLoop, calls=%fused_computation | loop fusion | flops 3932160 | bytes 4759552 | tf_op jit(solution)/shard_map/convert_element_type | solution.py:65
  23.7 5.7 %fusion.74 = f32[4,128,512]{2,1,0:T(8,128)} fusion(bf16[4,2048,512]{2,1,0:T(8,128)(2,1)} %param.18, f32[5,2048]{1,0:T(8,128)S(1)} %copy-done.24, f32[128,2048]{1,0:T(8,128)S(1)} %convert_subtract_fusion.1, f32[128,2048]{1,0:T(8,128)S(1)} %copy-done.7), kind=kOutput, calls=%fused_computation.194 | convolution fusion | flops 1077673984 | bytes 11575296 | tf_op jit(solution)/shard_map/itd,ide->ite/dot_general | solution.py:69
  40.5 4.6 %fusion.59 = f32[4,1,512]{2,1,0:T(1,128)S(1)} fusion(bf16[4,2048,512]{2,1,0:T(8,128)(2,1)} %param.18, bf16[4,2048,1]{1,0,2:T(4,128)(2,1)S(1)} %slice_bitcast_fusion.4), kind=kOutput, calls=%fused_computation.142 | convolution fusion | flops 8388608 | bytes 8413184 | tf_op jit(solution)/shard_map/itd,ide->ite/dot_general | solution.py:69
  51.7 2.2 %fusion.24 = f32[8,8,64,64]{2,3,1,0:T(8,128)S(1)} fusion(f32[8,8,16,64]{3,2,1,0:T(8,128)} %copy-done.5, f32[8,16]{1,0:T(8,128)S(1)} %compare_convert_fusion.1, f32[8,8,64]{2,1,0:T(8,128)S(1)} %bitcast.249, bf16[8,16,8,64]{3,2,1,0:T(8,128)(2,1)} %convert_element_type.115, f32[8,16,8,64]{3,2,1,0:T(8,128)S(1)} %reshape.620), kind=kOutput, calls=%fused_computation.51 | convolution fusion | flops 50528256 | bytes 1720832 | tf_op jit(solution)/shard_map/bhsc,bhsv->bhcv/dot_general | solution.py:127
  55.1 3.9 %collective-permute-start.1 = (f32[8,65,64]{1,2,0:T(8,128)}, f32[8,65,64]{1,2,0:T(8,128)S(1)}, u32[]{:S(2)}, u32[]{:S(2)}) collective-permute-start(f32[8,65,64]{1,2,0:T(8,128)} %pad_maximum_fusion), channel_id=1, source_target_pairs={{0,4},{4,8},{8,12},{12,16},{16,20},{20,24},{24,28},{28,32},{32,36}... | collective-permute-start | bytes 399368 | tf_op jit(solution)/shard_map/ppermute | solution.py:24
  61.2 1.8 %fusion.50 = f32[8,8,64,64]{2,3,1,0:T(8,128)} fusion(f32[8,8,64,64]{2,3,1,0:T(8,128)} %broadcast_dynamic-update-slice_fusion, f32[8,8,64,64]{2,3,1,0:T(8,128)} %copy-done.1, f32[8,64]{1,0:T(8,128)S(1)} %get-tuple-element.98), kind=kLoop, calls=%fused_computation.118 | loop fusion | flops 32768 | bytes 526336
  63.0 1.8 %constant_dynamic-update-slice_fusion.2 = (f32[8,8,64,64]{2,3,1,0:T(8,128)}, f32[1,8,64,64]{2,3,1,0:T(8,128)S(1)}) fusion(f32[8,8,64,64]{2,3,1,0:T(8,128)} %fusion.50, f32[8,8,64,64]{2,3,1,0:T(8,128)} %copy-done.1, f32[8,64]{1,0:T(8,128)S(1)} %get-tuple-element.98, f32[8,64]{1,0:T(8,128)} %copy-done.32), kind=kLoop, calls=%fused_computation.133 | loop fusion | flops 98304 | bytes 923648
  69.5 1.9 %collective-permute-start.2 = (f32[8,65,64]{1,2,0:T(8,128)S(1)}, f32[8,65,64]{1,2,0:T(8,128)S(1)}, u32[]{:S(2)}, u32[]{:S(2)}) collective-permute-start(f32[8,65,64]{1,2,0:T(8,128)S(1)} %collective-permute-done.1), channel_id=1, source_target_pairs={{0,4},{4,8},{8,12},{12,16},{16,20},{20,24},{24,28},{28,32},{32,36}... | collective-permute-start | bytes 399368 | tf_op jit(solution)/shard_map/ppermute | solution.py:24
  72.9 4.3 %collective-permute-done.2 = f32[8,65,64]{1,2,0:T(8,128)S(1)} collective-permute-done((f32[8,65,64]{1,2,0:T(8,128)S(1)}, f32[8,65,64]{1,2,0:T(8,128)S(1)}, u32[]{:S(2)}, u32[]{:S(2)}) %collective-permute-start.2) | collective-permute-done | bytes 133152 | tf_op jit(solution)/shard_map/ppermute | solution.py:24
  77.7 3.8 %collective-permute-start.3 = (f32[8,65,64]{1,2,0:T(8,128)S(1)}, f32[8,65,64]{1,2,0:T(8,128)}, u32[]{:S(2)}, u32[]{:S(2)}) collective-permute-start(f32[8,65,64]{1,2,0:T(8,128)S(1)} %pad_maximum_fusion.1), channel_id=1, source_target_pairs={{0,8},{4,12},{8,16},{12,20},{16,24},{20,28},{24,32},{28,36},{32,40... | collective-permute-start | bytes 399368 | tf_op jit(solution)/shard_map/ppermute | solution.py:24
  85.1 2.9 %collective-permute-done.3 = f32[8,65,64]{1,2,0:T(8,128)} collective-permute-done((f32[8,65,64]{1,2,0:T(8,128)S(1)}, f32[8,65,64]{1,2,0:T(8,128)}, u32[]{:S(2)}, u32[]{:S(2)}) %collective-permute-start.3) | collective-permute-done | bytes 133152 | tf_op jit(solution)/shard_map/ppermute | solution.py:24
  90.4 5.1 %collective-permute-start.4 = (f32[8,65,64]{1,2,0:T(8,128)S(1)}, f32[8,65,64]{1,2,0:T(8,128)}, u32[]{:S(2)}, u32[]{:S(2)}) collective-permute-start(f32[8,65,64]{1,2,0:T(8,128)S(1)} %pad_maximum_fusion.2), channel_id=1, source_target_pairs={{0,16},{4,20},{8,24},{12,28},{16,32},{20,36},{24,40},{28,44},{32,4... | collective-permute-start | bytes 399368 | tf_op jit(solution)/shard_map/ppermute | solution.py:24
  99.1 8.4 %collective-permute-done.4 = f32[8,65,64]{1,2,0:T(8,128)} collective-permute-done((f32[8,65,64]{1,2,0:T(8,128)S(1)}, f32[8,65,64]{1,2,0:T(8,128)}, u32[]{:S(2)}, u32[]{:S(2)}) %collective-permute-start.4) | collective-permute-done | bytes 133152 | tf_op jit(solution)/shard_map/ppermute | solution.py:24
  110.0 1.9 %collective-permute-start.5 = (f32[8,65,64]{1,2,0:T(8,128)S(1)}, f32[8,65,64]{1,2,0:T(8,128)}, u32[]{:S(2)}, u32[]{:S(2)}) collective-permute-start(f32[8,65,64]{1,2,0:T(8,128)S(1)} %pad_maximum_fusion.3), channel_id=1, source_target_pairs={{0,32},{4,36},{8,40},{12,44},{16,48},{20,52},{24,56},{28,60},{32,6... | collective-permute-start | bytes 399368 | tf_op jit(solution)/shard_map/ppermute | solution.py:24
  115.5 10.8 %collective-permute-done.5 = f32[8,65,64]{1,2,0:T(8,128)} collective-permute-done((f32[8,65,64]{1,2,0:T(8,128)S(1)}, f32[8,65,64]{1,2,0:T(8,128)}, u32[]{:S(2)}, u32[]{:S(2)}) %collective-permute-start.5) | collective-permute-done | bytes 133152 | tf_op jit(solution)/shard_map/ppermute | solution.py:24
  130.8 6.1 %collective-permute-start.6 = (f32[8,65,64]{1,2,0:T(8,128)S(1)}, f32[8,65,64]{1,2,0:T(8,128)S(1)}, u32[]{:S(2)}, u32[]{:S(2)}) collective-permute-start(f32[8,65,64]{1,2,0:T(8,128)S(1)} %pad_maximum_fusion.4), channel_id=1, source_target_pairs={{0,64},{4,68},{8,72},{12,76},{16,80},{20,84},{24,88},{28,92},{32,9... | collective-permute-start | bytes 399368 | tf_op jit(solution)/shard_map/ppermute | solution.py:24
  136.9 1.7 %fusion.7 = f32[8,16,8,64]{3,1,2,0:T(8,128)S(1)} fusion(f32[2,8,16,16]{3,2,1,0:T(8,128)} %copy.223, f32[2,8,16,16]{3,2,1,0:T(8,128)} %copy.217, f32[2,8,16,16]{3,2,1,0:T(8,128)} %copy.211, f32[2,8,16,16]{3,2,1,0:T(8,128)} %copy.205, f32[8,16,8]{1,2,0:T(8,128)} %bitcast.263, bf16[8,16,8,64]{3,2,1,0:T(8,128)(2,1)} %convert_element_type.115), kind=kOutput, calls=%fused_computation.23 | convolution fusion | flops 12828672 | bytes 462848 | tf_op jit(solution)/shard_map/bhts,bhsv->bhtv/dot_general | solution.py:181
  138.6 4.0 %collective-permute-done.6 = f32[8,65,64]{1,2,0:T(8,128)S(1)} collective-permute-done((f32[8,65,64]{1,2,0:T(8,128)S(1)}, f32[8,65,64]{1,2,0:T(8,128)S(1)}, u32[]{:S(2)}, u32[]{:S(2)}) %collective-permute-start.6) | collective-permute-done | bytes 133152 | tf_op jit(solution)/shard_map/ppermute | solution.py:24
  144.5 3.4 %fusion.6 = f32[8,16,8,64]{3,1,2,0:T(8,128)S(1)} fusion(f32[8,16,8,64]{3,1,2,0:T(8,128)S(1)} %fusion.7, f32[8,8,64,64]{2,3,1,0:T(8,128)S(1)} %copy-done.8, f32[8,8,16,64]{3,2,1,0:T(8,128)S(1)} %get-tuple-element.121, f32[8,16]{1,0:T(8,128)S(1)} %copy-done.33, f32[8,16,8,64]{3,2,1,0:T(8,128)S(1)} %reshape.621), kind=kOutput, calls=%fused_computation.22 | convolution fusion | flops 50528256 | bytes 2097664 | tf_op jit(solution)/shard_map/bhtc,bhcv->bhtv/dot_general | solution.py:183
  147.9 6.0 %collective-permute-done.7 = f32[8,65,64]{1,2,0:T(8,128)S(1)} collective-permute-done((f32[8,65,64]{1,2,0:T(8,128)S(1)}, f32[8,65,64]{1,2,0:T(8,128)S(1)}, u32[]{:S(2)}, u32[]{:S(2)}) %collective-permute-start.7) | collective-permute-done | bytes 133152 | tf_op jit(solution)/shard_map/ppermute | solution.py:24
  157.7 12.2 %all_to_all.5 = bf16[4,128,512]{2,1,0:T(8,128)(2,1)S(1)} all-to-all(bf16[4,128,512]{2,1,0:T(8,128)(2,1)S(1)} %bitcast.234), channel_id=1, replica_groups=mesh['seq_hi'=8,'seq_lo'=8,'tp'=4] {'tp'}, dimensions={0} | all-to-all | bytes 1048576 | tf_op jit(solution)/shard_map/all_to_all | solution.py:198
  (212 shorter events, 52.2 us)
Async XLA Ops:
  0.0 156.1 %copy-start = (bf16[512,2048]{1,0:T(8,128)(2,1)S(1)}, bf16[512,2048]{1,0:T(8,128)(2,1)}, u32[]{:S(2)}) copy-start(bf16[512,2048]{1,0:T(8,128)(2,1)} %param.25) | copy-start | bytes 6291460
  0.0 18.0 %copy-start.45 = (s32[4]{0:T(128)S(1)}, s32[4]{0:T(128)}, u32[]{:S(2)}) copy-start(s32[4]{0:T(128)} %param.14) | copy-start | bytes 52
  16.1 21.4 %collective-permute-start = (bf16[1,2048]{1,0:T(2,128)(2,1)S(1)}, bf16[1,2048]{1,0:T(2,128)(2,1)S(1)}, u32[]{:S(2)}, u32[]{:S(2)}) collective-permute-start(bf16[1,2048]{1,0:T(2,128)(2,1)S(1)} %get-tuple-element.87), channel_id=1, source_target_pairs={{0,4},{4,8},{8,12},{12,16},{16,20},{20,24},{24,28},{28,32},{32,36}... | collective-permute-start | bytes 12296 | tf_op jit(solution)/shard_map/ppermute | solution.py:24
  23.7 14.3 %copy-start.25 = (bf16[64,512]{1,0:T(8,128)(2,1)S(1)}, bf16[64,512]{1,0:T(8,128)(2,1)}, u32[]{:S(2)}) copy-start(bf16[64,512]{1,0:T(8,128)(2,1)} %param.20) | copy-start | bytes 196612
  55.1 14.4 %collective-permute-start.1 = (f32[8,65,64]{1,2,0:T(8,128)}, f32[8,65,64]{1,2,0:T(8,128)S(1)}, u32[]{:S(2)}, u32[]{:S(2)}) collective-permute-start(f32[8,65,64]{1,2,0:T(8,128)} %pad_maximum_fusion), channel_id=1, source_target_pairs={{0,4},{4,8},{8,12},{12,16},{16,20},{20,24},{24,28},{28,32},{32,36}... | collective-permute-start | bytes 399368 | tf_op jit(solution)/shard_map/ppermute | solution.py:24
  68.7 12.8 %copy-start.19 = (f32[2,8,16,64]{3,2,1,0:T(8,128)S(1)}, f32[2,8,16,64]{3,2,1,0:T(8,128)}, u32[]{:S(2)}) copy-start(f32[2,8,16,64]{3,2,1,0:T(8,128)} %get-tuple-element.25) | copy-start | bytes 196612
  68.7 12.8 %copy-start.20 = (f32[2,8,16,64]{3,2,1,0:T(8,128)S(1)}, f32[2,8,16,64]{3,2,1,0:T(8,128)}, u32[]{:S(2)}) copy-start(f32[2,8,16,64]{3,2,1,0:T(8,128)} %get-tuple-element.26) | copy-start | bytes 196612
  68.7 12.8 %copy-start.38 = (pred[2,16,16]{2,1,0:T(8,128)(4,1)S(1)}, pred[2,16,16]{2,1,0:T(8,128)(4,1)}, u32[]{:S(2)}) copy-start(pred[2,16,16]{2,1,0:T(8,128)(4,1)} %get-tuple-element.113) | copy-start | bytes 1540
  69.5 7.7 %collective-permute-start.2 = (f32[8,65,64]{1,2,0:T(8,128)S(1)}, f32[8,65,64]{1,2,0:T(8,128)S(1)}, u32[]{:S(2)}, u32[]{:S(2)}) collective-permute-start(f32[8,65,64]{1,2,0:T(8,128)S(1)} %collective-permute-done.1), channel_id=1, source_target_pairs={{0,4},{4,8},{8,12},{12,16},{16,20},{20,24},{24,28},{28,32},{32,36}... | collective-permute-start | bytes 399368 | tf_op jit(solution)/shard_map/ppermute | solution.py:24
  77.7 10.3 %collective-permute-start.3 = (f32[8,65,64]{1,2,0:T(8,128)S(1)}, f32[8,65,64]{1,2,0:T(8,128)}, u32[]{:S(2)}, u32[]{:S(2)}) collective-permute-start(f32[8,65,64]{1,2,0:T(8,128)S(1)} %pad_maximum_fusion.1), channel_id=1, source_target_pairs={{0,8},{4,12},{8,16},{12,20},{16,24},{20,28},{24,32},{28,36},{32,40... | collective-permute-start | bytes 399368 | tf_op jit(solution)/shard_map/ppermute | solution.py:24
  81.9 13.6 %copy-start.37 = (pred[2,16,16]{2,1,0:T(8,128)(4,1)S(1)}, pred[2,16,16]{2,1,0:T(8,128)(4,1)}, u32[]{:S(2)}) copy-start(pred[2,16,16]{2,1,0:T(8,128)(4,1)} %get-tuple-element.114) | copy-start | bytes 1540
  85.1 10.5 %copy-start.16 = (f32[2,8,16,64]{3,2,1,0:T(8,128)S(1)}, f32[2,8,16,64]{3,2,1,0:T(8,128)}, u32[]{:S(2)}) copy-start(f32[2,8,16,64]{3,2,1,0:T(8,128)} %get-tuple-element.31) | copy-start | bytes 196612
  90.4 17.1 %collective-permute-start.4 = (f32[8,65,64]{1,2,0:T(8,128)S(1)}, f32[8,65,64]{1,2,0:T(8,128)}, u32[]{:S(2)}, u32[]{:S(2)}) collective-permute-start(f32[8,65,64]{1,2,0:T(8,128)S(1)} %pad_maximum_fusion.2), channel_id=1, source_target_pairs={{0,16},{4,20},{8,24},{12,28},{16,32},{20,36},{24,40},{28,44},{32,4... | collective-permute-start | bytes 399368 | tf_op jit(solution)/shard_map/ppermute | solution.py:24
  96.0 15.9 %copy-start.36 = (pred[2,16,16]{2,1,0:T(8,128)(4,1)S(1)}, pred[2,16,16]{2,1,0:T(8,128)(4,1)}, u32[]{:S(2)}) copy-start(pred[2,16,16]{2,1,0:T(8,128)(4,1)} %get-tuple-element.115) | copy-start | bytes 1540
  99.1 12.8 %copy-start.11 = (f32[2,8,16,64]{3,2,1,0:T(8,128)S(1)}, f32[2,8,16,64]{3,2,1,0:T(8,128)}, u32[]{:S(2)}) copy-start(f32[2,8,16,64]{3,2,1,0:T(8,128)} %get-tuple-element.35) | copy-start | bytes 196612
  99.1 12.8 %copy-start.12 = (f32[2,8,16,64]{3,2,1,0:T(8,128)S(1)}, f32[2,8,16,64]{3,2,1,0:T(8,128)}, u32[]{:S(2)}) copy-start(f32[2,8,16,64]{3,2,1,0:T(8,128)} %get-tuple-element.36) | copy-start | bytes 196612
  110.0 16.3 %collective-permute-start.5 = (f32[8,65,64]{1,2,0:T(8,128)S(1)}, f32[8,65,64]{1,2,0:T(8,128)}, u32[]{:S(2)}, u32[]{:S(2)}) collective-permute-start(f32[8,65,64]{1,2,0:T(8,128)S(1)} %pad_maximum_fusion.3), channel_id=1, source_target_pairs={{0,32},{4,36},{8,40},{12,44},{16,48},{20,52},{24,56},{28,60},{32,6... | collective-permute-start | bytes 399368 | tf_op jit(solution)/shard_map/ppermute | solution.py:24
  112.4 16.4 %copy-start.35 = (pred[2,16,16]{2,1,0:T(8,128)(4,1)S(1)}, pred[2,16,16]{2,1,0:T(8,128)(4,1)}, u32[]{:S(2)}) copy-start(pred[2,16,16]{2,1,0:T(8,128)(4,1)} %get-tuple-element.116) | copy-start | bytes 1540
  115.5 13.2 %copy-start.10 = (f32[2,8,16,64]{3,2,1,0:T(8,128)S(1)}, f32[2,8,16,64]{3,2,1,0:T(8,128)}, u32[]{:S(2)}) copy-start(f32[2,8,16,64]{3,2,1,0:T(8,128)} %get-tuple-element.41) | copy-start | bytes 196612
  130.8 13.7 %copy-start.8 = (f32[8,8,64,64]{2,3,1,0:T(8,128)S(1)}, f32[8,8,64,64]{2,3,1,0:T(8,128)}, u32[]{:S(2)}) copy-start(f32[8,8,64,64]{2,3,1,0:T(8,128)} %add_dynamic-update-slice_fusion) | copy-start | bytes 3145732
  130.8 13.7 %copy-start.33 = (f32[8,16]{1,0:T(8,128)S(1)}, f32[8,16]{1,0:T(8,128)}, u32[]{:S(2)}) copy-start(f32[8,16]{1,0:T(8,128)} %get-tuple-element.123) | copy-start | bytes 1540
  130.8 11.8 %collective-permute-start.6 = (f32[8,65,64]{1,2,0:T(8,128)S(1)}, f32[8,65,64]{1,2,0:T(8,128)S(1)}, u32[]{:S(2)}, u32[]{:S(2)}) collective-permute-start(f32[8,65,64]{1,2,0:T(8,128)S(1)} %pad_maximum_fusion.4), channel_id=1, source_target_pairs={{0,64},{4,68},{8,72},{12,76},{16,80},{20,84},{24,88},{28,92},{32,9... | collective-permute-start | bytes 399368 | tf_op jit(solution)/shard_map/ppermute | solution.py:24
  143.2 10.8 %collective-permute-start.7 = (f32[8,65,64]{1,2,0:T(8,128)S(1)}, f32[8,65,64]{1,2,0:T(8,128)S(1)}, u32[]{:S(2)}, u32[]{:S(2)}) collective-permute-start(f32[8,65,64]{1,2,0:T(8,128)S(1)} %pad_maximum_fusion.5), channel_id=1, source_target_pairs={{0,128},{4,132},{8,136},{12,140},{16,144},{20,148},{24,152},{28,15... | collective-permute-start | bytes 399368 | tf_op jit(solution)/shard_map/ppermute | solution.py:24
  157.6 12.3 %copy-start.23 = (bf16[128,512]{1,0:T(8,128)(2,1)S(1)}, bf16[128,512]{1,0:T(8,128)(2,1)}, u32[]{:S(2)}) copy-start(bf16[128,512]{1,0:T(8,128)(2,1)} %param.13) | copy-start | bytes 393220
  (30 other events, 132.1 us)

commit v14 on v8

--- a/solution.py
+++ b/solution.py
@@ -51,7 +51,9 @@
     mixing_values_divided = local_width // CHANNELS_ONE_HEAD
     block = min(32, rows)
     blocks = rows // block
-    full = lax.all_gather(tier_source_concatenated, "tp", axis=1, tiled=True)
+    parts = lax.axis_size("tp")
+    copies = jnp.broadcast_to(tier_source_concatenated[None], (parts,) + tier_source_concatenated.shape)
+    full = lax.all_to_all(copies, "tp", 0, 0, tiled=True).transpose(1, 0, 2).reshape(rows, -1)
     normed = layer_norm(
         full.astype(jnp.float32), tier_standardize_scale, tier_standardize_offset, 1e-05
     ).astype(jnp.bfloat16)

time: 163 us -> 168 us (1.031)
  blocking collectives: 25.8 us -> 17.1 us
  local copies, waits for them, and re-layouts: 15.7 us -> 23.3 us
  other arithmetic: 42.7 us -> 44.9 us
  waiting for transfers between devices: 21.4 us -> 23.5 us
    all_gather x1 -> x0, blocking collectives: 13.5 us -> none  [body(): full = lax.all_gather(tier_source_concatenated, 'tp', axis=1, tiled=True)]
    all_to_all x1, blocking collectives: 12.3 us -> 17.1 us  [body(): pieces = lax.all_to_all(pieces, 'tp', 0, 0, tiled=True)]
    all_to_all x0 -> x1, starting transfers between devices: none -> 4.29 us  [body(): lax.all_to_all(copies, 'tp', 0, 0, tiled=True).transpose(1, 0, 2)]
    ppermute x8, starting transfers between devices: 29.9 us -> 26.5 us  [from_behind(): return lax.ppermute(block, axis, route)]
    sub x0 -> x1, local copies, waits for them, and re-layouts: none -> 2.59 us  [blend(): delta = previous.astype(jnp.float32) - base]
    ppermute x8, waiting for transfers between devices: 21.4 us -> 23.5 us  [from_behind(): return lax.ppermute(block, axis, route)]
    broadcast_in_dim x0 -> x1, local copies, waits for them, and re-layouts: none -> 1.88 us  [body(): jnp.broadcast_to(tier_source_concatenated[None], (parts,) + tier_source_c...]
  transfers between devices with their start and end apart: 8 -> 9, of which waited for: 6 -> 7; matrix products, arithmetic and copies ran while one was open for 30% -> 30% of each run, Pallas kernels for 0% -> 0%
where the time goes in v14:
time: 168 us; the launch traced here: 165 us
  other arithmetic  44.9 us (27%)
  starting transfers between devices  30.8 us (18%)
  waiting for transfers between devices  23.5 us (14%)
  local copies, waits for them, and re-layouts  23.3 us (14%)
  matrix products  21.7 us (13%)
  blocking collectives  17.1 us (10%)
  between operations  3.26 us (2%)
    ppermute x8, starting transfers between devices, from_behind(): return lax.ppermute(block, axis, route)  26.5 us
    ppermute x8, waiting for transfers between devices, from_behind(): return lax.ppermute(block, axis, route)  23.5 us
    all_to_all x1, blocking collectives, body(): pieces = lax.all_to_all(pieces, 'tp', 0, 0, tiled=True)  17.1 us
    unnamed x4, other arithmetic  15.1 us
    dot_general x2, matrix products, project(): jnp.einsum('itd,ide->ite', mixed[:4], mapping_matrices_pile, preferred_el...  10.3 us
    select_n x4, other arithmetic, block_scores(): weight = jnp.where(pair_ok[None, :, :, None], jnp.exp(gap), 0.0)  5.69 us
    dot_general x4, local copies, waits for them, and re-layouts, block_scores(): jnp.einsum('htc,hsc,htsc->hts', recept_b, key_b, weight, precision=highest)  4.79 us
    all_to_all x1, starting transfers between devices, body(): lax.all_to_all(copies, 'tp', 0, 0, tiled=True).transpose(1, 0, 2)  4.29 us
  transfers between devices with their start and end apart: 9, of which 7 were waited for; matrix products, arithmetic and copies ran while one was open for 30% of the time, Pallas kernels for 0%

profile of v14, /device:TPU:48, one launch (start us, length us, event | category | flops | bytes accessed | tf_op | source)
XLA Modules:
  0.0 164.5 jit_solution(10829887360750913850)
XLA Ops:
  1.9 4.3 %all-to-all-start = ((bf16[4,128,512]{2,1,0:T(8,128)(2,1)}), bf16[4,128,512]{2,1,0:T(8,128)(2,1)S(1)}, u32[]{:S(2)}, u32[]{:S(2)}) async-start(bf16[4,128,512]{2,1,0:T(8,128)(2,1)} %broadcast_in_dim.39), calls=%async_computation | async-start | bytes 1048576 | tf_op jit(solution)/shard_map/all_to_all | solution.py:56
  23.9 2.6 %copy.220 = f32[128,2048]{1,0:T(8,128)} copy(f32[128,2048]{0,1:T(8,128)} %convert_subtract_fusion.1) | data formatting | bytes 2097152 | tf_op jit(solution)/shard_map/sub | solution.py:66
  26.5 2.0 %collective-permute-start = (bf16[1,2048]{0,1:T(8,128)(2,1)}, bf16[1,2048]{0,1:T(8,128)(2,1)S(1)}, u32[]{:S(2)}, u32[]{:S(2)}) collective-permute-start(bf16[1,2048]{0,1:T(8,128)(2,1)} %slice.316), channel_id=1, source_target_pairs={{0,4},{4,8},{8,12},{12,16},{16,20},{20,24},{24,28},{28,32},{32,36}... | collective-permute-start | bytes 12296 | tf_op jit(solution)/shard_map/ppermute | solution.py:24
  28.6 2.2 %add_convert_fusion = bf16[5,128,2048]{2,1,0:T(8,128)(2,1)S(1)} fusion(f32[5,2048]{1,0:T(8,128)S(1)} %copy-done.21, f32[128,2048]{1,0:T(8,128)} %copy.220, f32[128,2048]{1,0:T(8,128)} %copy.219), kind=kLoop, calls=%fused_computation | loop fusion | flops 3932160 | bytes 4759552 | tf_op jit(solution)/shard_map/convert_element_type | solution.py:67
  30.8 5.7 %fusion.76 = f32[4,128,512]{2,1,0:T(8,128)} fusion(bf16[4,2048,512]{2,1,0:T(8,128)(2,1)} %param.18, f32[5,2048]{1,0:T(8,128)S(1)} %copy-done.21, f32[128,2048]{1,0:T(8,128)S(1)} %copy-done.6, f32[128,2048]{1,0:T(8,128)S(1)} %copy-done.5), kind=kOutput, calls=%fused_computation.186 | convolution fusion | flops 1077673984 | bytes 11575296 | tf_op jit(solution)/shard_map/itd,ide->ite/dot_general | solution.py:71
  40.8 4.6 %fusion.58 = f32[4,1,512]{2,1,0:T(1,128)S(1)} fusion(bf16[4,2048,512]{2,1,0:T(8,128)(2,1)} %param.18, bf16[4,2048,1]{1,0,2:T(4,128)(2,1)S(1)} %slice_bitcast_fusion.20), kind=kOutput, calls=%fused_computation.140 | convolution fusion | flops 8388608 | bytes 8413184 | tf_op jit(solution)/shard_map/itd,ide->ite/dot_general | solution.py:71
  51.4 1.9 %multiply_bitcast_fusion = (f32[1,8,64]{2,1,0:T(8,128)}, f32[1,8,1,64]{3,1,2,0:T(8,128)S(1)}, f32[1,8,64]{2,1,0:T(8,128)}) fusion(f32[]{:T(128)S(6)} %mul.391, f32[1,8,1,64]{3,1,2,0:T(8,128)} %bitcast.260, f32[1,8,1,64]{3,1,2,0:T(8,128)} %bitcast.259, f32[]{:T(128)} %bitcast.28), kind=kLoop, calls=%fused_computation.168 | loop fusion | flops 1536 | bytes 10248 | tf_op jit(solution)/shard_map/mul | solution.py:138
  54.9 2.0 %fusion.30 = f32[4,8,64,64]{2,3,1,0:T(8,128)S(1)} fusion(f32[4,8,32,64]{3,2,1,0:T(8,128)} %copy-done.3, f32[4,32]{1,0:T(4,128)} %compare_convert_fusion.1, f32[4,8,64]{2,1,0:T(8,128)S(1)} %bitcast.250, bf16[4,32,8,64]{3,2,1,0:T(8,128)(2,1)} %convert_element_type.141, f32[4,32,8,64]{3,2,1,0:T(8,128)S(1)} %reshape.576), kind=kOutput, calls=%fused_computation.60 | convolution fusion | flops 50528256 | bytes 1188352 | tf_op jit(solution)/shard_map/bhsc,bhsv->bhcv/dot_general | solution.py:129
  58.1 3.4 %collective-permute-start.1 = (f32[8,65,64]{1,2,0:T(8,128)S(1)}, f32[8,65,64]{1,2,0:T(8,128)S(1)}, u32[]{:S(2)}, u32[]{:S(2)}) collective-permute-start(f32[8,65,64]{1,2,0:T(8,128)S(1)} %pad_maximum_fusion), channel_id=1, source_target_pairs={{0,4},{4,8},{8,12},{12,16},{16,20},{20,24},{24,28},{28,32},{32,36}... | collective-permute-start | bytes 399368 | tf_op jit(solution)/shard_map/ppermute | solution.py:24
  63.3 2.5 %collective-permute-done.1 = f32[8,65,64]{1,2,0:T(8,128)S(1)} collective-permute-done((f32[8,65,64]{1,2,0:T(8,128)S(1)}, f32[8,65,64]{1,2,0:T(8,128)S(1)}, u32[]{:S(2)}, u32[]{:S(2)}) %collective-permute-start.1) | collective-permute-done | bytes 133152 | tf_op jit(solution)/shard_map/ppermute | solution.py:24
  68.6 4.9 %collective-permute-done.2 = f32[8,65,64]{1,2,0:T(8,128)S(1)} collective-permute-done((f32[8,65,64]{1,2,0:T(8,128)S(1)}, f32[8,65,64]{1,2,0:T(8,128)S(1)}, u32[]{:S(2)}, u32[]{:S(2)}) %collective-permute-start.2) | collective-permute-done | bytes 133152 | tf_op jit(solution)/shard_map/ppermute | solution.py:24
  74.0 4.0 %collective-permute-start.3 = (f32[8,65,64]{1,2,0:T(8,128)S(1)}, f32[8,65,64]{1,2,0:T(8,128)S(1)}, u32[]{:S(2)}, u32[]{:S(2)}) collective-permute-start(f32[8,65,64]{1,2,0:T(8,128)S(1)} %pad_maximum_fusion.1), channel_id=1, source_target_pairs={{0,8},{4,12},{8,16},{12,20},{16,24},{20,28},{24,32},{28,36},{32,40... | collective-permute-start | bytes 399368 | tf_op jit(solution)/shard_map/ppermute | solution.py:24
  78.8 4.1 %fusion.3 = f32[8,32,32]{1,2,0:T(8,128)} fusion(f32[8,32,32,64]{3,2,1,0:T(8,128)S(1)} %exponential_select_fusion.3, f32[8,64,32]{1,2,0:T(8,128)S(1)} %bitcast.248, f32[8,64,32]{1,2,0:T(8,128)S(1)} %bitcast.247), kind=kLoop, calls=%fused_computation.8 | loop fusion | flops 1564672 | bytes 2260992
  84.6 3.2 %collective-permute-done.3 = f32[8,65,64]{1,2,0:T(8,128)S(1)} collective-permute-done((f32[8,65,64]{1,2,0:T(8,128)S(1)}, f32[8,65,64]{1,2,0:T(8,128)S(1)}, u32[]{:S(2)}, u32[]{:S(2)}) %collective-permute-start.3) | collective-permute-done | bytes 133152 | tf_op jit(solution)/shard_map/ppermute | solution.py:24
  88.3 6.8 %collective-permute-start.4 = (f32[8,65,64]{1,2,0:T(8,128)S(1)}, f32[8,65,64]{1,2,0:T(8,128)S(1)}, u32[]{:S(2)}, u32[]{:S(2)}) collective-permute-start(f32[8,65,64]{1,2,0:T(8,128)S(1)} %pad_maximum_fusion.2), channel_id=1, source_target_pairs={{0,16},{4,20},{8,24},{12,28},{16,32},{20,36},{24,40},{28,44},{32,4... | collective-permute-start | bytes 399368 | tf_op jit(solution)/shard_map/ppermute | solution.py:24
  96.9 4.1 %fusion.2 = f32[8,32,32]{1,2,0:T(8,128)} fusion(f32[8,32,32,64]{3,2,1,0:T(8,128)S(1)} %exponential_select_fusion.2, f32[8,64,32]{1,2,0:T(8,128)S(1)} %bitcast.246, f32[8,64,32]{1,2,0:T(8,128)S(1)} %bitcast.245), kind=kLoop, calls=%fused_computation.6 | loop fusion | flops 1564672 | bytes 2260992
  104.4 4.9 %collective-permute-start.5 = (f32[8,65,64]{1,2,0:T(8,128)S(1)}, f32[8,65,64]{1,2,0:T(8,128)S(1)}, u32[]{:S(2)}, u32[]{:S(2)}) collective-permute-start(f32[8,65,64]{1,2,0:T(8,128)S(1)} %pad_maximum_fusion.3), channel_id=1, source_target_pairs={{0,32},{4,36},{8,40},{12,44},{16,48},{20,52},{24,56},{28,60},{32,6... | collective-permute-start | bytes 399368 | tf_op jit(solution)/shard_map/ppermute | solution.py:24
  110.7 3.4 %fusion.1 = f32[8,32,32]{1,2,0:T(8,128)S(1)} fusion(f32[8,32,32,64]{3,2,1,0:T(8,128)S(1)} %exponential_select_fusion.1, f32[8,64,32]{1,2,0:T(8,128)S(1)} %bitcast.244, f32[8,64,32]{1,2,0:T(8,128)S(1)} %bitcast.243), kind=kLoop, calls=%fused_computation.4 | loop fusion | flops 1564672 | bytes 2260992
  114.9 5.5 %collective-permute-done.5 = f32[8,65,64]{1,2,0:T(8,128)S(1)} collective-permute-done((f32[8,65,64]{1,2,0:T(8,128)S(1)}, f32[8,65,64]{1,2,0:T(8,128)S(1)}, u32[]{:S(2)}, u32[]{:S(2)}) %collective-permute-start.5) | collective-permute-done | bytes 133152 | tf_op jit(solution)/shard_map/ppermute | solution.py:24
  120.9 1.9 %collective-permute-start.6 = (f32[8,65,64]{1,2,0:T(8,128)S(1)}, f32[8,65,64]{1,2,0:T(8,128)}, u32[]{:S(2)}, u32[]{:S(2)}) collective-permute-start(f32[8,65,64]{1,2,0:T(8,128)S(1)} %pad_maximum_fusion.4), channel_id=1, source_target_pairs={{0,64},{4,68},{8,72},{12,76},{16,80},{20,84},{24,88},{28,92},{32,9... | collective-permute-start | bytes 399368 | tf_op jit(solution)/shard_map/ppermute | solution.py:24
  124.6 3.4 %fusion = f32[8,32,32]{1,2,0:T(8,128)S(1)} fusion(f32[8,32,32,64]{3,2,1,0:T(8,128)S(1)} %exponential_select_fusion, f32[8,64,32]{1,2,0:T(8,128)S(1)} %bitcast.242, f32[8,64,32]{1,2,0:T(8,128)S(1)} %bitcast.241), kind=kLoop, calls=%fused_computation.2 | loop fusion | flops 1564672 | bytes 2260992
  134.7 2.5 %fusion.4 = f32[4,32,8,64]{3,1,2,0:T(8,128)S(1)} fusion(f32[4,32,8,64]{3,1,2,0:T(8,128)S(1)} %fusion.5, f32[1,8,64,64]{2,3,1,0:T(8,128)S(1)} %copy-done.11, f32[1,8,64,64]{2,3,1,0:T(8,128)S(1)} %copy-done.12, f32[1,8,64,64]{2,3,1,0:T(8,128)S(1)} %copy-done.13, f32[4]{0:T(128)} %pad.7.clone, f32[4,8,32,64]{3,2,1,0:T(8,128)S(1)} %copy-done.2, ...), kind=kOutput, calls=%fused_computation.18 | convolution fusion | flops 50921472 | bytes 1442320 | tf_op jit(solution)/shard_map/bhtc,bhcv->bhtv/dot_general | solution.py:181
  137.2 5.6 %collective-permute-done.7 = f32[8,65,64]{1,2,0:T(8,128)S(1)} collective-permute-done((f32[8,65,64]{1,2,0:T(8,128)S(1)}, f32[8,65,64]{1,2,0:T(8,128)S(1)}, u32[]{:S(2)}, u32[]{:S(2)}) %collective-permute-start.7) | collective-permute-done | bytes 133152 | tf_op jit(solution)/shard_map/ppermute | solution.py:24
  146.6 17.1 %all_to_all.10 = bf16[4,128,512]{2,1,0:T(8,128)(2,1)S(1)} all-to-all(bf16[4,128,512]{2,1,0:T(8,128)(2,1)S(1)} %bitcast.235), channel_id=1, replica_groups=mesh['seq_hi'=8,'seq_lo'=8,'tp'=4] {'tp'}, dimensions={0} | all-to-all | bytes 1048576 | tf_op jit(solution)/shard_map/all_to_all | solution.py:196
  (180 shorter events, 58.5 us)
Async XLA Ops:
  0.0 145.1 %copy-start = (bf16[512,2048]{1,0:T(8,128)(2,1)S(1)}, bf16[512,2048]{1,0:T(8,128)(2,1)}, u32[]{:S(2)}) copy-start(bf16[512,2048]{1,0:T(8,128)(2,1)} %param.25) | copy-start | bytes 6291460
  0.0 22.3 %copy-start.23 = (f32[2048]{0:T(1024)S(1)}, f32[2048]{0:T(1024)}, u32[]{:S(2)}) copy-start(f32[2048]{0:T(1024)} %param.16) | copy-start | bytes 24580
  0.0 22.3 %copy-start.24 = (f32[2048]{0:T(1024)S(1)}, f32[2048]{0:T(1024)}, u32[]{:S(2)}) copy-start(f32[2048]{0:T(1024)} %param.15) | copy-start | bytes 24580
  1.9 16.0 %all-to-all-start = ((bf16[4,128,512]{2,1,0:T(8,128)(2,1)}), bf16[4,128,512]{2,1,0:T(8,128)(2,1)S(1)}, u32[]{:S(2)}, u32[]{:S(2)}) async-start(bf16[4,128,512]{2,1,0:T(8,128)(2,1)} %broadcast_in_dim.39), calls=%async_computation | async-start | bytes 1048576 | tf_op jit(solution)/shard_map/all_to_all | solution.py:56
  18.4 10.1 %copy-start.21 = (f32[5,2048]{1,0:T(8,128)S(1)}, f32[5,2048]{1,0:T(8,128)}, u32[]{:S(2)}) copy-start(f32[5,2048]{1,0:T(8,128)} %param.17) | copy-start | bytes 122884
  26.5 10.8 %collective-permute-start = (bf16[1,2048]{0,1:T(8,128)(2,1)}, bf16[1,2048]{0,1:T(8,128)(2,1)S(1)}, u32[]{:S(2)}, u32[]{:S(2)}) collective-permute-start(bf16[1,2048]{0,1:T(8,128)(2,1)} %slice.316), channel_id=1, source_target_pairs={{0,4},{4,8},{8,12},{12,16},{16,20},{20,24},{24,28},{28,32},{32,36}... | collective-permute-start | bytes 12296 | tf_op jit(solution)/shard_map/ppermute | solution.py:24
  56.9 10.8 %copy-start.26 = (f32[8,64]{1,0:T(8,128)S(1)}, f32[8,64]{1,0:T(8,128)}, u32[]{:S(2)}) copy-start(f32[8,64]{1,0:T(8,128)} %mul.412) | copy-start | bytes 6148
  58.0 20.1 %copy-start.25 = (pred[32,32]{1,0:T(8,128)(4,1)S(1)}, pred[32,32]{1,0:T(8,128)(4,1)}, u32[]{:S(2)}) copy-start(pred[32,32]{1,0:T(8,128)(4,1)} %get-tuple-element.116) | copy-start | bytes 3076
  58.1 7.7 %collective-permute-start.1 = (f32[8,65,64]{1,2,0:T(8,128)S(1)}, f32[8,65,64]{1,2,0:T(8,128)S(1)}, u32[]{:S(2)}, u32[]{:S(2)}) collective-permute-start(f32[8,65,64]{1,2,0:T(8,128)S(1)} %pad_maximum_fusion), channel_id=1, source_target_pairs={{0,4},{4,8},{8,12},{12,16},{16,20},{20,24},{24,28},{28,32},{32,36}... | collective-permute-start | bytes 399368 | tf_op jit(solution)/shard_map/ppermute | solution.py:24
  65.8 7.7 %collective-permute-start.2 = (f32[8,65,64]{1,2,0:T(8,128)S(1)}, f32[8,65,64]{1,2,0:T(8,128)S(1)}, u32[]{:S(2)}, u32[]{:S(2)}) collective-permute-start(f32[8,65,64]{1,2,0:T(8,128)S(1)} %collective-permute-done.1), channel_id=1, source_target_pairs={{0,4},{4,8},{8,12},{12,16},{16,20},{20,24},{24,28},{28,32},{32,36}... | collective-permute-start | bytes 399368 | tf_op jit(solution)/shard_map/ppermute | solution.py:24
  74.0 13.7 %collective-permute-start.3 = (f32[8,65,64]{1,2,0:T(8,128)S(1)}, f32[8,65,64]{1,2,0:T(8,128)S(1)}, u32[]{:S(2)}, u32[]{:S(2)}) collective-permute-start(f32[8,65,64]{1,2,0:T(8,128)S(1)} %pad_maximum_fusion.1), channel_id=1, source_target_pairs={{0,8},{4,12},{8,16},{12,20},{16,24},{20,28},{24,32},{28,36},{32,40... | collective-permute-start | bytes 399368 | tf_op jit(solution)/shard_map/ppermute | solution.py:24
  84.6 12.3 %copy-start.18 = (f32[8,32,64]{2,1,0:T(8,128)S(1)}, f32[8,32,64]{2,1,0:T(8,128)}, u32[]{:S(2)}) copy-start(f32[8,32,64]{2,1,0:T(8,128)} %get-tuple-element.32) | copy-start | bytes 196612
  84.6 12.3 %copy-start.19 = (f32[8,32,64]{2,1,0:T(8,128)S(1)}, f32[8,32,64]{2,1,0:T(8,128)}, u32[]{:S(2)}) copy-start(f32[8,32,64]{2,1,0:T(8,128)} %get-tuple-element.33) | copy-start | bytes 196612
  88.3 15.6 %collective-permute-start.4 = (f32[8,65,64]{1,2,0:T(8,128)S(1)}, f32[8,65,64]{1,2,0:T(8,128)S(1)}, u32[]{:S(2)}, u32[]{:S(2)}) collective-permute-start(f32[8,65,64]{1,2,0:T(8,128)S(1)} %pad_maximum_fusion.2), channel_id=1, source_target_pairs={{0,16},{4,20},{8,24},{12,28},{16,32},{20,36},{24,40},{28,44},{32,4... | collective-permute-start | bytes 399368 | tf_op jit(solution)/shard_map/ppermute | solution.py:24
  104.4 16.0 %collective-permute-start.5 = (f32[8,65,64]{1,2,0:T(8,128)S(1)}, f32[8,65,64]{1,2,0:T(8,128)S(1)}, u32[]{:S(2)}, u32[]{:S(2)}) collective-permute-start(f32[8,65,64]{1,2,0:T(8,128)S(1)} %pad_maximum_fusion.3), channel_id=1, source_target_pairs={{0,32},{4,36},{8,40},{12,44},{16,48},{20,52},{24,56},{28,60},{32,6... | collective-permute-start | bytes 399368 | tf_op jit(solution)/shard_map/ppermute | solution.py:24
  114.9 9.6 %copy-start.14 = (f32[8,32,64]{2,1,0:T(8,128)S(1)}, f32[8,32,64]{2,1,0:T(8,128)}, u32[]{:S(2)}) copy-start(f32[8,32,64]{2,1,0:T(8,128)} %get-tuple-element.42) | copy-start | bytes 196612
  114.9 9.6 %copy-start.15 = (f32[8,32,64]{2,1,0:T(8,128)S(1)}, f32[8,32,64]{2,1,0:T(8,128)}, u32[]{:S(2)}) copy-start(f32[8,32,64]{2,1,0:T(8,128)} %get-tuple-element.43) | copy-start | bytes 196612
  120.9 9.7 %collective-permute-start.6 = (f32[8,65,64]{1,2,0:T(8,128)S(1)}, f32[8,65,64]{1,2,0:T(8,128)}, u32[]{:S(2)}, u32[]{:S(2)}) collective-permute-start(f32[8,65,64]{1,2,0:T(8,128)S(1)} %pad_maximum_fusion.4), channel_id=1, source_target_pairs={{0,64},{4,68},{8,72},{12,76},{16,80},{20,84},{24,88},{28,92},{32,9... | collective-permute-start | bytes 399368 | tf_op jit(solution)/shard_map/ppermute | solution.py:24
  124.6 10.1 %copy-start.2 = (f32[4,8,32,64]{3,2,1,0:T(8,128)S(1)}, f32[4,8,32,64]{3,2,1,0:T(8,128)}, u32[]{:S(2)}) copy-start(f32[4,8,32,64]{3,2,1,0:T(8,128)} %get-tuple-element.99) | copy-start | bytes 786436
  128.8 14.1 %copy-start.30 = (f32[4,32]{1,0:T(4,128)S(1)}, f32[4,32]{1,0:T(4,128)}, u32[]{:S(2)}) copy-start(f32[4,32]{1,0:T(4,128)} %get-tuple-element.101) | copy-start | bytes 1540
  133.1 9.8 %collective-permute-start.7 = (f32[8,65,64]{1,2,0:T(8,128)S(1)}, f32[8,65,64]{1,2,0:T(8,128)S(1)}, u32[]{:S(2)}, u32[]{:S(2)}) collective-permute-start(f32[8,65,64]{1,2,0:T(8,128)S(1)} %pad_maximum_fusion.5), channel_id=1, source_target_pairs={{0,128},{4,132},{8,136},{12,140},{16,144},{20,148},{24,152},{28,15... | collective-permute-start | bytes 399368 | tf_op jit(solution)/shard_map/ppermute | solution.py:24
  134.7 10.5 %copy-start.31 = (f32[512]{0:T(512)S(1)}, f32[512]{0:T(512)}, u32[]{:S(2)}) copy-start(f32[512]{0:T(512)} %param.24) | copy-start | bytes 6148
  134.7 10.5 %copy-start.32 = (f32[512]{0:T(512)S(1)}, f32[512]{0:T(512)}, u32[]{:S(2)}) copy-start(f32[512]{0:T(512)} %param.23) | copy-start | bytes 6148
  144.7 19.2 %copy-start.20 = (bf16[128,512]{1,0:T(8,128)(2,1)S(1)}, bf16[128,512]{1,0:T(8,128)(2,1)}, u32[]{:S(2)}) copy-start(bf16[128,512]{1,0:T(8,128)(2,1)} %param.13) | copy-start | bytes 393220
  (20 other events, 115.8 us)

commit v15 on v8

--- a/solution.py
+++ b/solution.py
@@ -161,13 +161,13 @@
     prefix = from_behind(packed, SEQ, 1)
     distance = 1
     while distance < devices:
-        prefix = combine(from_behind(prefix, SEQ, distance), prefix)
-        distance *= 2
         index = len(scores)
         if index < blocks:
             operands = (incl[index], excl[index], gating_rows_tile[index], query_array_tile[index])
             prefix, operands = lax.optimization_barrier((prefix, operands))
             scores.append(block_scores(index, *operands))
+        prefix = combine(from_behind(prefix, SEQ, distance), prefix)
+        distance *= 2
     for index in range(len(scores), blocks):
         scores.append(
             block_scores(index, incl[index], excl[index], gating_rows_tile[index], query_array_tile[index])

time: 163 us -> 166 us (1.018); the launches traced: 160 us -> 165 us
  waiting for transfers between devices: 21.4 us -> 28 us
    ppermute x8, waiting for transfers between devices: 21.4 us -> 28 us  [from_behind(): return lax.ppermute(block, axis, route)]
  transfers between devices with their start and end apart: 8 -> 8, of which waited for: 6 -> 7; matrix products, arithmetic and copies ran while one was open for 30% -> 28% of each run, Pallas kernels for 0% -> 0%
where the time goes in v15:
time: 166 us; the launch traced here: 165 us
  other arithmetic  41.9 us (25%)
  starting transfers between devices  30.5 us (18%)
  waiting for transfers between devices  28 us (17%)
  blocking collectives  25.6 us (15%)
  matrix products  21 us (13%)
  local copies, waits for them, and re-layouts  14.9 us (9%)
  between operations  3.42 us (2%)
    ppermute x8, starting transfers between devices, from_behind(): return lax.ppermute(block, axis, route)  30.5 us
    ppermute x8, waiting for transfers between devices, from_behind(): return lax.ppermute(block, axis, route)  28 us
    unnamed x4, other arithmetic  14.4 us
    all_gather x1, blocking collectives, body(): full = lax.all_gather(tier_source_concatenated, 'tp', axis=1, tiled=True)  13.5 us
    all_to_all x1, blocking collectives, body(): pieces = lax.all_to_all(pieces, 'tp', 0, 0, tiled=True)  12.1 us
    dot_general x2, matrix products, project(): jnp.einsum('itd,ide->ite', mixed[:4], mapping_matrices_pile, preferred_el...  10.3 us
    select_n x4, other arithmetic, block_scores(): weight = jnp.where(pair_ok[None, :, :, None], jnp.exp(gap), 0.0)  5.69 us
    dot_general x4, local copies, waits for them, and re-layouts, block_scores(): jnp.einsum('htc,hsc,htsc->hts', recept_b, key_b, weight, precision=highest)  3.92 us
  transfers between devices with their start and end apart: 8, of which 7 were waited for; matrix products, arithmetic and copies ran while one was open for 28% of the time, Pallas kernels for 0%

profile of v15, /device:TPU:48, one launch (start us, length us, event | category | flops | bytes accessed | tf_op | source)
XLA Modules:
  0.0 165.3 jit_solution(14000006792405194639)
XLA Ops:
  0.0 13.5 %all_gather.3 = bf16[128,2048]{1,0:T(8,128)(2,1)S(1)} all-gather(bf16[128,512]{1,0:T(8,128)(2,1)} %param.13), channel_id=1, replica_groups=mesh['seq_hi'=8,'seq_lo'=8,'tp'=4] {'tp'}, dimensions={1}, use_global_device_ids=true | all-gather | bytes 655360 | tf_op jit(solution)/shard_map/all_gather | solution.py:54
  13.9 2.1 %fusion.83 = (f32[128,2048]{1,0:T(8,128)}, bf16[128,2048]{1,0:T(8,128)(2,1)S(1)}) fusion(f32[2048]{0:T(1024)} %param.16, f32[2048]{0:T(1024)} %param.15, f32[128]{0:T(128)S(1)} %add_rsqrt_fusion.1, f32[128]{0:T(128)S(1)} %broadcast_multiply_fusion.1, bf16[128,2048]{1,0:T(8,128)(2,1)S(1)} %all_gather.3), kind=kLoop, calls=%fused_computation.190 | loop fusion | flops 1835008 | bytes 2114560 | tf_op jit(solution)/shard_map/convert_element_type | solution.py:63
  16.1 1.9 %collective-permute-start = (bf16[1,2048]{1,0:T(2,128)(2,1)S(1)}, bf16[1,2048]{1,0:T(2,128)(2,1)S(1)}, u32[]{:S(2)}, u32[]{:S(2)}) collective-permute-start(bf16[1,2048]{1,0:T(2,128)(2,1)S(1)} %get-tuple-element.80), channel_id=1, source_target_pairs={{0,4},{4,8},{8,12},{12,16},{16,20},{20,24},{24,28},{28,32},{32,36}... | collective-permute-start | bytes 12296 | tf_op jit(solution)/shard_map/ppermute | solution.py:24
  22.4 1.8 %add_convert_fusion = bf16[5,128,2048]{2,1,0:T(8,128)(2,1)S(1)} fusion(f32[5,2048]{1,0:T(8,128)S(1)} %copy-done.22, f32[128,2048]{1,0:T(8,128)S(1)} %convert_subtract_fusion.1, f32[128,2048]{1,0:T(8,128)} %get-tuple-element.54), kind=kLoop, calls=%fused_computation | loop fusion | flops 3932160 | bytes 4759552 | tf_op jit(solution)/shard_map/convert_element_type | solution.py:65
  24.3 5.7 %fusion.80 = f32[4,128,512]{2,1,0:T(8,128)} fusion(bf16[4,2048,512]{2,1,0:T(8,128)(2,1)} %param.18, f32[5,2048]{1,0:T(8,128)S(1)} %copy-done.22, f32[128,2048]{1,0:T(8,128)S(1)} %convert_subtract_fusion.1, f32[128,2048]{1,0:T(8,128)S(1)} %copy-done.5), kind=kOutput, calls=%fused_computation.187 | convolution fusion | flops 1077673984 | bytes 11575296 | tf_op jit(solution)/shard_map/itd,ide->ite/dot_general | solution.py:69
  39.6 4.6 %fusion.60 = f32[4,1,512]{2,1,0:T(1,128)S(1)} fusion(bf16[4,2048,512]{2,1,0:T(8,128)(2,1)} %param.18, bf16[4,2048,1]{1,0,2:T(4,128)(2,1)S(1)} %slice_bitcast_fusion.20), kind=kOutput, calls=%fused_computation.137 | convolution fusion | flops 8388608 | bytes 8413184 | tf_op jit(solution)/shard_map/itd,ide->ite/dot_general | solution.py:69
  50.0 1.9 %multiply_bitcast_fusion = (f32[1,8,64]{2,1,0:T(8,128)}, f32[1,8,1,64]{3,1,2,0:T(8,128)S(1)}, f32[1,8,64]{2,1,0:T(8,128)}) fusion(f32[]{:T(128)S(6)} %mul.381, f32[1,8,1,64]{3,1,2,0:T(8,128)} %bitcast.250, f32[1,8,1,64]{3,1,2,0:T(8,128)} %bitcast.249, f32[]{:T(128)} %bitcast.28), kind=kLoop, calls=%fused_computation.169 | loop fusion | flops 1536 | bytes 10248 | tf_op jit(solution)/shard_map/mul | solution.py:136
  53.6 2.0 %fusion.31 = f32[4,8,64,64]{2,3,1,0:T(8,128)S(1)} fusion(f32[4,8,32,64]{3,2,1,0:T(8,128)} %copy-done.3, f32[4,32]{1,0:T(4,128)} %compare_convert_fusion.1, f32[4,8,64]{2,1,0:T(8,128)S(1)} %bitcast.238, bf16[4,32,8,64]{3,2,1,0:T(8,128)(2,1)} %convert_element_type.115, f32[4,32,8,64]{3,2,1,0:T(8,128)S(1)} %reshape.504), kind=kOutput, calls=%fused_computation.58 | convolution fusion | flops 50528256 | bytes 1188352 | tf_op jit(solution)/shard_map/bhsc,bhsv->bhcv/dot_general | solution.py:127
  56.8 3.9 %collective-permute-start.1 = (f32[8,65,64]{1,2,0:T(8,128)S(1)}, f32[8,65,64]{1,2,0:T(8,128)S(1)}, u32[]{:S(2)}, u32[]{:S(2)}) collective-permute-start(f32[8,65,64]{1,2,0:T(8,128)S(1)} %pad_maximum_fusion), channel_id=1, source_target_pairs={{0,4},{4,8},{8,12},{12,16},{16,20},{20,24},{24,28},{28,32},{32,36}... | collective-permute-start | bytes 399368 | tf_op jit(solution)/shard_map/ppermute | solution.py:24
  64.5 2.1 %collective-permute-start.2 = (f32[8,65,64]{1,2,0:T(8,128)S(1)}, f32[8,65,64]{1,2,0:T(8,128)S(1)}, u32[]{:S(2)}, u32[]{:S(2)}) collective-permute-start(f32[8,65,64]{1,2,0:T(8,128)S(1)} %collective-permute-done.1), channel_id=1, source_target_pairs={{0,4},{4,8},{8,12},{12,16},{16,20},{20,24},{24,28},{28,32},{32,36}... | collective-permute-start | bytes 399368 | tf_op jit(solution)/shard_map/ppermute | solution.py:24
  67.4 3.4 %fusion.3 = f32[8,32,32]{1,2,0:T(8,128)S(1)} fusion(f32[8,32,32,64]{3,2,1,0:T(8,128)S(1)} %exponential_select_fusion.3, f32[8,64,32]{1,2,0:T(8,128)S(1)} %bitcast.236, f32[8,64,32]{1,2,0:T(8,128)S(1)} %bitcast.235), kind=kLoop, calls=%fused_computation.8 | loop fusion | flops 1564672 | bytes 2260992
  72.7 3.8 %collective-permute-start.3 = (f32[8,65,64]{1,2,0:T(8,128)S(1)}, f32[8,65,64]{1,2,0:T(8,128)S(1)}, u32[]{:S(2)}, u32[]{:S(2)}) collective-permute-start(f32[8,65,64]{1,2,0:T(8,128)S(1)} %pad_maximum_fusion.1), channel_id=1, source_target_pairs={{0,8},{4,12},{8,16},{12,20},{16,24},{20,28},{24,32},{28,36},{32,40... | collective-permute-start | bytes 399368 | tf_op jit(solution)/shard_map/ppermute | solution.py:24
  78.4 4.1 %fusion.2 = f32[8,32,32]{1,2,0:T(8,128)} fusion(f32[8,32,32,64]{3,2,1,0:T(8,128)S(1)} %exponential_select_fusion.2, f32[8,64,32]{1,2,0:T(8,128)S(1)} %bitcast.234, f32[8,64,32]{1,2,0:T(8,128)S(1)} %bitcast.233), kind=kLoop, calls=%fused_computation.6 | loop fusion | flops 1564672 | bytes 2260992
  84.8 8.9 %collective-permute-start.4 = (f32[8,65,64]{1,2,0:T(8,128)S(1)}, f32[8,65,64]{1,2,0:T(8,128)S(1)}, u32[]{:S(2)}, u32[]{:S(2)}) collective-permute-start(f32[8,65,64]{1,2,0:T(8,128)S(1)} %pad_maximum_fusion.2), channel_id=1, source_target_pairs={{0,16},{4,20},{8,24},{12,28},{16,32},{20,36},{24,40},{28,44},{32,4... | collective-permute-start | bytes 399368 | tf_op jit(solution)/shard_map/ppermute | solution.py:24
  95.2 3.4 %fusion.1 = f32[8,32,32]{1,2,0:T(8,128)S(1)} fusion(f32[8,32,32,64]{3,2,1,0:T(8,128)S(1)} %exponential_select_fusion.1, f32[8,64,32]{1,2,0:T(8,128)S(1)} %bitcast.232, f32[8,64,32]{1,2,0:T(8,128)S(1)} %bitcast.231), kind=kLoop, calls=%fused_computation.4 | loop fusion | flops 1564672 | bytes 2260992
  99.4 5.1 %collective-permute-done.4 = f32[8,65,64]{1,2,0:T(8,128)S(1)} collective-permute-done((f32[8,65,64]{1,2,0:T(8,128)S(1)}, f32[8,65,64]{1,2,0:T(8,128)S(1)}, u32[]{:S(2)}, u32[]{:S(2)}) %collective-permute-start.4) | collective-permute-done | bytes 133152 | tf_op jit(solution)/shard_map/ppermute | solution.py:24
  105.0 5.2 %collective-permute-start.5 = (f32[8,65,64]{1,2,0:T(8,128)S(1)}, f32[8,65,64]{1,2,0:T(8,128)}, u32[]{:S(2)}, u32[]{:S(2)}) collective-permute-start(f32[8,65,64]{1,2,0:T(8,128)S(1)} %pad_maximum_fusion.3), channel_id=1, source_target_pairs={{0,32},{4,36},{8,40},{12,44},{16,48},{20,52},{24,56},{28,60},{32,6... | collective-permute-start | bytes 399368 | tf_op jit(solution)/shard_map/ppermute | solution.py:24
  112.0 3.4 %fusion = f32[8,32,32]{1,2,0:T(8,128)S(1)} fusion(f32[8,32,32,64]{3,2,1,0:T(8,128)S(1)} %exponential_select_fusion, f32[8,64,32]{1,2,0:T(8,128)S(1)} %bitcast.230, f32[8,64,32]{1,2,0:T(8,128)S(1)} %bitcast.229), kind=kLoop, calls=%fused_computation.2 | loop fusion | flops 1564672 | bytes 2260992
  116.3 8.5 %collective-permute-done.5 = f32[8,65,64]{1,2,0:T(8,128)} collective-permute-done((f32[8,65,64]{1,2,0:T(8,128)S(1)}, f32[8,65,64]{1,2,0:T(8,128)}, u32[]{:S(2)}, u32[]{:S(2)}) %collective-permute-start.5) | collective-permute-done | bytes 133152 | tf_op jit(solution)/shard_map/ppermute | solution.py:24
  127.2 3.0 %collective-permute-start.6 = (f32[8,65,64]{1,2,0:T(8,128)S(1)}, f32[8,65,64]{1,2,0:T(8,128)S(1)}, u32[]{:S(2)}, u32[]{:S(2)}) collective-permute-start(f32[8,65,64]{1,2,0:T(8,128)S(1)} %pad_maximum_fusion.4), channel_id=1, source_target_pairs={{0,64},{4,68},{8,72},{12,76},{16,80},{20,84},{24,88},{28,92},{32,9... | collective-permute-start | bytes 399368 | tf_op jit(solution)/shard_map/ppermute | solution.py:24
  132.0 5.3 %collective-permute-done.6 = f32[8,65,64]{1,2,0:T(8,128)S(1)} collective-permute-done((f32[8,65,64]{1,2,0:T(8,128)S(1)}, f32[8,65,64]{1,2,0:T(8,128)S(1)}, u32[]{:S(2)}, u32[]{:S(2)}) %collective-permute-start.6) | collective-permute-done | bytes 133152 | tf_op jit(solution)/shard_map/ppermute | solution.py:24
  139.4 1.9 %fusion.6 = f32[4,32,8,64]{3,1,2,0:T(8,128)S(1)} fusion(f32[4,32,8,64]{3,1,2,0:T(8,128)S(1)} %fusion.7, f32[1,8,64,64]{2,3,1,0:T(8,128)S(1)} %copy-done.10, f32[1,8,64,64]{2,3,1,0:T(8,128)S(1)} %copy-done.11, f32[1,8,64,64]{2,3,1,0:T(8,128)S(1)} %copy-done.12, f32[4]{0:T(128)S(1)} %copy-done.35, f32[4,8,32,64]{3,2,1,0:T(8,128)S(1)} %copy-done.2, ...), kind=kOutput, calls=%fused_computation.20 | convolution fusion | flops 50921472 | bytes 1442320 | tf_op jit(solution)/shard_map/bhtc,bhcv->bhtv/dot_general | solution.py:179
  141.3 7.3 %collective-permute-done.7 = f32[8,65,64]{1,2,0:T(8,128)S(1)} collective-permute-done((f32[8,65,64]{1,2,0:T(8,128)S(1)}, f32[8,65,64]{1,2,0:T(8,128)S(1)}, u32[]{:S(2)}, u32[]{:S(2)}) %collective-permute-start.7) | collective-permute-done | bytes 133152 | tf_op jit(solution)/shard_map/ppermute | solution.py:24
  152.4 12.1 %all_to_all.5 = bf16[4,128,512]{2,1,0:T(8,128)(2,1)S(1)} all-to-all(bf16[4,128,512]{2,1,0:T(8,128)(2,1)S(1)} %bitcast.223), channel_id=1, replica_groups=mesh['seq_hi'=8,'seq_lo'=8,'tp'=4] {'tp'}, dimensions={0} | all-to-all | bytes 1048576 | tf_op jit(solution)/shard_map/all_to_all | solution.py:194
  (179 shorter events, 46.6 us)
Async XLA Ops:
  0.0 150.8 %copy-start = (bf16[512,2048]{1,0:T(8,128)(2,1)S(1)}, bf16[512,2048]{1,0:T(8,128)(2,1)}, u32[]{:S(2)}) copy-start(bf16[512,2048]{1,0:T(8,128)(2,1)} %param.25) | copy-start | bytes 6291460
  0.0 22.4 %copy-start.22 = (f32[5,2048]{1,0:T(8,128)S(1)}, f32[5,2048]{1,0:T(8,128)}, u32[]{:S(2)}) copy-start(f32[5,2048]{1,0:T(8,128)} %param.17) | copy-start | bytes 122884
  16.1 20.6 %collective-permute-start = (bf16[1,2048]{1,0:T(2,128)(2,1)S(1)}, bf16[1,2048]{1,0:T(2,128)(2,1)S(1)}, u32[]{:S(2)}, u32[]{:S(2)}) collective-permute-start(bf16[1,2048]{1,0:T(2,128)(2,1)S(1)} %get-tuple-element.80), channel_id=1, source_target_pairs={{0,4},{4,8},{8,12},{12,16},{16,20},{20,24},{24,28},{28,32},{32,36}... | collective-permute-start | bytes 12296 | tf_op jit(solution)/shard_map/ppermute | solution.py:24
  24.3 12.8 %copy-start.23 = (bf16[64,512]{1,0:T(8,128)(2,1)S(1)}, bf16[64,512]{1,0:T(8,128)(2,1)}, u32[]{:S(2)}) copy-start(bf16[64,512]{1,0:T(8,128)(2,1)} %param.20) | copy-start | bytes 196612
  56.8 7.7 %collective-permute-start.1 = (f32[8,65,64]{1,2,0:T(8,128)S(1)}, f32[8,65,64]{1,2,0:T(8,128)S(1)}, u32[]{:S(2)}, u32[]{:S(2)}) collective-permute-start(f32[8,65,64]{1,2,0:T(8,128)S(1)} %pad_maximum_fusion), channel_id=1, source_target_pairs={{0,4},{4,8},{8,12},{12,16},{16,20},{20,24},{24,28},{28,32},{32,36}... | collective-permute-start | bytes 399368 | tf_op jit(solution)/shard_map/ppermute | solution.py:24
  64.5 7.7 %collective-permute-start.2 = (f32[8,65,64]{1,2,0:T(8,128)S(1)}, f32[8,65,64]{1,2,0:T(8,128)S(1)}, u32[]{:S(2)}, u32[]{:S(2)}) collective-permute-start(f32[8,65,64]{1,2,0:T(8,128)S(1)} %collective-permute-done.1), channel_id=1, source_target_pairs={{0,4},{4,8},{8,12},{12,16},{16,20},{20,24},{24,28},{28,32},{32,36}... | collective-permute-start | bytes 399368 | tf_op jit(solution)/shard_map/ppermute | solution.py:24
  72.7 11.5 %collective-permute-start.3 = (f32[8,65,64]{1,2,0:T(8,128)S(1)}, f32[8,65,64]{1,2,0:T(8,128)S(1)}, u32[]{:S(2)}, u32[]{:S(2)}) collective-permute-start(f32[8,65,64]{1,2,0:T(8,128)S(1)} %pad_maximum_fusion.1), channel_id=1, source_target_pairs={{0,8},{4,12},{8,16},{12,20},{16,24},{20,28},{24,32},{28,36},{32,40... | collective-permute-start | bytes 399368 | tf_op jit(solution)/shard_map/ppermute | solution.py:24
  78.3 15.4 %copy-start.15 = (f32[8,32,64]{2,1,0:T(8,128)S(1)}, f32[8,32,64]{2,1,0:T(8,128)}, u32[]{:S(2)}) copy-start(f32[8,32,64]{2,1,0:T(8,128)} %get-tuple-element.35) | copy-start | bytes 196612
  78.3 15.4 %copy-start.16 = (f32[8,32,64]{2,1,0:T(8,128)S(1)}, f32[8,32,64]{2,1,0:T(8,128)}, u32[]{:S(2)}) copy-start(f32[8,32,64]{2,1,0:T(8,128)} %get-tuple-element.36) | copy-start | bytes 196612
  84.8 19.8 %collective-permute-start.4 = (f32[8,65,64]{1,2,0:T(8,128)S(1)}, f32[8,65,64]{1,2,0:T(8,128)S(1)}, u32[]{:S(2)}, u32[]{:S(2)}) collective-permute-start(f32[8,65,64]{1,2,0:T(8,128)S(1)} %pad_maximum_fusion.2), channel_id=1, source_target_pairs={{0,16},{4,20},{8,24},{12,28},{16,32},{20,36},{24,40},{28,44},{32,4... | collective-permute-start | bytes 399368 | tf_op jit(solution)/shard_map/ppermute | solution.py:24
  99.4 12.6 %copy-start.13 = (f32[8,32,64]{2,1,0:T(8,128)S(1)}, f32[8,32,64]{2,1,0:T(8,128)}, u32[]{:S(2)}) copy-start(f32[8,32,64]{2,1,0:T(8,128)} %get-tuple-element.42) | copy-start | bytes 196612
  99.4 12.6 %copy-start.14 = (f32[8,32,64]{2,1,0:T(8,128)S(1)}, f32[8,32,64]{2,1,0:T(8,128)}, u32[]{:S(2)}) copy-start(f32[8,32,64]{2,1,0:T(8,128)} %get-tuple-element.43) | copy-start | bytes 196612
  105.0 19.7 %collective-permute-start.5 = (f32[8,65,64]{1,2,0:T(8,128)S(1)}, f32[8,65,64]{1,2,0:T(8,128)}, u32[]{:S(2)}, u32[]{:S(2)}) collective-permute-start(f32[8,65,64]{1,2,0:T(8,128)S(1)} %pad_maximum_fusion.3), channel_id=1, source_target_pairs={{0,32},{4,36},{8,40},{12,44},{16,48},{20,52},{24,56},{28,60},{32,6... | collective-permute-start | bytes 399368 | tf_op jit(solution)/shard_map/ppermute | solution.py:24
  115.5 23.9 %copy-start.2 = (f32[4,8,32,64]{3,2,1,0:T(8,128)S(1)}, f32[4,8,32,64]{3,2,1,0:T(8,128)}, u32[]{:S(2)}) copy-start(f32[4,8,32,64]{3,2,1,0:T(8,128)} %get-tuple-element.101) | copy-start | bytes 786436
  116.2 23.1 %copy-start.10 = (f32[1,8,64,64]{2,3,1,0:T(8,128)S(1)}, f32[1,8,64,64]{2,3,1,0:T(8,128)}, u32[]{:S(2)}) copy-start(f32[1,8,64,64]{2,3,1,0:T(8,128)} %get-tuple-element.51) | copy-start | bytes 393220
  116.2 23.1 %copy-start.11 = (f32[1,8,64,64]{2,3,1,0:T(8,128)S(1)}, f32[1,8,64,64]{2,3,1,0:T(8,128)}, u32[]{:S(2)}) copy-start(f32[1,8,64,64]{2,3,1,0:T(8,128)} %get-tuple-element.52) | copy-start | bytes 393220
  116.2 23.2 %copy-start.12 = (f32[1,8,64,64]{2,3,1,0:T(8,128)S(1)}, f32[1,8,64,64]{2,3,1,0:T(8,128)}, u32[]{:S(2)}) copy-start(f32[1,8,64,64]{2,3,1,0:T(8,128)} %get-tuple-element.53) | copy-start | bytes 393220
  116.2 23.2 %copy-start.29 = (f32[4,32]{1,0:T(4,128)S(1)}, f32[4,32]{1,0:T(4,128)}, u32[]{:S(2)}) copy-start(f32[4,32]{1,0:T(4,128)} %get-tuple-element.103) | copy-start | bytes 1540
  116.2 23.2 %copy-start.35 = (f32[4]{0:T(128)S(1)}, f32[4]{0:T(128)}, u32[]{:S(2)}) copy-start(f32[4]{0:T(128)} %pad.9.clone) | copy-start | bytes 52
  127.2 10.1 %collective-permute-start.6 = (f32[8,65,64]{1,2,0:T(8,128)S(1)}, f32[8,65,64]{1,2,0:T(8,128)S(1)}, u32[]{:S(2)}, u32[]{:S(2)}) collective-permute-start(f32[8,65,64]{1,2,0:T(8,128)S(1)} %pad_maximum_fusion.4), channel_id=1, source_target_pairs={{0,64},{4,68},{8,72},{12,76},{16,80},{20,84},{24,88},{28,92},{32,9... | collective-permute-start | bytes 399368 | tf_op jit(solution)/shard_map/ppermute | solution.py:24
  137.8 10.8 %collective-permute-start.7 = (f32[8,65,64]{1,2,0:T(8,128)S(1)}, f32[8,65,64]{1,2,0:T(8,128)S(1)}, u32[]{:S(2)}, u32[]{:S(2)}) collective-permute-start(f32[8,65,64]{1,2,0:T(8,128)S(1)} %pad_maximum_fusion.5), channel_id=1, source_target_pairs={{0,128},{4,132},{8,136},{12,140},{16,144},{20,148},{24,152},{28,15... | collective-permute-start | bytes 399368 | tf_op jit(solution)/shard_map/ppermute | solution.py:24
  139.4 11.4 %copy-start.30 = (f32[512]{0:T(512)S(1)}, f32[512]{0:T(512)}, u32[]{:S(2)}) copy-start(f32[512]{0:T(512)} %param.24) | copy-start | bytes 6148
  139.4 11.4 %copy-start.31 = (f32[512]{0:T(512)S(1)}, f32[512]{0:T(512)}, u32[]{:S(2)}) copy-start(f32[512]{0:T(512)} %param.23) | copy-start | bytes 6148
  150.4 14.2 %copy-start.21 = (bf16[128,512]{1,0:T(8,128)(2,1)S(1)}, bf16[128,512]{1,0:T(8,128)(2,1)}, u32[]{:S(2)}) copy-start(bf16[128,512]{1,0:T(8,128)(2,1)} %param.13) | copy-start | bytes 393220
  (21 other events, 148.7 us)

commit v16 on v8

--- a/solution.py
+++ b/solution.py
@@ -164,7 +164,7 @@
         prefix = combine(from_behind(prefix, SEQ, distance), prefix)
         distance *= 2
         index = len(scores)
-        if index < blocks:
+        if index < blocks and distance > 2:
             operands = (incl[index], excl[index], gating_rows_tile[index], query_array_tile[index])
             prefix, operands = lax.optimization_barrier((prefix, operands))
             scores.append(block_scores(index, *operands))

time: 163 us -> 171 us (1.049)
  the two profiles are of different devices: /device:TPU:48 before, /device:TPU:96 now
where the time goes in v16:
time: 171 us; the launch traced here: 170 us
  other arithmetic  42.7 us (25%)
  starting transfers between devices  42.1 us (25%)
  blocking collectives  25.6 us (15%)
  matrix products  23 us (13%)
  local copies, waits for them, and re-layouts  17.2 us (10%)
  waiting for transfers between devices  16.4 us (10%)
  between operations  3.27 us (2%)
    ppermute x8, starting transfers between devices, from_behind(): return lax.ppermute(block, axis, route)  42.1 us
    ppermute x8, waiting for transfers between devices, from_behind(): return lax.ppermute(block, axis, route)  16.4 us
    unnamed x4, other arithmetic  16.4 us
    all_gather x1, blocking collectives, body(): full = lax.all_gather(tier_source_concatenated, 'tp', axis=1, tiled=True)  13.5 us
    all_to_all x1, blocking collectives, body(): pieces = lax.all_to_all(pieces, 'tp', 0, 0, tiled=True)  12.2 us
    dot_general x2, matrix products, project(): jnp.einsum('itd,ide->ite', mixed[:4], mapping_matrices_pile, preferred_el...  10.3 us
    dot_general x4, local copies, waits for them, and re-layouts, block_scores(): jnp.einsum('htc,hsc,htsc->hts', recept_b, key_b, weight, precision=highest)  5.96 us
    select_n x4, other arithmetic, block_scores(): weight = jnp.where(pair_ok[None, :, :, None], jnp.exp(gap), 0.0)  5.75 us
  transfers between devices with their start and end apart: 8, of which 4 were waited for; matrix products, arithmetic and copies ran while one was open for 31% of the time, Pallas kernels for 0%

profile of v16, /device:TPU:96, one launch (start us, length us, event | category | flops | bytes accessed | tf_op | source)
XLA Modules:
  0.0 170.3 jit_solution(2583807705151156315)
XLA Ops:
  0.0 13.5 %all_gather.3 = bf16[128,2048]{1,0:T(8,128)(2,1)S(1)} all-gather(bf16[128,512]{1,0:T(8,128)(2,1)} %param.13), channel_id=1, replica_groups=mesh['seq_hi'=8,'seq_lo'=8,'tp'=4] {'tp'}, dimensions={1}, use_global_device_ids=true | all-gather | bytes 655360 | tf_op jit(solution)/shard_map/all_gather | solution.py:54
  13.9 2.1 %fusion.82 = (f32[128,2048]{1,0:T(8,128)}, bf16[128,2048]{1,0:T(8,128)(2,1)S(1)}) fusion(f32[2048]{0:T(1024)} %param.16, f32[2048]{0:T(1024)} %param.15, f32[128]{0:T(128)S(1)} %add_rsqrt_fusion.1, f32[128]{0:T(128)S(1)} %broadcast_multiply_fusion.1, bf16[128,2048]{1,0:T(8,128)(2,1)S(1)} %all_gather.3), kind=kLoop, calls=%fused_computation.191 | loop fusion | flops 1835008 | bytes 2114560 | tf_op jit(solution)/shard_map/convert_element_type | solution.py:63
  16.1 1.9 %collective-permute-start = (bf16[1,2048]{1,0:T(2,128)(2,1)S(1)}, bf16[1,2048]{1,0:T(2,128)(2,1)S(1)}, u32[]{:S(2)}, u32[]{:S(2)}) collective-permute-start(bf16[1,2048]{1,0:T(2,128)(2,1)S(1)} %get-tuple-element.78), channel_id=1, source_target_pairs={{0,4},{4,8},{8,12},{12,16},{16,20},{20,24},{24,28},{28,32},{32,36}... | collective-permute-start | bytes 12296 | tf_op jit(solution)/shard_map/ppermute | solution.py:24
  22.4 1.8 %add_convert_fusion = bf16[5,128,2048]{2,1,0:T(8,128)(2,1)S(1)} fusion(f32[5,2048]{1,0:T(8,128)S(1)} %copy-done.16, f32[128,2048]{1,0:T(8,128)S(1)} %convert_subtract_fusion.1, f32[128,2048]{1,0:T(8,128)} %get-tuple-element.52), kind=kLoop, calls=%fused_computation | loop fusion | flops 3932160 | bytes 4759552 | tf_op jit(solution)/shard_map/convert_element_type | solution.py:65
  24.3 5.7 %fusion.80 = f32[4,128,512]{2,1,0:T(8,128)} fusion(bf16[4,2048,512]{2,1,0:T(8,128)(2,1)} %param.18, f32[5,2048]{1,0:T(8,128)S(1)} %copy-done.16, f32[128,2048]{1,0:T(8,128)S(1)} %convert_subtract_fusion.1, f32[128,2048]{1,0:T(8,128)S(1)} %copy-done.5), kind=kOutput, calls=%fused_computation.189 | convolution fusion | flops 1077673984 | bytes 11575296 | tf_op jit(solution)/shard_map/itd,ide->ite/dot_general | solution.py:69
  39.6 4.6 %fusion.60 = f32[4,1,512]{2,1,0:T(1,128)S(1)} fusion(bf16[4,2048,512]{2,1,0:T(8,128)(2,1)} %param.18, bf16[4,2048,1]{1,0,2:T(4,128)(2,1)S(1)} %slice_bitcast_fusion.20), kind=kOutput, calls=%fused_computation.139 | convolution fusion | flops 8388608 | bytes 8413184 | tf_op jit(solution)/shard_map/itd,ide->ite/dot_general | solution.py:69
  50.2 1.9 %multiply_bitcast_fusion = (f32[1,8,64]{2,1,0:T(8,128)}, f32[1,8,1,64]{3,1,2,0:T(8,128)S(1)}, f32[1,8,64]{2,1,0:T(8,128)}) fusion(f32[]{:T(128)S(6)} %mul.381, f32[1,8,1,64]{3,1,2,0:T(8,128)} %bitcast.250, f32[1,8,1,64]{3,1,2,0:T(8,128)} %bitcast.249, f32[]{:T(128)} %bitcast.28), kind=kLoop, calls=%fused_computation.171 | loop fusion | flops 1536 | bytes 10248 | tf_op jit(solution)/shard_map/mul | solution.py:136
  53.6 2.0 %fusion.31 = f32[4,8,64,64]{2,3,1,0:T(8,128)S(1)} fusion(f32[4,8,32,64]{3,2,1,0:T(8,128)} %copy-done.3, f32[4,32]{1,0:T(4,128)} %compare_convert_fusion.1, f32[4,8,64]{2,1,0:T(8,128)S(1)} %bitcast.238, bf16[4,32,8,64]{3,2,1,0:T(8,128)(2,1)} %convert_element_type.115, f32[4,32,8,64]{3,2,1,0:T(8,128)S(1)} %reshape.504), kind=kOutput, calls=%fused_computation.58 | convolution fusion | flops 50528256 | bytes 1188352 | tf_op jit(solution)/shard_map/bhsc,bhsv->bhcv/dot_general | solution.py:127
  56.0 5.1 %collective-permute-start.1 = (f32[8,65,64]{1,2,0:T(8,128)S(1)}, f32[8,65,64]{1,2,0:T(8,128)S(1)}, u32[]{:S(2)}, u32[]{:S(2)}) collective-permute-start(f32[8,65,64]{1,2,0:T(8,128)S(1)} %pad_maximum_fusion), channel_id=1, source_target_pairs={{0,4},{4,8},{8,12},{12,16},{16,20},{20,24},{24,28},{28,32},{32,36}... | collective-permute-start | bytes 399368 | tf_op jit(solution)/shard_map/ppermute | solution.py:24
  64.5 1.9 %collective-permute-start.2 = (f32[8,65,64]{1,2,0:T(8,128)S(1)}, f32[8,65,64]{1,2,0:T(8,128)S(1)}, u32[]{:S(2)}, u32[]{:S(2)}) collective-permute-start(f32[8,65,64]{1,2,0:T(8,128)S(1)} %collective-permute-done.1), channel_id=1, source_target_pairs={{0,4},{4,8},{8,12},{12,16},{16,20},{20,24},{24,28},{28,32},{32,36}... | collective-permute-start | bytes 399368 | tf_op jit(solution)/shard_map/ppermute | solution.py:24
  66.5 5.6 %collective-permute-done.2 = f32[8,65,64]{1,2,0:T(8,128)S(1)} collective-permute-done((f32[8,65,64]{1,2,0:T(8,128)S(1)}, f32[8,65,64]{1,2,0:T(8,128)S(1)}, u32[]{:S(2)}, u32[]{:S(2)}) %collective-permute-start.2) | collective-permute-done | bytes 133152 | tf_op jit(solution)/shard_map/ppermute | solution.py:24
  72.8 6.6 %collective-permute-start.3 = (f32[8,65,64]{1,2,0:T(8,128)S(1)}, f32[8,65,64]{1,2,0:T(8,128)S(1)}, u32[]{:S(2)}, u32[]{:S(2)}) collective-permute-start(f32[8,65,64]{1,2,0:T(8,128)S(1)} %pad_maximum_fusion.1), channel_id=1, source_target_pairs={{0,8},{4,12},{8,16},{12,20},{16,24},{20,28},{24,32},{28,36},{32,40... | collective-permute-start | bytes 399368 | tf_op jit(solution)/shard_map/ppermute | solution.py:24
  80.2 3.4 %collective-permute-done.3 = f32[8,65,64]{1,2,0:T(8,128)S(1)} collective-permute-done((f32[8,65,64]{1,2,0:T(8,128)S(1)}, f32[8,65,64]{1,2,0:T(8,128)S(1)}, u32[]{:S(2)}, u32[]{:S(2)}) %collective-permute-start.3) | collective-permute-done | bytes 133152 | tf_op jit(solution)/shard_map/ppermute | solution.py:24
  84.0 3.6 %collective-permute-start.4 = (f32[8,65,64]{1,2,0:T(8,128)S(1)}, f32[8,65,64]{1,2,0:T(8,128)S(1)}, u32[]{:S(2)}, u32[]{:S(2)}) collective-permute-start(f32[8,65,64]{1,2,0:T(8,128)S(1)} %pad_maximum_fusion.2), channel_id=1, source_target_pairs={{0,16},{4,20},{8,24},{12,28},{16,32},{20,36},{24,40},{28,44},{32,4... | collective-permute-start | bytes 399368 | tf_op jit(solution)/shard_map/ppermute | solution.py:24
  88.4 4.1 %fusion.3 = f32[8,32,32]{1,2,0:T(8,128)} fusion(f32[8,32,32,64]{3,2,1,0:T(8,128)S(1)} %exponential_select_fusion.3, f32[8,64,32]{1,2,0:T(8,128)S(1)} %bitcast.236, f32[8,64,32]{1,2,0:T(8,128)S(1)} %bitcast.235), kind=kLoop, calls=%fused_computation.8 | loop fusion | flops 1564672 | bytes 2260992
  94.1 6.0 %collective-permute-done.4 = f32[8,65,64]{1,2,0:T(8,128)S(1)} collective-permute-done((f32[8,65,64]{1,2,0:T(8,128)S(1)}, f32[8,65,64]{1,2,0:T(8,128)S(1)}, u32[]{:S(2)}, u32[]{:S(2)}) %collective-permute-start.4) | collective-permute-done | bytes 133152 | tf_op jit(solution)/shard_map/ppermute | solution.py:24
  103.8 4.1 %fusion.2 = f32[8,32,32]{1,2,0:T(8,128)} fusion(f32[8,32,32,64]{3,2,1,0:T(8,128)S(1)} %exponential_select_fusion.2, f32[8,64,32]{1,2,0:T(8,128)S(1)} %bitcast.234, f32[8,64,32]{1,2,0:T(8,128)S(1)} %bitcast.233), kind=kLoop, calls=%fused_computation.6 | loop fusion | flops 1564672 | bytes 2260992
  111.3 13.9 %collective-permute-start.6 = (f32[8,65,64]{1,2,0:T(8,128)S(1)}, f32[8,65,64]{1,2,0:T(8,128)S(1)}, u32[]{:S(2)}, u32[]{:S(2)}) collective-permute-start(f32[8,65,64]{1,2,0:T(8,128)S(1)} %pad_maximum_fusion.4), channel_id=1, source_target_pairs={{0,64},{4,68},{8,72},{12,76},{16,80},{20,84},{24,88},{28,92},{32,9... | collective-permute-start | bytes 399368 | tf_op jit(solution)/shard_map/ppermute | solution.py:24
  127.0 4.1 %fusion.1 = f32[8,32,32]{1,2,0:T(8,128)} fusion(f32[8,32,32,64]{3,2,1,0:T(8,128)S(1)} %exponential_select_fusion.1, f32[8,64,32]{1,2,0:T(8,128)S(1)} %bitcast.232, f32[8,64,32]{1,2,0:T(8,128)S(1)} %bitcast.231), kind=kLoop, calls=%fused_computation.4 | loop fusion | flops 1564672 | bytes 2260992
  133.3 7.8 %collective-permute-start.7 = (f32[8,65,64]{1,2,0:T(8,128)S(1)}, f32[8,65,64]{1,2,0:T(8,128)}, u32[]{:S(2)}, u32[]{:S(2)}) collective-permute-start(f32[8,65,64]{1,2,0:T(8,128)S(1)} %pad_maximum_fusion.5), channel_id=1, source_target_pairs={{0,128},{4,132},{8,136},{12,140},{16,144},{20,148},{24,152},{28,15... | collective-permute-start | bytes 399368 | tf_op jit(solution)/shard_map/ppermute | solution.py:24
  142.5 4.1 %fusion = f32[8,32,32]{1,2,0:T(8,128)} fusion(f32[8,32,32,64]{3,2,1,0:T(8,128)S(1)} %exponential_select_fusion, f32[8,64,32]{1,2,0:T(8,128)S(1)} %bitcast.230, f32[8,64,32]{1,2,0:T(8,128)S(1)} %bitcast.229), kind=kLoop, calls=%fused_computation.2 | loop fusion | flops 1564672 | bytes 2260992
  149.3 3.0 %fusion.6 = f32[4,32,8,64]{3,1,2,0:T(8,128)S(1)} fusion(f32[4,32,8,64]{3,1,2,0:T(8,128)S(1)} %fusion.7, f32[1,8,64,64]{2,3,1,0:T(8,128)} %get-tuple-element.47, f32[1,8,64,64]{2,3,1,0:T(8,128)} %get-tuple-element.48, f32[1,8,64,64]{2,3,1,0:T(8,128)} %get-tuple-element.49, f32[4]{0:T(128)} %pad.5.clone, f32[4,8,32,64]{3,2,1,0:T(8,128)S(1)} %copy-done.2, ...), kind=kOutput, calls=%fused_computation.20 | convolution fusion | flops 50921472 | bytes 1442320 | tf_op jit(solution)/shard_map/bhtc,bhcv->bhtv/dot_general | solution.py:179
  152.6 1.8 %fusion.87 = (f32[4,32,8]{1,2,0:T(8,128)S(1)}, f32[4,32,8,64]{3,1,2,0:T(8,128)S(1)}) fusion(f32[4,32,8,64]{3,1,2,0:T(8,128)S(1)} %fusion.6, f32[4,8,64]{2,1,0:T(8,128)S(1)} %pad_maximum_fusion.6, f32[4,32]{1,0:T(4,128)S(1)} %copy-done.26, f32[4,8,32,64]{3,2,1,0:T(8,128)S(1)} %copy-done.2, f32[4,32,8,64]{3,2,1,0:T(8,128)S(1)} %reshape.505, ...), kind=kOutput, calls=%fused_computation.195 | convolution fusion | flops 50723840 | bytes 1329664 | tf_op jit(solution)/shard_map/bhtc,hcv->bhtv/dot_general | solution.py:182
  157.4 12.2 %all_to_all.5 = bf16[4,128,512]{2,1,0:T(8,128)(2,1)S(1)} all-to-all(bf16[4,128,512]{2,1,0:T(8,128)(2,1)S(1)} %bitcast.223), channel_id=1, replica_groups=mesh['seq_hi'=8,'seq_lo'=8,'tp'=4] {'tp'}, dimensions={0} | all-to-all | bytes 1048576 | tf_op jit(solution)/shard_map/all_to_all | solution.py:194
  (172 shorter events, 46.1 us)
Async XLA Ops:
  0.0 155.8 %copy-start = (bf16[512,2048]{1,0:T(8,128)(2,1)S(1)}, bf16[512,2048]{1,0:T(8,128)(2,1)}, u32[]{:S(2)}) copy-start(bf16[512,2048]{1,0:T(8,128)(2,1)} %param.25) | copy-start | bytes 6291460
  0.0 22.4 %copy-start.16 = (f32[5,2048]{1,0:T(8,128)S(1)}, f32[5,2048]{1,0:T(8,128)}, u32[]{:S(2)}) copy-start(f32[5,2048]{1,0:T(8,128)} %param.17) | copy-start | bytes 122884
  16.1 20.6 %collective-permute-start = (bf16[1,2048]{1,0:T(2,128)(2,1)S(1)}, bf16[1,2048]{1,0:T(2,128)(2,1)S(1)}, u32[]{:S(2)}, u32[]{:S(2)}) collective-permute-start(bf16[1,2048]{1,0:T(2,128)(2,1)S(1)} %get-tuple-element.78), channel_id=1, source_target_pairs={{0,4},{4,8},{8,12},{12,16},{16,20},{20,24},{24,28},{28,32},{32,36}... | collective-permute-start | bytes 12296 | tf_op jit(solution)/shard_map/ppermute | solution.py:24
  24.3 12.9 %copy-start.17 = (bf16[64,512]{1,0:T(8,128)(2,1)S(1)}, bf16[64,512]{1,0:T(8,128)(2,1)}, u32[]{:S(2)}) copy-start(bf16[64,512]{1,0:T(8,128)(2,1)} %param.20) | copy-start | bytes 196612
  50.2 11.8 %copy-start.18 = (f32[8,64]{1,0:T(8,128)}, f32[8,64]{1,0:T(8,128)S(1)}, u32[]{:S(2)}) copy-start(f32[8,64]{1,0:T(8,128)S(1)} %get-tuple-element.87) | copy-start | bytes 6148
  50.2 11.8 %copy-start.19 = (f32[8,64]{1,0:T(8,128)}, f32[8,64]{1,0:T(8,128)S(1)}, u32[]{:S(2)}) copy-start(f32[8,64]{1,0:T(8,128)S(1)} %get-tuple-element.88) | copy-start | bytes 6148
  50.2 11.8 %copy-start.20 = (f32[8,64]{1,0:T(8,128)}, f32[8,64]{1,0:T(8,128)S(1)}, u32[]{:S(2)}) copy-start(f32[8,64]{1,0:T(8,128)S(1)} %get-tuple-element.89) | copy-start | bytes 6148
  55.7 10.7 %copy-start.23 = (f32[1,8,64]{2,1,0:T(8,128)S(1)}, f32[1,8,64]{2,1,0:T(8,128)}, u32[]{:S(2)}) copy-start(f32[1,8,64]{2,1,0:T(8,128)} %get-tuple-element.45) | copy-start | bytes 6148
  55.7 10.7 %copy-start.24 = (f32[1,8,64]{2,1,0:T(8,128)S(1)}, f32[1,8,64]{2,1,0:T(8,128)}, u32[]{:S(2)}) copy-start(f32[1,8,64]{2,1,0:T(8,128)} %get-tuple-element.90) | copy-start | bytes 6148
  55.7 10.7 %copy-start.25 = (f32[1,8,1,64]{3,2,1,0:T(1,128)S(1)}, f32[1,8,1,64]{3,2,1,0:T(1,128)}, u32[]{:S(2)}) copy-start(f32[1,8,1,64]{3,2,1,0:T(1,128)} %get-tuple-element.54) | copy-start | bytes 6148
  55.7 10.7 %copy-start.31 = (f32[4]{0:T(128)S(1)}, f32[4]{0:T(128)}, u32[]{:S(2)}) copy-start(f32[4]{0:T(128)} %pad.1.clone) | copy-start | bytes 52
  56.0 23.4 %copy-start.22 = (f32[8,64]{1,0:T(8,128)S(1)}, f32[8,64]{1,0:T(8,128)}, u32[]{:S(2)}) copy-start(f32[8,64]{1,0:T(8,128)} %mul.406) | copy-start | bytes 6148
  56.0 8.5 %collective-permute-start.1 = (f32[8,65,64]{1,2,0:T(8,128)S(1)}, f32[8,65,64]{1,2,0:T(8,128)S(1)}, u32[]{:S(2)}, u32[]{:S(2)}) collective-permute-start(f32[8,65,64]{1,2,0:T(8,128)S(1)} %pad_maximum_fusion), channel_id=1, source_target_pairs={{0,4},{4,8},{8,12},{12,16},{16,20},{20,24},{24,28},{28,32},{32,36}... | collective-permute-start | bytes 399368 | tf_op jit(solution)/shard_map/ppermute | solution.py:24
  62.8 24.7 %copy-start.21 = (pred[32,32]{1,0:T(8,128)(4,1)S(1)}, pred[32,32]{1,0:T(8,128)(4,1)}, u32[]{:S(2)}) copy-start(pred[32,32]{1,0:T(8,128)(4,1)} %get-tuple-element.116) | copy-start | bytes 3076
  64.5 7.7 %collective-permute-start.2 = (f32[8,65,64]{1,2,0:T(8,128)S(1)}, f32[8,65,64]{1,2,0:T(8,128)S(1)}, u32[]{:S(2)}, u32[]{:S(2)}) collective-permute-start(f32[8,65,64]{1,2,0:T(8,128)S(1)} %collective-permute-done.1), channel_id=1, source_target_pairs={{0,4},{4,8},{8,12},{12,16},{16,20},{20,24},{24,28},{28,32},{32,36}... | collective-permute-start | bytes 399368 | tf_op jit(solution)/shard_map/ppermute | solution.py:24
  72.8 10.9 %collective-permute-start.3 = (f32[8,65,64]{1,2,0:T(8,128)S(1)}, f32[8,65,64]{1,2,0:T(8,128)S(1)}, u32[]{:S(2)}, u32[]{:S(2)}) collective-permute-start(f32[8,65,64]{1,2,0:T(8,128)S(1)} %pad_maximum_fusion.1), channel_id=1, source_target_pairs={{0,8},{4,12},{8,16},{12,20},{16,24},{20,28},{24,32},{28,36},{32,40... | collective-permute-start | bytes 399368 | tf_op jit(solution)/shard_map/ppermute | solution.py:24
  84.0 16.2 %collective-permute-start.4 = (f32[8,65,64]{1,2,0:T(8,128)S(1)}, f32[8,65,64]{1,2,0:T(8,128)S(1)}, u32[]{:S(2)}, u32[]{:S(2)}) collective-permute-start(f32[8,65,64]{1,2,0:T(8,128)S(1)} %pad_maximum_fusion.2), channel_id=1, source_target_pairs={{0,16},{4,20},{8,24},{12,28},{16,32},{20,36},{24,40},{28,44},{32,4... | collective-permute-start | bytes 399368 | tf_op jit(solution)/shard_map/ppermute | solution.py:24
  100.7 10.1 %collective-permute-start.5 = (f32[8,65,64]{1,2,0:T(8,128)S(1)}, f32[8,65,64]{1,2,0:T(8,128)S(1)}, u32[]{:S(2)}, u32[]{:S(2)}) collective-permute-start(f32[8,65,64]{1,2,0:T(8,128)S(1)} %pad_maximum_fusion.3), channel_id=1, source_target_pairs={{0,32},{4,36},{8,40},{12,44},{16,48},{20,52},{24,56},{28,60},{32,6... | collective-permute-start | bytes 399368 | tf_op jit(solution)/shard_map/ppermute | solution.py:24
  109.5 17.5 %copy-start.11 = (f32[8,32,64]{2,1,0:T(8,128)S(1)}, f32[8,32,64]{2,1,0:T(8,128)}, u32[]{:S(2)}) copy-start(f32[8,32,64]{2,1,0:T(8,128)} %get-tuple-element.37) | copy-start | bytes 196612
  109.5 17.5 %copy-start.12 = (f32[8,32,64]{2,1,0:T(8,128)S(1)}, f32[8,32,64]{2,1,0:T(8,128)}, u32[]{:S(2)}) copy-start(f32[8,32,64]{2,1,0:T(8,128)} %get-tuple-element.38) | copy-start | bytes 196612
  111.3 21.4 %collective-permute-start.6 = (f32[8,65,64]{1,2,0:T(8,128)S(1)}, f32[8,65,64]{1,2,0:T(8,128)S(1)}, u32[]{:S(2)}, u32[]{:S(2)}) collective-permute-start(f32[8,65,64]{1,2,0:T(8,128)S(1)} %pad_maximum_fusion.4), channel_id=1, source_target_pairs={{0,64},{4,68},{8,72},{12,76},{16,80},{20,84},{24,88},{28,92},{32,9... | collective-permute-start | bytes 399368 | tf_op jit(solution)/shard_map/ppermute | solution.py:24
  132.8 9.8 %copy-start.10 = (f32[8,32,64]{2,1,0:T(8,128)S(1)}, f32[8,32,64]{2,1,0:T(8,128)}, u32[]{:S(2)}) copy-start(f32[8,32,64]{2,1,0:T(8,128)} %get-tuple-element.43) | copy-start | bytes 196612
  133.3 19.3 %collective-permute-start.7 = (f32[8,65,64]{1,2,0:T(8,128)S(1)}, f32[8,65,64]{1,2,0:T(8,128)}, u32[]{:S(2)}, u32[]{:S(2)}) collective-permute-start(f32[8,65,64]{1,2,0:T(8,128)S(1)} %pad_maximum_fusion.5), channel_id=1, source_target_pairs={{0,128},{4,132},{8,136},{12,140},{16,144},{20,148},{24,152},{28,15... | collective-permute-start | bytes 399368 | tf_op jit(solution)/shard_map/ppermute | solution.py:24
  155.4 14.2 %copy-start.15 = (bf16[128,512]{1,0:T(8,128)(2,1)S(1)}, bf16[128,512]{1,0:T(8,128)(2,1)}, u32[]{:S(2)}) copy-start(bf16[128,512]{1,0:T(8,128)(2,1)} %param.13) | copy-start | bytes 393220
  (17 other events, 106.4 us)

commit v17 on v16

--- a/solution.py
+++ b/solution.py
@@ -157,7 +157,7 @@
         weight = jnp.where(pair_ok[None, :, :, None], jnp.exp(gap), 0.0)
         return jnp.einsum("htc,hsc,htsc->hts", recept_b, key_b, weight, precision=highest)
 
-    scores = []
+    scores = [block_scores(0, incl[0], excl[0], gating_rows_tile[0], query_array_tile[0])]
     prefix = from_behind(packed, SEQ, 1)
     distance = 1
     while distance < devices:

time: 171 us -> 176 us (1.029)
  the two profiles are of different devices: /device:TPU:96 before, /device:TPU:48 now
where the time goes in v17:
time: 176 us; the launch traced here: 175 us
  other arithmetic  46.9 us (27%)
  waiting for transfers between devices  28.2 us (16%)
  starting transfers between devices  27.7 us (16%)
  blocking collectives  26.1 us (15%)
  matrix products  21.7 us (12%)
  local copies, waits for them, and re-layouts  21.2 us (12%)
  between operations  3.31 us (2%)
    ppermute x8, waiting for transfers between devices, from_behind(): return lax.ppermute(block, axis, route)  28.2 us
    ppermute x8, starting transfers between devices, from_behind(): return lax.ppermute(block, axis, route)  27.7 us
    unnamed x4, other arithmetic  15.7 us
    all_gather x1, blocking collectives, body(): full = lax.all_gather(tier_source_concatenated, 'tp', axis=1, tiled=True)  13.5 us
    all_to_all x1, blocking collectives, body(): pieces = lax.all_to_all(pieces, 'tp', 0, 0, tiled=True)  12.6 us
    dot_general x2, matrix products, project(): jnp.einsum('itd,ide->ite', mixed[:4], mapping_matrices_pile, preferred_el...  10.3 us
    dot_general x4, local copies, waits for them, and re-layouts, block_scores(): jnp.einsum('htc,hsc,htsc->hts', recept_b, key_b, weight, precision=highest)  5.72 us
    select_n x4, other arithmetic, block_scores(): weight = jnp.where(pair_ok[None, :, :, None], jnp.exp(gap), 0.0)  5.01 us
  transfers between devices with their start and end apart: 8, of which 5 were waited for; matrix products, arithmetic and copies ran while one was open for 30% of the time, Pallas kernels for 0%

profile of v17, /device:TPU:48, one launch (start us, length us, event | category | flops | bytes accessed | tf_op | source)
XLA Modules:
  0.0 175.2 jit_solution(18399363739691396631)
XLA Ops:
  0.0 13.5 %all_gather.3 = bf16[128,2048]{1,0:T(8,128)(2,1)S(1)} all-gather(bf16[128,512]{1,0:T(8,128)(2,1)} %param.13), channel_id=1, replica_groups=mesh['seq_hi'=8,'seq_lo'=8,'tp'=4] {'tp'}, dimensions={1}, use_global_device_ids=true | all-gather | bytes 655360 | tf_op jit(solution)/shard_map/all_gather | solution.py:54
  13.9 2.1 %fusion.85 = (f32[128,2048]{1,0:T(8,128)}, bf16[128,2048]{1,0:T(8,128)(2,1)S(1)}) fusion(f32[2048]{0:T(1024)} %param.16, f32[2048]{0:T(1024)} %param.15, f32[128]{0:T(128)S(1)} %add_rsqrt_fusion.1, f32[128]{0:T(128)S(1)} %broadcast_multiply_fusion.1, bf16[128,2048]{1,0:T(8,128)(2,1)S(1)} %all_gather.3), kind=kLoop, calls=%fused_computation.193 | loop fusion | flops 1835008 | bytes 2114560 | tf_op jit(solution)/shard_map/convert_element_type | solution.py:63
  16.1 1.9 %collective-permute-start = (bf16[1,2048]{1,0:T(2,128)(2,1)S(1)}, bf16[1,2048]{1,0:T(2,128)(2,1)S(1)}, u32[]{:S(2)}, u32[]{:S(2)}) collective-permute-start(bf16[1,2048]{1,0:T(2,128)(2,1)S(1)} %get-tuple-element.68), channel_id=1, source_target_pairs={{0,4},{4,8},{8,12},{12,16},{16,20},{20,24},{24,28},{28,32},{32,36}... | collective-permute-start | bytes 12296 | tf_op jit(solution)/shard_map/ppermute | solution.py:24
  24.4 5.7 %fusion.82 = f32[4,128,512]{2,1,0:T(8,128)} fusion(bf16[4,2048,512]{2,1,0:T(8,128)(2,1)} %param.18, f32[5,2048]{1,0:T(8,128)S(1)} %copy-done.14, f32[128,2048]{1,0:T(8,128)S(1)} %convert_subtract_fusion.1, f32[128,2048]{1,0:T(8,128)S(1)} %copy-done.2), kind=kOutput, calls=%fused_computation.190 | convolution fusion | flops 1077673984 | bytes 11575296 | tf_op jit(solution)/shard_map/itd,ide->ite/dot_general | solution.py:69
  40.8 4.6 %fusion.60 = f32[4,1,512]{2,1,0:T(1,128)S(1)} fusion(bf16[4,2048,512]{2,1,0:T(8,128)(2,1)} %param.18, bf16[4,2048,1]{1,0,2:T(4,128)(2,1)S(1)} %slice_bitcast_fusion.20), kind=kOutput, calls=%fused_computation.138 | convolution fusion | flops 8388608 | bytes 8413184 | tf_op jit(solution)/shard_map/itd,ide->ite/dot_general | solution.py:69
  53.5 1.9 %multiply_bitcast_fusion = (f32[1,8,64]{2,1,0:T(8,128)}, f32[1,8,1,64]{3,1,2,0:T(8,128)S(1)}, f32[1,8,64]{2,1,0:T(8,128)}) fusion(f32[]{:T(128)S(6)} %mul.381, f32[1,8,1,64]{3,1,2,0:T(8,128)} %bitcast.256, f32[1,8,1,64]{3,1,2,0:T(8,128)} %bitcast.255, f32[]{:T(128)} %bitcast.38), kind=kLoop, calls=%fused_computation.170 | loop fusion | flops 1536 | bytes 10248 | tf_op jit(solution)/shard_map/mul | solution.py:136
  62.5 4.1 %collective-permute-start.1 = (f32[8,65,64]{1,2,0:T(8,128)}, f32[8,65,64]{1,2,0:T(8,128)}, u32[]{:S(2)}, u32[]{:S(2)}) collective-permute-start(f32[8,65,64]{1,2,0:T(8,128)} %pad_maximum_fusion), channel_id=1, source_target_pairs={{0,4},{4,8},{8,12},{12,16},{16,20},{20,24},{24,28},{28,32},{32,36}... | collective-permute-start | bytes 399368 | tf_op jit(solution)/shard_map/ppermute | solution.py:24
  69.2 4.1 %fusion.3 = f32[8,32,32]{1,2,0:T(8,128)} fusion(f32[8,32,32,64]{3,2,1,0:T(8,128)S(1)} %exponential_select_fusion.3, f32[8,64,32]{1,2,0:T(8,128)S(1)} %get-tuple-element.109, f32[8,64,32]{1,2,0:T(8,128)S(1)} %get-tuple-element.110), kind=kLoop, calls=%fused_computation.8 | loop fusion | flops 1564672 | bytes 2260992
  74.9 2.1 %slice_bitcast_fusion.4 = (f32[8,32,64]{2,1,0:T(8,128)}, f32[8,32,64]{2,1,0:T(8,128)}, f32[8,32,64]{2,1,0:T(8,128)S(1)}, f32[8,32,64]{2,1,0:T(8,128)S(1)}, f32[8,32,64]{2,1,0:T(8,128)}, /*index=5*/f32[8,32,64]{2,1,0:T(8,128)}) fusion(f32[4,8,32,64]{3,2,1,0:T(8,128)} %get-tuple-element.71, f32[4,8,32,64]{3,2,1,0:T(8,128)} %get-tuple-element.73), kind=kLoop, calls=%fused_computation.115 | loop fusion | bytes 786432 | tf_op jit(solution)/shard_map/squeeze | solution.py:168
  77.0 1.9 %collective-permute-start.2 = (f32[8,65,64]{1,2,0:T(8,128)}, f32[8,65,64]{1,2,0:T(8,128)S(1)}, u32[]{:S(2)}, u32[]{:S(2)}) collective-permute-start(f32[8,65,64]{1,2,0:T(8,128)} %collective-permute-done.1), channel_id=1, source_target_pairs={{0,4},{4,8},{8,12},{12,16},{16,20},{20,24},{24,28},{28,32},{32,36}... | collective-permute-start | bytes 399368 | tf_op jit(solution)/shard_map/ppermute | solution.py:24
  79.6 5.2 %collective-permute-done.2 = f32[8,65,64]{1,2,0:T(8,128)S(1)} collective-permute-done((f32[8,65,64]{1,2,0:T(8,128)}, f32[8,65,64]{1,2,0:T(8,128)S(1)}, u32[]{:S(2)}, u32[]{:S(2)}) %collective-permute-start.2) | collective-permute-done | bytes 133152 | tf_op jit(solution)/shard_map/ppermute | solution.py:24
  87.3 3.8 %collective-permute-start.3 = (f32[8,65,64]{1,2,0:T(8,128)S(1)}, f32[8,65,64]{1,2,0:T(8,128)S(1)}, u32[]{:S(2)}, u32[]{:S(2)}) collective-permute-start(f32[8,65,64]{1,2,0:T(8,128)S(1)} %pad_maximum_fusion.1), channel_id=1, source_target_pairs={{0,8},{4,12},{8,16},{12,20},{16,24},{20,28},{24,32},{28,36},{32,40... | collective-permute-start | bytes 399368 | tf_op jit(solution)/shard_map/ppermute | solution.py:24
  92.7 5.1 %collective-permute-done.3 = f32[8,65,64]{1,2,0:T(8,128)S(1)} collective-permute-done((f32[8,65,64]{1,2,0:T(8,128)S(1)}, f32[8,65,64]{1,2,0:T(8,128)S(1)}, u32[]{:S(2)}, u32[]{:S(2)}) %collective-permute-start.3) | collective-permute-done | bytes 133152 | tf_op jit(solution)/shard_map/ppermute | solution.py:24
  98.1 4.8 %collective-permute-start.4 = (f32[8,65,64]{1,2,0:T(8,128)S(1)}, f32[8,65,64]{1,2,0:T(8,128)S(1)}, u32[]{:S(2)}, u32[]{:S(2)}) collective-permute-start(f32[8,65,64]{1,2,0:T(8,128)S(1)} %pad_maximum_fusion.2), channel_id=1, source_target_pairs={{0,16},{4,20},{8,24},{12,28},{16,32},{20,36},{24,40},{28,44},{32,4... | collective-permute-start | bytes 399368 | tf_op jit(solution)/shard_map/ppermute | solution.py:24
  103.7 4.1 %fusion.2 = f32[8,32,32]{1,2,0:T(8,128)} fusion(f32[8,32,32,64]{3,2,1,0:T(8,128)S(1)} %exponential_select_fusion.2, f32[8,64,32]{1,2,0:T(8,128)S(1)} %bitcast.242, f32[8,64,32]{1,2,0:T(8,128)S(1)} %bitcast.241), kind=kLoop, calls=%fused_computation.6 | loop fusion | flops 1564672 | bytes 2260992
  109.5 5.5 %collective-permute-done.4 = f32[8,65,64]{1,2,0:T(8,128)S(1)} collective-permute-done((f32[8,65,64]{1,2,0:T(8,128)S(1)}, f32[8,65,64]{1,2,0:T(8,128)S(1)}, u32[]{:S(2)}, u32[]{:S(2)}) %collective-permute-start.4) | collective-permute-done | bytes 133152 | tf_op jit(solution)/shard_map/ppermute | solution.py:24
  115.5 2.1 %collective-permute-start.5 = (f32[8,65,64]{1,2,0:T(8,128)S(1)}, f32[8,65,64]{1,2,0:T(8,128)S(1)}, u32[]{:S(2)}, u32[]{:S(2)}) collective-permute-start(f32[8,65,64]{1,2,0:T(8,128)S(1)} %pad_maximum_fusion.3), channel_id=1, source_target_pairs={{0,32},{4,36},{8,40},{12,44},{16,48},{20,52},{24,56},{28,60},{32,6... | collective-permute-start | bytes 399368 | tf_op jit(solution)/shard_map/ppermute | solution.py:24
  119.4 4.1 %fusion.1 = f32[8,32,32]{1,2,0:T(8,128)} fusion(f32[8,32,32,64]{3,2,1,0:T(8,128)S(1)} %exponential_select_fusion.1, f32[8,64,32]{1,2,0:T(8,128)S(1)} %bitcast.240, f32[8,64,32]{1,2,0:T(8,128)S(1)} %bitcast.239), kind=kLoop, calls=%fused_computation.4 | loop fusion | flops 1564672 | bytes 2260992
  125.1 5.3 %collective-permute-done.5 = f32[8,65,64]{1,2,0:T(8,128)S(1)} collective-permute-done((f32[8,65,64]{1,2,0:T(8,128)S(1)}, f32[8,65,64]{1,2,0:T(8,128)S(1)}, u32[]{:S(2)}, u32[]{:S(2)}) %collective-permute-start.5) | collective-permute-done | bytes 133152 | tf_op jit(solution)/shard_map/ppermute | solution.py:24
  130.9 7.4 %collective-permute-start.6 = (f32[8,65,64]{1,2,0:T(8,128)S(1)}, f32[8,65,64]{1,2,0:T(8,128)S(1)}, u32[]{:S(2)}, u32[]{:S(2)}) collective-permute-start(f32[8,65,64]{1,2,0:T(8,128)S(1)} %pad_maximum_fusion.4), channel_id=1, source_target_pairs={{0,64},{4,68},{8,72},{12,76},{16,80},{20,84},{24,88},{28,92},{32,9... | collective-permute-start | bytes 399368 | tf_op jit(solution)/shard_map/ppermute | solution.py:24
  140.1 3.4 %fusion = f32[8,32,32]{1,2,0:T(8,128)S(1)} fusion(f32[8,32,32,64]{3,2,1,0:T(8,128)S(1)} %exponential_select_fusion, f32[8,64,32]{1,2,0:T(8,128)S(1)} %bitcast.238, f32[8,64,32]{1,2,0:T(8,128)S(1)} %bitcast.237), kind=kLoop, calls=%fused_computation.2 | loop fusion | flops 1564672 | bytes 2260992
  148.3 2.5 %fusion.6 = f32[4,32,8,64]{3,1,2,0:T(8,128)S(1)} fusion(f32[4,32,8,64]{3,1,2,0:T(8,128)S(1)} %fusion.7, f32[1,8,64,64]{2,3,1,0:T(8,128)S(1)} %copy-done.4, f32[1,8,64,64]{2,3,1,0:T(8,128)S(1)} %copy-done.5, f32[1,8,64,64]{2,3,1,0:T(8,128)S(1)} %copy-done.6, f32[4]{0:T(128)} %pad.7.clone, f32[4,8,32,64]{3,2,1,0:T(8,128)S(1)} %get-tuple-element.92, ...), kind=kOutput, calls=%fused_computation.20 | convolution fusion | flops 50987008 | bytes 1311248 | tf_op jit(solution)/shard_map/bhtc,bhcv->bhtv/dot_general | solution.py:179
  150.8 7.2 %collective-permute-done.7 = f32[8,65,64]{1,2,0:T(8,128)S(1)} collective-permute-done((f32[8,65,64]{1,2,0:T(8,128)S(1)}, f32[8,65,64]{1,2,0:T(8,128)S(1)}, u32[]{:S(2)}, u32[]{:S(2)}) %collective-permute-start.7) | collective-permute-done | bytes 133152 | tf_op jit(solution)/shard_map/ppermute | solution.py:24
  161.8 12.6 %all_to_all.5 = bf16[4,128,512]{2,1,0:T(8,128)(2,1)S(1)} all-to-all(bf16[4,128,512]{2,1,0:T(8,128)(2,1)S(1)} %bitcast.233), channel_id=1, replica_groups=mesh['seq_hi'=8,'seq_lo'=8,'tp'=4] {'tp'}, dimensions={0} | all-to-all | bytes 1048576 | tf_op jit(solution)/shard_map/all_to_all | solution.py:194
  (154 shorter events, 56.8 us)
Async XLA Ops:
  0.0 160.3 %copy-start = (bf16[512,2048]{1,0:T(8,128)(2,1)S(1)}, bf16[512,2048]{1,0:T(8,128)(2,1)}, u32[]{:S(2)}) copy-start(bf16[512,2048]{1,0:T(8,128)(2,1)} %param.25) | copy-start | bytes 6291460
  0.0 22.5 %copy-start.14 = (f32[5,2048]{1,0:T(8,128)S(1)}, f32[5,2048]{1,0:T(8,128)}, u32[]{:S(2)}) copy-start(f32[5,2048]{1,0:T(8,128)} %param.17) | copy-start | bytes 122884
  16.1 20.8 %collective-permute-start = (bf16[1,2048]{1,0:T(2,128)(2,1)S(1)}, bf16[1,2048]{1,0:T(2,128)(2,1)S(1)}, u32[]{:S(2)}, u32[]{:S(2)}) collective-permute-start(bf16[1,2048]{1,0:T(2,128)(2,1)S(1)} %get-tuple-element.68), channel_id=1, source_target_pairs={{0,4},{4,8},{8,12},{12,16},{16,20},{20,24},{24,28},{28,32},{32,36}... | collective-permute-start | bytes 12296 | tf_op jit(solution)/shard_map/ppermute | solution.py:24
  24.3 13.0 %copy-start.15 = (bf16[64,512]{1,0:T(8,128)(2,1)S(1)}, bf16[64,512]{1,0:T(8,128)(2,1)}, u32[]{:S(2)}) copy-start(bf16[64,512]{1,0:T(8,128)(2,1)} %param.20) | copy-start | bytes 196612
  58.8 9.6 %copy-start.17 = (pred[32,32]{1,0:T(8,128)(4,1)S(1)}, pred[32,32]{1,0:T(8,128)(4,1)}, u32[]{:S(2)}) copy-start(pred[32,32]{1,0:T(8,128)(4,1)} %get-tuple-element.108) | copy-start | bytes 3076
  62.5 14.5 %collective-permute-start.1 = (f32[8,65,64]{1,2,0:T(8,128)}, f32[8,65,64]{1,2,0:T(8,128)}, u32[]{:S(2)}, u32[]{:S(2)}) collective-permute-start(f32[8,65,64]{1,2,0:T(8,128)} %pad_maximum_fusion), channel_id=1, source_target_pairs={{0,4},{4,8},{8,12},{12,16},{16,20},{20,24},{24,28},{28,32},{32,36}... | collective-permute-start | bytes 399368 | tf_op jit(solution)/shard_map/ppermute | solution.py:24
  69.1 22.0 %copy-start.1 = (bf16[4,32,8,64]{3,2,1,0:T(8,128)(2,1)S(1)}, bf16[4,32,8,64]{3,2,1,0:T(8,128)(2,1)}, u32[]{:S(2)}) copy-start(bf16[4,32,8,64]{3,2,1,0:T(8,128)(2,1)} %convert_element_type.111) | copy-start | bytes 393220
  74.9 28.0 %copy-start.9 = (f32[8,32,64]{2,1,0:T(8,128)S(1)}, f32[8,32,64]{2,1,0:T(8,128)}, u32[]{:S(2)}) copy-start(f32[8,32,64]{2,1,0:T(8,128)} %get-tuple-element.21) | copy-start | bytes 196612
  74.9 28.0 %copy-start.10 = (f32[8,32,64]{2,1,0:T(8,128)S(1)}, f32[8,32,64]{2,1,0:T(8,128)}, u32[]{:S(2)}) copy-start(f32[8,32,64]{2,1,0:T(8,128)} %get-tuple-element.20) | copy-start | bytes 196612
  74.9 28.0 %copy-start.16 = (pred[32,32]{1,0:T(8,128)(4,1)S(1)}, pred[32,32]{1,0:T(8,128)(4,1)}, u32[]{:S(2)}) copy-start(pred[32,32]{1,0:T(8,128)(4,1)} %get-tuple-element.107) | copy-start | bytes 3076
  77.0 7.9 %collective-permute-start.2 = (f32[8,65,64]{1,2,0:T(8,128)}, f32[8,65,64]{1,2,0:T(8,128)S(1)}, u32[]{:S(2)}, u32[]{:S(2)}) collective-permute-start(f32[8,65,64]{1,2,0:T(8,128)} %collective-permute-done.1), channel_id=1, source_target_pairs={{0,4},{4,8},{8,12},{12,16},{16,20},{20,24},{24,28},{28,32},{32,36}... | collective-permute-start | bytes 399368 | tf_op jit(solution)/shard_map/ppermute | solution.py:24
  87.3 10.4 %collective-permute-start.3 = (f32[8,65,64]{1,2,0:T(8,128)S(1)}, f32[8,65,64]{1,2,0:T(8,128)S(1)}, u32[]{:S(2)}, u32[]{:S(2)}) collective-permute-start(f32[8,65,64]{1,2,0:T(8,128)S(1)} %pad_maximum_fusion.1), channel_id=1, source_target_pairs={{0,8},{4,12},{8,16},{12,20},{16,24},{20,28},{24,32},{28,36},{32,40... | collective-permute-start | bytes 399368 | tf_op jit(solution)/shard_map/ppermute | solution.py:24
  98.1 16.9 %collective-permute-start.4 = (f32[8,65,64]{1,2,0:T(8,128)S(1)}, f32[8,65,64]{1,2,0:T(8,128)S(1)}, u32[]{:S(2)}, u32[]{:S(2)}) collective-permute-start(f32[8,65,64]{1,2,0:T(8,128)S(1)} %pad_maximum_fusion.2), channel_id=1, source_target_pairs={{0,16},{4,20},{8,24},{12,28},{16,32},{20,36},{24,40},{28,44},{32,4... | collective-permute-start | bytes 399368 | tf_op jit(solution)/shard_map/ppermute | solution.py:24
  109.5 9.9 %copy-start.11 = (f32[8,32,64]{2,1,0:T(8,128)S(1)}, f32[8,32,64]{2,1,0:T(8,128)}, u32[]{:S(2)}) copy-start(f32[8,32,64]{2,1,0:T(8,128)} %get-tuple-element.27) | copy-start | bytes 196612
  109.5 9.9 %copy-start.12 = (f32[8,32,64]{2,1,0:T(8,128)S(1)}, f32[8,32,64]{2,1,0:T(8,128)}, u32[]{:S(2)}) copy-start(f32[8,32,64]{2,1,0:T(8,128)} %get-tuple-element.28) | copy-start | bytes 196612
  115.5 14.9 %collective-permute-start.5 = (f32[8,65,64]{1,2,0:T(8,128)S(1)}, f32[8,65,64]{1,2,0:T(8,128)S(1)}, u32[]{:S(2)}, u32[]{:S(2)}) collective-permute-start(f32[8,65,64]{1,2,0:T(8,128)S(1)} %pad_maximum_fusion.3), channel_id=1, source_target_pairs={{0,32},{4,36},{8,40},{12,44},{16,48},{20,52},{24,56},{28,60},{32,6... | collective-permute-start | bytes 399368 | tf_op jit(solution)/shard_map/ppermute | solution.py:24
  125.1 14.9 %copy-start.7 = (f32[8,32,64]{2,1,0:T(8,128)S(1)}, f32[8,32,64]{2,1,0:T(8,128)}, u32[]{:S(2)}) copy-start(f32[8,32,64]{2,1,0:T(8,128)} %get-tuple-element.32) | copy-start | bytes 196612
  125.1 14.9 %copy-start.8 = (f32[8,32,64]{2,1,0:T(8,128)S(1)}, f32[8,32,64]{2,1,0:T(8,128)}, u32[]{:S(2)}) copy-start(f32[8,32,64]{2,1,0:T(8,128)} %get-tuple-element.33) | copy-start | bytes 196612
  130.9 15.2 %collective-permute-start.6 = (f32[8,65,64]{1,2,0:T(8,128)S(1)}, f32[8,65,64]{1,2,0:T(8,128)S(1)}, u32[]{:S(2)}, u32[]{:S(2)}) collective-permute-start(f32[8,65,64]{1,2,0:T(8,128)S(1)} %pad_maximum_fusion.4), channel_id=1, source_target_pairs={{0,64},{4,68},{8,72},{12,76},{16,80},{20,84},{24,88},{28,92},{32,9... | collective-permute-start | bytes 399368 | tf_op jit(solution)/shard_map/ppermute | solution.py:24
  144.3 13.8 %copy-start.18 = (f32[4,32]{1,0:T(4,128)S(1)}, f32[4,32]{1,0:T(4,128)}, u32[]{:S(2)}) copy-start(f32[4,32]{1,0:T(4,128)} %get-tuple-element.94) | copy-start | bytes 1540
  146.7 11.3 %collective-permute-start.7 = (f32[8,65,64]{1,2,0:T(8,128)S(1)}, f32[8,65,64]{1,2,0:T(8,128)S(1)}, u32[]{:S(2)}, u32[]{:S(2)}) collective-permute-start(f32[8,65,64]{1,2,0:T(8,128)S(1)} %pad_maximum_fusion.5), channel_id=1, source_target_pairs={{0,128},{4,132},{8,136},{12,140},{16,144},{20,148},{24,152},{28,15... | collective-permute-start | bytes 399368 | tf_op jit(solution)/shard_map/ppermute | solution.py:24
  148.3 12.0 %copy-start.19 = (f32[512]{0:T(512)S(1)}, f32[512]{0:T(512)}, u32[]{:S(2)}) copy-start(f32[512]{0:T(512)} %param.24) | copy-start | bytes 6148
  148.3 12.0 %copy-start.20 = (f32[512]{0:T(512)S(1)}, f32[512]{0:T(512)}, u32[]{:S(2)}) copy-start(f32[512]{0:T(512)} %param.23) | copy-start | bytes 6148
  159.8 14.7 %copy-start.13 = (bf16[128,512]{1,0:T(8,128)(2,1)S(1)}, bf16[128,512]{1,0:T(8,128)(2,1)}, u32[]{:S(2)}) copy-start(bf16[128,512]{1,0:T(8,128)(2,1)} %param.13) | copy-start | bytes 393220
  (8 other events, 46.6 us)
